TPU v7x, 32 devices: a whole 2x2x4 slice. The times are simulated.
32 devices in a mesh: group: 2 (over y), ctx: 8 (over z, x), head: 2 (over core).
Axes of the slice: x: 2, y: 2, z: 4, core: 2. Of those that a mesh axis runs over, the one named last changes fastest.
Arguments:
- queries: bfloat16 [4096, 4096], P(('group', 'ctx'), 'head'), parts along dimension 0, may hold values from -7 to 7
- keys: bfloat16 [4096, 1024], P(('group', 'ctx'), 'head'), parts along dimension 0, may hold values from -4 to 4
- values: bfloat16 [4096, 1024], P(('group', 'ctx'), 'head'), parts along dimension 0, may hold values from -24 to 24
- doc_of_block: int32 [32], P('group'), parts along dimension 0, may hold values from 0 to 4, never falling along the last dimension, each value on 1 to 8 neighbouring positions
- out_weight: bfloat16 [4096, 4096], P('ctx', 'head'), may hold values from -0.09375 to 0.09375
Outputs:
- mixed: bfloat16 [4096, 4096], P(('group', 'ctx'), 'head'), parts along dimension 0
There are 2 independent parts, one for each index of `group`. A program takes and returns all parts, laid end to end along the dimension named above; an argument that names none is the same for every part. Nothing has to cross between parts.
Inputs may be any that keep to these rules, and one draw needn't show every extreme that they name: `doc_of_block`: blocks of one document are consecutive, and a document covers at most 8 blocks.
All inputs are finite; a program needn't handle non-finite values.
Results may differ from a plain program's by a relative error of at most 0.006.
Values may be sent and summed in bfloat16 or wider, within the bound.
No kernel may reach another device: no remote copies, remote signals or barrier semaphores. Data moves between devices by JAX's collectives and lax.ppermute only.
A program may use at most 64 MiB of HBM per device.

v0:
```python
import math

import jax
import jax.numpy as jnp
from jax import lax
from jax.sharding import PartitionSpec as P

HEAD_SIZE = 128
BLOCK_TOKENS = 128


def passed_along(array, axis, by):
    peers = lax.axis_size(axis)
    pairs = [(i, i + by) for i in range(peers) if 0 <= i + by < peers]
    return lax.ppermute(array, axis, pairs)


def lookup_docs(positions, doc_of_block):
    block_ids = jnp.floor_divide(positions, BLOCK_TOKENS)
    table_ids = jnp.arange(doc_of_block.shape[0], dtype=jnp.int32)
    matches = block_ids[:, None] == table_ids[None, :]
    return jnp.max(jnp.where(matches, doc_of_block[None, :], -1), axis=1)


def update(state_now, query_head_rows, key_piece, value_piece, visible):
    running_max, summed, totals = state_now
    rows_here = key_piece.shape[0]
    kv_heads = query_head_rows.shape[1]
    key_head_rows = key_piece.reshape(rows_here, kv_heads, HEAD_SIZE)
    value_head_rows = value_piece.reshape(rows_here, kv_heads, HEAD_SIZE)
    score_scale = 1.0 / math.sqrt(HEAD_SIZE)
    scores = (
        jnp.einsum(
            "qhgd,khd->hgqk", query_head_rows, key_head_rows, preferred_element_type=jnp.float32
        )
        * score_scale
    )
    scores = jnp.where(visible, scores, -1e30)
    new_max = jnp.maximum(running_max, jnp.max(scores, axis=-1))
    weights = jnp.where(visible, jnp.exp(scores - new_max[..., None]), 0.0)
    rescale = jnp.exp(running_max - new_max)
    products = jnp.einsum(
        "hgqk,khd->hgqd",
        weights.astype(jnp.bfloat16),
        value_head_rows,
        preferred_element_type=jnp.float32,
    )
    summed = summed * rescale[..., None] + products
    totals = totals * rescale + jnp.sum(weights, axis=-1)
    return (new_max, summed, totals)


def fresh_state(kv_heads, group_width, rows_here):
    return (
        jnp.full((kv_heads, group_width, rows_here), -1e30, jnp.float32),
        jnp.zeros((kv_heads, group_width, rows_here, HEAD_SIZE), jnp.float32),
        jnp.zeros((kv_heads, group_width, rows_here), jnp.float32),
    )


def finish(state_now, rows_here, q_heads):
    running_max, summed, totals = state_now
    attended = summed / totals[..., None]
    return (
        jnp.transpose(attended, (2, 0, 1, 3))
        .reshape(rows_here, q_heads * HEAD_SIZE)
        .astype(jnp.bfloat16)
    )


def per_device(queries, keys, values, doc_of_block, out_weight):
    tok_rows = queries.shape[0]
    kv_heads = keys.shape[1] // HEAD_SIZE
    q_heads = queries.shape[1] // HEAD_SIZE
    group_width = q_heads // kv_heads
    ctx_count = lax.axis_size("ctx")
    reach_devs = min(8, ctx_count // 2)
    ctx_index = lax.axis_index("ctx")
    query_start = ctx_index * tok_rows
    query_pos = query_start + jnp.arange(tok_rows, dtype=jnp.int32)
    query_doc = lookup_docs(query_pos, doc_of_block)
    query_head_rows = queries.reshape(tok_rows, kv_heads, group_width, HEAD_SIZE)

    def attend(state_now, key_piece, value_piece, key_start):
        key_pos = key_start + jnp.arange(key_piece.shape[0], dtype=jnp.int32)
        key_doc = lookup_docs(key_pos, doc_of_block)
        visible = (key_doc[None, :] == query_doc[:, None]) & (
            key_pos[None, :] <= query_pos[:, None]
        )
        return update(state_now, query_head_rows, key_piece, value_piece, visible)

    initial_state = fresh_state(kv_heads, group_width, tok_rows)
    state_now = attend(initial_state, keys, values, query_start)
    for distance in range(1, reach_devs + 1):
        prior_keys, prior_values = passed_along((keys, values), "ctx", distance)
        state_now = attend(state_now, prior_keys, prior_values, query_start - distance * tok_rows)
    attended = finish(state_now, tok_rows, q_heads)
    features = lax.all_gather(attended, "head", axis=1, tiled=True)
    mixed = jnp.dot(
        features,
        lax.all_gather(out_weight, "ctx", axis=0, tiled=True),
        preferred_element_type=jnp.float32,
    )
    return mixed.astype(jnp.bfloat16)


def solution(mesh):
    return jax.shard_map(
        per_device,
        mesh=mesh,
        in_specs=(
            P(("group", "ctx"), "head"),
            P(("group", "ctx"), "head"),
            P(("group", "ctx"), "head"),
            P("group"),
            P("ctx", "head"),
        ),
        out_specs=P(("group", "ctx"), "head"),
        check_vma=False,
    )
```

profile of v0, /device:TPU:0, one launch (start us, length us, event | category | flops | bytes accessed | tf_op | source)
XLA Modules:
  0.0 352.3 jit_solution(2587613839477615480)
XLA Ops:
  6.5 1.1 copy.50
  7.6 6.0 %collective-permute-start.6 = (bf16[256,512]{0,1:T(8,128)(2,1)S(1)}, bf16[256,512]{0,1:T(8,128)(2,1)S(1)}, u32[]{:S(2)}, u32[]{:S(2)}) collective-permute-start(bf16[256,512]{0,1:T(8,128)(2,1)S(1)} %copy.50), channel_id=1, source_target_pairs={{0,8},{2,10},{4,12},{6,14},{1,9},{3,11},{5,13},{7,15},{16,24},{18,... | collective-permute-start | bytes 786440 | tf_op jit(solution)/shard_map/ppermute | solution.py:15
  13.6 4.4 %collective-permute-start.4 = (bf16[256,512]{0,1:T(8,128)(2,1)S(1)}, bf16[256,512]{0,1:T(8,128)(2,1)S(1)}, u32[]{:S(2)}, u32[]{:S(2)}) collective-permute-start(bf16[256,512]{0,1:T(8,128)(2,1)S(1)} %copy.50), channel_id=1, source_target_pairs={{0,6},{2,8},{4,10},{6,12},{8,14},{1,7},{3,9},{5,11},{7,13},{9,15},... | collective-permute-start | bytes 786440 | tf_op jit(solution)/shard_map/ppermute | solution.py:15
  18.0 1.3 collective-permute-start.2
  19.4 3.1 collective-permute-start
  22.5 2.7 collective-permute-start.1
  25.2 1.0 reshape.264
  26.2 0.0 copy-start.4
  26.2 1.9 copy.87
  28.2 1.8 reshape.265
  30.0 0.8 select_reduce_fusion
  30.7 0.5 compare_and_fusion.4
  31.3 1.0 fusion
  32.3 0.0 collective-permute-done.6
  32.3 2.6 collective-permute-start.3
  34.9 2.9 fusion.4
  37.8 0.0 collective-permute-done.4
  37.8 2.6 collective-permute-start.5
  40.4 3.0 fusion.3
  43.4 0.0 collective-permute-done.2
  43.4 4.1 %collective-permute-start.7 = (bf16[256,512]{1,0:T(8,128)(2,1)S(1)}, bf16[256,512]{1,0:T(8,128)(2,1)S(1)}, u32[]{:S(2)}, u32[]{:S(2)}) collective-permute-start(bf16[256,512]{1,0:T(8,128)(2,1)S(1)} %copy-done.4), channel_id=1, source_target_pairs={{0,8},{2,10},{4,12},{6,14},{1,9},{3,11},{5,13},{7,15},{16,24},{18,... | collective-permute-start | bytes 786440 | tf_op jit(solution)/shard_map/ppermute | solution.py:15
  47.5 3.0 fusion.2
  50.5 0.0 collective-permute-done
  50.5 1.0 fusion.1
  51.6 1.0 fusion.5
  52.6 2.5 fusion.23
  55.2 1.0 fusion.7
  56.2 0.0 collective-permute-done.1
  56.2 0.1 copy.53
  56.4 4.9 %fusion.21 = f32[4,4,256,128]{2,3,1,0:T(8,128)} fusion(bf16[256,4,128,1]{0,2,3,1:T(8,128)(2,1)S(1)} %bitcast.249, f32[4,256,256,4]{2,1,3,0:T(8,128)} %copy-done.3, f32[4,4,256]{2,1,0:T(4,128)S(1)} %get-tuple-element.17, pred[256,256]{0,1:T(8,128)(4,1)S(1)} %get-tuple-element.22), kind=kOutput, calls=%fused_computation.29 | convolution fusion | flops 273678336 | bytes 6635520 | tf_op jit(solution)/shard_map/hgqk,khd->hgqd/dot_general | solution.py:42
  61.2 1.0 fusion.9
  62.3 0.0 collective-permute-done.3
  62.3 1.1 copy.58
  63.4 4.9 %fusion.19 = f32[4,4,256,128]{2,3,1,0:T(8,128)} fusion(bf16[256,4,128,1]{0,2,3,1:T(8,128)(2,1)S(1)} %bitcast.250, f32[4,256,256,4]{2,1,3,0:T(8,128)} %get-tuple-element.31, f32[4,4,256]{2,1,0:T(4,128)S(1)} %get-tuple-element.16, pred[256,256]{0,1:T(8,128)(4,1)S(1)} %get-tuple-element.24), kind=kOutput, calls=%fused_computation.28 | convolution fusion | flops 273678336 | bytes 6635520 | tf_op jit(solution)/shard_map/hgqk,khd->hgqd/dot_general | solution.py:42
  68.3 1.0 fusion.11
  69.3 0.0 collective-permute-done.5
  69.3 0.1 copy.63
  69.5 4.9 %fusion.17 = f32[4,4,256,128]{2,3,1,0:T(8,128)} fusion(bf16[256,4,128,1]{0,2,3,1:T(8,128)(2,1)S(1)} %bitcast.251, f32[4,256,256,4]{2,1,3,0:T(8,128)} %get-tuple-element.29, f32[4,4,256]{2,1,0:T(4,128)S(1)} %get-tuple-element.15, pred[256,256]{0,1:T(8,128)(4,1)S(1)} %get-tuple-element.23), kind=kOutput, calls=%fused_computation.27 | convolution fusion | flops 273678336 | bytes 6635520 | tf_op jit(solution)/shard_map/hgqk,khd->hgqd/dot_general | solution.py:42
  74.4 1.0 fusion.13
  75.5 0.0 collective-permute-done.7
  75.5 0.4 copy.68
  75.8 7.4 %fusion.26 = bf16[256,4,4,128]{0,3,2,1:T(8,128)(2,1)} fusion(f32[4,4,256,128]{2,3,1,0:T(8,128)} %fusion.17, f32[4,4,256,128]{2,3,1,0:T(8,128)} %fusion.19, f32[4,4,256,128]{2,3,1,0:T(8,128)} %fusion.21, f32[4,4,256,128]{2,3,1,0:T(8,128)} %fusion.23, f32[256,4,4]{0,2,1:T(4,128)S(1)} %get-tuple-element.10, f32[256,4,4]{0,2,1:T(4,128)S(1)} %get-tuple-element.13, ...), kind=kOutput, calls=%fused_computation.33 | convolution fusion | flops 279445504 | bytes 14073856 | tf_op jit(solution)/shard_map/hgqk,khd->hgqd/dot_general | solution.py:42
  83.2 0.0 all-gather.3.cloned.1.call-update
  83.2 0.0 all-gather.5.cloned.1.call-start
  83.3 0.7 all-gather.5.cloned.1.call-update
  84.0 19.0 %all-gather.3.cloned.1.call-done = bf16[256,4096]{0,1:T(8,128)(2,1)} async-done(((bf16[256,2048]{0,1:T(8,128)(2,1)}), bf16[256,4096]{0,1:T(8,128)(2,1)}) %all-gather.3.cloned.1.call-update) | async-done | bytes 2097168 | tf_op jit(solution)/shard_map/all_gather | solution.py:98
  103.0 230.6 %all-gather.5.cloned.1.call-done = bf16[4096,2048]{1,0:T(8,128)(2,1)} async-done(((bf16[512,2048]{1,0:T(8,128)(2,1)}), bf16[4096,2048]{1,0:T(8,128)(2,1)}) %all-gather.5.cloned.1.call-update) | async-done | bytes 16777232 | tf_op jit(solution)/shard_map/all_gather | solution.py:101
  333.6 11.9 %convolution_convert_fusion = bf16[256,2048]{1,0:T(8,128)(2,1)} fusion(bf16[256,4096]{0,1:T(8,128)(2,1)} %all-gather.3.cloned.1.call-done, bf16[4096,2048]{1,0:T(8,128)(2,1)} %all-gather.5.cloned.1.call-done), kind=kOutput, calls=%fused_computation.25 | convolution fusion | flops 4295491584 | bytes 19922944 | tf_op jit(solution)/shard_map/dot_general | solution.py:99
  (19 shorter events, 0.1 us)
Async XLA Ops:
  6.5 96.4 %all-gather.3.cloned.1.call-start = ((), (), s32[]{:S(2)}) async-start(), calls=%async_computation | async-start | bytes 3145728 | tf_op jit(solution)/shard_map/all_gather | solution.py:98
  7.6 24.6 %collective-permute-start.6 = (bf16[256,512]{0,1:T(8,128)(2,1)S(1)}, bf16[256,512]{0,1:T(8,128)(2,1)S(1)}, u32[]{:S(2)}, u32[]{:S(2)}) collective-permute-start(bf16[256,512]{0,1:T(8,128)(2,1)S(1)} %copy.50), channel_id=1, source_target_pairs={{0,8},{2,10},{4,12},{6,14},{1,9},{3,11},{5,13},{7,15},{16,24},{18,... | collective-permute-start | bytes 786440 | tf_op jit(solution)/shard_map/ppermute | solution.py:15
  13.6 24.2 %collective-permute-start.4 = (bf16[256,512]{0,1:T(8,128)(2,1)S(1)}, bf16[256,512]{0,1:T(8,128)(2,1)S(1)}, u32[]{:S(2)}, u32[]{:S(2)}) collective-permute-start(bf16[256,512]{0,1:T(8,128)(2,1)S(1)} %copy.50), channel_id=1, source_target_pairs={{0,6},{2,8},{4,10},{6,12},{8,14},{1,7},{3,9},{5,11},{7,13},{9,15},... | collective-permute-start | bytes 786440 | tf_op jit(solution)/shard_map/ppermute | solution.py:15
  18.0 25.4 %collective-permute-start.2 = (bf16[256,512]{0,1:T(8,128)(2,1)S(1)}, bf16[256,512]{0,1:T(8,128)(2,1)S(1)}, u32[]{:S(2)}, u32[]{:S(2)}) collective-permute-start(bf16[256,512]{0,1:T(8,128)(2,1)S(1)} %copy.50), channel_id=1, source_target_pairs={{0,4},{2,6},{4,8},{6,10},{8,12},{10,14},{1,5},{3,7},{5,9},{7,11},{... | collective-permute-start | bytes 786440 | tf_op jit(solution)/shard_map/ppermute | solution.py:15
  19.4 31.1 %collective-permute-start = (bf16[256,512]{0,1:T(8,128)(2,1)S(1)}, bf16[256,512]{0,1:T(8,128)(2,1)S(1)}, u32[]{:S(2)}, u32[]{:S(2)}) collective-permute-start(bf16[256,512]{0,1:T(8,128)(2,1)S(1)} %copy.50), channel_id=1, source_target_pairs={{0,2},{2,4},{4,6},{6,8},{8,10},{10,12},{12,14},{1,3},{3,5},{5,7},{... | collective-permute-start | bytes 786440 | tf_op jit(solution)/shard_map/ppermute | solution.py:15
  22.5 33.7 %collective-permute-start.1 = (bf16[256,512]{1,0:T(8,128)(2,1)}, bf16[256,512]{1,0:T(8,128)(2,1)S(1)}, u32[]{:S(2)}, u32[]{:S(2)}) collective-permute-start(bf16[256,512]{1,0:T(8,128)(2,1)} %param.7), channel_id=1, source_target_pairs={{0,2},{2,4},{4,6},{6,8},{8,10},{10,12},{12,14},{1,3},{3,5},{5,7},{... | collective-permute-start | bytes 786440 | tf_op jit(solution)/shard_map/ppermute | solution.py:15
  26.2 6.1 %copy-start.4 = (bf16[256,512]{1,0:T(8,128)(2,1)S(1)}, bf16[256,512]{1,0:T(8,128)(2,1)}, u32[]{:S(2)}) copy-start(bf16[256,512]{1,0:T(8,128)(2,1)} %param.7) | copy-start | bytes 786436
  32.3 30.0 %collective-permute-start.3 = (bf16[256,512]{1,0:T(8,128)(2,1)S(1)}, bf16[256,512]{1,0:T(8,128)(2,1)}, u32[]{:S(2)}, u32[]{:S(2)}) collective-permute-start(bf16[256,512]{1,0:T(8,128)(2,1)S(1)} %copy-done.4), channel_id=1, source_target_pairs={{0,4},{2,6},{4,8},{6,10},{8,12},{10,14},{1,5},{3,7},{5,9},{7,11},{... | collective-permute-start | bytes 786440 | tf_op jit(solution)/shard_map/ppermute | solution.py:15
  37.8 31.5 %collective-permute-start.5 = (bf16[256,512]{1,0:T(8,128)(2,1)S(1)}, bf16[256,512]{1,0:T(8,128)(2,1)S(1)}, u32[]{:S(2)}, u32[]{:S(2)}) collective-permute-start(bf16[256,512]{1,0:T(8,128)(2,1)S(1)} %copy-done.4), channel_id=1, source_target_pairs={{0,6},{2,8},{4,10},{6,12},{8,14},{1,7},{3,9},{5,11},{7,13},{9,15},... | collective-permute-start | bytes 786440 | tf_op jit(solution)/shard_map/ppermute | solution.py:15
  43.4 32.0 %collective-permute-start.7 = (bf16[256,512]{1,0:T(8,128)(2,1)S(1)}, bf16[256,512]{1,0:T(8,128)(2,1)S(1)}, u32[]{:S(2)}, u32[]{:S(2)}) collective-permute-start(bf16[256,512]{1,0:T(8,128)(2,1)S(1)} %copy-done.4), channel_id=1, source_target_pairs={{0,8},{2,10},{4,12},{6,14},{1,9},{3,11},{5,13},{7,15},{16,24},{18,... | collective-permute-start | bytes 786440 | tf_op jit(solution)/shard_map/ppermute | solution.py:15
  50.5 2.1 copy-start.5
  51.5 3.6 %copy-start.3 = (f32[4,256,256,4]{2,1,3,0:T(8,128)}, f32[4,256,256,4]{2,1,3,0:T(8,128)S(1)}, u32[]{:S(2)}) copy-start(f32[4,256,256,4]{2,1,3,0:T(8,128)S(1)} %get-tuple-element.33) | copy-start | bytes 12582916
  56.4 4.9 %copy-start.2 = (f32[4,256,256,4]{2,1,3,0:T(8,128)S(1)}, f32[4,256,256,4]{2,1,3,0:T(8,128)}, u32[]{:S(2)}) copy-start(f32[4,256,256,4]{2,1,3,0:T(8,128)} %get-tuple-element.31) | copy-start | bytes 12582916
  63.4 4.9 %copy-start.1 = (f32[4,256,256,4]{2,1,3,0:T(8,128)S(1)}, f32[4,256,256,4]{2,1,3,0:T(8,128)}, u32[]{:S(2)}) copy-start(f32[4,256,256,4]{2,1,3,0:T(8,128)} %get-tuple-element.29) | copy-start | bytes 12582916
  69.5 4.9 %copy-start = (f32[4,256,256,4]{2,1,3,0:T(8,128)S(1)}, f32[4,256,256,4]{2,1,3,0:T(8,128)}, u32[]{:S(2)}) copy-start(f32[4,256,256,4]{2,1,3,0:T(8,128)} %get-tuple-element.27) | copy-start | bytes 12582916
  83.2 250.4 %all-gather.5.cloned.1.call-start = ((), (), s32[]{:S(2)}) async-start(), calls=%async_computation.1 | async-start | bytes 18874368 | tf_op jit(solution)/shard_map/all_gather | solution.py:101
Sparse Core Ops, SparseCore 0:
  83.3 19.5 all-gather.2
  105.1 228.4 all-gather.4
where the time goes:
time: 353 us; the launch traced here: 352 us
  waiting for transfers between devices  250 us (71%)
  matrix products  47.2 us (13%)
  starting transfers between devices  26.9 us (8%)
  between operations  13.7 us (4%)
  local copies, waits for them, and re-layouts  7.47 us (2%)
  other arithmetic  6.66 us (2%)
    all_gather x1, waiting for transfers between devices, per_device(): lax.all_gather(out_weight, 'ctx', axis=0, tiled=True)  231 us
    ppermute x8, starting transfers between devices, passed_along(): return lax.ppermute(array, axis, pairs)  26.9 us
    dot_general x5, matrix products, update(): jnp.einsum('hgqk,khd->hgqd', weights.astype(jnp.bfloat16), value_head_row...  24.5 us
    all_gather x1, waiting for transfers between devices, per_device(): features = lax.all_gather(attended, 'head', axis=1, tiled=True)  19 us
    dot_general x1, matrix products, per_device(): jnp.dot(features, lax.all_gather(out_weight, 'ctx', axis=0, tiled=True),...  11.9 us
    dot_general x5, matrix products, update(): jnp.einsum('qhgd,khd->hgqk', query_head_rows, key_head_rows, preferred_el...  10.8 us
  transfers between devices with their start and end apart: 10, of which 2 were waited for; matrix products, arithmetic and copies ran while one was open for 12% of the time, Pallas kernels for 0%

commit v1 on v0

--- a/solution.py
+++ b/solution.py
@@ -95,12 +95,20 @@
         prior_keys, prior_values = passed_along((keys, values), "ctx", distance)
         state_now = attend(state_now, prior_keys, prior_values, query_start - distance * tok_rows)
     attended = finish(state_now, tok_rows, q_heads)
-    features = lax.all_gather(attended, "head", axis=1, tiled=True)
-    mixed = jnp.dot(
-        features,
-        lax.all_gather(out_weight, "ctx", axis=0, tiled=True),
-        preferred_element_type=jnp.float32,
-    )
+    head_count = lax.axis_size("head")
+    head_index = lax.axis_index("head")
+    feature_rows = attended.shape[1]
+    weight_rows = lax.all_gather(out_weight, "ctx", axis=0, tiled=True)
+
+    def project(piece, source):
+        rows = lax.dynamic_slice_in_dim(weight_rows, source * feature_rows, feature_rows, 0)
+        return jnp.dot(piece, rows, preferred_element_type=jnp.float32)
+
+    mixed = project(attended, head_index)
+    for shift in range(1, head_count):
+        pairs = [(i, (i + shift) % head_count) for i in range(head_count)]
+        piece = lax.ppermute(attended, "head", pairs)
+        mixed = mixed + project(piece, (head_index + head_count - shift) % head_count)
     return mixed.astype(jnp.bfloat16)
 
 

time: 353 us -> 315 us (0.89)
  matrix products: 47.2 us -> 26.5 us
  waiting for transfers between devices: 250 us -> 234 us
    all_gather x2 -> x1, waiting for transfers between devices: 250 us -> 203 us  [per_device(): weight_rows = lax.all_gather(out_weight, 'ctx', axis=0, tiled=True)]
    ppermute x8, waiting for transfers between devices: 0.02 us -> 29.6 us  [passed_along(): return lax.ppermute(array, axis, pairs)]
    dot_general x5, matrix products: 24.5 us -> 7.07 us  [update(): jnp.einsum('hgqk,khd->hgqd', weights.astype(jnp.bfloat16), value_head_row...]
    ppermute x4, local copies, waits for them, and re-layouts: 1.7 us -> 6.21 us  [passed_along(): return lax.ppermute(array, axis, pairs)]
    dot_general x5, matrix products: 10.8 us -> 6.95 us  [update(): jnp.einsum('qhgd,khd->hgqk', query_head_rows, key_head_rows, preferred_el...]
    dot_general x1 -> x2, matrix products: 11.9 us -> 12.4 us  [project(): return jnp.dot(piece, rows, preferred_element_type=jnp.float32)]
  transfers between devices with their start and end apart: 10 -> 10, of which waited for: 2 -> 5; matrix products, arithmetic and copies ran while one was open for 12% -> 11% of each run, Pallas kernels for 0% -> 0%
where the time goes in v1:
time: 315 us; the launch traced here: 314 us
  waiting for transfers between devices  234 us (74%)
  matrix products  26.5 us (8%)
  starting transfers between devices  24.2 us (8%)
  between operations  13.7 us (4%)
  local copies, waits for them, and re-layouts  10.3 us (3%)
  other arithmetic  6.05 us (2%)
    all_gather x1, waiting for transfers between devices, per_device(): weight_rows = lax.all_gather(out_weight, 'ctx', axis=0, tiled=True)  203 us
    ppermute x8, waiting for transfers between devices, passed_along(): return lax.ppermute(array, axis, pairs)  29.6 us
    ppermute x8, starting transfers between devices, passed_along(): return lax.ppermute(array, axis, pairs)  24.1 us
    dot_general x2, matrix products, project(): return jnp.dot(piece, rows, preferred_element_type=jnp.float32)  12.4 us
    dot_general x5, matrix products, update(): jnp.einsum('hgqk,khd->hgqd', weights.astype(jnp.bfloat16), value_head_row...  7.07 us
    dot_general x5, matrix products, update(): jnp.einsum('qhgd,khd->hgqk', query_head_rows, key_head_rows, preferred_el...  6.95 us
  transfers between devices with their start and end apart: 10, of which 5 were waited for; matrix products, arithmetic and copies ran while one was open for 11% of the time, Pallas kernels for 0%

profile of v1, /device:TPU:0, one launch (start us, length us, event | category | flops | bytes accessed | tf_op | source)
XLA Modules:
  0.0 314.3 jit_solution(14603484617698803601)
XLA Ops:
  6.5 0.7 all-gather.2.cloned.1.call-update
  7.3 5.6 %collective-permute-start.1 = (bf16[256,512]{1,0:T(8,128)(2,1)}, bf16[256,512]{1,0:T(8,128)(2,1)}, u32[]{:S(2)}, u32[]{:S(2)}) collective-permute-start(bf16[256,512]{1,0:T(8,128)(2,1)} %param.7), channel_id=1, source_target_pairs={{0,2},{2,4},{4,6},{6,8},{8,10},{10,12},{12,14},{1,3},{3,5},{5,7},{... | collective-permute-start | bytes 786440 | tf_op jit(solution)/shard_map/ppermute | solution.py:15
  12.9 3.5 %collective-permute-start.3 = (bf16[256,512]{1,0:T(8,128)(2,1)}, bf16[256,512]{1,0:T(8,128)(2,1)}, u32[]{:S(2)}, u32[]{:S(2)}) collective-permute-start(bf16[256,512]{1,0:T(8,128)(2,1)} %param.7), channel_id=1, source_target_pairs={{0,4},{2,6},{4,8},{6,10},{8,12},{10,14},{1,5},{3,7},{5,9},{7,11},{... | collective-permute-start | bytes 786440 | tf_op jit(solution)/shard_map/ppermute | solution.py:15
  16.3 4.5 %collective-permute-start.5 = (bf16[256,512]{1,0:T(8,128)(2,1)}, bf16[256,512]{1,0:T(8,128)(2,1)}, u32[]{:S(2)}, u32[]{:S(2)}) collective-permute-start(bf16[256,512]{1,0:T(8,128)(2,1)} %param.7), channel_id=1, source_target_pairs={{0,6},{2,8},{4,10},{6,12},{8,14},{1,7},{3,9},{5,11},{7,13},{9,15},... | collective-permute-start | bytes 786440 | tf_op jit(solution)/shard_map/ppermute | solution.py:15
  20.8 1.3 collective-permute-start.7
  22.1 1.1 copy.50
  23.2 1.3 collective-permute-start.6
  24.6 1.0 reshape.264
  25.6 1.1 copy.87
  26.7 0.8 reshape.265
  27.6 0.1 select_reduce_fusion
  27.7 0.5 compare_and_fusion.4
  28.2 2.9 fusion.4
  31.1 0.0 collective-permute-done.1
  31.1 1.6 collective-permute-start.4
  32.7 1.8 copy.53
  34.5 0.0 collective-permute-done.3
  34.5 1.7 collective-permute-start.2
  36.2 1.8 copy.58
  38.0 0.0 collective-permute-done.5
  38.0 4.7 %collective-permute-start = (bf16[256,512]{0,1:T(8,128)(2,1)S(1)}, bf16[256,512]{0,1:T(8,128)(2,1)S(1)}, u32[]{:S(2)}, u32[]{:S(2)}) collective-permute-start(bf16[256,512]{0,1:T(8,128)(2,1)S(1)} %copy.50), channel_id=1, source_target_pairs={{0,2},{2,4},{4,6},{6,8},{8,10},{10,12},{12,14},{1,3},{3,5},{5,7},{... | collective-permute-start | bytes 786440 | tf_op jit(solution)/shard_map/ppermute | solution.py:15
  42.7 1.8 copy.63
  44.5 0.3 collective-permute-done.7
  44.8 0.8 copy.68
  45.6 10.3 %collective-permute-done.6 = bf16[256,512]{0,1:T(8,128)(2,1)S(1)} collective-permute-done((bf16[256,512]{0,1:T(8,128)(2,1)S(1)}, bf16[256,512]{0,1:T(8,128)(2,1)S(1)}, u32[]{:S(2)}, u32[]{:S(2)}) %collective-permute-start.6) | collective-permute-done | bytes 262176 | tf_op jit(solution)/shard_map/ppermute | solution.py:15
  55.9 1.0 fusion.8
  56.9 10.2 %collective-permute-done.4 = bf16[256,512]{0,1:T(8,128)(2,1)S(1)} collective-permute-done((bf16[256,512]{0,1:T(8,128)(2,1)S(1)}, bf16[256,512]{0,1:T(8,128)(2,1)S(1)}, u32[]{:S(2)}, u32[]{:S(2)}) %collective-permute-start.4) | collective-permute-done | bytes 262176 | tf_op jit(solution)/shard_map/ppermute | solution.py:15
  67.1 1.0 fusion.7
  68.2 8.8 %collective-permute-done.2 = bf16[256,512]{0,1:T(8,128)(2,1)S(1)} collective-permute-done((bf16[256,512]{0,1:T(8,128)(2,1)S(1)}, bf16[256,512]{0,1:T(8,128)(2,1)S(1)}, u32[]{:S(2)}, u32[]{:S(2)}) %collective-permute-start.2) | collective-permute-done | bytes 262176 | tf_op jit(solution)/shard_map/ppermute | solution.py:15
  77.0 1.0 fusion.6
  78.0 1.0 fusion.5
  79.0 1.1 fusion.11
  80.1 1.1 fusion.13
  81.2 1.1 fusion.15
  82.2 1.1 fusion.17
  83.3 0.1 copy-done
  83.3 1.0 fusion.9
  84.4 0.1 bitcast_add_fusion.5
  84.5 1.2 fusion.33
  85.7 1.2 fusion.31
  87.0 0.0 copy-start.5
  87.0 1.4 fusion.29
  88.5 1.2 fusion.27
  89.7 1.9 fusion.36
  91.6 0.1 collective-permute-start.8
  91.7 203.2 %all-gather.2.cloned.1.call-done = bf16[4096,2048]{1,0:T(8,128)(2,1)} async-done(((bf16[512,2048]{1,0:T(8,128)(2,1)}), bf16[4096,2048]{1,0:T(8,128)(2,1)}) %all-gather.2.cloned.1.call-update) | async-done | bytes 16777232 | tf_op jit(solution)/shard_map/all_gather | solution.py:101
  295.0 5.7 %fusion.2 = f32[256,2048]{1,0:T(8,128)S(1)} fusion(bf16[256,2048]{0,1:T(8,128)(2,1)S(1)} %bitcast.252, bf16[4096,2048]{1,0:T(8,128)(2,1)} %all-gather.2.cloned.1.call-done, s32[]{:T(128)S(6)} %select_n.119), kind=kOutput, calls=%fused_computation.2 | convolution fusion | flops 2147483648 | bytes 11534340 | tf_op jit(solution)/shard_map/dot_general | solution.py:105
  300.7 6.7 %fusion.22 = bf16[256,2048]{1,0:T(8,128)(2,1)} fusion(f32[256,2048]{1,0:T(8,128)S(1)} %fusion.2, bf16[256,2048]{0,1:T(8,128)(2,1)S(1)} %collective-permute-done.8, bf16[4096,2048]{1,0:T(8,128)(2,1)} %all-gather.2.cloned.1.call-done, s32[]{:T(128)S(6)} %select_n.121), kind=kOutput, calls=%fused_computation.30 | convolution fusion | flops 2148532224 | bytes 12582916 | tf_op jit(solution)/shard_map/dot_general | solution.py:105
  (21 shorter events, 0.1 us)
Async XLA Ops:
  6.5 20.1 %copy-start.1 = (bf16[256,2048]{1,0:T(8,128)(2,1)S(1)}, bf16[256,2048]{1,0:T(8,128)(2,1)}, u32[]{:S(2)}) copy-start(bf16[256,2048]{1,0:T(8,128)(2,1)} %param.5) | copy-start | bytes 3145732
  6.5 21.0 %copy-start.6 = (s32[16]{0:T(128)S(1)}, s32[16]{0:T(128)}, u32[]{:S(2)}) copy-start(s32[16]{0:T(128)} %param.8) | copy-start | bytes 196
  6.5 288.4 %all-gather.2.cloned.1.call-start = ((), (), s32[]{:S(2)}) async-start(), calls=%async_computation | async-start | bytes 18874368 | tf_op jit(solution)/shard_map/all_gather | solution.py:101
  7.3 23.8 %collective-permute-start.1 = (bf16[256,512]{1,0:T(8,128)(2,1)}, bf16[256,512]{1,0:T(8,128)(2,1)}, u32[]{:S(2)}, u32[]{:S(2)}) collective-permute-start(bf16[256,512]{1,0:T(8,128)(2,1)} %param.7), channel_id=1, source_target_pairs={{0,2},{2,4},{4,6},{6,8},{8,10},{10,12},{12,14},{1,3},{3,5},{5,7},{... | collective-permute-start | bytes 786440 | tf_op jit(solution)/shard_map/ppermute | solution.py:15
  12.9 21.6 %collective-permute-start.3 = (bf16[256,512]{1,0:T(8,128)(2,1)}, bf16[256,512]{1,0:T(8,128)(2,1)}, u32[]{:S(2)}, u32[]{:S(2)}) collective-permute-start(bf16[256,512]{1,0:T(8,128)(2,1)} %param.7), channel_id=1, source_target_pairs={{0,4},{2,6},{4,8},{6,10},{8,12},{10,14},{1,5},{3,7},{5,9},{7,11},{... | collective-permute-start | bytes 786440 | tf_op jit(solution)/shard_map/ppermute | solution.py:15
  16.3 21.7 %collective-permute-start.5 = (bf16[256,512]{1,0:T(8,128)(2,1)}, bf16[256,512]{1,0:T(8,128)(2,1)}, u32[]{:S(2)}, u32[]{:S(2)}) collective-permute-start(bf16[256,512]{1,0:T(8,128)(2,1)} %param.7), channel_id=1, source_target_pairs={{0,6},{2,8},{4,10},{6,12},{8,14},{1,7},{3,9},{5,11},{7,13},{9,15},... | collective-permute-start | bytes 786440 | tf_op jit(solution)/shard_map/ppermute | solution.py:15
  20.8 24.0 %collective-permute-start.7 = (bf16[256,512]{1,0:T(8,128)(2,1)}, bf16[256,512]{1,0:T(8,128)(2,1)S(1)}, u32[]{:S(2)}, u32[]{:S(2)}) collective-permute-start(bf16[256,512]{1,0:T(8,128)(2,1)} %param.7), channel_id=1, source_target_pairs={{0,8},{2,10},{4,12},{6,14},{1,9},{3,11},{5,13},{7,15},{16,24},{18,... | collective-permute-start | bytes 786440 | tf_op jit(solution)/shard_map/ppermute | solution.py:15
  23.2 32.7 %collective-permute-start.6 = (bf16[256,512]{0,1:T(8,128)(2,1)S(1)}, bf16[256,512]{0,1:T(8,128)(2,1)S(1)}, u32[]{:S(2)}, u32[]{:S(2)}) collective-permute-start(bf16[256,512]{0,1:T(8,128)(2,1)S(1)} %copy.50), channel_id=1, source_target_pairs={{0,8},{2,10},{4,12},{6,14},{1,9},{3,11},{5,13},{7,15},{16,24},{18,... | collective-permute-start | bytes 786440 | tf_op jit(solution)/shard_map/ppermute | solution.py:15
  31.1 36.1 %collective-permute-start.4 = (bf16[256,512]{0,1:T(8,128)(2,1)S(1)}, bf16[256,512]{0,1:T(8,128)(2,1)S(1)}, u32[]{:S(2)}, u32[]{:S(2)}) collective-permute-start(bf16[256,512]{0,1:T(8,128)(2,1)S(1)} %copy.50), channel_id=1, source_target_pairs={{0,6},{2,8},{4,10},{6,12},{8,14},{1,7},{3,9},{5,11},{7,13},{9,15},... | collective-permute-start | bytes 786440 | tf_op jit(solution)/shard_map/ppermute | solution.py:15
  34.5 42.5 %collective-permute-start.2 = (bf16[256,512]{0,1:T(8,128)(2,1)S(1)}, bf16[256,512]{0,1:T(8,128)(2,1)S(1)}, u32[]{:S(2)}, u32[]{:S(2)}) collective-permute-start(bf16[256,512]{0,1:T(8,128)(2,1)S(1)} %copy.50), channel_id=1, source_target_pairs={{0,4},{2,6},{4,8},{6,10},{8,12},{10,14},{1,5},{3,7},{5,9},{7,11},{... | collective-permute-start | bytes 786440 | tf_op jit(solution)/shard_map/ppermute | solution.py:15
  38.0 40.0 %collective-permute-start = (bf16[256,512]{0,1:T(8,128)(2,1)S(1)}, bf16[256,512]{0,1:T(8,128)(2,1)S(1)}, u32[]{:S(2)}, u32[]{:S(2)}) collective-permute-start(bf16[256,512]{0,1:T(8,128)(2,1)S(1)} %copy.50), channel_id=1, source_target_pairs={{0,2},{2,4},{4,6},{6,8},{8,10},{10,12},{12,14},{1,3},{3,5},{5,7},{... | collective-permute-start | bytes 786440 | tf_op jit(solution)/shard_map/ppermute | solution.py:15
  81.2 2.2 copy-start
  84.4 1.3 copy-start.2
  85.7 1.3 copy-start.3
  87.0 1.5 copy-start.5
  88.4 1.3 copy-start.4
  91.6 209.1 %collective-permute-start.8 = (bf16[256,2048]{0,1:T(8,128)(2,1)S(1)}, bf16[256,2048]{0,1:T(8,128)(2,1)S(1)}, u32[]{:S(2)}, u32[]{:S(2)}) collective-permute-start(bf16[256,2048]{0,1:T(8,128)(2,1)S(1)} %bitcast.251), channel_id=1, source_target_pairs={{0,1},{1,0},{2,3},{3,2},{4,5},{5,4},{6,7},{7,6},{8,9},{9,8},{10,11... | collective-permute-start | bytes 3145736 | tf_op jit(solution)/shard_map/ppermute | solution.py:110
Sparse Core Ops, SparseCore 0:
  9.5 285.4 all-gather.1

commit v2 on v0

--- a/solution.py
+++ b/solution.py
@@ -68,6 +68,53 @@
     )
 
 
+def head_features(attended):
+    head_count = lax.axis_size("head")
+    head_index = lax.axis_index("head")
+    received = [attended]
+    for shift in range(1, head_count):
+        pairs = [(i, (i + shift) % head_count) for i in range(head_count)]
+        received.append(lax.ppermute(attended, "head", pairs))
+    pieces = []
+    for source in range(head_count):
+        shift_of = (head_index + head_count - source) % head_count
+        piece = received[0]
+        for shift in range(1, head_count):
+            piece = jnp.where(shift_of == shift, received[shift], piece)
+        pieces.append(piece)
+    return jnp.concatenate(pieces, axis=1)
+
+
+def ring_project(features, out_weight):
+    count = lax.axis_size("ctx")
+    order = [i for i in range(0, count, 2)] + sorted(range(1, count, 2), reverse=True)
+    position_of = [0] * count
+    for position, index in enumerate(order):
+        position_of[index] = position
+    ctx_index = lax.axis_index("ctx")
+    position = jnp.asarray(position_of, jnp.int32)[ctx_index]
+    order_table = jnp.asarray(order, jnp.int32)
+    rows = out_weight.shape[0]
+
+    def term(block, source):
+        piece = lax.dynamic_slice_in_dim(features, source * rows, rows, 1)
+        return jnp.dot(piece, block, preferred_element_type=jnp.float32)
+
+    mixed = term(out_weight, ctx_index)
+    ahead = [(order[p], order[(p + 1) % count]) for p in range(count)]
+    behind = [(order[p], order[(p - 1) % count]) for p in range(count)]
+    forward = backward = out_weight
+    forward_steps = count // 2
+    backward_steps = count - 1 - forward_steps
+    for step in range(1, forward_steps + 1):
+        forward = lax.ppermute(forward, "ctx", ahead)
+        mixed = mixed + term(forward, order_table[(position + count - step) % count])
+        if step <= backward_steps:
+            backward = lax.ppermute(backward, "ctx", behind)
+            mixed = mixed + term(backward, order_table[(position + step) % count])
+    return mixed
+
+
 def per_device(queries, keys, values, doc_of_block, out_weight):
     tok_rows = queries.shape[0]
     kv_heads = keys.shape[1] // HEAD_SIZE
@@ -95,12 +142,8 @@
         prior_keys, prior_values = passed_along((keys, values), "ctx", distance)
         state_now = attend(state_now, prior_keys, prior_values, query_start - distance * tok_rows)
     attended = finish(state_now, tok_rows, q_heads)
-    features = lax.all_gather(attended, "head", axis=1, tiled=True)
-    mixed = jnp.dot(
-        features,
-        lax.all_gather(out_weight, "ctx", axis=0, tiled=True),
-        preferred_element_type=jnp.float32,
-    )
+    features = head_features(attended)
+    mixed = ring_project(features, out_weight)
     return mixed.astype(jnp.bfloat16)
 
 

time: 353 us -> 238 us (0.67)
  waiting for transfers between devices: 250 us -> 115 us
  starting transfers between devices: 26.9 us -> 45.5 us
  between operations: 13.7 us -> 9.6 us
  local copies, waits for them, and re-layouts: 7.47 us -> 11.1 us
    all_gather x2 -> x0, waiting for transfers between devices: 250 us -> none  [the longest x1 231 us: per_device(): lax.all_gather(out_weight, 'ctx', axis=0, tiled=True)]
    ppermute x0 -> x8, waiting for transfers between devices: none -> 86.2 us  [the longest x4 77.3 us: ring_project(): forward = lax.ppermute(forward, 'ctx', ahead)]
    ppermute x8, waiting for transfers between devices: 0.02 us -> 29 us  [passed_along(): return lax.ppermute(array, axis, pairs)]
    ppermute x0 -> x8, starting transfers between devices: none -> 17.8 us  [the longest x4 17.6 us: ring_project(): forward = lax.ppermute(forward, 'ctx', ahead)]
    dot_general x1 -> x8, matrix products: 11.9 us -> 18.1 us  [term(): return jnp.dot(piece, block, preferred_element_type=jnp.float32)]
    dot_general x5, matrix products: 24.5 us -> 19.1 us  [update(): jnp.einsum('hgqk,khd->hgqd', weights.astype(jnp.bfloat16), value_head_row...]
  transfers between devices with their start and end apart: 10 -> 16, of which waited for: 2 -> 5; matrix products, arithmetic and copies ran while one was open for 12% -> 26% of each run, Pallas kernels for 0% -> 0%
where the time goes in v2:
time: 238 us; the launch traced here: 237 us
  waiting for transfers between devices  115 us (48%)
  matrix products  46.2 us (19%)
  starting transfers between devices  45.5 us (19%)
  local copies, waits for them, and re-layouts  11.1 us (5%)
  between operations  9.6 us (4%)
  other arithmetic  9.19 us (4%)
    ppermute x4, waiting for transfers between devices, ring_project(): forward = lax.ppermute(forward, 'ctx', ahead)  77.3 us
    ppermute x8, waiting for transfers between devices, passed_along(): return lax.ppermute(array, axis, pairs)  29 us
    ppermute x8, starting transfers between devices, passed_along(): return lax.ppermute(array, axis, pairs)  27.6 us
    dot_general x5, matrix products, update(): jnp.einsum('hgqk,khd->hgqd', weights.astype(jnp.bfloat16), value_head_row...  19.1 us
    dot_general x8, matrix products, term(): return jnp.dot(piece, block, preferred_element_type=jnp.float32)  18.1 us
    ppermute x4, starting transfers between devices, ring_project(): forward = lax.ppermute(forward, 'ctx', ahead)  17.6 us
    dot_general x5, matrix products, update(): jnp.einsum('qhgd,khd->hgqk', query_head_rows, key_head_rows, preferred_el...  9.07 us
    ppermute x3, waiting for transfers between devices, ring_project(): backward = lax.ppermute(backward, 'ctx', behind)  8.84 us
  transfers between devices with their start and end apart: 16, of which 5 were waited for; matrix products, arithmetic and copies ran while one was open for 26% of the time, Pallas kernels for 0%

profile of v2, /device:TPU:0, one launch (start us, length us, event | category | flops | bytes accessed | tf_op | source)
XLA Modules:
  0.0 236.8 jit_solution(5006324753632147928)
XLA Ops:
  0.0 1.8 copy.52
  1.8 6.0 %collective-permute-start.6 = (bf16[256,512]{0,1:T(8,128)(2,1)}, bf16[256,512]{0,1:T(8,128)(2,1)S(1)}, u32[]{:S(2)}, u32[]{:S(2)}) collective-permute-start(bf16[256,512]{0,1:T(8,128)(2,1)} %copy.52), channel_id=1, source_target_pairs={{0,8},{2,10},{4,12},{6,14},{1,9},{3,11},{5,13},{7,15},{16,24},{18,... | collective-permute-start | bytes 786440 | tf_op jit(solution)/shard_map/ppermute | solution.py:15
  7.8 4.4 %collective-permute-start.4 = (bf16[256,512]{0,1:T(8,128)(2,1)}, bf16[256,512]{0,1:T(8,128)(2,1)S(1)}, u32[]{:S(2)}, u32[]{:S(2)}) collective-permute-start(bf16[256,512]{0,1:T(8,128)(2,1)} %copy.52), channel_id=1, source_target_pairs={{0,6},{2,8},{4,10},{6,12},{8,14},{1,7},{3,9},{5,11},{7,13},{9,15},... | collective-permute-start | bytes 786440 | tf_op jit(solution)/shard_map/ppermute | solution.py:15
  12.2 2.0 collective-permute-start.2
  14.2 3.8 %collective-permute-start = (bf16[256,512]{0,1:T(8,128)(2,1)}, bf16[256,512]{0,1:T(8,128)(2,1)}, u32[]{:S(2)}, u32[]{:S(2)}) collective-permute-start(bf16[256,512]{0,1:T(8,128)(2,1)} %copy.52), channel_id=1, source_target_pairs={{0,2},{2,4},{4,6},{6,8},{8,10},{10,12},{12,14},{1,3},{3,5},{5,7},{... | collective-permute-start | bytes 786440 | tf_op jit(solution)/shard_map/ppermute | solution.py:15
  18.0 2.0 collective-permute-start.1
  20.1 1.0 reshape.292
  21.1 1.8 copy.89
  23.0 1.8 reshape.293
  26.1 1.0 fusion
  27.0 2.0 collective-permute-start.3
  29.1 2.9 %fusion.4 = (f32[4,4,256]{2,1,0:T(4,128)S(1)}, f32[4,256,256,4]{2,1,3,0:T(8,128)}) fusion(pred[256,256]{0,1:T(8,128)(4,1)S(1)} %get-tuple-element.27, bf16[256,4,128,1]{0,2,3,1:T(8,128)(2,1)S(1)} %bitcast.266, bf16[256,4,4,128]{3,2,1,0:T(4,128)(2,1)S(1)} %reshape.293), kind=kOutput, calls=%fused_computation.30 | convolution fusion | flops 271577088 | bytes 5586944 | tf_op jit(solution)/shard_map/qhgd,khd->hgqk/dot_general | solution.py:33
  32.0 3.6 %collective-permute-start.5 = (bf16[256,512]{1,0:T(8,128)(2,1)}, bf16[256,512]{1,0:T(8,128)(2,1)}, u32[]{:S(2)}, u32[]{:S(2)}) collective-permute-start(bf16[256,512]{1,0:T(8,128)(2,1)} %param.9), channel_id=1, source_target_pairs={{0,6},{2,8},{4,10},{6,12},{8,14},{1,7},{3,9},{5,11},{7,13},{9,15},... | collective-permute-start | bytes 786440 | tf_op jit(solution)/shard_map/ppermute | solution.py:15
  35.6 1.0 fusion.3
  36.7 3.2 %collective-permute-start.9 = (bf16[512,2048]{1,0:T(8,128)(2,1)}, bf16[512,2048]{1,0:T(8,128)(2,1)S(1)}, u32[]{:S(2)}, u32[]{:S(2)}) collective-permute-start(bf16[512,2048]{1,0:T(8,128)(2,1)} %param.11), channel_id=1, source_target_pairs={{0,4},{4,8},{8,12},{12,14},{14,10},{10,6},{6,2},{2,0},{1,5},{5,9},... | collective-permute-start | bytes 6291464 | tf_op jit(solution)/shard_map/ppermute | solution.py:110
  39.8 2.0 fusion.2
  41.9 2.2 fusion.1
  44.2 1.0 fusion.11
  45.2 1.0 fusion.7
  46.3 1.0 fusion.5
  47.3 2.6 %fusion.27 = f32[4,4,256,128]{2,3,1,0:T(8,128)} fusion(bf16[256,4,128,1]{0,2,3,1:T(8,128)(2,1)S(1)} %bitcast.267, f32[4,256,256,4]{2,1,3,0:T(8,128)S(1)} %get-tuple-element.44, f32[4,4,256]{2,1,0:T(4,128)S(1)} %get-tuple-element.22, pred[256,256]{0,1:T(8,128)(4,1)S(1)} %get-tuple-element.23), kind=kOutput, calls=%fused_computation.53 | convolution fusion | flops 273678336 | bytes 6635520 | tf_op jit(solution)/shard_map/hgqk,khd->hgqd/dot_general | solution.py:42
  49.8 35.9 %collective-permute-done.9 = bf16[512,2048]{1,0:T(8,128)(2,1)S(1)} collective-permute-done((bf16[512,2048]{1,0:T(8,128)(2,1)}, bf16[512,2048]{1,0:T(8,128)(2,1)S(1)}, u32[]{:S(2)}, u32[]{:S(2)}) %collective-permute-start.9) | collective-permute-done | bytes 2097184 | tf_op jit(solution)/shard_map/ppermute | solution.py:110
  85.8 2.8 %collective-permute-start.11 = (bf16[512,2048]{1,0:T(8,128)(2,1)S(1)}, bf16[512,2048]{1,0:T(8,128)(2,1)}, u32[]{:S(2)}, u32[]{:S(2)}) collective-permute-start(bf16[512,2048]{1,0:T(8,128)(2,1)S(1)} %collective-permute-done.9), channel_id=1, source_target_pairs={{0,4},{4,8},{8,12},{12,14},{14,10},{10,6},{6,2},{2,0},{1,5},{5,9},... | collective-permute-start | bytes 6291464 | tf_op jit(solution)/shard_map/ppermute | solution.py:110
  88.6 1.6 fusion.9
  90.2 3.7 %collective-permute-start.7 = (bf16[256,512]{1,0:T(8,128)(2,1)}, bf16[256,512]{1,0:T(8,128)(2,1)S(1)}, u32[]{:S(2)}, u32[]{:S(2)}) collective-permute-start(bf16[256,512]{1,0:T(8,128)(2,1)} %param.9), channel_id=1, source_target_pairs={{0,8},{2,10},{4,12},{6,14},{1,9},{3,11},{5,13},{7,15},{16,24},{18,... | collective-permute-start | bytes 786440 | tf_op jit(solution)/shard_map/ppermute | solution.py:15
  94.0 1.1 copy.55
  95.1 1.1 copy.60
  96.2 1.1 copy.65
  97.3 4.9 %fusion.25 = f32[4,4,256,128]{2,3,1,0:T(8,128)} fusion(bf16[256,4,128,1]{0,2,3,1:T(8,128)(2,1)S(1)} %bitcast.269, f32[4,256,256,4]{2,1,3,0:T(8,128)} %copy-done.5, f32[4,4,256]{2,1,0:T(4,128)} %copy-done.12, pred[256,256]{0,1:T(8,128)(4,1)S(1)} %get-tuple-element.24), kind=kOutput, calls=%fused_computation.52 | convolution fusion | flops 273678336 | bytes 6635520 | tf_op jit(solution)/shard_map/hgqk,khd->hgqd/dot_general | solution.py:42
  102.1 2.6 %fusion.23 = f32[4,4,256,128]{2,3,1,0:T(8,128)} fusion(bf16[256,4,128,1]{0,2,3,1:T(8,128)(2,1)S(1)} %bitcast.270, f32[4,256,256,4]{2,1,3,0:T(8,128)S(1)} %copy-done.4, f32[4,4,256]{2,1,0:T(4,128)S(1)} %copy-done.11, pred[256,256]{0,1:T(8,128)(4,1)S(1)} %get-tuple-element.26), kind=kOutput, calls=%fused_computation.51 | convolution fusion | flops 273678336 | bytes 6635520 | tf_op jit(solution)/shard_map/hgqk,khd->hgqd/dot_general | solution.py:42
  104.8 2.6 %fusion.21 = f32[4,4,256,128]{2,3,1,0:T(8,128)} fusion(bf16[256,4,128,1]{0,2,3,1:T(8,128)(2,1)S(1)} %bitcast.271, f32[4,256,256,4]{2,1,3,0:T(8,128)S(1)} %copy-done.2, f32[4,4,256]{2,1,0:T(4,128)S(1)} %copy-done.9, pred[256,256]{0,1:T(8,128)(4,1)S(1)} %get-tuple-element.25), kind=kOutput, calls=%fused_computation.50 | convolution fusion | flops 273678336 | bytes 6635520 | tf_op jit(solution)/shard_map/hgqk,khd->hgqd/dot_general | solution.py:42
  107.3 1.0 fusion.13
  109.1 29.0 %collective-permute-done.7 = bf16[256,512]{1,0:T(8,128)(2,1)S(1)} collective-permute-done((bf16[256,512]{1,0:T(8,128)(2,1)}, bf16[256,512]{1,0:T(8,128)(2,1)S(1)}, u32[]{:S(2)}, u32[]{:S(2)}) %collective-permute-start.7) | collective-permute-done | bytes 262176 | tf_op jit(solution)/shard_map/ppermute | solution.py:15
  138.3 9.2 %collective-permute-start.13 = (bf16[512,2048]{1,0:T(8,128)(2,1)}, bf16[512,2048]{1,0:T(8,128)(2,1)}, u32[]{:S(2)}, u32[]{:S(2)}) collective-permute-start(bf16[512,2048]{1,0:T(8,128)(2,1)} %collective-permute-done.11), channel_id=1, source_target_pairs={{0,4},{4,8},{8,12},{12,14},{14,10},{10,6},{6,2},{2,0},{1,5},{5,9},... | collective-permute-start | bytes 6291464 | tf_op jit(solution)/shard_map/ppermute | solution.py:110
  147.5 6.5 %fusion.30 = bf16[256,4,4,128]{0,3,2,1:T(8,128)(2,1)S(1)} fusion(f32[4,4,256,128]{2,3,1,0:T(8,128)} %fusion.21, f32[4,4,256,128]{2,3,1,0:T(8,128)} %fusion.23, f32[4,4,256,128]{2,3,1,0:T(8,128)} %fusion.25, f32[4,4,256,128]{2,3,1,0:T(8,128)} %fusion.27, f32[256,4,4]{0,2,1:T(4,128)} %get-tuple-element.10, f32[256,4,4]{0,2,1:T(4,128)} %get-tuple-element.13, ...), kind=kOutput, calls=%fused_computation.56 | convolution fusion | flops 279445504 | bytes 14073856 | tf_op jit(solution)/shard_map/hgqk,khd->hgqd/dot_general | solution.py:42
  164.6 1.4 broadcast_select_fusion
  166.0 1.1 fusion.82
  167.1 23.4 %collective-permute-done.13 = bf16[512,2048]{1,0:T(8,128)(2,1)} collective-permute-done((bf16[512,2048]{1,0:T(8,128)(2,1)}, bf16[512,2048]{1,0:T(8,128)(2,1)}, u32[]{:S(2)}, u32[]{:S(2)}) %collective-permute-start.13) | collective-permute-done | bytes 2097184 | tf_op jit(solution)/shard_map/ppermute | solution.py:110
  190.5 2.5 %collective-permute-start.15 = (bf16[512,2048]{1,0:T(8,128)(2,1)}, bf16[512,2048]{1,0:T(8,128)(2,1)S(1)}, u32[]{:S(2)}, u32[]{:S(2)}) collective-permute-start(bf16[512,2048]{1,0:T(8,128)(2,1)} %collective-permute-done.13), channel_id=1, source_target_pairs={{0,4},{4,8},{8,12},{12,14},{14,10},{10,6},{6,2},{2,0},{1,5},{5,9},... | collective-permute-start | bytes 6291464 | tf_op jit(solution)/shard_map/ppermute | solution.py:110
  193.0 2.7 %fusion.84 = f32[256,2048]{1,0:T(8,128)S(1)} fusion(bf16[512,2048]{1,0:T(8,128)(2,1)} %collective-permute-done.10, s32[]{:T(128)S(6)} %select_n.220, bf16[256,2048]{0,1:T(8,128)(2,1)S(1)} %get-tuple-element.19, bf16[256,2048]{0,1:T(8,128)(2,1)S(1)} %get-tuple-element.18), kind=kOutput, calls=%fused_computation.111 | convolution fusion | flops 537395200 | bytes 6291460 | tf_op jit(solution)/shard_map/dot_general | solution.py:101
  195.7 2.8 %fusion.17 = f32[256,2048]{1,0:T(8,128)S(1)} fusion(f32[256,2048]{1,0:T(8,128)S(1)} %fusion.84, f32[256,2048]{1,0:T(8,128)S(1)} %fusion.82, bf16[512,2048]{1,0:T(8,128)(2,1)} %param.11, s32[]{:T(128)S(6)} %select_n.213, bf16[256,2048]{0,1:T(8,128)(2,1)S(1)} %get-tuple-element.19, bf16[256,2048]{0,1:T(8,128)(2,1)S(1)} %get-tuple-element.18), kind=kOutput, calls=%fused_computation.47 | convolution fusion | flops 538443776 | bytes 10485764 | tf_op jit(solution)/shard_map/dot_general | solution.py:101
  198.5 2.7 %fusion.87 = f32[256,2048]{1,0:T(8,128)S(1)} fusion(bf16[512,2048]{1,0:T(8,128)(2,1)} %collective-permute-done.12, s32[]{:T(128)S(6)} %select_n.226, bf16[256,2048]{0,1:T(8,128)(2,1)S(1)} %get-tuple-element.19, bf16[256,2048]{0,1:T(8,128)(2,1)S(1)} %get-tuple-element.18), kind=kOutput, calls=%fused_computation.112 | convolution fusion | flops 537395200 | bytes 6291460 | tf_op jit(solution)/shard_map/dot_general | solution.py:101
  201.2 2.8 %fusion.16 = f32[256,2048]{1,0:T(8,128)S(1)} fusion(f32[256,2048]{1,0:T(8,128)S(1)} %fusion.87, f32[256,2048]{1,0:T(8,128)S(1)} %fusion.17, bf16[512,2048]{1,0:T(8,128)(2,1)} %collective-permute-done.11, s32[]{:T(128)S(6)} %select_n.223, bf16[256,2048]{0,1:T(8,128)(2,1)S(1)} %get-tuple-element.19, bf16[256,2048]{0,1:T(8,128)(2,1)S(1)} %get-tuple-element.18), kind=kOutput, calls=%fused_computation.45 | convolution fusion | flops 538443776 | bytes 10485764 | tf_op jit(solution)/shard_map/dot_general | solution.py:101
  204.0 8.8 %collective-permute-done.14 = bf16[512,2048]{1,0:T(8,128)(2,1)S(1)} collective-permute-done((bf16[512,2048]{1,0:T(8,128)(2,1)}, bf16[512,2048]{1,0:T(8,128)(2,1)S(1)}, u32[]{:S(2)}, u32[]{:S(2)}) %collective-permute-start.14) | collective-permute-done | bytes 2097184 | tf_op jit(solution)/shard_map/ppermute | solution.py:113
  212.8 1.1 fusion.90
  213.9 2.8 %fusion.15 = f32[256,2048]{1,0:T(8,128)S(1)} fusion(f32[256,2048]{1,0:T(8,128)S(1)} %fusion.90, f32[256,2048]{1,0:T(8,128)S(1)} %fusion.16, bf16[512,2048]{1,0:T(8,128)(2,1)} %collective-permute-done.13, s32[]{:T(128)S(6)} %select_n.229, bf16[256,2048]{0,1:T(8,128)(2,1)S(1)} %get-tuple-element.19, bf16[256,2048]{0,1:T(8,128)(2,1)S(1)} %get-tuple-element.18), kind=kOutput, calls=%fused_computation.43 | convolution fusion | flops 538443776 | bytes 10485764 | tf_op jit(solution)/shard_map/dot_general | solution.py:101
  216.7 18.0 %collective-permute-done.15 = bf16[512,2048]{1,0:T(8,128)(2,1)S(1)} collective-permute-done((bf16[512,2048]{1,0:T(8,128)(2,1)}, bf16[512,2048]{1,0:T(8,128)(2,1)S(1)}, u32[]{:S(2)}, u32[]{:S(2)}) %collective-permute-start.15) | collective-permute-done | bytes 2097184 | tf_op jit(solution)/shard_map/ppermute | solution.py:110
  234.7 2.1 fusion.18
  (57 shorter events, 3.8 us)
Async XLA Ops:
  1.8 25.2 %collective-permute-start.6 = (bf16[256,512]{0,1:T(8,128)(2,1)}, bf16[256,512]{0,1:T(8,128)(2,1)S(1)}, u32[]{:S(2)}, u32[]{:S(2)}) collective-permute-start(bf16[256,512]{0,1:T(8,128)(2,1)} %copy.52), channel_id=1, source_target_pairs={{0,8},{2,10},{4,12},{6,14},{1,9},{3,11},{5,13},{7,15},{16,24},{18,... | collective-permute-start | bytes 786440 | tf_op jit(solution)/shard_map/ppermute | solution.py:15
  7.8 24.2 %collective-permute-start.4 = (bf16[256,512]{0,1:T(8,128)(2,1)}, bf16[256,512]{0,1:T(8,128)(2,1)S(1)}, u32[]{:S(2)}, u32[]{:S(2)}) collective-permute-start(bf16[256,512]{0,1:T(8,128)(2,1)} %copy.52), channel_id=1, source_target_pairs={{0,6},{2,8},{4,10},{6,12},{8,14},{1,7},{3,9},{5,11},{7,13},{9,15},... | collective-permute-start | bytes 786440 | tf_op jit(solution)/shard_map/ppermute | solution.py:15
  12.2 24.5 %collective-permute-start.2 = (bf16[256,512]{0,1:T(8,128)(2,1)}, bf16[256,512]{0,1:T(8,128)(2,1)}, u32[]{:S(2)}, u32[]{:S(2)}) collective-permute-start(bf16[256,512]{0,1:T(8,128)(2,1)} %copy.52), channel_id=1, source_target_pairs={{0,4},{2,6},{4,8},{6,10},{8,12},{10,14},{1,5},{3,7},{5,9},{7,11},{... | collective-permute-start | bytes 786440 | tf_op jit(solution)/shard_map/ppermute | solution.py:15
  14.2 27.6 %collective-permute-start = (bf16[256,512]{0,1:T(8,128)(2,1)}, bf16[256,512]{0,1:T(8,128)(2,1)}, u32[]{:S(2)}, u32[]{:S(2)}) collective-permute-start(bf16[256,512]{0,1:T(8,128)(2,1)} %copy.52), channel_id=1, source_target_pairs={{0,2},{2,4},{4,6},{6,8},{8,10},{10,12},{12,14},{1,3},{3,5},{5,7},{... | collective-permute-start | bytes 786440 | tf_op jit(solution)/shard_map/ppermute | solution.py:15
  18.0 72.2 %collective-permute-start.1 = (bf16[256,512]{1,0:T(8,128)(2,1)}, bf16[256,512]{1,0:T(8,128)(2,1)}, u32[]{:S(2)}, u32[]{:S(2)}) collective-permute-start(bf16[256,512]{1,0:T(8,128)(2,1)} %param.9), channel_id=1, source_target_pairs={{0,2},{2,4},{4,6},{6,8},{8,10},{10,12},{12,14},{1,3},{3,5},{5,7},{... | collective-permute-start | bytes 786440 | tf_op jit(solution)/shard_map/ppermute | solution.py:15
  27.0 68.0 %collective-permute-start.3 = (bf16[256,512]{1,0:T(8,128)(2,1)}, bf16[256,512]{1,0:T(8,128)(2,1)}, u32[]{:S(2)}, u32[]{:S(2)}) collective-permute-start(bf16[256,512]{1,0:T(8,128)(2,1)} %param.9), channel_id=1, source_target_pairs={{0,4},{2,6},{4,8},{6,10},{8,12},{10,14},{1,5},{3,7},{5,9},{7,11},{... | collective-permute-start | bytes 786440 | tf_op jit(solution)/shard_map/ppermute | solution.py:15
  32.0 64.2 %collective-permute-start.5 = (bf16[256,512]{1,0:T(8,128)(2,1)}, bf16[256,512]{1,0:T(8,128)(2,1)}, u32[]{:S(2)}, u32[]{:S(2)}) collective-permute-start(bf16[256,512]{1,0:T(8,128)(2,1)} %param.9), channel_id=1, source_target_pairs={{0,6},{2,8},{4,10},{6,12},{8,14},{1,7},{3,9},{5,11},{7,13},{9,15},... | collective-permute-start | bytes 786440 | tf_op jit(solution)/shard_map/ppermute | solution.py:15
  36.6 7.5 %copy-start.1 = (f32[4,256,256,4]{2,1,3,0:T(8,128)}, f32[4,256,256,4]{2,1,3,0:T(8,128)S(1)}, u32[]{:S(2)}) copy-start(f32[4,256,256,4]{2,1,3,0:T(8,128)S(1)} %get-tuple-element.38) | copy-start | bytes 12582916
  36.7 49.1 %collective-permute-start.9 = (bf16[512,2048]{1,0:T(8,128)(2,1)}, bf16[512,2048]{1,0:T(8,128)(2,1)S(1)}, u32[]{:S(2)}, u32[]{:S(2)}) collective-permute-start(bf16[512,2048]{1,0:T(8,128)(2,1)} %param.11), channel_id=1, source_target_pairs={{0,4},{4,8},{8,12},{12,14},{14,10},{10,6},{6,2},{2,0},{1,5},{5,9},... | collective-permute-start | bytes 6291464 | tf_op jit(solution)/shard_map/ppermute | solution.py:110
  41.8 46.8 %copy-start.3 = (f32[4,256,256,4]{2,1,3,0:T(8,128)}, f32[4,256,256,4]{2,1,3,0:T(8,128)S(1)}, u32[]{:S(2)}) copy-start(f32[4,256,256,4]{2,1,3,0:T(8,128)S(1)} %get-tuple-element.40) | copy-start | bytes 12582916
  41.8 66.6 %collective-permute-start.10 = (bf16[512,2048]{1,0:T(8,128)(2,1)}, bf16[512,2048]{1,0:T(8,128)(2,1)}, u32[]{:S(2)}, u32[]{:S(2)}) collective-permute-start(bf16[512,2048]{1,0:T(8,128)(2,1)} %param.11), channel_id=1, source_target_pairs={{0,2},{4,0},{8,4},{12,8},{14,12},{10,14},{6,10},{2,6},{1,3},{5,1},... | collective-permute-start | bytes 6291464 | tf_op jit(solution)/shard_map/ppermute | solution.py:113
  44.1 2.2 copy-start.5
  44.1 2.1 copy-start.8
  44.1 44.4 %copy-start.10 = (f32[4,4,256]{2,1,0:T(4,128)}, f32[4,4,256]{2,1,0:T(4,128)S(1)}, u32[]{:S(2)}) copy-start(f32[4,4,256]{2,1,0:T(4,128)S(1)} %get-tuple-element.16) | copy-start | bytes 49156
  44.1 46.1 %copy-start.12 = (f32[4,4,256]{2,1,0:T(4,128)}, f32[4,4,256]{2,1,0:T(4,128)S(1)}, u32[]{:S(2)}) copy-start(f32[4,4,256]{2,1,0:T(4,128)S(1)} %get-tuple-element.17) | copy-start | bytes 49156
  45.2 2.1 copy-start.6
  85.8 52.5 %collective-permute-start.11 = (bf16[512,2048]{1,0:T(8,128)(2,1)S(1)}, bf16[512,2048]{1,0:T(8,128)(2,1)}, u32[]{:S(2)}, u32[]{:S(2)}) collective-permute-start(bf16[512,2048]{1,0:T(8,128)(2,1)S(1)} %collective-permute-done.9), channel_id=1, source_target_pairs={{0,4},{4,8},{8,12},{12,14},{14,10},{10,6},{6,2},{2,0},{1,5},{5,9},... | collective-permute-start | bytes 6291464 | tf_op jit(solution)/shard_map/ppermute | solution.py:110
  90.2 48.0 %collective-permute-start.7 = (bf16[256,512]{1,0:T(8,128)(2,1)}, bf16[256,512]{1,0:T(8,128)(2,1)S(1)}, u32[]{:S(2)}, u32[]{:S(2)}) collective-permute-start(bf16[256,512]{1,0:T(8,128)(2,1)} %param.9), channel_id=1, source_target_pairs={{0,8},{2,10},{4,12},{6,14},{1,9},{3,11},{5,13},{7,15},{16,24},{18,... | collective-permute-start | bytes 786440 | tf_op jit(solution)/shard_map/ppermute | solution.py:15
  97.2 4.9 %copy-start.4 = (f32[4,256,256,4]{2,1,3,0:T(8,128)S(1)}, f32[4,256,256,4]{2,1,3,0:T(8,128)}, u32[]{:S(2)}) copy-start(f32[4,256,256,4]{2,1,3,0:T(8,128)} %copy-done.3) | copy-start | bytes 12582916
  97.2 4.9 %copy-start.11 = (f32[4,4,256]{2,1,0:T(4,128)S(1)}, f32[4,4,256]{2,1,0:T(4,128)}, u32[]{:S(2)}) copy-start(f32[4,4,256]{2,1,0:T(4,128)} %copy-done.10) | copy-start | bytes 49156
  102.1 2.6 %copy-start.2 = (f32[4,256,256,4]{2,1,3,0:T(8,128)S(1)}, f32[4,256,256,4]{2,1,3,0:T(8,128)}, u32[]{:S(2)}) copy-start(f32[4,256,256,4]{2,1,3,0:T(8,128)} %copy-done.1) | copy-start | bytes 12582916
  102.1 2.6 %copy-start.9 = (f32[4,4,256]{2,1,0:T(4,128)S(1)}, f32[4,4,256]{2,1,0:T(4,128)}, u32[]{:S(2)}) copy-start(f32[4,4,256]{2,1,0:T(4,128)} %copy-done.8) | copy-start | bytes 49156
  104.8 2.6 %copy-start = (f32[4,256,256,4]{2,1,3,0:T(8,128)S(1)}, f32[4,256,256,4]{2,1,3,0:T(8,128)}, u32[]{:S(2)}) copy-start(f32[4,256,256,4]{2,1,3,0:T(8,128)} %get-tuple-element.36) | copy-start | bytes 12582916
  104.8 3.7 %copy-start.7 = (f32[4,4,256]{2,1,0:T(4,128)S(1)}, f32[4,4,256]{2,1,0:T(4,128)}, u32[]{:S(2)}) copy-start(f32[4,4,256]{2,1,0:T(4,128)} %fusion.9) | copy-start | bytes 49156
  108.4 56.1 %collective-permute-start.12 = (bf16[512,2048]{1,0:T(8,128)(2,1)}, bf16[512,2048]{1,0:T(8,128)(2,1)}, u32[]{:S(2)}, u32[]{:S(2)}) collective-permute-start(bf16[512,2048]{1,0:T(8,128)(2,1)} %collective-permute-done.10), channel_id=1, source_target_pairs={{0,2},{4,0},{8,4},{12,8},{14,12},{10,14},{6,10},{2,6},{1,3},{5,1},... | collective-permute-start | bytes 6291464 | tf_op jit(solution)/shard_map/ppermute | solution.py:113
  138.3 52.2 %collective-permute-start.13 = (bf16[512,2048]{1,0:T(8,128)(2,1)}, bf16[512,2048]{1,0:T(8,128)(2,1)}, u32[]{:S(2)}, u32[]{:S(2)}) collective-permute-start(bf16[512,2048]{1,0:T(8,128)(2,1)} %collective-permute-done.11), channel_id=1, source_target_pairs={{0,4},{4,8},{8,12},{12,14},{14,10},{10,6},{6,2},{2,0},{1,5},{5,9},... | collective-permute-start | bytes 6291464 | tf_op jit(solution)/shard_map/ppermute | solution.py:110
  147.5 6.6 %copy-start.14 = (s32[8]{0:T(128)S(1)}, s32[8]{0:T(128)}, u32[]{:S(2)}) copy-start(s32[8]{0:T(128)} %constant.172.clone) | copy-start | bytes 100
  147.5 11.8 %copy-start.13 = (s32[8]{0:T(128)S(1)}, s32[8]{0:T(128)}, u32[]{:S(2)}) copy-start(s32[8]{0:T(128)} %constant.173.clone) | copy-start | bytes 100
  154.0 10.6 %collective-permute-start.8 = (bf16[256,2048]{0,1:T(8,128)(2,1)S(1)}, bf16[256,2048]{0,1:T(8,128)(2,1)}, u32[]{:S(2)}, u32[]{:S(2)}) collective-permute-start(bf16[256,2048]{0,1:T(8,128)(2,1)S(1)} %bitcast.263), channel_id=1, source_target_pairs={{0,1},{1,0},{2,3},{3,2},{4,5},{5,4},{6,7},{7,6},{8,9},{9,8},{10,11... | collective-permute-start | bytes 3145736 | tf_op jit(solution)/shard_map/ppermute | solution.py:77
  164.5 48.3 %collective-permute-start.14 = (bf16[512,2048]{1,0:T(8,128)(2,1)}, bf16[512,2048]{1,0:T(8,128)(2,1)S(1)}, u32[]{:S(2)}, u32[]{:S(2)}) collective-permute-start(bf16[512,2048]{1,0:T(8,128)(2,1)} %collective-permute-done.12), channel_id=1, source_target_pairs={{0,2},{4,0},{8,4},{12,8},{14,12},{10,14},{6,10},{2,6},{1,3},{5,1},... | collective-permute-start | bytes 6291464 | tf_op jit(solution)/shard_map/ppermute | solution.py:113
  190.5 44.2 %collective-permute-start.15 = (bf16[512,2048]{1,0:T(8,128)(2,1)}, bf16[512,2048]{1,0:T(8,128)(2,1)S(1)}, u32[]{:S(2)}, u32[]{:S(2)}) collective-permute-start(bf16[512,2048]{1,0:T(8,128)(2,1)} %collective-permute-done.13), channel_id=1, source_target_pairs={{0,4},{4,8},{8,12},{12,14},{14,10},{10,6},{6,2},{2,0},{1,5},{5,9},... | collective-permute-start | bytes 6291464 | tf_op jit(solution)/shard_map/ppermute | solution.py:110

commit v3 on v2

--- a/solution.py
+++ b/solution.py
@@ -107,6 +107,13 @@
     forward_steps = count // 2
     backward_steps = count - 1 - forward_steps
     for step in range(1, forward_steps + 1):
+        if step > backward_steps:
+            half = out_weight.shape[1] // 2
+            forward = lax.ppermute(forward[:, :half], "ctx", ahead)
+            backward = lax.ppermute(backward[:, half:], "ctx", behind)
+            joined = jnp.concatenate([forward, backward], axis=1)
+            mixed = mixed + term(joined, order_table[(position + count - step) % count])
+            break
         forward = lax.ppermute(forward, "ctx", ahead)
         mixed = mixed + term(forward, order_table[(position + count - step) % count])
         if step <= backward_steps:

time: 238 us -> 247 us (1.038)
  other arithmetic: 9.19 us -> 19.7 us
  matrix products: 46.2 us -> 41.7 us
  waiting for transfers between devices: 115 us -> 119 us
  starting transfers between devices: 45.5 us -> 41.7 us
  local copies, waits for them, and re-layouts: 11.1 us -> 14.5 us
    ppermute x8, waiting for transfers between devices: 29 us -> 0.02 us  [passed_along(): return lax.ppermute(array, axis, pairs)]
    ppermute x4 -> x3, starting transfers between devices: 17.6 us -> 1.31 us  [ring_project(): forward = lax.ppermute(forward, 'ctx', ahead)]
    ppermute x0 -> x2, waiting for transfers between devices: none -> 15 us  [the longest x1 14.5 us: ring_project(): forward = lax.ppermute(forward[:, :half], 'ctx', ahead)]
    ppermute x3, waiting for transfers between devices: 8.84 us -> 20.5 us  [ring_project(): backward = lax.ppermute(backward, 'ctx', behind)]
    dot_general x5, matrix products: 19.1 us -> 7.8 us  [update(): jnp.einsum('hgqk,khd->hgqd', weights.astype(jnp.bfloat16), value_head_row...]
    ppermute x3, starting transfers between devices: 0.18 us -> 11.2 us  [ring_project(): backward = lax.ppermute(backward, 'ctx', behind)]
    reduce_sum x5, other arithmetic: 5.77 us -> 15.8 us  [update(): totals = totals * rescale + jnp.sum(weights, axis=-1)]
    ppermute x4 -> x3, waiting for transfers between devices: 77.3 us -> 83.9 us  [ring_project(): forward = lax.ppermute(forward, 'ctx', ahead)]
  transfers between devices with their start and end apart: 16 -> 17, of which waited for: 5 -> 5; matrix products, arithmetic and copies ran while one was open for 26% -> 28% of each run, Pallas kernels for 0% -> 0%
where the time goes in v3:
time: 247 us; the launch traced here: 246 us
  waiting for transfers between devices  119 us (48%)
  starting transfers between devices  41.7 us (17%)
  matrix products  41.7 us (17%)
  other arithmetic  19.7 us (8%)
  local copies, waits for them, and re-layouts  14.5 us (6%)
  between operations  9.4 us (4%)
    ppermute x3, waiting for transfers between devices, ring_project(): forward = lax.ppermute(forward, 'ctx', ahead)  83.9 us
    ppermute x8, starting transfers between devices, passed_along(): return lax.ppermute(array, axis, pairs)  26.8 us
    ppermute x3, waiting for transfers between devices, ring_project(): backward = lax.ppermute(backward, 'ctx', behind)  20.5 us
    dot_general x8, matrix products, term(): return jnp.dot(piece, block, preferred_element_type=jnp.float32)  18.3 us
    reduce_sum x5, other arithmetic, update(): totals = totals * rescale + jnp.sum(weights, axis=-1)  15.8 us
    dot_general x5, matrix products, update(): jnp.einsum('qhgd,khd->hgqk', query_head_rows, key_head_rows, preferred_el...  15.6 us
    ppermute x1, waiting for transfers between devices, ring_project(): forward = lax.ppermute(forward[:, :half], 'ctx', ahead)  14.5 us
    ppermute x3, starting transfers between devices, ring_project(): backward = lax.ppermute(backward, 'ctx', behind)  11.2 us
  transfers between devices with their start and end apart: 17, of which 5 were waited for; matrix products, arithmetic and copies ran while one was open for 28% of the time, Pallas kernels for 0%

profile of v3, /device:TPU:0, one launch (start us, length us, event | category | flops | bytes accessed | tf_op | source)
XLA Modules:
  0.0 246.3 jit_solution(17235062751499556806)
XLA Ops:
  0.0 1.1 copy.52
  1.1 6.0 %collective-permute-start.6 = (bf16[256,512]{0,1:T(8,128)(2,1)S(1)}, bf16[256,512]{0,1:T(8,128)(2,1)S(1)}, u32[]{:S(2)}, u32[]{:S(2)}) collective-permute-start(bf16[256,512]{0,1:T(8,128)(2,1)S(1)} %copy.52), channel_id=1, source_target_pairs={{0,8},{2,10},{4,12},{6,14},{1,9},{3,11},{5,13},{7,15},{16,24},{18,... | collective-permute-start | bytes 786440 | tf_op jit(solution)/shard_map/ppermute | solution.py:15
  7.1 4.4 %collective-permute-start.4 = (bf16[256,512]{0,1:T(8,128)(2,1)S(1)}, bf16[256,512]{0,1:T(8,128)(2,1)S(1)}, u32[]{:S(2)}, u32[]{:S(2)}) collective-permute-start(bf16[256,512]{0,1:T(8,128)(2,1)S(1)} %copy.52), channel_id=1, source_target_pairs={{0,6},{2,8},{4,10},{6,12},{8,14},{1,7},{3,9},{5,11},{7,13},{9,15},... | collective-permute-start | bytes 786440 | tf_op jit(solution)/shard_map/ppermute | solution.py:15
  11.5 1.3 collective-permute-start.2
  12.8 3.8 %collective-permute-start = (bf16[256,512]{0,1:T(8,128)(2,1)S(1)}, bf16[256,512]{0,1:T(8,128)(2,1)}, u32[]{:S(2)}, u32[]{:S(2)}) collective-permute-start(bf16[256,512]{0,1:T(8,128)(2,1)S(1)} %copy.52), channel_id=1, source_target_pairs={{0,2},{2,4},{4,6},{6,8},{8,10},{10,12},{12,14},{1,3},{3,5},{5,7},{... | collective-permute-start | bytes 786440 | tf_op jit(solution)/shard_map/ppermute | solution.py:15
  16.6 2.2 collective-permute-start.5
  19.9 1.8 copy.89
  21.7 1.8 reshape.293
  24.8 2.9 %fusion = (f32[4,4,256]{2,1,0:T(4,128)S(1)}, f32[4,256,256,4]{2,1,3,0:T(8,128)}) fusion(pred[256,256]{0,1:T(8,128)(4,1)S(1)} %get-tuple-element.23, bf16[256,4,4,128]{3,2,1,0:T(4,128)(2,1)S(1)} %reshape.293, bf16[256,4,128,1]{2,1,0,3:T(4,128)(2,1)S(1)} %bitcast.262), kind=kOutput, calls=%fused_computation.26 | convolution fusion | flops 271577088 | bytes 5586944 | tf_op jit(solution)/shard_map/qhgd,khd->hgqk/dot_general | solution.py:33
  27.7 2.0 collective-permute-start.3
  29.7 2.9 %fusion.4 = (f32[4,4,256]{2,1,0:T(4,128)S(1)}, f32[4,256,256,4]{2,1,3,0:T(8,128)}) fusion(pred[256,256]{0,1:T(8,128)(4,1)S(1)} %get-tuple-element.27, bf16[256,4,128,1]{0,2,3,1:T(8,128)(2,1)S(1)} %bitcast.265, bf16[256,4,4,128]{3,2,1,0:T(4,128)(2,1)S(1)} %reshape.293), kind=kOutput, calls=%fused_computation.30 | convolution fusion | flops 271577088 | bytes 5586944 | tf_op jit(solution)/shard_map/qhgd,khd->hgqk/dot_general | solution.py:33
  32.6 3.1 %collective-permute-start.1 = (bf16[256,512]{1,0:T(8,128)(2,1)}, bf16[256,512]{1,0:T(8,128)(2,1)}, u32[]{:S(2)}, u32[]{:S(2)}) collective-permute-start(bf16[256,512]{1,0:T(8,128)(2,1)} %param.9), channel_id=1, source_target_pairs={{0,2},{2,4},{4,6},{6,8},{8,10},{10,12},{12,14},{1,3},{3,5},{5,7},{... | collective-permute-start | bytes 786440 | tf_op jit(solution)/shard_map/ppermute | solution.py:15
  35.8 2.9 %fusion.3 = (f32[4,4,256]{2,1,0:T(4,128)S(1)}, f32[4,256,256,4]{2,1,3,0:T(8,128)}) fusion(pred[256,256]{0,1:T(8,128)(4,1)S(1)} %get-tuple-element.25, bf16[256,4,128,1]{0,2,3,1:T(8,128)(2,1)S(1)} %bitcast.264, bf16[256,4,4,128]{3,2,1,0:T(4,128)(2,1)S(1)} %reshape.293), kind=kOutput, calls=%fused_computation.29 | convolution fusion | flops 271577088 | bytes 5586944 | tf_op jit(solution)/shard_map/qhgd,khd->hgqk/dot_general | solution.py:33
  38.7 4.0 %collective-permute-start.7 = (bf16[256,512]{1,0:T(8,128)(2,1)}, bf16[256,512]{1,0:T(8,128)(2,1)}, u32[]{:S(2)}, u32[]{:S(2)}) collective-permute-start(bf16[256,512]{1,0:T(8,128)(2,1)} %param.9), channel_id=1, source_target_pairs={{0,8},{2,10},{4,12},{6,14},{1,9},{3,11},{5,13},{7,15},{16,24},{18,... | collective-permute-start | bytes 786440 | tf_op jit(solution)/shard_map/ppermute | solution.py:15
  42.7 2.9 %fusion.2 = (f32[4,4,256]{2,1,0:T(4,128)S(1)}, f32[4,256,256,4]{2,1,3,0:T(8,128)}) fusion(pred[256,256]{0,1:T(8,128)(4,1)S(1)} %get-tuple-element.26, bf16[256,4,128,1]{0,2,3,1:T(8,128)(2,1)S(1)} %bitcast.263, bf16[256,4,4,128]{3,2,1,0:T(4,128)(2,1)S(1)} %reshape.293), kind=kOutput, calls=%fused_computation.28 | convolution fusion | flops 271577088 | bytes 5586944 | tf_op jit(solution)/shard_map/qhgd,khd->hgqk/dot_general | solution.py:33
  45.6 1.3 collective-permute-start.9
  46.9 3.9 %fusion.1 = (f32[4,4,256]{2,1,0:T(4,128)S(1)}, f32[4,256,256,4]{2,1,3,0:T(8,128)}) fusion(pred[256,256]{0,1:T(8,128)(4,1)S(1)} %get-tuple-element.24, bf16[256,4,128,1]{0,2,3,1:T(8,128)(2,1)} %bitcast.62, bf16[256,4,4,128]{3,2,1,0:T(4,128)(2,1)S(1)} %reshape.293), kind=kOutput, calls=%fused_computation.27 | convolution fusion | flops 271577088 | bytes 5586944 | tf_op jit(solution)/shard_map/qhgd,khd->hgqk/dot_general | solution.py:33
  51.5 4.6 %collective-permute-start.10 = (bf16[512,2048]{1,0:T(8,128)(2,1)}, bf16[512,2048]{1,0:T(8,128)(2,1)}, u32[]{:S(2)}, u32[]{:S(2)}) collective-permute-start(bf16[512,2048]{1,0:T(8,128)(2,1)} %param.11), channel_id=1, source_target_pairs={{0,2},{4,0},{8,4},{12,8},{14,12},{10,14},{6,10},{2,6},{1,3},{5,1},... | collective-permute-start | bytes 6291464 | tf_op jit(solution)/shard_map/ppermute | solution.py:120
  56.1 1.1 copy.65
  57.1 3.8 %fusion.11 = f32[4,4,256]{2,1,0:T(4,128)} fusion(f32[4,256,256,4]{2,1,3,0:T(8,128)} %get-tuple-element.38, f32[4,4,256]{2,1,0:T(4,128)S(1)} %get-tuple-element.15, pred[256,256]{0,1:T(8,128)(4,1)S(1)} %get-tuple-element.25), kind=kLoop, calls=%fused_computation.37 | loop fusion | flops 5238784 | bytes 4292608 | tf_op jit(solution)/shard_map/reduce_sum | solution.py:49
  60.9 1.1 copy.60
  62.0 3.8 %fusion.13 = f32[4,4,256]{2,1,0:T(4,128)} fusion(f32[4,256,256,4]{2,1,3,0:T(8,128)} %get-tuple-element.36, f32[4,4,256]{2,1,0:T(4,128)S(1)} %get-tuple-element.14, pred[256,256]{0,1:T(8,128)(4,1)S(1)} %get-tuple-element.27), kind=kLoop, calls=%fused_computation.39 | loop fusion | flops 5238784 | bytes 4292608 | tf_op jit(solution)/shard_map/reduce_sum | solution.py:49
  65.8 1.1 copy.55
  66.9 3.8 %fusion.7 = f32[4,4,256]{2,1,0:T(4,128)} fusion(f32[4,256,256,4]{2,1,3,0:T(8,128)} %get-tuple-element.42, f32[4,4,256]{2,1,0:T(4,128)S(1)} %get-tuple-element.17, pred[256,256]{0,1:T(8,128)(4,1)S(1)} %get-tuple-element.24), kind=kLoop, calls=%fused_computation.33 | loop fusion | flops 5238784 | bytes 4292608 | tf_op jit(solution)/shard_map/reduce_sum | solution.py:49
  70.8 1.1 copy.70
  71.9 3.4 %fusion.9 = f32[4,4,256]{2,1,0:T(4,128)S(1)} fusion(f32[4,256,256,4]{2,1,3,0:T(8,128)} %get-tuple-element.40, f32[4,4,256]{2,1,0:T(4,128)} %get-tuple-element.16, pred[256,256]{0,1:T(8,128)(4,1)S(1)} %get-tuple-element.26), kind=kLoop, calls=%fused_computation.35 | loop fusion | flops 5238784 | bytes 4292608 | tf_op jit(solution)/shard_map/reduce_sum | solution.py:49
  76.6 1.2 fusion.22
  78.6 1.2 fusion.24
  80.2 1.2 fusion.26
  81.5 20.5 %collective-permute-done.10 = bf16[512,2048]{1,0:T(8,128)(2,1)} collective-permute-done((bf16[512,2048]{1,0:T(8,128)(2,1)}, bf16[512,2048]{1,0:T(8,128)(2,1)}, u32[]{:S(2)}, u32[]{:S(2)}) %collective-permute-start.10) | collective-permute-done | bytes 2097184 | tf_op jit(solution)/shard_map/ppermute | solution.py:120
  102.0 4.1 %collective-permute-start.12 = (bf16[512,2048]{1,0:T(8,128)(2,1)}, bf16[512,2048]{1,0:T(8,128)(2,1)}, u32[]{:S(2)}, u32[]{:S(2)}) collective-permute-start(bf16[512,2048]{1,0:T(8,128)(2,1)} %collective-permute-done.10), channel_id=1, source_target_pairs={{0,2},{4,0},{8,4},{12,8},{14,12},{10,14},{6,10},{2,6},{1,3},{5,1},... | collective-permute-start | bytes 6291464 | tf_op jit(solution)/shard_map/ppermute | solution.py:120
  106.2 1.2 fusion.28
  107.5 2.9 %fusion.35 = bf16[256,4,4,128]{0,3,2,1:T(8,128)(2,1)} fusion(f32[4,4,256,128]{2,3,1,0:T(8,128)S(1)} %fusion.22, f32[4,4,256,128]{2,3,1,0:T(8,128)S(1)} %fusion.24, f32[4,4,256,128]{2,3,1,0:T(8,128)S(1)} %fusion.26, f32[4,4,256,128]{2,3,1,0:T(8,128)S(1)} %fusion.28, f32[256,4,4]{0,2,1:T(4,128)S(1)} %get-tuple-element.10, ...), kind=kOutput, calls=%fused_computation.60 | convolution fusion | flops 279445504 | bytes 14073856 | tf_op jit(solution)/shard_map/hgqk,khd->hgqd/dot_general | solution.py:42
  110.4 57.8 %collective-permute-done.11 = bf16[512,2048]{1,0:T(8,128)(2,1)} collective-permute-done((bf16[512,2048]{1,0:T(8,128)(2,1)S(1)}, bf16[512,2048]{1,0:T(8,128)(2,1)}, u32[]{:S(2)}, u32[]{:S(2)}) %collective-permute-start.11) | collective-permute-done | bytes 2097184 | tf_op jit(solution)/shard_map/ppermute | solution.py:117
  168.2 2.5 %collective-permute-start.14 = (bf16[512,2048]{1,0:T(8,128)(2,1)}, bf16[512,2048]{1,0:T(8,128)(2,1)S(1)}, u32[]{:S(2)}, u32[]{:S(2)}) collective-permute-start(bf16[512,2048]{1,0:T(8,128)(2,1)} %collective-permute-done.12), channel_id=1, source_target_pairs={{0,2},{4,0},{8,4},{12,8},{14,12},{10,14},{6,10},{2,6},{1,3},{5,1},... | collective-permute-start | bytes 6291464 | tf_op jit(solution)/shard_map/ppermute | solution.py:120
  181.0 1.8 broadcast_select_fusion
  183.2 1.1 fusion.87
  184.3 2.7 %fusion.89 = f32[256,2048]{1,0:T(8,128)S(1)} fusion(bf16[512,2048]{1,0:T(8,128)(2,1)} %collective-permute-done.10, s32[]{:T(128)S(6)} %select_n.220, bf16[256,2048]{0,1:T(8,128)(2,1)S(1)} %get-tuple-element.19, bf16[256,2048]{0,1:T(8,128)(2,1)S(1)} %get-tuple-element.18), kind=kOutput, calls=%fused_computation.115 | convolution fusion | flops 537395200 | bytes 6291460 | tf_op jit(solution)/shard_map/dot_general | solution.py:101
  187.0 2.8 %fusion.17 = f32[256,2048]{1,0:T(8,128)S(1)} fusion(f32[256,2048]{1,0:T(8,128)S(1)} %fusion.89, f32[256,2048]{1,0:T(8,128)S(1)} %fusion.87, bf16[512,2048]{1,0:T(8,128)(2,1)} %param.11, s32[]{:T(128)S(6)} %select_n.213, bf16[256,2048]{0,1:T(8,128)(2,1)S(1)} %get-tuple-element.19, bf16[256,2048]{0,1:T(8,128)(2,1)S(1)} %get-tuple-element.18), kind=kOutput, calls=%fused_computation.46 | convolution fusion | flops 538443776 | bytes 10485764 | tf_op jit(solution)/shard_map/dot_general | solution.py:101
  189.9 26.1 %collective-permute-done.13 = bf16[512,2048]{1,0:T(8,128)(2,1)} collective-permute-done((bf16[512,2048]{1,0:T(8,128)(2,1)}, bf16[512,2048]{1,0:T(8,128)(2,1)}, u32[]{:S(2)}, u32[]{:S(2)}) %collective-permute-start.13) | collective-permute-done | bytes 2097184 | tf_op jit(solution)/shard_map/ppermute | solution.py:117
  215.9 1.3 slice.8
  217.4 2.3 collective-permute-start.16
  219.7 2.7 %fusion.92 = f32[256,2048]{1,0:T(8,128)S(1)} fusion(bf16[512,2048]{1,0:T(8,128)(2,1)} %collective-permute-done.12, s32[]{:T(128)S(6)} %select_n.226, bf16[256,2048]{0,1:T(8,128)(2,1)S(1)} %get-tuple-element.19, bf16[256,2048]{0,1:T(8,128)(2,1)S(1)} %get-tuple-element.18), kind=kOutput, calls=%fused_computation.116 | convolution fusion | flops 537395200 | bytes 6291460 | tf_op jit(solution)/shard_map/dot_general | solution.py:101
  222.4 2.8 %fusion.16 = f32[256,2048]{1,0:T(8,128)S(1)} fusion(f32[256,2048]{1,0:T(8,128)S(1)} %fusion.92, f32[256,2048]{1,0:T(8,128)S(1)} %fusion.17, bf16[512,2048]{1,0:T(8,128)(2,1)} %collective-permute-done.11, s32[]{:T(128)S(6)} %select_n.223, bf16[256,2048]{0,1:T(8,128)(2,1)S(1)} %get-tuple-element.19, bf16[256,2048]{0,1:T(8,128)(2,1)S(1)} %get-tuple-element.18), kind=kOutput, calls=%fused_computation.44 | convolution fusion | flops 538443776 | bytes 10485764 | tf_op jit(solution)/shard_map/dot_general | solution.py:101
  225.3 1.1 fusion.95
  226.4 14.5 %collective-permute-done.15 = bf16[512,1024]{1,0:T(8,128)(2,1)S(1)} collective-permute-done((bf16[512,1024]{1,0:T(8,128)(2,1)S(1)}, bf16[512,1024]{1,0:T(8,128)(2,1)S(1)}, u32[]{:S(2)}, u32[]{:S(2)}) %collective-permute-start.15) | collective-permute-done | bytes 1048608 | tf_op jit(solution)/shard_map/ppermute | solution.py:112
  241.4 1.2 fusion.30
  242.5 3.8 %fusion.19 = bf16[256,2048]{1,0:T(8,128)(2,1)} fusion(f32[256,2048]{1,0:T(8,128)S(1)} %fusion.30, f32[256,2048]{1,0:T(8,128)S(1)} %fusion.95, f32[256,2048]{1,0:T(8,128)S(1)} %fusion.16, bf16[512,2048]{1,0:T(8,128)(2,1)} %collective-permute-done.13, s32[]{:T(128)S(6)} %select_n.229, bf16[256,2048]{0,1:T(8,128)(2,1)S(1)} %get-tuple-element.19, ...), kind=kOutput, calls=%fused_computation.48 | convolution fusion | flops 539492352 | bytes 11534340 | tf_op jit(solution)/shard_map/dot_general | solution.py:101
  (73 shorter events, 7.9 us)
Async XLA Ops:
  1.1 26.6 %collective-permute-start.6 = (bf16[256,512]{0,1:T(8,128)(2,1)S(1)}, bf16[256,512]{0,1:T(8,128)(2,1)S(1)}, u32[]{:S(2)}, u32[]{:S(2)}) collective-permute-start(bf16[256,512]{0,1:T(8,128)(2,1)S(1)} %copy.52), channel_id=1, source_target_pairs={{0,8},{2,10},{4,12},{6,14},{1,9},{3,11},{5,13},{7,15},{16,24},{18,... | collective-permute-start | bytes 786440 | tf_op jit(solution)/shard_map/ppermute | solution.py:15
  7.1 25.6 %collective-permute-start.4 = (bf16[256,512]{0,1:T(8,128)(2,1)S(1)}, bf16[256,512]{0,1:T(8,128)(2,1)S(1)}, u32[]{:S(2)}, u32[]{:S(2)}) collective-permute-start(bf16[256,512]{0,1:T(8,128)(2,1)S(1)} %copy.52), channel_id=1, source_target_pairs={{0,6},{2,8},{4,10},{6,12},{8,14},{1,7},{3,9},{5,11},{7,13},{9,15},... | collective-permute-start | bytes 786440 | tf_op jit(solution)/shard_map/ppermute | solution.py:15
  11.5 27.2 %collective-permute-start.2 = (bf16[256,512]{0,1:T(8,128)(2,1)S(1)}, bf16[256,512]{0,1:T(8,128)(2,1)S(1)}, u32[]{:S(2)}, u32[]{:S(2)}) collective-permute-start(bf16[256,512]{0,1:T(8,128)(2,1)S(1)} %copy.52), channel_id=1, source_target_pairs={{0,4},{2,6},{4,8},{6,10},{8,12},{10,14},{1,5},{3,7},{5,9},{7,11},{... | collective-permute-start | bytes 786440 | tf_op jit(solution)/shard_map/ppermute | solution.py:15
  12.8 32.8 %collective-permute-start = (bf16[256,512]{0,1:T(8,128)(2,1)S(1)}, bf16[256,512]{0,1:T(8,128)(2,1)}, u32[]{:S(2)}, u32[]{:S(2)}) collective-permute-start(bf16[256,512]{0,1:T(8,128)(2,1)S(1)} %copy.52), channel_id=1, source_target_pairs={{0,2},{2,4},{4,6},{6,8},{8,10},{10,12},{12,14},{1,3},{3,5},{5,7},{... | collective-permute-start | bytes 786440 | tf_op jit(solution)/shard_map/ppermute | solution.py:15
  16.6 34.8 %collective-permute-start.5 = (bf16[256,512]{1,0:T(8,128)(2,1)}, bf16[256,512]{1,0:T(8,128)(2,1)}, u32[]{:S(2)}, u32[]{:S(2)}) collective-permute-start(bf16[256,512]{1,0:T(8,128)(2,1)} %param.9), channel_id=1, source_target_pairs={{0,6},{2,8},{4,10},{6,12},{8,14},{1,7},{3,9},{5,11},{7,13},{9,15},... | collective-permute-start | bytes 786440 | tf_op jit(solution)/shard_map/ppermute | solution.py:15
  27.7 33.2 %collective-permute-start.3 = (bf16[256,512]{1,0:T(8,128)(2,1)}, bf16[256,512]{1,0:T(8,128)(2,1)}, u32[]{:S(2)}, u32[]{:S(2)}) collective-permute-start(bf16[256,512]{1,0:T(8,128)(2,1)} %param.9), channel_id=1, source_target_pairs={{0,4},{2,6},{4,8},{6,10},{8,12},{10,14},{1,5},{3,7},{5,9},{7,11},{... | collective-permute-start | bytes 786440 | tf_op jit(solution)/shard_map/ppermute | solution.py:15
  32.6 33.2 %collective-permute-start.1 = (bf16[256,512]{1,0:T(8,128)(2,1)}, bf16[256,512]{1,0:T(8,128)(2,1)}, u32[]{:S(2)}, u32[]{:S(2)}) collective-permute-start(bf16[256,512]{1,0:T(8,128)(2,1)} %param.9), channel_id=1, source_target_pairs={{0,2},{2,4},{4,6},{6,8},{8,10},{10,12},{12,14},{1,3},{3,5},{5,7},{... | collective-permute-start | bytes 786440 | tf_op jit(solution)/shard_map/ppermute | solution.py:15
  38.7 32.1 %collective-permute-start.7 = (bf16[256,512]{1,0:T(8,128)(2,1)}, bf16[256,512]{1,0:T(8,128)(2,1)}, u32[]{:S(2)}, u32[]{:S(2)}) collective-permute-start(bf16[256,512]{1,0:T(8,128)(2,1)} %param.9), channel_id=1, source_target_pairs={{0,8},{2,10},{4,12},{6,14},{1,9},{3,11},{5,13},{7,15},{16,24},{18,... | collective-permute-start | bytes 786440 | tf_op jit(solution)/shard_map/ppermute | solution.py:15
  45.6 60.5 %collective-permute-start.9 = (bf16[512,2048]{1,0:T(8,128)(2,1)}, bf16[512,2048]{1,0:T(8,128)(2,1)S(1)}, u32[]{:S(2)}, u32[]{:S(2)}) collective-permute-start(bf16[512,2048]{1,0:T(8,128)(2,1)} %param.11), channel_id=1, source_target_pairs={{0,4},{4,8},{8,12},{12,14},{14,10},{10,6},{6,2},{2,0},{1,5},{5,9},... | collective-permute-start | bytes 6291464 | tf_op jit(solution)/shard_map/ppermute | solution.py:117
  51.4 14.4 %copy-start.8 = (f32[4,4,256]{2,1,0:T(4,128)}, f32[4,4,256]{2,1,0:T(4,128)S(1)}, u32[]{:S(2)}) copy-start(f32[4,4,256]{2,1,0:T(4,128)S(1)} %get-tuple-element.14) | copy-start | bytes 49156
  51.4 14.4 %copy-start.17 = (f32[4,4,256]{2,1,0:T(4,128)}, f32[4,4,256]{2,1,0:T(4,128)S(1)}, u32[]{:S(2)}) copy-start(f32[4,4,256]{2,1,0:T(4,128)S(1)} %get-tuple-element.15) | copy-start | bytes 49156
  51.5 15.5 %copy-start.14 = (f32[4,4,256]{2,1,0:T(4,128)}, f32[4,4,256]{2,1,0:T(4,128)S(1)}, u32[]{:S(2)}) copy-start(f32[4,4,256]{2,1,0:T(4,128)S(1)} %get-tuple-element.17) | copy-start | bytes 49156
  51.5 50.5 %collective-permute-start.10 = (bf16[512,2048]{1,0:T(8,128)(2,1)}, bf16[512,2048]{1,0:T(8,128)(2,1)}, u32[]{:S(2)}, u32[]{:S(2)}) collective-permute-start(bf16[512,2048]{1,0:T(8,128)(2,1)} %param.11), channel_id=1, source_target_pairs={{0,2},{4,0},{8,4},{12,8},{14,12},{10,14},{6,10},{2,6},{1,3},{5,1},... | collective-permute-start | bytes 6291464 | tf_op jit(solution)/shard_map/ppermute | solution.py:120
  71.8 3.5 %copy-start = (f32[4,256,256,4]{2,1,3,0:T(8,128)S(1)}, f32[4,256,256,4]{2,1,3,0:T(8,128)}, u32[]{:S(2)}) copy-start(f32[4,256,256,4]{2,1,3,0:T(8,128)} %get-tuple-element.44) | copy-start | bytes 12582916
  71.9 3.5 %copy-start.10 = (f32[4,4,256]{2,1,0:T(4,128)S(1)}, f32[4,4,256]{2,1,0:T(4,128)}, u32[]{:S(2)}) copy-start(f32[4,4,256]{2,1,0:T(4,128)} %get-tuple-element.22) | copy-start | bytes 49156
  71.9 4.7 %copy-start.2 = (f32[4,256,256,4]{2,1,3,0:T(8,128)S(1)}, f32[4,256,256,4]{2,1,3,0:T(8,128)}, u32[]{:S(2)}) copy-start(f32[4,256,256,4]{2,1,3,0:T(8,128)} %get-tuple-element.38) | copy-start | bytes 12582916
  71.9 4.7 %copy-start.18 = (f32[4,4,256]{2,1,0:T(4,128)S(1)}, f32[4,4,256]{2,1,0:T(4,128)}, u32[]{:S(2)}) copy-start(f32[4,4,256]{2,1,0:T(4,128)} %copy-done.17) | copy-start | bytes 49156
  76.4 2.2 copy-start.3
  76.4 2.2 copy-start.16
  77.8 2.4 copy-start.4
  77.8 2.4 copy-start.15
  79.9 26.3 %copy-start.11 = (f32[4,4,256]{2,1,0:T(4,128)S(1)}, f32[4,4,256]{2,1,0:T(4,128)}, u32[]{:S(2)}) copy-start(f32[4,4,256]{2,1,0:T(4,128)} %fusion.11) | copy-start | bytes 49156
  79.9 26.3 %copy-start.12 = (f32[4,4,256]{2,1,0:T(4,128)S(1)}, f32[4,4,256]{2,1,0:T(4,128)}, u32[]{:S(2)}) copy-start(f32[4,4,256]{2,1,0:T(4,128)} %fusion.13) | copy-start | bytes 49156
  79.9 26.3 %copy-start.13 = (f32[4,4,256]{2,1,0:T(4,128)S(1)}, f32[4,4,256]{2,1,0:T(4,128)}, u32[]{:S(2)}) copy-start(f32[4,4,256]{2,1,0:T(4,128)} %fusion.7) | copy-start | bytes 49156
  79.9 26.3 %copy-start.7 = (bf16[256,512]{0,1:T(8,128)(2,1)S(1)}, bf16[256,512]{0,1:T(8,128)(2,1)}, u32[]{:S(2)}) copy-start(bf16[256,512]{0,1:T(8,128)(2,1)} %copy.89) | copy-start | bytes 786436
  81.4 26.0 %copy-start.1 = (f32[4,256,256,4]{2,1,3,0:T(8,128)S(1)}, f32[4,256,256,4]{2,1,3,0:T(8,128)}, u32[]{:S(2)}) copy-start(f32[4,256,256,4]{2,1,3,0:T(8,128)} %get-tuple-element.36) | copy-start | bytes 12582916
  81.5 26.0 %copy-start.9 = (f32[4,4,256]{2,1,0:T(4,128)S(1)}, f32[4,4,256]{2,1,0:T(4,128)}, u32[]{:S(2)}) copy-start(f32[4,4,256]{2,1,0:T(4,128)} %copy-done.8) | copy-start | bytes 49156
  102.0 66.2 %collective-permute-start.12 = (bf16[512,2048]{1,0:T(8,128)(2,1)}, bf16[512,2048]{1,0:T(8,128)(2,1)}, u32[]{:S(2)}, u32[]{:S(2)}) collective-permute-start(bf16[512,2048]{1,0:T(8,128)(2,1)} %collective-permute-done.10), channel_id=1, source_target_pairs={{0,2},{4,0},{8,4},{12,8},{14,12},{10,14},{6,10},{2,6},{1,3},{5,1},... | collective-permute-start | bytes 6291464 | tf_op jit(solution)/shard_map/ppermute | solution.py:120
  106.1 4.3 %copy-start.5 = (bf16[512,2048]{1,0:T(8,128)(2,1)}, bf16[512,2048]{1,0:T(8,128)(2,1)S(1)}, u32[]{:S(2)}) copy-start(bf16[512,2048]{1,0:T(8,128)(2,1)S(1)} %collective-permute-done.9) | copy-start | bytes 6291460
  106.1 62.1 %collective-permute-start.11 = (bf16[512,2048]{1,0:T(8,128)(2,1)S(1)}, bf16[512,2048]{1,0:T(8,128)(2,1)}, u32[]{:S(2)}, u32[]{:S(2)}) collective-permute-start(bf16[512,2048]{1,0:T(8,128)(2,1)S(1)} %collective-permute-done.9), channel_id=1, source_target_pairs={{0,4},{4,8},{8,12},{12,14},{14,10},{10,6},{6,2},{2,0},{1,5},{5,9},... | collective-permute-start | bytes 6291464 | tf_op jit(solution)/shard_map/ppermute | solution.py:117
  107.5 63.2 %copy-start.20 = (s32[8]{0:T(128)S(1)}, s32[8]{0:T(128)}, u32[]{:S(2)}) copy-start(s32[8]{0:T(128)} %constant.172.clone) | copy-start | bytes 100
  107.5 68.4 %copy-start.19 = (s32[8]{0:T(128)S(1)}, s32[8]{0:T(128)}, u32[]{:S(2)}) copy-start(s32[8]{0:T(128)} %constant.173.clone) | copy-start | bytes 100
  110.4 70.6 %collective-permute-start.8 = (bf16[256,2048]{0,1:T(8,128)(2,1)}, bf16[256,2048]{0,1:T(8,128)(2,1)}, u32[]{:S(2)}, u32[]{:S(2)}) collective-permute-start(bf16[256,2048]{0,1:T(8,128)(2,1)} %bitcast.44), channel_id=1, source_target_pairs={{0,1},{1,0},{2,3},{3,2},{4,5},{5,4},{6,7},{7,6},{8,9},{9,8},{10,11... | collective-permute-start | bytes 3145736 | tf_op jit(solution)/shard_map/ppermute | solution.py:77
  168.2 47.7 %collective-permute-start.13 = (bf16[512,2048]{1,0:T(8,128)(2,1)}, bf16[512,2048]{1,0:T(8,128)(2,1)}, u32[]{:S(2)}, u32[]{:S(2)}) collective-permute-start(bf16[512,2048]{1,0:T(8,128)(2,1)} %collective-permute-done.11), channel_id=1, source_target_pairs={{0,4},{4,8},{8,12},{12,14},{14,10},{10,6},{6,2},{2,0},{1,5},{5,9},... | collective-permute-start | bytes 6291464 | tf_op jit(solution)/shard_map/ppermute | solution.py:117
  168.2 49.1 %collective-permute-start.14 = (bf16[512,2048]{1,0:T(8,128)(2,1)}, bf16[512,2048]{1,0:T(8,128)(2,1)S(1)}, u32[]{:S(2)}, u32[]{:S(2)}) collective-permute-start(bf16[512,2048]{1,0:T(8,128)(2,1)} %collective-permute-done.12), channel_id=1, source_target_pairs={{0,2},{4,0},{8,4},{12,8},{14,12},{10,14},{6,10},{2,6},{1,3},{5,1},... | collective-permute-start | bytes 6291464 | tf_op jit(solution)/shard_map/ppermute | solution.py:120
  181.0 2.2 copy-start.6
  217.2 23.7 %collective-permute-start.15 = (bf16[512,1024]{1,0:T(8,128)(2,1)S(1)}, bf16[512,1024]{1,0:T(8,128)(2,1)S(1)}, u32[]{:S(2)}, u32[]{:S(2)}) collective-permute-start(bf16[512,1024]{1,0:T(8,128)(2,1)S(1)} %slice.8), channel_id=1, source_target_pairs={{0,4},{4,8},{8,12},{12,14},{14,10},{10,6},{6,2},{2,0},{1,5},{5,9},... | collective-permute-start | bytes 3145736 | tf_op jit(solution)/shard_map/ppermute | solution.py:112
  217.4 24.0 %collective-permute-start.16 = (bf16[512,1024]{1,0:T(8,128)(2,1)S(1)}, bf16[512,1024]{1,0:T(8,128)(2,1)S(1)}, u32[]{:S(2)}, u32[]{:S(2)}) collective-permute-start(bf16[512,1024]{1,0:T(8,128)(2,1)S(1)} %slice.9), channel_id=1, source_target_pairs={{0,2},{4,0},{8,4},{12,8},{14,12},{10,14},{6,10},{2,6},{1,3},{5,1},... | collective-permute-start | bytes 3145736 | tf_op jit(solution)/shard_map/ppermute | solution.py:113

commit v4 on v2

--- a/solution.py
+++ b/solution.py
@@ -85,35 +85,63 @@
     return jnp.concatenate(pieces, axis=1)
 
 
-def ring_project(features, out_weight):
+def ring_transfer(out_weight):
     count = lax.axis_size("ctx")
-    order = [i for i in range(0, count, 2)] + sorted(range(1, count, 2), reverse=True)
+    order = list(range(0, count, 2)) + sorted(range(1, count, 2), reverse=True)
     position_of = [0] * count
     for position, index in enumerate(order):
         position_of[index] = position
     ctx_index = lax.axis_index("ctx")
     position = jnp.asarray(position_of, jnp.int32)[ctx_index]
     order_table = jnp.asarray(order, jnp.int32)
-    rows = out_weight.shape[0]
+    columns = out_weight.shape[1]
+    groups = lax.axis_size("group")
+    group_index = lax.axis_index("group")
+    own = (columns // 3) // 128 * 128 if groups == 2 else 0
+    shared = columns - groups * own if own else columns
+    swap = [(0, 1), (1, 0)]
 
-    def term(block, source):
-        piece = lax.dynamic_slice_in_dim(features, source * rows, rows, 1)
-        return jnp.dot(piece, block, preferred_element_type=jnp.float32)
+    def carried(block):
+        if not own:
+            return block
+        mine = lax.dynamic_slice_in_dim(block, shared + group_index * own, own, 1)
+        return jnp.concatenate([block[:, :shared], mine], axis=1)
 
-    mixed = term(out_weight, ctx_index)
+    def other_of(block):
+        return lax.dynamic_slice_in_dim(block, shared + (1 - group_index) * own, own, 1)
+
+    arrivals = [(ctx_index, carried(out_weight), other_of(out_weight) if own else None)]
     ahead = [(order[p], order[(p + 1) % count]) for p in range(count)]
     behind = [(order[p], order[(p - 1) % count]) for p in range(count)]
-    forward = backward = out_weight
+    forward = backward = carried(out_weight)
     forward_steps = count // 2
     backward_steps = count - 1 - forward_steps
     for step in range(1, forward_steps + 1):
         forward = lax.ppermute(forward, "ctx", ahead)
-        mixed = mixed + term(forward, order_table[(position + count - step) % count])
+        crossed = lax.ppermute(forward[:, shared:], "group", swap) if own else None
+        arrivals.append((order_table[(position + count - step) % count], forward, crossed))
         if step <= backward_steps:
             backward = lax.ppermute(backward, "ctx", behind)
-            mixed = mixed + term(backward, order_table[(position + step) % count])
-    return mixed
+            crossed = lax.ppermute(backward[:, shared:], "group", swap) if own else None
+            arrivals.append((order_table[(position + step) % count], backward, crossed))
+    return arrivals, shared, own
 
+
+def ring_project(features, arrivals, shared, own, rows):
+    group_index = lax.axis_index("group")
+    parts = None
+    for source, carried_block, crossed in arrivals:
+        piece = lax.dynamic_slice_in_dim(features, source * rows, rows, 1)
+        terms = [jnp.dot(piece, carried_block, preferred_element_type=jnp.float32)]
+        if own:
+            terms.append(jnp.dot(piece, crossed, preferred_element_type=jnp.float32))
+        parts = terms if parts is None else [a + b for a, b in zip(parts, terms)]
+    if not own:
+        return parts[0]
+    mine, other = parts[0][:, shared:], parts[1]
+    first = jnp.where(group_index == 0, mine, other)
+    second = jnp.where(group_index == 0, other, mine)
+    return jnp.concatenate([parts[0][:, :shared], first, second], axis=1)
 
 def per_device(queries, keys, values, doc_of_block, out_weight):
     tok_rows = queries.shape[0]
@@ -136,6 +164,7 @@
         )
         return update(state_now, query_head_rows, key_piece, value_piece, visible)
 
+    arrivals, shared, own = ring_transfer(out_weight)
     initial_state = fresh_state(kv_heads, group_width, tok_rows)
     state_now = attend(initial_state, keys, values, query_start)
     for distance in range(1, reach_devs + 1):
@@ -143,7 +172,7 @@
         state_now = attend(state_now, prior_keys, prior_values, query_start - distance * tok_rows)
     attended = finish(state_now, tok_rows, q_heads)
     features = head_features(attended)
-    mixed = ring_project(features, out_weight)
+    mixed = ring_project(features, arrivals, shared, own, out_weight.shape[0])
     return mixed.astype(jnp.bfloat16)
 
 

time: 238 us -> 222 us (0.933)
  waiting for transfers between devices: 115 us -> 78.9 us
  matrix products: 46.2 us -> 56.1 us
  local copies, waits for them, and re-layouts: 11.1 us -> 17.2 us
  starting transfers between devices: 45.5 us -> 49.3 us
    ppermute x8, waiting for transfers between devices: 29 us -> 0.02 us  [passed_along(): return lax.ppermute(array, axis, pairs)]
    ppermute x7 -> x14, waiting for transfers between devices: 86.2 us -> 78.8 us  [the longest x4 35.4 us: ring_transfer(): forward = lax.ppermute(forward, 'ctx', ahead)]
    ppermute x7 -> x14, starting transfers between devices: 17.8 us -> 24.6 us  [the longest x3 10.3 us: ring_transfer(): backward = lax.ppermute(backward, 'ctx', behind)]
    slice x0 -> x9, local copies, waits for them, and re-layouts: none -> 4.88 us  [the longest x4 2.41 us: ring_transfer(): crossed = lax.ppermute(forward[:, shared:], 'group', swap) if own else None]
    dot_general x5, matrix products: 19.1 us -> 23.5 us  [update(): jnp.einsum('hgqk,khd->hgqd', weights.astype(jnp.bfloat16), value_head_row...]
    dot_general x5, matrix products: 9.07 us -> 12.7 us  [update(): jnp.einsum('qhgd,khd->hgqk', query_head_rows, key_head_rows, preferred_el...]
    ppermute x8, starting transfers between devices: 27.6 us -> 24.6 us  [passed_along(): return lax.ppermute(array, axis, pairs)]
    dot_general x8 -> x16, matrix products: 18.1 us -> 19.9 us  [the longest x8 12.1 us: ring_project(): terms = [jnp.dot(piece, carried_block, preferred_element_type=jnp.float32)]]
  transfers between devices with their start and end apart: 16 -> 23, of which waited for: 5 -> 9; matrix products, arithmetic and copies ran while one was open for 26% -> 35% of each run, Pallas kernels for 0% -> 0%
where the time goes in v4:
time: 222 us; the launch traced here: 221 us
  waiting for transfers between devices  78.9 us (36%)
  matrix products  56.1 us (25%)
  starting transfers between devices  49.3 us (22%)
  local copies, waits for them, and re-layouts  17.2 us (8%)
  other arithmetic  9.87 us (4%)
  between operations  9.57 us (4%)
    ppermute x4, waiting for transfers between devices, ring_transfer(): forward = lax.ppermute(forward, 'ctx', ahead)  35.4 us
    ppermute x8, starting transfers between devices, passed_along(): return lax.ppermute(array, axis, pairs)  24.6 us
    ppermute x3, waiting for transfers between devices, ring_transfer(): crossed = lax.ppermute(backward[:, shared:], 'group', swap) if own else None  24.4 us
    dot_general x5, matrix products, update(): jnp.einsum('hgqk,khd->hgqd', weights.astype(jnp.bfloat16), value_head_row...  23.5 us
    dot_general x5, matrix products, update(): jnp.einsum('qhgd,khd->hgqk', query_head_rows, key_head_rows, preferred_el...  12.7 us
    dot_general x8, matrix products, ring_project(): terms = [jnp.dot(piece, carried_block, preferred_element_type=jnp.float32)]  12.1 us
    ppermute x4, waiting for transfers between devices, ring_transfer(): crossed = lax.ppermute(forward[:, shared:], 'group', swap) if own else None  11.6 us
    ppermute x3, starting transfers between devices, ring_transfer(): backward = lax.ppermute(backward, 'ctx', behind)  10.3 us
  transfers between devices with their start and end apart: 23, of which 9 were waited for; matrix products, arithmetic and copies ran while one was open for 35% of the time, Pallas kernels for 0%

profile of v4, /device:TPU:0, one launch (start us, length us, event | category | flops | bytes accessed | tf_op | source)
XLA Modules:
  0.0 220.9 jit_solution(13090258058370153806)
XLA Ops:
  0.0 1.9 copy.52
  1.9 6.7 %collective-permute-start.6 = (bf16[256,512]{0,1:T(8,128)(2,1)}, bf16[256,512]{0,1:T(8,128)(2,1)}, u32[]{:S(2)}, u32[]{:S(2)}) collective-permute-start(bf16[256,512]{0,1:T(8,128)(2,1)} %copy.52), channel_id=1, source_target_pairs={{0,8},{2,10},{4,12},{6,14},{1,9},{3,11},{5,13},{7,15},{16,24},{18,... | collective-permute-start | bytes 786440 | tf_op jit(solution)/shard_map/ppermute | solution.py:15
  8.6 5.1 %collective-permute-start.4 = (bf16[256,512]{0,1:T(8,128)(2,1)}, bf16[256,512]{0,1:T(8,128)(2,1)}, u32[]{:S(2)}, u32[]{:S(2)}) collective-permute-start(bf16[256,512]{0,1:T(8,128)(2,1)} %copy.52), channel_id=1, source_target_pairs={{0,6},{2,8},{4,10},{6,12},{8,14},{1,7},{3,9},{5,11},{7,13},{9,15},... | collective-permute-start | bytes 786440 | tf_op jit(solution)/shard_map/ppermute | solution.py:15
  13.7 1.3 collective-permute-start.2
  15.0 2.4 %collective-permute-start = (bf16[256,512]{0,1:T(8,128)(2,1)}, bf16[256,512]{0,1:T(8,128)(2,1)S(1)}, u32[]{:S(2)}, u32[]{:S(2)}) collective-permute-start(bf16[256,512]{0,1:T(8,128)(2,1)} %copy.52), channel_id=1, source_target_pairs={{0,2},{2,4},{4,6},{6,8},{8,10},{10,12},{12,14},{1,3},{3,5},{5,7},{... | collective-permute-start | bytes 786440 | tf_op jit(solution)/shard_map/ppermute | solution.py:15
  17.4 2.7 %collective-permute-start.1 = (bf16[256,512]{1,0:T(8,128)(2,1)}, bf16[256,512]{1,0:T(8,128)(2,1)}, u32[]{:S(2)}, u32[]{:S(2)}) collective-permute-start(bf16[256,512]{1,0:T(8,128)(2,1)} %param.9), channel_id=1, source_target_pairs={{0,2},{2,4},{4,6},{6,8},{8,10},{10,12},{12,14},{1,3},{3,5},{5,7},{... | collective-permute-start | bytes 786440 | tf_op jit(solution)/shard_map/ppermute | solution.py:15
  21.8 1.8 copy.89
  24.4 1.2 slice.32
  25.6 1.2 constant_dynamic-slice_fusion
  26.8 1.2 compare_and_fusion.4
  29.1 1.3 pad_maximum_fusion
  30.3 2.0 collective-permute-start.3
  32.3 3.9 %fusion.4 = (f32[4,4,256]{2,1,0:T(4,128)S(1)}, f32[4,256,256,4]{2,1,3,0:T(8,128)}) fusion(pred[256,256]{0,1:T(8,128)(4,1)S(1)} %get-tuple-element.29, bf16[256,4,128,1]{0,2,3,1:T(8,128)(2,1)} %bitcast.74, bf16[256,4,4,128]{3,2,1,0:T(4,128)(2,1)S(1)} %reshape.293), kind=kOutput, calls=%fused_computation.30 | convolution fusion | flops 271577088 | bytes 5586944 | tf_op jit(solution)/shard_map/qhgd,khd->hgqk/dot_general | solution.py:33
  36.2 2.0 collective-permute-start.5
  38.3 3.9 %fusion.3 = (f32[4,4,256]{2,1,0:T(4,128)S(1)}, f32[4,256,256,4]{2,1,3,0:T(8,128)}) fusion(pred[256,256]{0,1:T(8,128)(4,1)S(1)} %get-tuple-element.27, bf16[256,4,128,1]{0,2,3,1:T(8,128)(2,1)} %bitcast.70, bf16[256,4,4,128]{3,2,1,0:T(4,128)(2,1)S(1)} %reshape.293), kind=kOutput, calls=%fused_computation.29 | convolution fusion | flops 271577088 | bytes 5586944 | tf_op jit(solution)/shard_map/qhgd,khd->hgqk/dot_general | solution.py:33
  42.2 2.4 %collective-permute-start.7 = (bf16[256,512]{1,0:T(8,128)(2,1)S(1)}, bf16[256,512]{1,0:T(8,128)(2,1)}, u32[]{:S(2)}, u32[]{:S(2)}) collective-permute-start(bf16[256,512]{1,0:T(8,128)(2,1)S(1)} %copy-done.5), channel_id=1, source_target_pairs={{0,8},{2,10},{4,12},{6,14},{1,9},{3,11},{5,13},{7,15},{16,24},{18,... | collective-permute-start | bytes 786440 | tf_op jit(solution)/shard_map/ppermute | solution.py:15
  44.5 3.0 %fusion.2 = (f32[4,4,256]{2,1,0:T(4,128)S(1)}, f32[4,256,256,4]{2,1,3,0:T(8,128)}) fusion(pred[256,256]{0,1:T(8,128)(4,1)S(1)} %get-tuple-element.28, bf16[256,4,128,1]{0,2,3,1:T(8,128)(2,1)S(1)} %bitcast.272, bf16[256,4,4,128]{3,2,1,0:T(4,128)(2,1)S(1)} %reshape.293), kind=kOutput, calls=%fused_computation.28 | convolution fusion | flops 271577088 | bytes 5586944 | tf_op jit(solution)/shard_map/qhgd,khd->hgqk/dot_general | solution.py:33
  47.5 1.3 collective-permute-start.9
  51.1 2.6 %fusion.26 = f32[4,4,256,128]{2,3,1,0:T(8,128)} fusion(bf16[256,4,128,1]{0,2,3,1:T(8,128)(2,1)S(1)} %bitcast.273, f32[4,256,256,4]{2,1,3,0:T(8,128)S(1)} %get-tuple-element.46, f32[4,4,256]{2,1,0:T(4,128)S(1)} %get-tuple-element.24, pred[256,256]{0,1:T(8,128)(4,1)S(1)} %get-tuple-element.25), kind=kOutput, calls=%fused_computation.52 | convolution fusion | flops 273678336 | bytes 6635520 | tf_op jit(solution)/shard_map/hgqk,khd->hgqd/dot_general | solution.py:42
  56.8 4.8 %fusion.24 = f32[4,4,256,128]{2,3,1,0:T(8,128)} fusion(bf16[256,4,128,1]{0,2,3,1:T(8,128)(2,1)S(1)} %bitcast.275, f32[4,256,256,4]{2,1,3,0:T(8,128)} %copy-done.3, f32[4,4,256]{2,1,0:T(4,128)S(1)} %get-tuple-element.17, pred[256,256]{0,1:T(8,128)(4,1)S(1)} %get-tuple-element.26), kind=kOutput, calls=%fused_computation.51 | convolution fusion | flops 273678336 | bytes 6635520 | tf_op jit(solution)/shard_map/hgqk,khd->hgqd/dot_general | solution.py:42
  62.7 1.1 copy.60
  63.8 4.8 %fusion.22 = f32[4,4,256,128]{2,3,1,0:T(8,128)} fusion(bf16[256,4,128,1]{0,2,3,1:T(8,128)(2,1)S(1)} %bitcast.276, f32[4,256,256,4]{2,1,3,0:T(8,128)} %get-tuple-element.42, f32[4,4,256]{2,1,0:T(4,128)S(1)} %get-tuple-element.16, pred[256,256]{0,1:T(8,128)(4,1)S(1)} %get-tuple-element.28), kind=kOutput, calls=%fused_computation.50 | convolution fusion | flops 273678336 | bytes 6635520 | tf_op jit(solution)/shard_map/hgqk,khd->hgqd/dot_general | solution.py:42
  70.8 4.8 %fusion.20 = f32[4,4,256,128]{2,3,1,0:T(8,128)} fusion(bf16[256,4,128,1]{0,2,3,1:T(8,128)(2,1)S(1)} %bitcast.277, f32[4,256,256,4]{2,1,3,0:T(8,128)} %get-tuple-element.40, f32[4,4,256]{2,1,0:T(4,128)S(1)} %get-tuple-element.15, pred[256,256]{0,1:T(8,128)(4,1)S(1)} %get-tuple-element.27), kind=kOutput, calls=%fused_computation.49 | convolution fusion | flops 273678336 | bytes 6635520 | tf_op jit(solution)/shard_map/hgqk,khd->hgqd/dot_general | solution.py:42
  77.9 6.4 %fusion.29 = bf16[256,4,4,128]{0,3,2,1:T(8,128)(2,1)S(1)} fusion(f32[4,4,256,128]{2,3,1,0:T(8,128)} %fusion.20, f32[4,4,256,128]{2,3,1,0:T(8,128)} %fusion.22, f32[4,4,256,128]{2,3,1,0:T(8,128)} %fusion.24, f32[4,4,256,128]{2,3,1,0:T(8,128)} %fusion.26, f32[256,4,4]{0,2,1:T(4,128)S(1)} %get-tuple-element.10, f32[256,4,4]{0,2,1:T(4,128)S(1)} %get-tuple-element.13, ...), kind=kOutput, calls=%fused_computation.55 | convolution fusion | flops 279445504 | bytes 14073856 | tf_op jit(solution)/shard_map/hgqk,khd->hgqd/dot_general | solution.py:42
  84.4 2.7 %collective-permute-start.11 = (bf16[512,1408]{1,0:T(8,128)(2,1)}, bf16[512,1408]{1,0:T(8,128)(2,1)}, u32[]{:S(2)}, u32[]{:S(2)}) collective-permute-start(bf16[512,1408]{1,0:T(8,128)(2,1)} %collective-permute-done.9), channel_id=1, source_target_pairs={{0,4},{4,8},{8,12},{12,14},{14,10},{10,6},{6,2},{2,0},{1,5},{5,9},... | collective-permute-start | bytes 4325384 | tf_op jit(solution)/shard_map/ppermute | solution.py:120
  97.5 3.5 %collective-permute-start.12 = (bf16[512,1408]{1,0:T(8,128)(2,1)}, bf16[512,1408]{1,0:T(8,128)(2,1)S(1)}, u32[]{:S(2)}, u32[]{:S(2)}) collective-permute-start(bf16[512,1408]{1,0:T(8,128)(2,1)} %collective-permute-done.10), channel_id=1, source_target_pairs={{0,2},{4,0},{8,4},{12,8},{14,12},{10,14},{6,10},{2,6},{1,3},{5,1},... | collective-permute-start | bytes 4325384 | tf_op jit(solution)/shard_map/ppermute | solution.py:124
  101.2 1.1 slice.44
  102.3 1.6 collective-permute-start.16
  103.9 1.1 slice.45
  105.6 2.3 %fusion.134 = f32[256,1408]{1,0:T(8,128)S(1)} fusion(bf16[512,1408]{1,0:T(8,128)(2,1)} %collective-permute-done.9, s32[]{:T(128)S(6)} %select_n.237, bf16[256,2048]{0,1:T(8,128)(2,1)S(1)} %get-tuple-element.19, bf16[256,2048]{0,1:T(8,128)(2,1)S(1)} %get-tuple-element.18), kind=kOutput, calls=%fused_computation.212 | convolution fusion | flops 369623040 | bytes 4980740 | tf_op jit(solution)/shard_map/dot_general | solution.py:135
  108.0 15.0 %collective-permute-done.11 = bf16[512,1408]{1,0:T(8,128)(2,1)} collective-permute-done((bf16[512,1408]{1,0:T(8,128)(2,1)}, bf16[512,1408]{1,0:T(8,128)(2,1)}, u32[]{:S(2)}, u32[]{:S(2)}) %collective-permute-start.11) | collective-permute-done | bytes 1441824 | tf_op jit(solution)/shard_map/ppermute | solution.py:120
  123.0 1.2 collective-permute-start.13
  124.2 2.3 %fusion.130 = f32[256,1408]{1,0:T(8,128)S(1)} fusion(bf16[512,1408]{1,0:T(8,128)(2,1)} %collective-permute-done.10, s32[]{:T(128)S(6)} %select_n.240, bf16[256,2048]{0,1:T(8,128)(2,1)S(1)} %get-tuple-element.19, bf16[256,2048]{0,1:T(8,128)(2,1)S(1)} %get-tuple-element.18), kind=kOutput, calls=%fused_computation.210 | convolution fusion | flops 369623040 | bytes 4980740 | tf_op jit(solution)/shard_map/dot_general | solution.py:135
  127.6 7.4 %collective-permute-done.12 = bf16[512,1408]{1,0:T(8,128)(2,1)S(1)} collective-permute-done((bf16[512,1408]{1,0:T(8,128)(2,1)}, bf16[512,1408]{1,0:T(8,128)(2,1)S(1)}, u32[]{:S(2)}, u32[]{:S(2)}) %collective-permute-start.12) | collective-permute-done | bytes 1441824 | tf_op jit(solution)/shard_map/ppermute | solution.py:124
  135.0 5.8 %collective-permute-start.14 = (bf16[512,1408]{1,0:T(8,128)(2,1)S(1)}, bf16[512,1408]{1,0:T(8,128)(2,1)S(1)}, u32[]{:S(2)}, u32[]{:S(2)}) collective-permute-start(bf16[512,1408]{1,0:T(8,128)(2,1)S(1)} %collective-permute-done.12), channel_id=1, source_target_pairs={{0,2},{4,0},{8,4},{12,8},{14,12},{10,14},{6,10},{2,6},{1,3},{5,1},... | collective-permute-start | bytes 4325384 | tf_op jit(solution)/shard_map/ppermute | solution.py:124
  142.4 1.1 slice.46
  143.6 1.6 collective-permute-start.18
  146.8 9.7 %collective-permute-done.13 = bf16[512,1408]{1,0:T(8,128)(2,1)S(1)} collective-permute-done((bf16[512,1408]{1,0:T(8,128)(2,1)}, bf16[512,1408]{1,0:T(8,128)(2,1)S(1)}, u32[]{:S(2)}, u32[]{:S(2)}) %collective-permute-start.13) | collective-permute-done | bytes 1441824 | tf_op jit(solution)/shard_map/ppermute | solution.py:120
  157.6 2.4 %fusion.16 = f32[256,1408]{1,0:T(8,128)S(1)} fusion(f32[256,1408]{1,0:T(8,128)S(1)} %fusion.123, f32[256,1408]{1,0:T(8,128)S(1)} %fusion.17, bf16[512,1408]{1,0:T(8,128)(2,1)} %collective-permute-done.11, s32[]{:T(128)S(6)} %select_n.243, bf16[256,2048]{0,1:T(8,128)(2,1)S(1)} %get-tuple-element.19, bf16[256,2048]{0,1:T(8,128)(2,1)S(1)} %get-tuple-element.18), kind=kOutput, calls=%fused_computation.45 | convolution fusion | flops 370343936 | bytes 7864324 | tf_op jit(solution)/shard_map/dot_general | solution.py:135
  160.0 1.3 collective-permute-done.18
  162.1 11.1 %collective-permute-done.19 = bf16[512,640]{1,0:T(8,128)(2,1)S(1)} collective-permute-done((bf16[512,640]{1,0:T(8,128)(2,1)S(1)}, bf16[512,640]{1,0:T(8,128)(2,1)S(1)}, u32[]{:S(2)}, u32[]{:S(2)}) %collective-permute-start.19) | collective-permute-done | bytes 655392 | tf_op jit(solution)/shard_map/ppermute | solution.py:125
  174.1 1.6 collective-permute-start.20
  178.4 10.7 %collective-permute-done.15 = bf16[512,1408]{1,0:T(8,128)(2,1)S(1)} collective-permute-done((bf16[512,1408]{1,0:T(8,128)(2,1)S(1)}, bf16[512,1408]{1,0:T(8,128)(2,1)S(1)}, u32[]{:S(2)}, u32[]{:S(2)}) %collective-permute-start.15) | collective-permute-done | bytes 1441824 | tf_op jit(solution)/shard_map/ppermute | solution.py:120
  189.1 1.6 collective-permute-start.22
  192.6 13.2 %collective-permute-done.21 = bf16[512,640]{1,0:T(8,128)(2,1)S(1)} collective-permute-done((bf16[512,640]{1,0:T(8,128)(2,1)S(1)}, bf16[512,640]{1,0:T(8,128)(2,1)S(1)}, u32[]{:S(2)}, u32[]{:S(2)}) %collective-permute-start.21) | collective-permute-done | bytes 655392 | tf_op jit(solution)/shard_map/ppermute | solution.py:125
  207.7 9.2 %collective-permute-done.22 = bf16[512,640]{1,0:T(8,128)(2,1)S(1)} collective-permute-done((bf16[512,640]{1,0:T(8,128)(2,1)S(1)}, bf16[512,640]{1,0:T(8,128)(2,1)S(1)}, u32[]{:S(2)}, u32[]{:S(2)}) %collective-permute-start.22) | collective-permute-done | bytes 655392 | tf_op jit(solution)/shard_map/ppermute | solution.py:121
  217.7 2.1 select_convert_fusion.1
  219.8 1.1 pad_maximum_fusion.1
  (93 shorter events, 30.5 us)
Async XLA Ops:
  0.0 23.6 %copy-start.4 = (bf16[256,2048]{1,0:T(8,128)(2,1)S(1)}, bf16[256,2048]{1,0:T(8,128)(2,1)}, u32[]{:S(2)}) copy-start(bf16[256,2048]{1,0:T(8,128)(2,1)} %param.7) | copy-start | bytes 3145732
  1.9 28.5 %collective-permute-start.6 = (bf16[256,512]{0,1:T(8,128)(2,1)}, bf16[256,512]{0,1:T(8,128)(2,1)}, u32[]{:S(2)}, u32[]{:S(2)}) collective-permute-start(bf16[256,512]{0,1:T(8,128)(2,1)} %copy.52), channel_id=1, source_target_pairs={{0,8},{2,10},{4,12},{6,14},{1,9},{3,11},{5,13},{7,15},{16,24},{18,... | collective-permute-start | bytes 786440 | tf_op jit(solution)/shard_map/ppermute | solution.py:15
  8.6 27.7 %collective-permute-start.4 = (bf16[256,512]{0,1:T(8,128)(2,1)}, bf16[256,512]{0,1:T(8,128)(2,1)}, u32[]{:S(2)}, u32[]{:S(2)}) collective-permute-start(bf16[256,512]{0,1:T(8,128)(2,1)} %copy.52), channel_id=1, source_target_pairs={{0,6},{2,8},{4,10},{6,12},{8,14},{1,7},{3,9},{5,11},{7,13},{9,15},... | collective-permute-start | bytes 786440 | tf_op jit(solution)/shard_map/ppermute | solution.py:15
  13.7 28.5 %collective-permute-start.2 = (bf16[256,512]{0,1:T(8,128)(2,1)}, bf16[256,512]{0,1:T(8,128)(2,1)S(1)}, u32[]{:S(2)}, u32[]{:S(2)}) collective-permute-start(bf16[256,512]{0,1:T(8,128)(2,1)} %copy.52), channel_id=1, source_target_pairs={{0,4},{2,6},{4,8},{6,10},{8,12},{10,14},{1,5},{3,7},{5,9},{7,11},{... | collective-permute-start | bytes 786440 | tf_op jit(solution)/shard_map/ppermute | solution.py:15
  15.0 32.5 %collective-permute-start = (bf16[256,512]{0,1:T(8,128)(2,1)}, bf16[256,512]{0,1:T(8,128)(2,1)S(1)}, u32[]{:S(2)}, u32[]{:S(2)}) collective-permute-start(bf16[256,512]{0,1:T(8,128)(2,1)} %copy.52), channel_id=1, source_target_pairs={{0,2},{2,4},{4,6},{6,8},{8,10},{10,12},{12,14},{1,3},{3,5},{5,7},{... | collective-permute-start | bytes 786440 | tf_op jit(solution)/shard_map/ppermute | solution.py:15
  17.4 37.3 %collective-permute-start.1 = (bf16[256,512]{1,0:T(8,128)(2,1)}, bf16[256,512]{1,0:T(8,128)(2,1)}, u32[]{:S(2)}, u32[]{:S(2)}) collective-permute-start(bf16[256,512]{1,0:T(8,128)(2,1)} %param.9), channel_id=1, source_target_pairs={{0,2},{2,4},{4,6},{6,8},{8,10},{10,12},{12,14},{1,3},{3,5},{5,7},{... | collective-permute-start | bytes 786440 | tf_op jit(solution)/shard_map/ppermute | solution.py:15
  23.6 3.1 %copy-start.14 = (s32[16]{0:T(128)S(1)}, s32[16]{0:T(128)}, u32[]{:S(2)}) copy-start(s32[16]{0:T(128)} %param.10) | copy-start | bytes 196
  29.1 1.3 copy-start.5
  30.3 32.4 %collective-permute-start.3 = (bf16[256,512]{1,0:T(8,128)(2,1)S(1)}, bf16[256,512]{1,0:T(8,128)(2,1)}, u32[]{:S(2)}, u32[]{:S(2)}) collective-permute-start(bf16[256,512]{1,0:T(8,128)(2,1)S(1)} %copy-done.5), channel_id=1, source_target_pairs={{0,4},{2,6},{4,8},{6,10},{8,12},{10,14},{1,5},{3,7},{5,9},{7,11},{... | collective-permute-start | bytes 786440 | tf_op jit(solution)/shard_map/ppermute | solution.py:15
  36.2 13.6 %copy-start.7 = (f32[4,4,256]{2,1,0:T(4,128)}, f32[4,4,256]{2,1,0:T(4,128)S(1)}, u32[]{:S(2)}) copy-start(f32[4,4,256]{2,1,0:T(4,128)S(1)} %get-tuple-element.37) | copy-start | bytes 49156
  36.2 33.5 %collective-permute-start.5 = (bf16[256,512]{1,0:T(8,128)(2,1)S(1)}, bf16[256,512]{1,0:T(8,128)(2,1)}, u32[]{:S(2)}, u32[]{:S(2)}) collective-permute-start(bf16[256,512]{1,0:T(8,128)(2,1)S(1)} %copy-done.5), channel_id=1, source_target_pairs={{0,6},{2,8},{4,10},{6,12},{8,14},{1,7},{3,9},{5,11},{7,13},{9,15},... | collective-permute-start | bytes 786440 | tf_op jit(solution)/shard_map/ppermute | solution.py:15
  42.2 7.7 %copy-start.9 = (f32[4,4,256]{2,1,0:T(4,128)}, f32[4,4,256]{2,1,0:T(4,128)S(1)}, u32[]{:S(2)}) copy-start(f32[4,4,256]{2,1,0:T(4,128)S(1)} %get-tuple-element.39) | copy-start | bytes 49156
  42.2 34.6 %collective-permute-start.7 = (bf16[256,512]{1,0:T(8,128)(2,1)S(1)}, bf16[256,512]{1,0:T(8,128)(2,1)}, u32[]{:S(2)}, u32[]{:S(2)}) collective-permute-start(bf16[256,512]{1,0:T(8,128)(2,1)S(1)} %copy-done.5), channel_id=1, source_target_pairs={{0,8},{2,10},{4,12},{6,14},{1,9},{3,11},{5,13},{7,15},{16,24},{18,... | collective-permute-start | bytes 786440 | tf_op jit(solution)/shard_map/ppermute | solution.py:15
  47.5 2.4 %copy-start.11 = (f32[4,4,256]{2,1,0:T(4,128)}, f32[4,4,256]{2,1,0:T(4,128)S(1)}, u32[]{:S(2)}) copy-start(f32[4,4,256]{2,1,0:T(4,128)S(1)} %get-tuple-element.41) | copy-start | bytes 49156
  47.5 36.9 %collective-permute-start.9 = (bf16[512,1408]{1,0:T(8,128)(2,1)}, bf16[512,1408]{1,0:T(8,128)(2,1)}, u32[]{:S(2)}, u32[]{:S(2)}) collective-permute-start(bf16[512,1408]{1,0:T(8,128)(2,1)} %pad_maximum_fusion), channel_id=1, source_target_pairs={{0,4},{4,8},{8,12},{12,14},{14,10},{10,6},{6,2},{2,0},{1,5},{5,9},... | collective-permute-start | bytes 4325384 | tf_op jit(solution)/shard_map/ppermute | solution.py:120
  49.9 3.8 %copy-start.3 = (f32[4,256,256,4]{2,1,3,0:T(8,128)}, f32[4,256,256,4]{2,1,3,0:T(8,128)S(1)}, u32[]{:S(2)}) copy-start(f32[4,256,256,4]{2,1,3,0:T(8,128)S(1)} %get-tuple-element.44) | copy-start | bytes 12582916
  49.9 1.2 copy-start.6
  54.7 42.7 %collective-permute-start.10 = (bf16[512,1408]{1,0:T(8,128)(2,1)}, bf16[512,1408]{1,0:T(8,128)(2,1)}, u32[]{:S(2)}, u32[]{:S(2)}) collective-permute-start(bf16[512,1408]{1,0:T(8,128)(2,1)} %pad_maximum_fusion), channel_id=1, source_target_pairs={{0,2},{4,0},{8,4},{12,8},{14,12},{10,14},{6,10},{2,6},{1,3},{5,1},... | collective-permute-start | bytes 4325384 | tf_op jit(solution)/shard_map/ppermute | solution.py:124
  56.8 4.9 %copy-start.2 = (f32[4,256,256,4]{2,1,3,0:T(8,128)S(1)}, f32[4,256,256,4]{2,1,3,0:T(8,128)}, u32[]{:S(2)}) copy-start(f32[4,256,256,4]{2,1,3,0:T(8,128)} %get-tuple-element.42) | copy-start | bytes 12582916
  63.8 4.9 %copy-start.1 = (f32[4,256,256,4]{2,1,3,0:T(8,128)S(1)}, f32[4,256,256,4]{2,1,3,0:T(8,128)}, u32[]{:S(2)}) copy-start(f32[4,256,256,4]{2,1,3,0:T(8,128)} %get-tuple-element.40) | copy-start | bytes 12582916
  70.8 4.8 %copy-start = (f32[4,256,256,4]{2,1,3,0:T(8,128)S(1)}, f32[4,256,256,4]{2,1,3,0:T(8,128)}, u32[]{:S(2)}) copy-start(f32[4,256,256,4]{2,1,3,0:T(8,128)} %get-tuple-element.38) | copy-start | bytes 12582916
  75.6 1.1 copy-start.8
  75.6 1.1 copy-start.10
  75.6 1.1 copy-start.12
  77.9 9.2 %copy-start.15 = (s32[8]{0:T(128)S(1)}, s32[8]{0:T(128)}, u32[]{:S(2)}) copy-start(s32[8]{0:T(128)} %constant.183.clone) | copy-start | bytes 100
  77.9 14.5 %copy-start.13 = (s32[8]{0:T(128)S(1)}, s32[8]{0:T(128)}, u32[]{:S(2)}) copy-start(s32[8]{0:T(128)} %constant.184.clone) | copy-start | bytes 100
  84.3 16.7 %collective-permute-start.8 = (bf16[256,2048]{0,1:T(8,128)(2,1)S(1)}, bf16[256,2048]{0,1:T(8,128)(2,1)S(1)}, u32[]{:S(2)}, u32[]{:S(2)}) collective-permute-start(bf16[256,2048]{0,1:T(8,128)(2,1)S(1)} %bitcast.269), channel_id=1, source_target_pairs={{0,1},{1,0},{2,3},{3,2},{4,5},{5,4},{6,7},{7,6},{8,9},{9,8},{10,11... | collective-permute-start | bytes 3145736 | tf_op jit(solution)/shard_map/ppermute | solution.py:77
  84.4 38.6 %collective-permute-start.11 = (bf16[512,1408]{1,0:T(8,128)(2,1)}, bf16[512,1408]{1,0:T(8,128)(2,1)}, u32[]{:S(2)}, u32[]{:S(2)}) collective-permute-start(bf16[512,1408]{1,0:T(8,128)(2,1)} %collective-permute-done.9), channel_id=1, source_target_pairs={{0,4},{4,8},{8,12},{12,14},{14,10},{10,6},{6,2},{2,0},{1,5},{5,9},... | collective-permute-start | bytes 4325384 | tf_op jit(solution)/shard_map/ppermute | solution.py:120
  97.5 37.5 %collective-permute-start.12 = (bf16[512,1408]{1,0:T(8,128)(2,1)}, bf16[512,1408]{1,0:T(8,128)(2,1)S(1)}, u32[]{:S(2)}, u32[]{:S(2)}) collective-permute-start(bf16[512,1408]{1,0:T(8,128)(2,1)} %collective-permute-done.10), channel_id=1, source_target_pairs={{0,2},{4,0},{8,4},{12,8},{14,12},{10,14},{6,10},{2,6},{1,3},{5,1},... | collective-permute-start | bytes 4325384 | tf_op jit(solution)/shard_map/ppermute | solution.py:124
  102.3 38.5 %collective-permute-start.16 = (bf16[512,640]{1,0:T(8,128)(2,1)S(1)}, bf16[512,640]{1,0:T(8,128)(2,1)S(1)}, u32[]{:S(2)}, u32[]{:S(2)}) collective-permute-start(bf16[512,640]{1,0:T(8,128)(2,1)S(1)} %slice.44), channel_id=1, source_target_pairs={{0,16},{16,0},{1,17},{17,1},{2,18},{18,2},{3,19},{19,3},{4,20},{20... | collective-permute-start | bytes 1966088 | tf_op jit(solution)/shard_map/ppermute | solution.py:121
  105.1 36.5 %collective-permute-start.17 = (bf16[512,640]{1,0:T(8,128)(2,1)S(1)}, bf16[512,640]{1,0:T(8,128)(2,1)S(1)}, u32[]{:S(2)}, u32[]{:S(2)}) collective-permute-start(bf16[512,640]{1,0:T(8,128)(2,1)S(1)} %slice.45), channel_id=1, source_target_pairs={{0,16},{16,0},{1,17},{17,1},{2,18},{18,2},{3,19},{19,3},{4,20},{20... | collective-permute-start | bytes 1966088 | tf_op jit(solution)/shard_map/ppermute | solution.py:125
  123.0 33.6 %collective-permute-start.13 = (bf16[512,1408]{1,0:T(8,128)(2,1)}, bf16[512,1408]{1,0:T(8,128)(2,1)S(1)}, u32[]{:S(2)}, u32[]{:S(2)}) collective-permute-start(bf16[512,1408]{1,0:T(8,128)(2,1)} %collective-permute-done.11), channel_id=1, source_target_pairs={{0,4},{4,8},{8,12},{12,14},{14,10},{10,6},{6,2},{2,0},{1,5},{5,9},... | collective-permute-start | bytes 4325384 | tf_op jit(solution)/shard_map/ppermute | solution.py:120
  135.0 40.7 %collective-permute-start.14 = (bf16[512,1408]{1,0:T(8,128)(2,1)S(1)}, bf16[512,1408]{1,0:T(8,128)(2,1)S(1)}, u32[]{:S(2)}, u32[]{:S(2)}) collective-permute-start(bf16[512,1408]{1,0:T(8,128)(2,1)S(1)} %collective-permute-done.12), channel_id=1, source_target_pairs={{0,2},{4,0},{8,4},{12,8},{14,12},{10,14},{6,10},{2,6},{1,3},{5,1},... | collective-permute-start | bytes 4325384 | tf_op jit(solution)/shard_map/ppermute | solution.py:124
  143.6 17.7 %collective-permute-start.18 = (bf16[512,640]{1,0:T(8,128)(2,1)S(1)}, bf16[512,640]{1,0:T(8,128)(2,1)S(1)}, u32[]{:S(2)}, u32[]{:S(2)}) collective-permute-start(bf16[512,640]{1,0:T(8,128)(2,1)S(1)} %slice.46), channel_id=1, source_target_pairs={{0,16},{16,0},{1,17},{17,1},{2,18},{18,2},{3,19},{19,3},{4,20},{20... | collective-permute-start | bytes 1966088 | tf_op jit(solution)/shard_map/ppermute | solution.py:121
  145.2 28.0 %collective-permute-start.19 = (bf16[512,640]{1,0:T(8,128)(2,1)S(1)}, bf16[512,640]{1,0:T(8,128)(2,1)S(1)}, u32[]{:S(2)}, u32[]{:S(2)}) collective-permute-start(bf16[512,640]{1,0:T(8,128)(2,1)S(1)} %slice.47), channel_id=1, source_target_pairs={{0,16},{16,0},{1,17},{17,1},{2,18},{18,2},{3,19},{19,3},{4,20},{20... | collective-permute-start | bytes 1966088 | tf_op jit(solution)/shard_map/ppermute | solution.py:125
  156.6 32.5 %collective-permute-start.15 = (bf16[512,1408]{1,0:T(8,128)(2,1)S(1)}, bf16[512,1408]{1,0:T(8,128)(2,1)S(1)}, u32[]{:S(2)}, u32[]{:S(2)}) collective-permute-start(bf16[512,1408]{1,0:T(8,128)(2,1)S(1)} %collective-permute-done.13), channel_id=1, source_target_pairs={{0,4},{4,8},{8,12},{12,14},{14,10},{10,6},{6,2},{2,0},{1,5},{5,9},... | collective-permute-start | bytes 4325384 | tf_op jit(solution)/shard_map/ppermute | solution.py:120
  174.1 17.7 %collective-permute-start.20 = (bf16[512,640]{1,0:T(8,128)(2,1)S(1)}, bf16[512,640]{1,0:T(8,128)(2,1)S(1)}, u32[]{:S(2)}, u32[]{:S(2)}) collective-permute-start(bf16[512,640]{1,0:T(8,128)(2,1)S(1)} %slice.48), channel_id=1, source_target_pairs={{0,16},{16,0},{1,17},{17,1},{2,18},{18,2},{3,19},{19,3},{4,20},{20... | collective-permute-start | bytes 1966088 | tf_op jit(solution)/shard_map/ppermute | solution.py:121
  175.7 30.1 %collective-permute-start.21 = (bf16[512,640]{1,0:T(8,128)(2,1)S(1)}, bf16[512,640]{1,0:T(8,128)(2,1)S(1)}, u32[]{:S(2)}, u32[]{:S(2)}) collective-permute-start(bf16[512,640]{1,0:T(8,128)(2,1)S(1)} %slice.49), channel_id=1, source_target_pairs={{0,16},{16,0},{1,17},{17,1},{2,18},{18,2},{3,19},{19,3},{4,20},{20... | collective-permute-start | bytes 1966088 | tf_op jit(solution)/shard_map/ppermute | solution.py:125
  189.1 27.8 %collective-permute-start.22 = (bf16[512,640]{1,0:T(8,128)(2,1)S(1)}, bf16[512,640]{1,0:T(8,128)(2,1)S(1)}, u32[]{:S(2)}, u32[]{:S(2)}) collective-permute-start(bf16[512,640]{1,0:T(8,128)(2,1)S(1)} %slice.50), channel_id=1, source_target_pairs={{0,16},{16,0},{1,17},{17,1},{2,18},{18,2},{3,19},{19,3},{4,20},{20... | collective-permute-start | bytes 1966088 | tf_op jit(solution)/shard_map/ppermute | solution.py:121

commit v5 on v4

--- a/solution.py
+++ b/solution.py
@@ -167,6 +167,9 @@
     arrivals, shared, own = ring_transfer(out_weight)
     initial_state = fresh_state(kv_heads, group_width, tok_rows)
     state_now = attend(initial_state, keys, values, query_start)
+    first_block = arrivals[1][1]
+    first_block, keys, values = lax.optimization_barrier((first_block, keys, values))
+    arrivals[1] = (arrivals[1][0], first_block, arrivals[1][2])
     for distance in range(1, reach_devs + 1):
         prior_keys, prior_values = passed_along((keys, values), "ctx", distance)
         state_now = attend(state_now, prior_keys, prior_values, query_start - distance * tok_rows)

time: 222 us -> 257 us (1.16)
  waiting for transfers between devices: 78.9 us -> 109 us
  starting transfers between devices: 49.3 us -> 57.2 us
    ppermute x4, waiting for transfers between devices: 35.4 us -> 63.6 us  [ring_transfer(): forward = lax.ppermute(forward, 'ctx', ahead)]
    ppermute x8, starting transfers between devices: 24.6 us -> 34.9 us  [passed_along(): return lax.ppermute(array, axis, pairs)]
    ppermute x3, starting transfers between devices: 10.3 us -> 1.99 us  [ring_transfer(): backward = lax.ppermute(backward, 'ctx', behind)]
    ppermute x4, starting transfers between devices: 6.23 us -> 12.1 us  [ring_transfer(): forward = lax.ppermute(forward, 'ctx', ahead)]
    ppermute x3, waiting for transfers between devices: 7.39 us -> 11.2 us  [ring_transfer(): backward = lax.ppermute(backward, 'ctx', behind)]
  transfers between devices with their start and end apart: 23 -> 23, of which waited for: 9 -> 9; matrix products, arithmetic and copies ran while one was open for 35% -> 28% of each run, Pallas kernels for 0% -> 0%
where the time goes in v5:
time: 257 us; the launch traced here: 256 us
  waiting for transfers between devices  109 us (42%)
  starting transfers between devices  57.2 us (22%)
  matrix products  54.4 us (21%)
  local copies, waits for them, and re-layouts  17.2 us (7%)
  between operations  9.56 us (4%)
  other arithmetic  8.56 us (3%)
    ppermute x4, waiting for transfers between devices, ring_transfer(): forward = lax.ppermute(forward, 'ctx', ahead)  63.6 us
    ppermute x8, starting transfers between devices, passed_along(): return lax.ppermute(array, axis, pairs)  34.9 us
    ppermute x3, waiting for transfers between devices, ring_transfer(): crossed = lax.ppermute(backward[:, shared:], 'group', swap) if own else None  23.8 us
    dot_general x5, matrix products, update(): jnp.einsum('hgqk,khd->hgqd', weights.astype(jnp.bfloat16), value_head_row...  23.7 us
    ppermute x4, starting transfers between devices, ring_transfer(): forward = lax.ppermute(forward, 'ctx', ahead)  12.1 us
    dot_general x8, matrix products, ring_project(): terms = [jnp.dot(piece, carried_block, preferred_element_type=jnp.float32)]  12.1 us
    ppermute x3, waiting for transfers between devices, ring_transfer(): backward = lax.ppermute(backward, 'ctx', behind)  11.2 us
    dot_general x5, matrix products, update(): jnp.einsum('qhgd,khd->hgqk', query_head_rows, key_head_rows, preferred_el...  10.8 us
  transfers between devices with their start and end apart: 23, of which 9 were waited for; matrix products, arithmetic and copies ran while one was open for 28% of the time, Pallas kernels for 0%

profile of v5, /device:TPU:0, one launch (start us, length us, event | category | flops | bytes accessed | tf_op | source)
XLA Modules:
  0.0 255.8 jit_solution(543532978882072178)
XLA Ops:
  0.0 1.2 slice.32
  1.2 1.2 constant_dynamic-slice_fusion
  2.4 1.2 pad_maximum_fusion
  3.7 3.1 %collective-permute-start = (bf16[512,1408]{1,0:T(8,128)(2,1)}, bf16[512,1408]{1,0:T(8,128)(2,1)}, u32[]{:S(2)}, u32[]{:S(2)}) collective-permute-start(bf16[512,1408]{1,0:T(8,128)(2,1)} %pad_maximum_fusion), channel_id=1, source_target_pairs={{0,4},{4,8},{8,12},{12,14},{14,10},{10,6},{6,2},{2,0},{1,5},{5,9},... | collective-permute-start | bytes 4325384 | tf_op jit(solution)/shard_map/ppermute | solution.py:120
  8.5 1.8 copy.89
  11.1 27.5 %collective-permute-done = bf16[512,1408]{1,0:T(8,128)(2,1)} collective-permute-done((bf16[512,1408]{1,0:T(8,128)(2,1)}, bf16[512,1408]{1,0:T(8,128)(2,1)}, u32[]{:S(2)}, u32[]{:S(2)}) %collective-permute-start) | collective-permute-done | bytes 1441824 | tf_op jit(solution)/shard_map/ppermute | solution.py:120
  38.5 1.8 copy.52
  40.3 4.7 %collective-permute-start.7 = (bf16[256,512]{0,1:T(8,128)(2,1)}, bf16[256,512]{0,1:T(8,128)(2,1)S(1)}, u32[]{:S(2)}, u32[]{:S(2)}) collective-permute-start(bf16[256,512]{0,1:T(8,128)(2,1)} %copy.52), channel_id=1, source_target_pairs={{0,8},{2,10},{4,12},{6,14},{1,9},{3,11},{5,13},{7,15},{16,24},{18,... | collective-permute-start | bytes 786440 | tf_op jit(solution)/shard_map/ppermute | solution.py:15
  46.1 4.4 %collective-permute-start.5 = (bf16[256,512]{0,1:T(8,128)(2,1)}, bf16[256,512]{0,1:T(8,128)(2,1)S(1)}, u32[]{:S(2)}, u32[]{:S(2)}) collective-permute-start(bf16[256,512]{0,1:T(8,128)(2,1)} %copy.52), channel_id=1, source_target_pairs={{0,6},{2,8},{4,10},{6,12},{8,14},{1,7},{3,9},{5,11},{7,13},{9,15},... | collective-permute-start | bytes 786440 | tf_op jit(solution)/shard_map/ppermute | solution.py:15
  50.5 1.3 collective-permute-start.3
  51.8 3.1 %collective-permute-start.1 = (bf16[256,512]{0,1:T(8,128)(2,1)}, bf16[256,512]{0,1:T(8,128)(2,1)S(1)}, u32[]{:S(2)}, u32[]{:S(2)}) collective-permute-start(bf16[256,512]{0,1:T(8,128)(2,1)} %copy.52), channel_id=1, source_target_pairs={{0,2},{2,4},{4,6},{6,8},{8,10},{10,12},{12,14},{1,3},{3,5},{5,7},{... | collective-permute-start | bytes 786440 | tf_op jit(solution)/shard_map/ppermute | solution.py:15
  55.0 3.4 %collective-permute-start.2 = (bf16[256,512]{1,0:T(8,128)(2,1)S(1)}, bf16[256,512]{1,0:T(8,128)(2,1)}, u32[]{:S(2)}, u32[]{:S(2)}) collective-permute-start(bf16[256,512]{1,0:T(8,128)(2,1)S(1)} %copy-done.5), channel_id=1, source_target_pairs={{0,2},{2,4},{4,6},{6,8},{8,10},{10,12},{12,14},{1,3},{3,5},{5,7},{... | collective-permute-start | bytes 786440 | tf_op jit(solution)/shard_map/ppermute | solution.py:15
  58.4 2.9 %fusion.4 = (f32[4,4,256]{2,1,0:T(4,128)S(1)}, f32[4,256,256,4]{2,1,3,0:T(8,128)}) fusion(pred[256,256]{0,1:T(8,128)(4,1)S(1)} %get-tuple-element.35, bf16[256,4,128,1]{0,2,3,1:T(8,128)(2,1)S(1)} %bitcast.274, bf16[256,4,4,128]{3,2,1,0:T(4,128)(2,1)S(1)} %reshape.293), kind=kOutput, calls=%fused_computation.30 | convolution fusion | flops 271577088 | bytes 5586944 | tf_op jit(solution)/shard_map/qhgd,khd->hgqk/dot_general | solution.py:33
  61.3 10.6 %collective-permute-start.4 = (bf16[256,512]{1,0:T(8,128)(2,1)S(1)}, bf16[256,512]{1,0:T(8,128)(2,1)}, u32[]{:S(2)}, u32[]{:S(2)}) collective-permute-start(bf16[256,512]{1,0:T(8,128)(2,1)S(1)} %copy-done.5), channel_id=1, source_target_pairs={{0,4},{2,6},{4,8},{6,10},{8,12},{10,14},{1,5},{3,7},{5,9},{7,11},{... | collective-permute-start | bytes 786440 | tf_op jit(solution)/shard_map/ppermute | solution.py:15
  71.9 3.0 %fusion.3 = (f32[4,4,256]{2,1,0:T(4,128)S(1)}, f32[4,256,256,4]{2,1,3,0:T(8,128)}) fusion(pred[256,256]{0,1:T(8,128)(4,1)S(1)} %get-tuple-element.33, bf16[256,4,128,1]{0,2,3,1:T(8,128)(2,1)S(1)} %bitcast.273, bf16[256,4,4,128]{3,2,1,0:T(4,128)(2,1)S(1)} %reshape.293), kind=kOutput, calls=%fused_computation.29 | convolution fusion | flops 271577088 | bytes 5586944 | tf_op jit(solution)/shard_map/qhgd,khd->hgqk/dot_general | solution.py:33
  74.8 2.9 %collective-permute-start.6 = (bf16[256,512]{1,0:T(8,128)(2,1)S(1)}, bf16[256,512]{1,0:T(8,128)(2,1)}, u32[]{:S(2)}, u32[]{:S(2)}) collective-permute-start(bf16[256,512]{1,0:T(8,128)(2,1)S(1)} %copy-done.5), channel_id=1, source_target_pairs={{0,6},{2,8},{4,10},{6,12},{8,14},{1,7},{3,9},{5,11},{7,13},{9,15},... | collective-permute-start | bytes 786440 | tf_op jit(solution)/shard_map/ppermute | solution.py:15
  77.7 2.9 %fusion.2 = (f32[4,4,256]{2,1,0:T(4,128)S(1)}, f32[4,256,256,4]{2,1,3,0:T(8,128)}) fusion(pred[256,256]{0,1:T(8,128)(4,1)S(1)} %get-tuple-element.34, bf16[256,4,128,1]{0,2,3,1:T(8,128)(2,1)S(1)} %bitcast.272, bf16[256,4,4,128]{3,2,1,0:T(4,128)(2,1)S(1)} %reshape.293), kind=kOutput, calls=%fused_computation.28 | convolution fusion | flops 271577088 | bytes 5586944 | tf_op jit(solution)/shard_map/qhgd,khd->hgqk/dot_general | solution.py:33
  80.7 4.5 %collective-permute-start.8 = (bf16[256,512]{1,0:T(8,128)(2,1)S(1)}, bf16[256,512]{1,0:T(8,128)(2,1)}, u32[]{:S(2)}, u32[]{:S(2)}) collective-permute-start(bf16[256,512]{1,0:T(8,128)(2,1)S(1)} %copy-done.5), channel_id=1, source_target_pairs={{0,8},{2,10},{4,12},{6,14},{1,9},{3,11},{5,13},{7,15},{16,24},{18,... | collective-permute-start | bytes 786440 | tf_op jit(solution)/shard_map/ppermute | solution.py:15
  87.4 2.6 %fusion.26 = f32[4,4,256,128]{2,3,1,0:T(8,128)} fusion(bf16[256,4,128,1]{0,2,3,1:T(8,128)(2,1)S(1)} %bitcast.275, f32[4,256,256,4]{2,1,3,0:T(8,128)S(1)} %get-tuple-element.52, f32[4,4,256]{2,1,0:T(4,128)S(1)} %get-tuple-element.30, pred[256,256]{0,1:T(8,128)(4,1)S(1)} %get-tuple-element.31), kind=kOutput, calls=%fused_computation.52 | convolution fusion | flops 273678336 | bytes 6635520 | tf_op jit(solution)/shard_map/hgqk,khd->hgqd/dot_general | solution.py:42
  91.0 1.1 copy.55
  92.1 4.8 %fusion.24 = f32[4,4,256,128]{2,3,1,0:T(8,128)} fusion(bf16[256,4,128,1]{0,2,3,1:T(8,128)(2,1)S(1)} %bitcast.277, f32[4,256,256,4]{2,1,3,0:T(8,128)} %copy-done.3, f32[4,4,256]{2,1,0:T(4,128)S(1)} %get-tuple-element.23, pred[256,256]{0,1:T(8,128)(4,1)S(1)} %get-tuple-element.32), kind=kOutput, calls=%fused_computation.51 | convolution fusion | flops 273678336 | bytes 6635520 | tf_op jit(solution)/shard_map/hgqk,khd->hgqd/dot_general | solution.py:42
  98.0 1.1 copy.60
  99.1 4.9 %fusion.22 = f32[4,4,256,128]{2,3,1,0:T(8,128)} fusion(bf16[256,4,128,1]{0,2,3,1:T(8,128)(2,1)S(1)} %bitcast.278, f32[4,256,256,4]{2,1,3,0:T(8,128)} %get-tuple-element.48, f32[4,4,256]{2,1,0:T(4,128)S(1)} %get-tuple-element.22, pred[256,256]{0,1:T(8,128)(4,1)S(1)} %get-tuple-element.34), kind=kOutput, calls=%fused_computation.50 | convolution fusion | flops 273678336 | bytes 6635520 | tf_op jit(solution)/shard_map/hgqk,khd->hgqd/dot_general | solution.py:42
  105.0 1.1 copy.65
  106.1 4.8 %fusion.20 = f32[4,4,256,128]{2,3,1,0:T(8,128)} fusion(bf16[256,4,128,1]{0,2,3,1:T(8,128)(2,1)S(1)} %bitcast.279, f32[4,256,256,4]{2,1,3,0:T(8,128)} %get-tuple-element.46, f32[4,4,256]{2,1,0:T(4,128)S(1)} %get-tuple-element.21, pred[256,256]{0,1:T(8,128)(4,1)S(1)} %get-tuple-element.33), kind=kOutput, calls=%fused_computation.49 | convolution fusion | flops 273678336 | bytes 6635520 | tf_op jit(solution)/shard_map/hgqk,khd->hgqd/dot_general | solution.py:42
  113.2 6.6 %fusion.29 = bf16[256,4,4,128]{0,3,2,1:T(8,128)(2,1)S(1)} fusion(f32[4,4,256,128]{2,3,1,0:T(8,128)} %fusion.20, f32[4,4,256,128]{2,3,1,0:T(8,128)} %fusion.22, f32[4,4,256,128]{2,3,1,0:T(8,128)} %fusion.24, f32[4,4,256,128]{2,3,1,0:T(8,128)} %fusion.26, f32[256,4,4]{0,2,1:T(4,128)S(1)} %get-tuple-element.16, f32[256,4,4]{0,2,1:T(4,128)S(1)} %get-tuple-element.19, ...), kind=kOutput, calls=%fused_computation.55 | convolution fusion | flops 279445504 | bytes 14073856 | tf_op jit(solution)/shard_map/hgqk,khd->hgqd/dot_general | solution.py:42
  130.3 1.1 slice.44
  131.5 1.6 collective-permute-start.16
  133.1 1.1 slice.45
  134.8 2.0 collective-permute-start.12
  137.0 2.4 fusion.134
  139.3 14.8 %collective-permute-done.11 = bf16[512,1408]{1,0:T(8,128)(2,1)} collective-permute-done((bf16[512,1408]{1,0:T(8,128)(2,1)}, bf16[512,1408]{1,0:T(8,128)(2,1)}, u32[]{:S(2)}, u32[]{:S(2)}) %collective-permute-start.11) | collective-permute-done | bytes 1441824 | tf_op jit(solution)/shard_map/ppermute | solution.py:120
  154.2 6.6 %collective-permute-start.13 = (bf16[512,1408]{1,0:T(8,128)(2,1)}, bf16[512,1408]{1,0:T(8,128)(2,1)S(1)}, u32[]{:S(2)}, u32[]{:S(2)}) collective-permute-start(bf16[512,1408]{1,0:T(8,128)(2,1)} %collective-permute-done.11), channel_id=1, source_target_pairs={{0,4},{4,8},{8,12},{12,14},{14,10},{10,6},{6,2},{2,0},{1,5},{5,9},... | collective-permute-start | bytes 4325384 | tf_op jit(solution)/shard_map/ppermute | solution.py:120
  160.7 2.3 fusion.130
  164.1 11.2 %collective-permute-done.12 = bf16[512,1408]{1,0:T(8,128)(2,1)S(1)} collective-permute-done((bf16[512,1408]{1,0:T(8,128)(2,1)}, bf16[512,1408]{1,0:T(8,128)(2,1)S(1)}, u32[]{:S(2)}, u32[]{:S(2)}) %collective-permute-start.12) | collective-permute-done | bytes 1441824 | tf_op jit(solution)/shard_map/ppermute | solution.py:124
  177.0 1.1 slice.46
  178.1 1.6 collective-permute-start.18
  181.4 10.3 %collective-permute-done.13 = bf16[512,1408]{1,0:T(8,128)(2,1)S(1)} collective-permute-done((bf16[512,1408]{1,0:T(8,128)(2,1)}, bf16[512,1408]{1,0:T(8,128)(2,1)S(1)}, u32[]{:S(2)}, u32[]{:S(2)}) %collective-permute-start.13) | collective-permute-done | bytes 1441824 | tf_op jit(solution)/shard_map/ppermute | solution.py:120
  191.6 2.5 collective-permute-start.15
  194.1 2.4 fusion.16
  197.3 10.6 %collective-permute-done.19 = bf16[512,640]{1,0:T(8,128)(2,1)S(1)} collective-permute-done((bf16[512,640]{1,0:T(8,128)(2,1)S(1)}, bf16[512,640]{1,0:T(8,128)(2,1)S(1)}, u32[]{:S(2)}, u32[]{:S(2)}) %collective-permute-start.19) | collective-permute-done | bytes 655392 | tf_op jit(solution)/shard_map/ppermute | solution.py:125
  208.8 1.6 collective-permute-start.20
  213.1 11.0 %collective-permute-done.15 = bf16[512,1408]{1,0:T(8,128)(2,1)S(1)} collective-permute-done((bf16[512,1408]{1,0:T(8,128)(2,1)S(1)}, bf16[512,1408]{1,0:T(8,128)(2,1)S(1)}, u32[]{:S(2)}, u32[]{:S(2)}) %collective-permute-start.15) | collective-permute-done | bytes 1441824 | tf_op jit(solution)/shard_map/ppermute | solution.py:120
  224.1 1.6 collective-permute-start.22
  227.3 13.2 %collective-permute-done.21 = bf16[512,640]{1,0:T(8,128)(2,1)S(1)} collective-permute-done((bf16[512,640]{1,0:T(8,128)(2,1)S(1)}, bf16[512,640]{1,0:T(8,128)(2,1)S(1)}, u32[]{:S(2)}, u32[]{:S(2)}) %collective-permute-start.21) | collective-permute-done | bytes 655392 | tf_op jit(solution)/shard_map/ppermute | solution.py:125
  242.4 9.4 %collective-permute-done.22 = bf16[512,640]{1,0:T(8,128)(2,1)S(1)} collective-permute-done((bf16[512,640]{1,0:T(8,128)(2,1)S(1)}, bf16[512,640]{1,0:T(8,128)(2,1)S(1)}, u32[]{:S(2)}, u32[]{:S(2)}) %collective-permute-start.22) | collective-permute-done | bytes 655392 | tf_op jit(solution)/shard_map/ppermute | solution.py:121
  252.6 2.1 select_convert_fusion.1
  254.7 1.1 pad_maximum_fusion.1
  (81 shorter events, 26.1 us)
Async XLA Ops:
  1.2 5.6 %copy-start.4 = (bf16[256,2048]{1,0:T(8,128)(2,1)S(1)}, bf16[256,2048]{1,0:T(8,128)(2,1)}, u32[]{:S(2)}) copy-start(bf16[256,2048]{1,0:T(8,128)(2,1)} %param.7) | copy-start | bytes 3145732
  3.7 6.7 %copy-start.8 = (s32[16]{0:T(128)S(1)}, s32[16]{0:T(128)}, u32[]{:S(2)}) copy-start(s32[16]{0:T(128)} %param.10) | copy-start | bytes 196
  3.7 34.9 %collective-permute-start = (bf16[512,1408]{1,0:T(8,128)(2,1)}, bf16[512,1408]{1,0:T(8,128)(2,1)}, u32[]{:S(2)}, u32[]{:S(2)}) collective-permute-start(bf16[512,1408]{1,0:T(8,128)(2,1)} %pad_maximum_fusion), channel_id=1, source_target_pairs={{0,4},{4,8},{8,12},{12,14},{14,10},{10,6},{6,2},{2,0},{1,5},{5,9},... | collective-permute-start | bytes 4325384 | tf_op jit(solution)/shard_map/ppermute | solution.py:120
  6.7 126.3 %collective-permute-start.10 = (bf16[512,1408]{1,0:T(8,128)(2,1)}, bf16[512,1408]{1,0:T(8,128)(2,1)}, u32[]{:S(2)}, u32[]{:S(2)}) collective-permute-start(bf16[512,1408]{1,0:T(8,128)(2,1)} %pad_maximum_fusion), channel_id=1, source_target_pairs={{0,2},{4,0},{8,4},{12,8},{14,12},{10,14},{6,10},{2,6},{1,3},{5,1},... | collective-permute-start | bytes 4325384 | tf_op jit(solution)/shard_map/ppermute | solution.py:124
  40.3 14.6 %collective-permute-start.7 = (bf16[256,512]{0,1:T(8,128)(2,1)}, bf16[256,512]{0,1:T(8,128)(2,1)S(1)}, u32[]{:S(2)}, u32[]{:S(2)}) collective-permute-start(bf16[256,512]{0,1:T(8,128)(2,1)} %copy.52), channel_id=1, source_target_pairs={{0,8},{2,10},{4,12},{6,14},{1,9},{3,11},{5,13},{7,15},{16,24},{18,... | collective-permute-start | bytes 786440 | tf_op jit(solution)/shard_map/ppermute | solution.py:15
  45.1 9.9 %copy-start.5 = (bf16[256,512]{1,0:T(8,128)(2,1)S(1)}, bf16[256,512]{1,0:T(8,128)(2,1)}, u32[]{:S(2)}) copy-start(bf16[256,512]{1,0:T(8,128)(2,1)} %param.9) | copy-start | bytes 786436
  46.1 15.2 %collective-permute-start.5 = (bf16[256,512]{0,1:T(8,128)(2,1)}, bf16[256,512]{0,1:T(8,128)(2,1)S(1)}, u32[]{:S(2)}, u32[]{:S(2)}) collective-permute-start(bf16[256,512]{0,1:T(8,128)(2,1)} %copy.52), channel_id=1, source_target_pairs={{0,6},{2,8},{4,10},{6,12},{8,14},{1,7},{3,9},{5,11},{7,13},{9,15},... | collective-permute-start | bytes 786440 | tf_op jit(solution)/shard_map/ppermute | solution.py:15
  50.5 24.3 %collective-permute-start.3 = (bf16[256,512]{0,1:T(8,128)(2,1)}, bf16[256,512]{0,1:T(8,128)(2,1)S(1)}, u32[]{:S(2)}, u32[]{:S(2)}) collective-permute-start(bf16[256,512]{0,1:T(8,128)(2,1)} %copy.52), channel_id=1, source_target_pairs={{0,4},{2,6},{4,8},{6,10},{8,12},{10,14},{1,5},{3,7},{5,9},{7,11},{... | collective-permute-start | bytes 786440 | tf_op jit(solution)/shard_map/ppermute | solution.py:15
  51.8 28.8 %collective-permute-start.1 = (bf16[256,512]{0,1:T(8,128)(2,1)}, bf16[256,512]{0,1:T(8,128)(2,1)S(1)}, u32[]{:S(2)}, u32[]{:S(2)}) collective-permute-start(bf16[256,512]{0,1:T(8,128)(2,1)} %copy.52), channel_id=1, source_target_pairs={{0,2},{2,4},{4,6},{6,8},{8,10},{10,12},{12,14},{1,3},{3,5},{5,7},{... | collective-permute-start | bytes 786440 | tf_op jit(solution)/shard_map/ppermute | solution.py:15
  55.0 36.0 %collective-permute-start.2 = (bf16[256,512]{1,0:T(8,128)(2,1)S(1)}, bf16[256,512]{1,0:T(8,128)(2,1)}, u32[]{:S(2)}, u32[]{:S(2)}) collective-permute-start(bf16[256,512]{1,0:T(8,128)(2,1)S(1)} %copy-done.5), channel_id=1, source_target_pairs={{0,2},{2,4},{4,6},{6,8},{8,10},{10,12},{12,14},{1,3},{3,5},{5,7},{... | collective-permute-start | bytes 786440 | tf_op jit(solution)/shard_map/ppermute | solution.py:15
  61.3 36.7 %collective-permute-start.4 = (bf16[256,512]{1,0:T(8,128)(2,1)S(1)}, bf16[256,512]{1,0:T(8,128)(2,1)}, u32[]{:S(2)}, u32[]{:S(2)}) collective-permute-start(bf16[256,512]{1,0:T(8,128)(2,1)S(1)} %copy-done.5), channel_id=1, source_target_pairs={{0,4},{2,6},{4,8},{6,10},{8,12},{10,14},{1,5},{3,7},{5,9},{7,11},{... | collective-permute-start | bytes 786440 | tf_op jit(solution)/shard_map/ppermute | solution.py:15
  74.8 30.1 %collective-permute-start.6 = (bf16[256,512]{1,0:T(8,128)(2,1)S(1)}, bf16[256,512]{1,0:T(8,128)(2,1)}, u32[]{:S(2)}, u32[]{:S(2)}) collective-permute-start(bf16[256,512]{1,0:T(8,128)(2,1)S(1)} %copy-done.5), channel_id=1, source_target_pairs={{0,6},{2,8},{4,10},{6,12},{8,14},{1,7},{3,9},{5,11},{7,13},{9,15},... | collective-permute-start | bytes 786440 | tf_op jit(solution)/shard_map/ppermute | solution.py:15
  80.7 31.4 %collective-permute-start.8 = (bf16[256,512]{1,0:T(8,128)(2,1)S(1)}, bf16[256,512]{1,0:T(8,128)(2,1)}, u32[]{:S(2)}, u32[]{:S(2)}) collective-permute-start(bf16[256,512]{1,0:T(8,128)(2,1)S(1)} %copy-done.5), channel_id=1, source_target_pairs={{0,8},{2,10},{4,12},{6,14},{1,9},{3,11},{5,13},{7,15},{16,24},{18,... | collective-permute-start | bytes 786440 | tf_op jit(solution)/shard_map/ppermute | solution.py:15
  86.2 3.8 %copy-start.3 = (f32[4,256,256,4]{2,1,3,0:T(8,128)}, f32[4,256,256,4]{2,1,3,0:T(8,128)S(1)}, u32[]{:S(2)}) copy-start(f32[4,256,256,4]{2,1,3,0:T(8,128)S(1)} %get-tuple-element.50) | copy-start | bytes 12582916
  86.2 1.1 copy-start.6
  92.1 4.8 %copy-start.2 = (f32[4,256,256,4]{2,1,3,0:T(8,128)S(1)}, f32[4,256,256,4]{2,1,3,0:T(8,128)}, u32[]{:S(2)}) copy-start(f32[4,256,256,4]{2,1,3,0:T(8,128)} %get-tuple-element.48) | copy-start | bytes 12582916
  99.1 4.9 %copy-start.1 = (f32[4,256,256,4]{2,1,3,0:T(8,128)S(1)}, f32[4,256,256,4]{2,1,3,0:T(8,128)}, u32[]{:S(2)}) copy-start(f32[4,256,256,4]{2,1,3,0:T(8,128)} %get-tuple-element.46) | copy-start | bytes 12582916
  106.1 4.9 %copy-start = (f32[4,256,256,4]{2,1,3,0:T(8,128)S(1)}, f32[4,256,256,4]{2,1,3,0:T(8,128)}, u32[]{:S(2)}) copy-start(f32[4,256,256,4]{2,1,3,0:T(8,128)} %get-tuple-element.44) | copy-start | bytes 12582916
  113.1 6.8 %copy-start.9 = (s32[8]{0:T(128)S(1)}, s32[8]{0:T(128)}, u32[]{:S(2)}) copy-start(s32[8]{0:T(128)} %constant.183.clone) | copy-start | bytes 100
  113.2 12.1 %copy-start.7 = (s32[8]{0:T(128)S(1)}, s32[8]{0:T(128)}, u32[]{:S(2)}) copy-start(s32[8]{0:T(128)} %constant.184.clone) | copy-start | bytes 100
  119.8 17.0 %collective-permute-start.9 = (bf16[256,2048]{0,1:T(8,128)(2,1)S(1)}, bf16[256,2048]{0,1:T(8,128)(2,1)S(1)}, u32[]{:S(2)}, u32[]{:S(2)}) collective-permute-start(bf16[256,2048]{0,1:T(8,128)(2,1)S(1)} %bitcast.269), channel_id=1, source_target_pairs={{0,1},{1,0},{2,3},{3,2},{4,5},{5,4},{6,7},{7,6},{8,9},{9,8},{10,11... | collective-permute-start | bytes 3145736 | tf_op jit(solution)/shard_map/ppermute | solution.py:77
  119.9 34.3 %collective-permute-start.11 = (bf16[512,1408]{1,0:T(8,128)(2,1)}, bf16[512,1408]{1,0:T(8,128)(2,1)}, u32[]{:S(2)}, u32[]{:S(2)}) collective-permute-start(bf16[512,1408]{1,0:T(8,128)(2,1)} %collective-permute-done), channel_id=1, source_target_pairs={{0,4},{4,8},{8,12},{12,14},{14,10},{10,6},{6,2},{2,0},{1,5},{5,9},... | collective-permute-start | bytes 4325384 | tf_op jit(solution)/shard_map/ppermute | solution.py:120
  131.5 43.9 %collective-permute-start.16 = (bf16[512,640]{1,0:T(8,128)(2,1)S(1)}, bf16[512,640]{1,0:T(8,128)(2,1)S(1)}, u32[]{:S(2)}, u32[]{:S(2)}) collective-permute-start(bf16[512,640]{1,0:T(8,128)(2,1)S(1)} %slice.44), channel_id=1, source_target_pairs={{0,16},{16,0},{1,17},{17,1},{2,18},{18,2},{3,19},{19,3},{4,20},{20... | collective-permute-start | bytes 1966088 | tf_op jit(solution)/shard_map/ppermute | solution.py:121
  134.2 41.9 %collective-permute-start.17 = (bf16[512,640]{1,0:T(8,128)(2,1)S(1)}, bf16[512,640]{1,0:T(8,128)(2,1)S(1)}, u32[]{:S(2)}, u32[]{:S(2)}) collective-permute-start(bf16[512,640]{1,0:T(8,128)(2,1)S(1)} %slice.45), channel_id=1, source_target_pairs={{0,16},{16,0},{1,17},{17,1},{2,18},{18,2},{3,19},{19,3},{4,20},{20... | collective-permute-start | bytes 1966088 | tf_op jit(solution)/shard_map/ppermute | solution.py:125
  134.8 40.6 %collective-permute-start.12 = (bf16[512,1408]{1,0:T(8,128)(2,1)}, bf16[512,1408]{1,0:T(8,128)(2,1)S(1)}, u32[]{:S(2)}, u32[]{:S(2)}) collective-permute-start(bf16[512,1408]{1,0:T(8,128)(2,1)} %collective-permute-done.10), channel_id=1, source_target_pairs={{0,2},{4,0},{8,4},{12,8},{14,12},{10,14},{6,10},{2,6},{1,3},{5,1},... | collective-permute-start | bytes 4325384 | tf_op jit(solution)/shard_map/ppermute | solution.py:124
  154.2 37.5 %collective-permute-start.13 = (bf16[512,1408]{1,0:T(8,128)(2,1)}, bf16[512,1408]{1,0:T(8,128)(2,1)S(1)}, u32[]{:S(2)}, u32[]{:S(2)}) collective-permute-start(bf16[512,1408]{1,0:T(8,128)(2,1)} %collective-permute-done.11), channel_id=1, source_target_pairs={{0,4},{4,8},{8,12},{12,14},{14,10},{10,6},{6,2},{2,0},{1,5},{5,9},... | collective-permute-start | bytes 4325384 | tf_op jit(solution)/shard_map/ppermute | solution.py:120
  175.3 35.0 %collective-permute-start.14 = (bf16[512,1408]{1,0:T(8,128)(2,1)S(1)}, bf16[512,1408]{1,0:T(8,128)(2,1)S(1)}, u32[]{:S(2)}, u32[]{:S(2)}) collective-permute-start(bf16[512,1408]{1,0:T(8,128)(2,1)S(1)} %collective-permute-done.12), channel_id=1, source_target_pairs={{0,2},{4,0},{8,4},{12,8},{14,12},{10,14},{6,10},{2,6},{1,3},{5,1},... | collective-permute-start | bytes 4325384 | tf_op jit(solution)/shard_map/ppermute | solution.py:124
  178.1 18.4 %collective-permute-start.18 = (bf16[512,640]{1,0:T(8,128)(2,1)S(1)}, bf16[512,640]{1,0:T(8,128)(2,1)S(1)}, u32[]{:S(2)}, u32[]{:S(2)}) collective-permute-start(bf16[512,640]{1,0:T(8,128)(2,1)S(1)} %slice.46), channel_id=1, source_target_pairs={{0,16},{16,0},{1,17},{17,1},{2,18},{18,2},{3,19},{19,3},{4,20},{20... | collective-permute-start | bytes 1966088 | tf_op jit(solution)/shard_map/ppermute | solution.py:121
  179.8 28.1 %collective-permute-start.19 = (bf16[512,640]{1,0:T(8,128)(2,1)S(1)}, bf16[512,640]{1,0:T(8,128)(2,1)S(1)}, u32[]{:S(2)}, u32[]{:S(2)}) collective-permute-start(bf16[512,640]{1,0:T(8,128)(2,1)S(1)} %slice.47), channel_id=1, source_target_pairs={{0,16},{16,0},{1,17},{17,1},{2,18},{18,2},{3,19},{19,3},{4,20},{20... | collective-permute-start | bytes 1966088 | tf_op jit(solution)/shard_map/ppermute | solution.py:125
  191.6 32.4 %collective-permute-start.15 = (bf16[512,1408]{1,0:T(8,128)(2,1)S(1)}, bf16[512,1408]{1,0:T(8,128)(2,1)S(1)}, u32[]{:S(2)}, u32[]{:S(2)}) collective-permute-start(bf16[512,1408]{1,0:T(8,128)(2,1)S(1)} %collective-permute-done.13), channel_id=1, source_target_pairs={{0,4},{4,8},{8,12},{12,14},{14,10},{10,6},{6,2},{2,0},{1,5},{5,9},... | collective-permute-start | bytes 4325384 | tf_op jit(solution)/shard_map/ppermute | solution.py:120
  208.8 17.7 %collective-permute-start.20 = (bf16[512,640]{1,0:T(8,128)(2,1)S(1)}, bf16[512,640]{1,0:T(8,128)(2,1)S(1)}, u32[]{:S(2)}, u32[]{:S(2)}) collective-permute-start(bf16[512,640]{1,0:T(8,128)(2,1)S(1)} %slice.48), channel_id=1, source_target_pairs={{0,16},{16,0},{1,17},{17,1},{2,18},{18,2},{3,19},{19,3},{4,20},{20... | collective-permute-start | bytes 1966088 | tf_op jit(solution)/shard_map/ppermute | solution.py:121
  210.4 30.1 %collective-permute-start.21 = (bf16[512,640]{1,0:T(8,128)(2,1)S(1)}, bf16[512,640]{1,0:T(8,128)(2,1)S(1)}, u32[]{:S(2)}, u32[]{:S(2)}) collective-permute-start(bf16[512,640]{1,0:T(8,128)(2,1)S(1)} %slice.49), channel_id=1, source_target_pairs={{0,16},{16,0},{1,17},{17,1},{2,18},{18,2},{3,19},{19,3},{4,20},{20... | collective-permute-start | bytes 1966088 | tf_op jit(solution)/shard_map/ppermute | solution.py:125
  224.1 27.7 %collective-permute-start.22 = (bf16[512,640]{1,0:T(8,128)(2,1)S(1)}, bf16[512,640]{1,0:T(8,128)(2,1)S(1)}, u32[]{:S(2)}, u32[]{:S(2)}) collective-permute-start(bf16[512,640]{1,0:T(8,128)(2,1)S(1)} %slice.50), channel_id=1, source_target_pairs={{0,16},{16,0},{1,17},{17,1},{2,18},{18,2},{3,19},{19,3},{4,20},{20... | collective-permute-start | bytes 1966088 | tf_op jit(solution)/shard_map/ppermute | solution.py:121

commit v6 on v4

--- a/solution.py
+++ b/solution.py
@@ -168,7 +168,8 @@
     initial_state = fresh_state(kv_heads, group_width, tok_rows)
     state_now = attend(initial_state, keys, values, query_start)
     for distance in range(1, reach_devs + 1):
-        prior_keys, prior_values = passed_along((keys, values), "ctx", distance)
+        prior = passed_along(jnp.concatenate([keys, values], axis=1), "ctx", distance)
+        prior_keys, prior_values = prior[:, : keys.shape[1]], prior[:, keys.shape[1] :]
         state_now = attend(state_now, prior_keys, prior_values, query_start - distance * tok_rows)
     attended = finish(state_now, tok_rows, q_heads)
     features = head_features(attended)

time: 222 us -> 225 us (1.014)
  waiting for transfers between devices: 78.9 us -> 105 us
  matrix products: 56.1 us -> 32.1 us
  starting transfers between devices: 49.3 us -> 54.6 us
  local copies, waits for them, and re-layouts: 17.2 us -> 13.7 us
    ppermute x4, starting transfers between devices: 6.23 us -> 25.4 us  [ring_transfer(): forward = lax.ppermute(forward, 'ctx', ahead)]
    dot_general x5, matrix products: 23.5 us -> 7.1 us  [update(): jnp.einsum('hgqk,khd->hgqd', weights.astype(jnp.bfloat16), value_head_row...]
    ppermute x8 -> x4, waiting for transfers between devices: 0.02 us -> 12.4 us  [passed_along(): return lax.ppermute(array, axis, pairs)]
    ppermute x4, waiting for transfers between devices: 35.4 us -> 45.7 us  [ring_transfer(): forward = lax.ppermute(forward, 'ctx', ahead)]
    dot_general x5, matrix products: 12.7 us -> 5.07 us  [update(): jnp.einsum('qhgd,khd->hgqk', query_head_rows, key_head_rows, preferred_el...]
    ppermute x8 -> x4, starting transfers between devices: 24.6 us -> 17.2 us  [passed_along(): return lax.ppermute(array, axis, pairs)]
    ppermute x3, starting transfers between devices: 10.3 us -> 3.83 us  [ring_transfer(): backward = lax.ppermute(backward, 'ctx', behind)]
    ppermute x4 -> x0, local copies, waits for them, and re-layouts: 4.32 us -> none  [passed_along(): return lax.ppermute(array, axis, pairs)]
  transfers between devices with their start and end apart: 23 -> 19, of which waited for: 9 -> 12; matrix products, arithmetic and copies ran while one was open for 35% -> 21% of each run, Pallas kernels for 0% -> 0%
where the time goes in v6:
time: 225 us; the launch traced here: 224 us
  waiting for transfers between devices  105 us (47%)
  starting transfers between devices  54.6 us (24%)
  matrix products  32.1 us (14%)
  local copies, waits for them, and re-layouts  13.7 us (6%)
  between operations  9.47 us (4%)
  other arithmetic  9.42 us (4%)
    ppermute x4, waiting for transfers between devices, ring_transfer(): forward = lax.ppermute(forward, 'ctx', ahead)  45.7 us
    ppermute x4, starting transfers between devices, ring_transfer(): forward = lax.ppermute(forward, 'ctx', ahead)  25.4 us
    ppermute x3, waiting for transfers between devices, ring_transfer(): crossed = lax.ppermute(backward[:, shared:], 'group', swap) if own else None  24.1 us
    ppermute x4, starting transfers between devices, passed_along(): return lax.ppermute(array, axis, pairs)  17.2 us
    ppermute x4, waiting for transfers between devices, passed_along(): return lax.ppermute(array, axis, pairs)  12.4 us
    dot_general x8, matrix products, ring_project(): terms = [jnp.dot(piece, carried_block, preferred_element_type=jnp.float32)]  12.1 us
    ppermute x4, waiting for transfers between devices, ring_transfer(): crossed = lax.ppermute(forward[:, shared:], 'group', swap) if own else None  11.7 us
    ppermute x3, waiting for transfers between devices, ring_transfer(): backward = lax.ppermute(backward, 'ctx', behind)  11.2 us
  transfers between devices with their start and end apart: 19, of which 12 were waited for; matrix products, arithmetic and copies ran while one was open for 21% of the time, Pallas kernels for 0%

profile of v6, /device:TPU:0, one launch (start us, length us, event | category | flops | bytes accessed | tf_op | source)
XLA Modules:
  0.0 224.3 jit_solution(8393823099498419647)
XLA Ops:
  0.0 1.2 copy.77
  1.2 1.2 copy.46
  3.3 6.8 %collective-permute-start.3 = (bf16[256,1024]{0,1:T(8,128)(2,1)}, bf16[256,1024]{0,1:T(8,128)(2,1)}, u32[]{:S(2)}, u32[]{:S(2)}) collective-permute-start(bf16[256,1024]{0,1:T(8,128)(2,1)} %pad_maximum_fusion.2), channel_id=1, source_target_pairs={{0,8},{2,10},{4,12},{6,14},{1,9},{3,11},{5,13},{7,15},{16,24},{18,... | collective-permute-start | bytes 1572872 | tf_op jit(solution)/shard_map/ppermute | solution.py:15
  10.0 5.2 %collective-permute-start.2 = (bf16[256,1024]{0,1:T(8,128)(2,1)}, bf16[256,1024]{0,1:T(8,128)(2,1)}, u32[]{:S(2)}, u32[]{:S(2)}) collective-permute-start(bf16[256,1024]{0,1:T(8,128)(2,1)} %pad_maximum_fusion.2), channel_id=1, source_target_pairs={{0,6},{2,8},{4,10},{6,12},{8,14},{1,7},{3,9},{5,11},{7,13},{9,15},... | collective-permute-start | bytes 1572872 | tf_op jit(solution)/shard_map/ppermute | solution.py:15
  15.2 2.1 collective-permute-start.1
  17.4 3.1 %collective-permute-start = (bf16[256,1024]{0,1:T(8,128)(2,1)}, bf16[256,1024]{0,1:T(8,128)(2,1)}, u32[]{:S(2)}, u32[]{:S(2)}) collective-permute-start(bf16[256,1024]{0,1:T(8,128)(2,1)} %pad_maximum_fusion.2), channel_id=1, source_target_pairs={{0,2},{2,4},{4,6},{6,8},{8,10},{10,12},{12,14},{1,3},{3,5},{5,7},{... | collective-permute-start | bytes 1572872 | tf_op jit(solution)/shard_map/ppermute | solution.py:15
  20.7 1.2 pad_maximum_fusion
  22.1 1.8 reshape.293
  25.5 2.3 %collective-permute-start.6 = (bf16[512,1408]{1,0:T(8,128)(2,1)}, bf16[512,1408]{1,0:T(8,128)(2,1)}, u32[]{:S(2)}, u32[]{:S(2)}) collective-permute-start(bf16[512,1408]{1,0:T(8,128)(2,1)} %pad_maximum_fusion), channel_id=1, source_target_pairs={{0,2},{4,0},{8,4},{12,8},{14,12},{10,14},{6,10},{2,6},{1,3},{5,1},... | collective-permute-start | bytes 4325384 | tf_op jit(solution)/shard_map/ppermute | solution.py:124
  27.8 1.1 fusion.142
  29.9 3.3 %collective-permute-done.2 = bf16[256,1024]{0,1:T(8,128)(2,1)} collective-permute-done((bf16[256,1024]{0,1:T(8,128)(2,1)}, bf16[256,1024]{0,1:T(8,128)(2,1)}, u32[]{:S(2)}, u32[]{:S(2)}) %collective-permute-start.2) | collective-permute-done | bytes 524320 | tf_op jit(solution)/shard_map/ppermute | solution.py:15
  33.2 1.1 fusion.145
  35.3 9.1 %collective-permute-done.1 = bf16[256,1024]{0,1:T(8,128)(2,1)} collective-permute-done((bf16[256,1024]{0,1:T(8,128)(2,1)}, bf16[256,1024]{0,1:T(8,128)(2,1)}, u32[]{:S(2)}, u32[]{:S(2)}) %collective-permute-start.1) | collective-permute-done | bytes 524320 | tf_op jit(solution)/shard_map/ppermute | solution.py:15
  44.4 1.1 fusion.144
  46.5 1.1 fusion.143
  48.6 1.1 fusion.5
  49.7 1.2 fusion.26
  51.0 1.1 fusion.7
  52.0 1.2 fusion.24
  53.3 1.1 fusion.9
  54.3 1.2 fusion.22
  56.6 1.4 fusion.20
  59.2 1.9 fusion.29
  61.2 13.0 %collective-permute-done.5 = bf16[512,1408]{1,0:T(8,128)(2,1)} collective-permute-done((bf16[512,1408]{1,0:T(8,128)(2,1)}, bf16[512,1408]{1,0:T(8,128)(2,1)}, u32[]{:S(2)}, u32[]{:S(2)}) %collective-permute-start.5) | collective-permute-done | bytes 1441824 | tf_op jit(solution)/shard_map/ppermute | solution.py:120
  74.2 12.7 %collective-permute-start.7 = (bf16[512,1408]{1,0:T(8,128)(2,1)}, bf16[512,1408]{1,0:T(8,128)(2,1)}, u32[]{:S(2)}, u32[]{:S(2)}) collective-permute-start(bf16[512,1408]{1,0:T(8,128)(2,1)} %collective-permute-done.5), channel_id=1, source_target_pairs={{0,4},{4,8},{8,12},{12,14},{14,10},{10,6},{6,2},{2,0},{1,5},{5,9},... | collective-permute-start | bytes 4325384 | tf_op jit(solution)/shard_map/ppermute | solution.py:120
  97.2 1.1 slice.84
  98.3 1.6 collective-permute-start.12
  99.9 1.1 slice.85
  101.8 2.4 %fusion.134 = f32[256,1408]{1,0:T(8,128)S(1)} fusion(bf16[512,1408]{1,0:T(8,128)(2,1)} %collective-permute-done.5, s32[]{:T(128)S(6)} %select_n.237, bf16[256,2048]{0,1:T(8,128)(2,1)S(1)} %get-tuple-element.19, bf16[256,2048]{0,1:T(8,128)(2,1)S(1)} %get-tuple-element.18), kind=kOutput, calls=%fused_computation.213 | convolution fusion | flops 369623040 | bytes 4980740 | tf_op jit(solution)/shard_map/dot_general | solution.py:135
  104.2 14.0 %collective-permute-done.7 = bf16[512,1408]{1,0:T(8,128)(2,1)} collective-permute-done((bf16[512,1408]{1,0:T(8,128)(2,1)}, bf16[512,1408]{1,0:T(8,128)(2,1)}, u32[]{:S(2)}, u32[]{:S(2)}) %collective-permute-start.7) | collective-permute-done | bytes 1441824 | tf_op jit(solution)/shard_map/ppermute | solution.py:120
  118.2 10.3 %collective-permute-start.9 = (bf16[512,1408]{1,0:T(8,128)(2,1)}, bf16[512,1408]{1,0:T(8,128)(2,1)S(1)}, u32[]{:S(2)}, u32[]{:S(2)}) collective-permute-start(bf16[512,1408]{1,0:T(8,128)(2,1)} %collective-permute-done.7), channel_id=1, source_target_pairs={{0,4},{4,8},{8,12},{12,14},{14,10},{10,6},{6,2},{2,0},{1,5},{5,9},... | collective-permute-start | bytes 4325384 | tf_op jit(solution)/shard_map/ppermute | solution.py:120
  128.5 2.3 %fusion.130 = f32[256,1408]{1,0:T(8,128)S(1)} fusion(bf16[512,1408]{1,0:T(8,128)(2,1)} %collective-permute-done.6, s32[]{:T(128)S(6)} %select_n.240, bf16[256,2048]{0,1:T(8,128)(2,1)S(1)} %get-tuple-element.19, bf16[256,2048]{0,1:T(8,128)(2,1)S(1)} %get-tuple-element.18), kind=kOutput, calls=%fused_computation.211 | convolution fusion | flops 369623040 | bytes 4980740 | tf_op jit(solution)/shard_map/dot_general | solution.py:135
  131.9 11.2 %collective-permute-done.8 = bf16[512,1408]{1,0:T(8,128)(2,1)S(1)} collective-permute-done((bf16[512,1408]{1,0:T(8,128)(2,1)}, bf16[512,1408]{1,0:T(8,128)(2,1)S(1)}, u32[]{:S(2)}, u32[]{:S(2)}) %collective-permute-start.8) | collective-permute-done | bytes 1441824 | tf_op jit(solution)/shard_map/ppermute | solution.py:124
  143.1 1.6 collective-permute-start.10
  146.3 1.1 slice.86
  148.1 1.6 collective-permute-start.15
  150.6 8.7 %collective-permute-done.9 = bf16[512,1408]{1,0:T(8,128)(2,1)S(1)} collective-permute-done((bf16[512,1408]{1,0:T(8,128)(2,1)}, bf16[512,1408]{1,0:T(8,128)(2,1)S(1)}, u32[]{:S(2)}, u32[]{:S(2)}) %collective-permute-start.9) | collective-permute-done | bytes 1441824 | tf_op jit(solution)/shard_map/ppermute | solution.py:120
  159.4 2.5 %collective-permute-start.11 = (bf16[512,1408]{1,0:T(8,128)(2,1)S(1)}, bf16[512,1408]{1,0:T(8,128)(2,1)S(1)}, u32[]{:S(2)}, u32[]{:S(2)}) collective-permute-start(bf16[512,1408]{1,0:T(8,128)(2,1)S(1)} %collective-permute-done.9), channel_id=1, source_target_pairs={{0,4},{4,8},{8,12},{12,14},{14,10},{10,6},{6,2},{2,0},{1,5},{5,9},... | collective-permute-start | bytes 4325384 | tf_op jit(solution)/shard_map/ppermute | solution.py:120
  161.9 2.3 %fusion.16 = f32[256,1408]{1,0:T(8,128)S(1)} fusion(f32[256,1408]{1,0:T(8,128)S(1)} %fusion.123, f32[256,1408]{1,0:T(8,128)S(1)} %fusion.17, bf16[512,1408]{1,0:T(8,128)(2,1)} %collective-permute-done.7, s32[]{:T(128)S(6)} %select_n.243, bf16[256,2048]{0,1:T(8,128)(2,1)S(1)} %get-tuple-element.19, bf16[256,2048]{0,1:T(8,128)(2,1)S(1)} %get-tuple-element.18), kind=kOutput, calls=%fused_computation.45 | convolution fusion | flops 370343936 | bytes 7864324 | tf_op jit(solution)/shard_map/dot_general | solution.py:135
  165.9 10.9 %collective-permute-done.15 = bf16[512,640]{1,0:T(8,128)(2,1)S(1)} collective-permute-done((bf16[512,640]{1,0:T(8,128)(2,1)S(1)}, bf16[512,640]{1,0:T(8,128)(2,1)S(1)}, u32[]{:S(2)}, u32[]{:S(2)}) %collective-permute-start.15) | collective-permute-done | bytes 655392 | tf_op jit(solution)/shard_map/ppermute | solution.py:125
  178.3 1.6 collective-permute-start.17
  181.9 10.0 %collective-permute-done.11 = bf16[512,1408]{1,0:T(8,128)(2,1)S(1)} collective-permute-done((bf16[512,1408]{1,0:T(8,128)(2,1)S(1)}, bf16[512,1408]{1,0:T(8,128)(2,1)S(1)}, u32[]{:S(2)}, u32[]{:S(2)}) %collective-permute-start.11) | collective-permute-done | bytes 1441824 | tf_op jit(solution)/shard_map/ppermute | solution.py:120
  191.9 1.6 collective-permute-start.18
  193.5 1.8 collective-permute-done.16
  196.1 13.2 %collective-permute-done.17 = bf16[512,640]{1,0:T(8,128)(2,1)S(1)} collective-permute-done((bf16[512,640]{1,0:T(8,128)(2,1)S(1)}, bf16[512,640]{1,0:T(8,128)(2,1)S(1)}, u32[]{:S(2)}, u32[]{:S(2)}) %collective-permute-start.17) | collective-permute-done | bytes 655392 | tf_op jit(solution)/shard_map/ppermute | solution.py:125
  211.2 9.0 %collective-permute-done.18 = bf16[512,640]{1,0:T(8,128)(2,1)S(1)} collective-permute-done((bf16[512,640]{1,0:T(8,128)(2,1)S(1)}, bf16[512,640]{1,0:T(8,128)(2,1)S(1)}, u32[]{:S(2)}, u32[]{:S(2)}) %collective-permute-start.18) | collective-permute-done | bytes 655392 | tf_op jit(solution)/shard_map/ppermute | solution.py:121
  221.0 2.2 select_convert_fusion.1
  223.2 1.1 pad_maximum_fusion.1
  (68 shorter events, 24.2 us)
Async XLA Ops:
  0.0 20.5 %copy-start = (bf16[512,2048]{1,0:T(8,128)(2,1)S(1)}, bf16[512,2048]{1,0:T(8,128)(2,1)}, u32[]{:S(2)}) copy-start(bf16[512,2048]{1,0:T(8,128)(2,1)} %param.11) | copy-start | bytes 6291460
  1.2 19.2 %copy-start.2 = (bf16[256,512]{0,1:T(8,128)(2,1)}, bf16[256,512]{0,1:T(8,128)(2,1)S(1)}, u32[]{:S(2)}) copy-start(bf16[256,512]{0,1:T(8,128)(2,1)S(1)} %copy.77) | copy-start | bytes 786436
  3.3 22.2 %collective-permute-start.3 = (bf16[256,1024]{0,1:T(8,128)(2,1)}, bf16[256,1024]{0,1:T(8,128)(2,1)}, u32[]{:S(2)}, u32[]{:S(2)}) collective-permute-start(bf16[256,1024]{0,1:T(8,128)(2,1)} %pad_maximum_fusion.2), channel_id=1, source_target_pairs={{0,8},{2,10},{4,12},{6,14},{1,9},{3,11},{5,13},{7,15},{16,24},{18,... | collective-permute-start | bytes 1572872 | tf_op jit(solution)/shard_map/ppermute | solution.py:15
  10.0 23.1 %collective-permute-start.2 = (bf16[256,1024]{0,1:T(8,128)(2,1)}, bf16[256,1024]{0,1:T(8,128)(2,1)}, u32[]{:S(2)}, u32[]{:S(2)}) collective-permute-start(bf16[256,1024]{0,1:T(8,128)(2,1)} %pad_maximum_fusion.2), channel_id=1, source_target_pairs={{0,6},{2,8},{4,10},{6,12},{8,14},{1,7},{3,9},{5,11},{7,13},{9,15},... | collective-permute-start | bytes 1572872 | tf_op jit(solution)/shard_map/ppermute | solution.py:15
  15.2 29.2 %collective-permute-start.1 = (bf16[256,1024]{0,1:T(8,128)(2,1)}, bf16[256,1024]{0,1:T(8,128)(2,1)}, u32[]{:S(2)}, u32[]{:S(2)}) collective-permute-start(bf16[256,1024]{0,1:T(8,128)(2,1)} %pad_maximum_fusion.2), channel_id=1, source_target_pairs={{0,4},{2,6},{4,8},{6,10},{8,12},{10,14},{1,5},{3,7},{5,9},{7,11},{... | collective-permute-start | bytes 1572872 | tf_op jit(solution)/shard_map/ppermute | solution.py:15
  17.4 29.1 %collective-permute-start = (bf16[256,1024]{0,1:T(8,128)(2,1)}, bf16[256,1024]{0,1:T(8,128)(2,1)}, u32[]{:S(2)}, u32[]{:S(2)}) collective-permute-start(bf16[256,1024]{0,1:T(8,128)(2,1)} %pad_maximum_fusion.2), channel_id=1, source_target_pairs={{0,2},{2,4},{4,6},{6,8},{8,10},{10,12},{12,14},{1,3},{3,5},{5,7},{... | collective-permute-start | bytes 1572872 | tf_op jit(solution)/shard_map/ppermute | solution.py:15
  20.6 1.4 copy-start.1
  20.6 3.2 %copy-start.5 = (s32[16]{0:T(128)S(1)}, s32[16]{0:T(128)}, u32[]{:S(2)}) copy-start(s32[16]{0:T(128)} %param.10) | copy-start | bytes 196
  21.9 52.3 %collective-permute-start.5 = (bf16[512,1408]{1,0:T(8,128)(2,1)}, bf16[512,1408]{1,0:T(8,128)(2,1)}, u32[]{:S(2)}, u32[]{:S(2)}) collective-permute-start(bf16[512,1408]{1,0:T(8,128)(2,1)} %pad_maximum_fusion), channel_id=1, source_target_pairs={{0,4},{4,8},{8,12},{12,14},{14,10},{10,6},{6,2},{2,0},{1,5},{5,9},... | collective-permute-start | bytes 4325384 | tf_op jit(solution)/shard_map/ppermute | solution.py:120
  25.5 74.4 %collective-permute-start.6 = (bf16[512,1408]{1,0:T(8,128)(2,1)}, bf16[512,1408]{1,0:T(8,128)(2,1)}, u32[]{:S(2)}, u32[]{:S(2)}) collective-permute-start(bf16[512,1408]{1,0:T(8,128)(2,1)} %pad_maximum_fusion), channel_id=1, source_target_pairs={{0,2},{4,0},{8,4},{12,8},{14,12},{10,14},{6,10},{2,6},{1,3},{5,1},... | collective-permute-start | bytes 4325384 | tf_op jit(solution)/shard_map/ppermute | solution.py:124
  48.6 1.1 copy-start.3
  59.2 27.7 %copy-start.6 = (s32[8]{0:T(128)S(1)}, s32[8]{0:T(128)}, u32[]{:S(2)}) copy-start(s32[8]{0:T(128)} %constant.183.clone) | copy-start | bytes 100
  59.2 32.9 %copy-start.4 = (s32[8]{0:T(128)S(1)}, s32[8]{0:T(128)}, u32[]{:S(2)}) copy-start(s32[8]{0:T(128)} %constant.184.clone) | copy-start | bytes 100
  61.1 40.5 %collective-permute-start.4 = (bf16[256,2048]{0,1:T(8,128)(2,1)S(1)}, bf16[256,2048]{0,1:T(8,128)(2,1)S(1)}, u32[]{:S(2)}, u32[]{:S(2)}) collective-permute-start(bf16[256,2048]{0,1:T(8,128)(2,1)S(1)} %bitcast.269), channel_id=1, source_target_pairs={{0,1},{1,0},{2,3},{3,2},{4,5},{5,4},{6,7},{7,6},{8,9},{9,8},{10,11... | collective-permute-start | bytes 3145736 | tf_op jit(solution)/shard_map/ppermute | solution.py:77
  74.2 44.0 %collective-permute-start.7 = (bf16[512,1408]{1,0:T(8,128)(2,1)}, bf16[512,1408]{1,0:T(8,128)(2,1)}, u32[]{:S(2)}, u32[]{:S(2)}) collective-permute-start(bf16[512,1408]{1,0:T(8,128)(2,1)} %collective-permute-done.5), channel_id=1, source_target_pairs={{0,4},{4,8},{8,12},{12,14},{14,10},{10,6},{6,2},{2,0},{1,5},{5,9},... | collective-permute-start | bytes 4325384 | tf_op jit(solution)/shard_map/ppermute | solution.py:120
  98.3 46.3 %collective-permute-start.12 = (bf16[512,640]{1,0:T(8,128)(2,1)S(1)}, bf16[512,640]{1,0:T(8,128)(2,1)S(1)}, u32[]{:S(2)}, u32[]{:S(2)}) collective-permute-start(bf16[512,640]{1,0:T(8,128)(2,1)S(1)} %slice.84), channel_id=1, source_target_pairs={{0,16},{16,0},{1,17},{17,1},{2,18},{18,2},{3,19},{19,3},{4,20},{20... | collective-permute-start | bytes 1966088 | tf_op jit(solution)/shard_map/ppermute | solution.py:121
  101.0 44.4 %collective-permute-start.13 = (bf16[512,640]{1,0:T(8,128)(2,1)S(1)}, bf16[512,640]{1,0:T(8,128)(2,1)S(1)}, u32[]{:S(2)}, u32[]{:S(2)}) collective-permute-start(bf16[512,640]{1,0:T(8,128)(2,1)S(1)} %slice.85), channel_id=1, source_target_pairs={{0,16},{16,0},{1,17},{17,1},{2,18},{18,2},{3,19},{19,3},{4,20},{20... | collective-permute-start | bytes 1966088 | tf_op jit(solution)/shard_map/ppermute | solution.py:125
  101.6 41.4 %collective-permute-start.8 = (bf16[512,1408]{1,0:T(8,128)(2,1)}, bf16[512,1408]{1,0:T(8,128)(2,1)S(1)}, u32[]{:S(2)}, u32[]{:S(2)}) collective-permute-start(bf16[512,1408]{1,0:T(8,128)(2,1)} %collective-permute-done.6), channel_id=1, source_target_pairs={{0,2},{4,0},{8,4},{12,8},{14,12},{10,14},{6,10},{2,6},{1,3},{5,1},... | collective-permute-start | bytes 4325384 | tf_op jit(solution)/shard_map/ppermute | solution.py:124
  118.2 41.2 %collective-permute-start.9 = (bf16[512,1408]{1,0:T(8,128)(2,1)}, bf16[512,1408]{1,0:T(8,128)(2,1)S(1)}, u32[]{:S(2)}, u32[]{:S(2)}) collective-permute-start(bf16[512,1408]{1,0:T(8,128)(2,1)} %collective-permute-done.7), channel_id=1, source_target_pairs={{0,4},{4,8},{8,12},{12,14},{14,10},{10,6},{6,2},{2,0},{1,5},{5,9},... | collective-permute-start | bytes 4325384 | tf_op jit(solution)/shard_map/ppermute | solution.py:120
  143.1 35.2 %collective-permute-start.10 = (bf16[512,1408]{1,0:T(8,128)(2,1)S(1)}, bf16[512,1408]{1,0:T(8,128)(2,1)S(1)}, u32[]{:S(2)}, u32[]{:S(2)}) collective-permute-start(bf16[512,1408]{1,0:T(8,128)(2,1)S(1)} %collective-permute-done.8), channel_id=1, source_target_pairs={{0,2},{4,0},{8,4},{12,8},{14,12},{10,14},{6,10},{2,6},{1,3},{5,1},... | collective-permute-start | bytes 4325384 | tf_op jit(solution)/shard_map/ppermute | solution.py:124
  147.4 17.7 %collective-permute-start.14 = (bf16[512,640]{1,0:T(8,128)(2,1)S(1)}, bf16[512,640]{1,0:T(8,128)(2,1)S(1)}, u32[]{:S(2)}, u32[]{:S(2)}) collective-permute-start(bf16[512,640]{1,0:T(8,128)(2,1)S(1)} %slice.86), channel_id=1, source_target_pairs={{0,16},{16,0},{1,17},{17,1},{2,18},{18,2},{3,19},{19,3},{4,20},{20... | collective-permute-start | bytes 1966088 | tf_op jit(solution)/shard_map/ppermute | solution.py:121
  148.1 28.7 %collective-permute-start.15 = (bf16[512,640]{1,0:T(8,128)(2,1)S(1)}, bf16[512,640]{1,0:T(8,128)(2,1)S(1)}, u32[]{:S(2)}, u32[]{:S(2)}) collective-permute-start(bf16[512,640]{1,0:T(8,128)(2,1)S(1)} %slice.87), channel_id=1, source_target_pairs={{0,16},{16,0},{1,17},{17,1},{2,18},{18,2},{3,19},{19,3},{4,20},{20... | collective-permute-start | bytes 1966088 | tf_op jit(solution)/shard_map/ppermute | solution.py:125
  159.4 32.5 %collective-permute-start.11 = (bf16[512,1408]{1,0:T(8,128)(2,1)S(1)}, bf16[512,1408]{1,0:T(8,128)(2,1)S(1)}, u32[]{:S(2)}, u32[]{:S(2)}) collective-permute-start(bf16[512,1408]{1,0:T(8,128)(2,1)S(1)} %collective-permute-done.9), channel_id=1, source_target_pairs={{0,4},{4,8},{8,12},{12,14},{14,10},{10,6},{6,2},{2,0},{1,5},{5,9},... | collective-permute-start | bytes 4325384 | tf_op jit(solution)/shard_map/ppermute | solution.py:120
  177.7 17.7 %collective-permute-start.16 = (bf16[512,640]{1,0:T(8,128)(2,1)S(1)}, bf16[512,640]{1,0:T(8,128)(2,1)S(1)}, u32[]{:S(2)}, u32[]{:S(2)}) collective-permute-start(bf16[512,640]{1,0:T(8,128)(2,1)S(1)} %slice.88), channel_id=1, source_target_pairs={{0,16},{16,0},{1,17},{17,1},{2,18},{18,2},{3,19},{19,3},{4,20},{20... | collective-permute-start | bytes 1966088 | tf_op jit(solution)/shard_map/ppermute | solution.py:121
  178.3 31.1 %collective-permute-start.17 = (bf16[512,640]{1,0:T(8,128)(2,1)S(1)}, bf16[512,640]{1,0:T(8,128)(2,1)S(1)}, u32[]{:S(2)}, u32[]{:S(2)}) collective-permute-start(bf16[512,640]{1,0:T(8,128)(2,1)S(1)} %slice.89), channel_id=1, source_target_pairs={{0,16},{16,0},{1,17},{17,1},{2,18},{18,2},{3,19},{19,3},{4,20},{20... | collective-permute-start | bytes 1966088 | tf_op jit(solution)/shard_map/ppermute | solution.py:125
  191.9 28.3 %collective-permute-start.18 = (bf16[512,640]{1,0:T(8,128)(2,1)S(1)}, bf16[512,640]{1,0:T(8,128)(2,1)S(1)}, u32[]{:S(2)}, u32[]{:S(2)}) collective-permute-start(bf16[512,640]{1,0:T(8,128)(2,1)S(1)} %slice.90), channel_id=1, source_target_pairs={{0,16},{16,0},{1,17},{17,1},{2,18},{18,2},{3,19},{19,3},{4,20},{20... | collective-permute-start | bytes 1966088 | tf_op jit(solution)/shard_map/ppermute | solution.py:121

commit v7 on v4

--- a/solution.py
+++ b/solution.py
@@ -143,6 +143,18 @@
     second = jnp.where(group_index == 0, other, mine)
     return jnp.concatenate([parts[0][:, :shared], first, second], axis=1)
 
+def scatter_project(features, weight_columns):
+    count = lax.axis_size("ctx")
+    rows = weight_columns.shape[0]
+    tokens = features.shape[0]
+    chunks = features.reshape(tokens, count, rows)
+    mine = lax.all_to_all(chunks, "ctx", 1, 0, tiled=True).reshape(count * tokens, rows)
+    partial = jnp.dot(mine, weight_columns, preferred_element_type=jnp.float32)
+    return lax.psum_scatter(
+        partial.astype(jnp.bfloat16), "ctx", scatter_dimension=0, tiled=True
+    )
+
+
 def per_device(queries, keys, values, doc_of_block, out_weight):
     tok_rows = queries.shape[0]
     kv_heads = keys.shape[1] // HEAD_SIZE
@@ -164,7 +176,9 @@
         )
         return update(state_now, query_head_rows, key_piece, value_piece, visible)
 
-    arrivals, shared, own = ring_transfer(out_weight)
+    columns = out_weight.shape[1]
+    reduced = (columns // 4) // 128 * 128
+    arrivals, shared, own = ring_transfer(out_weight[:, : columns - reduced])
     initial_state = fresh_state(kv_heads, group_width, tok_rows)
     state_now = attend(initial_state, keys, values, query_start)
     for distance in range(1, reach_devs + 1):
@@ -173,7 +187,12 @@
     attended = finish(state_now, tok_rows, q_heads)
     features = head_features(attended)
     mixed = ring_project(features, arrivals, shared, own, out_weight.shape[0])
-    return mixed.astype(jnp.bfloat16)
+    late = [index for index in (3, 4) if index < len(arrivals)]
+    tied = lax.optimization_barrier((features, [arrivals[index][1] for index in late]))
+    for index, value in zip(late, tied[1]):
+        arrivals[index] = (arrivals[index][0], value, arrivals[index][2])
+    summed = scatter_project(tied[0], out_weight[:, columns - reduced :])
+    return jnp.concatenate([mixed.astype(jnp.bfloat16), summed], axis=1)
 
 
 def solution(mesh):

time: 222 us -> 295 us (1.33)
  waiting for transfers between devices: 78.9 us -> 113 us
  between operations: 9.57 us -> 23.1 us
  local copies, waits for them, and re-layouts: 17.2 us -> 26.8 us
  starting transfers between devices: 49.3 us -> 56.5 us
  matrix products: 56.1 us -> 61.7 us
    all_to_all x0 -> x1, waiting for transfers between devices: none -> 31.1 us  [scatter_project(): lax.all_to_all(chunks, 'ctx', 1, 0, tiled=True)]
    ppermute x3, waiting for transfers between devices: 24.4 us -> 0.01 us  [ring_transfer(): crossed = lax.ppermute(backward[:, shared:], 'group', swap) if own else None]
    ppermute x4, waiting for transfers between devices: 35.4 us -> 53.6 us  [ring_transfer(): forward = lax.ppermute(forward, 'ctx', ahead)]
    ppermute x4, waiting for transfers between devices: 11.6 us -> 26.6 us  [ring_transfer(): crossed = lax.ppermute(forward[:, shared:], 'group', swap) if own else None]
    all_to_all x0 -> x1, starting transfers between devices: none -> 12.9 us  [scatter_project(): lax.all_to_all(chunks, 'ctx', 1, 0, tiled=True)]
    ppermute x3, waiting for transfers between devices: 7.39 us -> 1.65 us  [ring_transfer(): backward = lax.ppermute(backward, 'ctx', behind)]
    dot_general x0 -> x1, matrix products: none -> 4.28 us  [scatter_project(): partial = jnp.dot(mine, weight_columns, preferred_element_type=jnp.float32)]
    all_to_all x0 -> x1, local copies, waits for them, and re-layouts: none -> 3.92 us  [scatter_project(): lax.all_to_all(chunks, 'ctx', 1, 0, tiled=True)]
  transfers between devices with their start and end apart: 23 -> 25, of which waited for: 9 -> 8; matrix products, arithmetic and copies ran while one was open for 35% -> 33% of each run, Pallas kernels for 0% -> 0%
where the time goes in v7:
time: 295 us; the launch traced here: 294 us
  waiting for transfers between devices  113 us (38%)
  matrix products  61.7 us (21%)
  starting transfers between devices  56.5 us (19%)
  local copies, waits for them, and re-layouts  26.8 us (9%)
  between operations  23.1 us (8%)
  other arithmetic  12.4 us (4%)
    ppermute x4, waiting for transfers between devices, ring_transfer(): forward = lax.ppermute(forward, 'ctx', ahead)  53.6 us
    all_to_all x1, waiting for transfers between devices, scatter_project(): lax.all_to_all(chunks, 'ctx', 1, 0, tiled=True)  31.1 us
    ppermute x4, waiting for transfers between devices, ring_transfer(): crossed = lax.ppermute(forward[:, shared:], 'group', swap) if own else None  26.6 us
    ppermute x8, starting transfers between devices, passed_along(): return lax.ppermute(array, axis, pairs)  24.3 us
    dot_general x5, matrix products, update(): jnp.einsum('hgqk,khd->hgqd', weights.astype(jnp.bfloat16), value_head_row...  23.5 us
    all_to_all x1, starting transfers between devices, scatter_project(): lax.all_to_all(chunks, 'ctx', 1, 0, tiled=True)  12.9 us
    dot_general x5, matrix products, update(): jnp.einsum('qhgd,khd->hgqk', query_head_rows, key_head_rows, preferred_el...  12.7 us
    dot_general x8, matrix products, ring_project(): terms = [jnp.dot(piece, carried_block, preferred_element_type=jnp.float32)]  11.9 us
  transfers between devices with their start and end apart: 25, of which 8 were waited for; matrix products, arithmetic and copies ran while one was open for 33% of the time, Pallas kernels for 0%

profile of v7, /device:TPU:0, one launch (start us, length us, event | category | flops | bytes accessed | tf_op | source)
XLA Modules:
  0.0 293.7 jit_solution(17026746603813641427)
XLA Ops:
  6.5 1.8 copy.77
  8.3 6.7 %collective-permute-start.6 = (bf16[256,512]{0,1:T(8,128)(2,1)}, bf16[256,512]{0,1:T(8,128)(2,1)}, u32[]{:S(2)}, u32[]{:S(2)}) collective-permute-start(bf16[256,512]{0,1:T(8,128)(2,1)} %copy.77), channel_id=1, source_target_pairs={{0,8},{2,10},{4,12},{6,14},{1,9},{3,11},{5,13},{7,15},{16,24},{18,... | collective-permute-start | bytes 786440 | tf_op jit(solution)/shard_map/ppermute | solution.py:15
  15.0 5.1 %collective-permute-start.4 = (bf16[256,512]{0,1:T(8,128)(2,1)}, bf16[256,512]{0,1:T(8,128)(2,1)}, u32[]{:S(2)}, u32[]{:S(2)}) collective-permute-start(bf16[256,512]{0,1:T(8,128)(2,1)} %copy.77), channel_id=1, source_target_pairs={{0,6},{2,8},{4,10},{6,12},{8,14},{1,7},{3,9},{5,11},{7,13},{9,15},... | collective-permute-start | bytes 786440 | tf_op jit(solution)/shard_map/ppermute | solution.py:15
  21.4 2.4 collective-permute-start
  23.9 2.7 collective-permute-start.1
  27.7 1.8 copy.115
  29.5 2.7 slice.40
  33.2 1.8 reshape.300
  39.0 2.0 collective-permute-start.3
  41.0 3.9 %fusion.4 = (f32[4,4,256]{2,1,0:T(4,128)S(1)}, f32[4,256,256,4]{2,1,3,0:T(8,128)}) fusion(pred[256,256]{0,1:T(8,128)(4,1)S(1)} %get-tuple-element.32, bf16[256,4,128,1]{0,2,3,1:T(8,128)(2,1)} %bitcast.78, bf16[256,4,4,128]{3,2,1,0:T(4,128)(2,1)S(1)} %reshape.300), kind=kOutput, calls=%fused_computation.31 | convolution fusion | flops 271577088 | bytes 5586944 | tf_op jit(solution)/shard_map/qhgd,khd->hgqk/dot_general | solution.py:33
  44.9 2.0 collective-permute-start.5
  46.9 3.9 %fusion.3 = (f32[4,4,256]{2,1,0:T(4,128)S(1)}, f32[4,256,256,4]{2,1,3,0:T(8,128)}) fusion(pred[256,256]{0,1:T(8,128)(4,1)S(1)} %get-tuple-element.30, bf16[256,4,128,1]{0,2,3,1:T(8,128)(2,1)} %bitcast.74, bf16[256,4,4,128]{3,2,1,0:T(4,128)(2,1)S(1)} %reshape.300), kind=kOutput, calls=%fused_computation.30 | convolution fusion | flops 271577088 | bytes 5586944 | tf_op jit(solution)/shard_map/qhgd,khd->hgqk/dot_general | solution.py:33
  50.8 2.0 collective-permute-start.7
  52.8 3.0 %fusion.2 = (f32[4,4,256]{2,1,0:T(4,128)S(1)}, f32[4,256,256,4]{2,1,3,0:T(8,128)}) fusion(pred[256,256]{0,1:T(8,128)(4,1)S(1)} %get-tuple-element.31, bf16[256,4,128,1]{0,2,3,1:T(8,128)(2,1)S(1)} %bitcast.280, bf16[256,4,4,128]{3,2,1,0:T(4,128)(2,1)S(1)} %reshape.300), kind=kOutput, calls=%fused_computation.29 | convolution fusion | flops 271577088 | bytes 5586944 | tf_op jit(solution)/shard_map/qhgd,khd->hgqk/dot_general | solution.py:33
  57.9 2.6 fusion.23
  61.6 2.2 collective-permute-start.10
  64.9 4.8 %fusion.21 = f32[4,4,256,128]{2,3,1,0:T(8,128)} fusion(bf16[256,4,128,1]{0,2,3,1:T(8,128)(2,1)S(1)} %bitcast.283, f32[4,256,256,4]{2,1,3,0:T(8,128)} %copy-done.3, f32[4,4,256]{2,1,0:T(4,128)S(1)} %get-tuple-element.19, pred[256,256]{0,1:T(8,128)(4,1)S(1)} %get-tuple-element.29), kind=kOutput, calls=%fused_computation.46 | convolution fusion | flops 273678336 | bytes 6635520 | tf_op jit(solution)/shard_map/hgqk,khd->hgqd/dot_general | solution.py:42
  71.9 4.9 %fusion.19 = f32[4,4,256,128]{2,3,1,0:T(8,128)} fusion(bf16[256,4,128,1]{0,2,3,1:T(8,128)(2,1)S(1)} %bitcast.284, f32[4,256,256,4]{2,1,3,0:T(8,128)} %get-tuple-element.45, f32[4,4,256]{2,1,0:T(4,128)S(1)} %get-tuple-element.18, pred[256,256]{0,1:T(8,128)(4,1)S(1)} %get-tuple-element.31), kind=kOutput, calls=%fused_computation.45 | convolution fusion | flops 273678336 | bytes 6635520 | tf_op jit(solution)/shard_map/hgqk,khd->hgqd/dot_general | solution.py:42
  78.9 4.8 %fusion.17 = f32[4,4,256,128]{2,3,1,0:T(8,128)} fusion(bf16[256,4,128,1]{0,2,3,1:T(8,128)(2,1)S(1)} %bitcast.285, f32[4,256,256,4]{2,1,3,0:T(8,128)} %get-tuple-element.43, f32[4,4,256]{2,1,0:T(4,128)S(1)} %get-tuple-element.17, pred[256,256]{0,1:T(8,128)(4,1)S(1)} %get-tuple-element.30), kind=kOutput, calls=%fused_computation.44 | convolution fusion | flops 273678336 | bytes 6635520 | tf_op jit(solution)/shard_map/hgqk,khd->hgqd/dot_general | solution.py:42
  85.9 6.4 %fusion.26 = bf16[256,4,4,128]{0,3,2,1:T(8,128)(2,1)S(1)} fusion(f32[4,4,256,128]{2,3,1,0:T(8,128)} %fusion.17, f32[4,4,256,128]{2,3,1,0:T(8,128)} %fusion.19, f32[4,4,256,128]{2,3,1,0:T(8,128)} %fusion.21, f32[4,4,256,128]{2,3,1,0:T(8,128)} %fusion.23, f32[256,4,4]{0,2,1:T(4,128)S(1)} %get-tuple-element.12, f32[256,4,4]{0,2,1:T(4,128)S(1)} %get-tuple-element.15, ...), kind=kOutput, calls=%fused_computation.50 | convolution fusion | flops 279445504 | bytes 14073856 | tf_op jit(solution)/shard_map/hgqk,khd->hgqd/dot_general | solution.py:42
  92.6 4.4 %collective-permute-start.12 = (bf16[512,1024]{1,0:T(8,128)(2,1)}, bf16[512,1024]{1,0:T(8,128)(2,1)}, u32[]{:S(2)}, u32[]{:S(2)}) collective-permute-start(bf16[512,1024]{1,0:T(8,128)(2,1)} %collective-permute-done.10), channel_id=1, source_target_pairs={{0,2},{4,0},{8,4},{12,8},{14,12},{10,14},{6,10},{2,6},{1,3},{5,1},... | collective-permute-start | bytes 3145736 | tf_op jit(solution)/shard_map/ppermute | solution.py:124
  97.0 1.7 broadcast_select_fusion.1
  100.2 20.8 %collective-permute-done.11 = bf16[512,1024]{1,0:T(8,128)(2,1)} collective-permute-done((bf16[512,1024]{1,0:T(8,128)(2,1)}, bf16[512,1024]{1,0:T(8,128)(2,1)}, u32[]{:S(2)}, u32[]{:S(2)}) %collective-permute-start.11) | collective-permute-done | bytes 1048608 | tf_op jit(solution)/shard_map/ppermute | solution.py:120
  121.0 1.6 collective-permute-done.12
  122.6 12.9 %all-to-all-start = ((bf16[256,8,512]{0,2,1:T(8,128)(2,1)}), bf16[256,8,512]{0,2,1:T(8,128)(2,1)}, u32[]{:S(2)}, u32[]{:S(2)}) async-start(bf16[256,8,512]{0,2,1:T(8,128)(2,1)} %bitcast.275), calls=%async_computation | async-start | bytes 4194304 | tf_op jit(solution)/shard_map/all_to_all | solution.py:151
  146.3 1.9 slice.53
  149.7 1.9 slice.54
  152.1 31.1 %all-to-all-done = bf16[256,8,512]{0,2,1:T(8,128)(2,1)} async-done(((bf16[256,8,512]{0,2,1:T(8,128)(2,1)}), bf16[256,8,512]{0,2,1:T(8,128)(2,1)}, u32[]{:S(2)}, u32[]{:S(2)}) %all-to-all-start) | async-done | bytes 2097184 | tf_op jit(solution)/shard_map/all_to_all | solution.py:151
  183.2 3.9 %copy.97 = bf16[8,256,1,512]{3,1,0,2:T(8,128)(2,1)} copy(bf16[8,256,1,512]{1,3,0,2:T(8,128)(2,1)} %bitcast.61) | data formatting | bytes 4194304 | tf_op jit(solution)/shard_map/all_to_all | solution.py:151
  187.1 4.3 %convolution_convert_fusion = bf16[2048,512]{1,0:T(8,128)(2,1)} fusion(bf16[2048,512]{1,0:T(8,128)(2,1)} %bitcast.276, bf16[512,2048]{1,0:T(8,128)(2,1)} %param.11), kind=kOutput, calls=%fused_computation.32 | convolution fusion | flops 1074790400 | bytes 4718592 | tf_op jit(solution)/shard_map/dot_general | solution.py:152
  191.4 2.1 fusion.138
  193.5 2.1 fusion.134
  196.4 1.8 fusion.136
  198.3 1.8 fusion.132
  201.2 1.6 collective-permute-start.18
  204.4 2.0 collective-permute-start.14
  206.4 2.1 fusion.127
  208.5 2.1 fusion.57
  210.6 5.4 %collective-permute-done.18 = bf16[512,512]{1,0:T(8,128)(2,1)S(1)} collective-permute-done((bf16[512,512]{1,0:T(8,128)(2,1)S(1)}, bf16[512,512]{1,0:T(8,128)(2,1)S(1)}, u32[]{:S(2)}, u32[]{:S(2)}) %collective-permute-start.18) | collective-permute-done | bytes 524320 | tf_op jit(solution)/shard_map/ppermute | solution.py:121
  216.8 20.3 %collective-permute-done.13 = bf16[512,1024]{1,0:T(8,128)(2,1)S(1)} collective-permute-done((bf16[512,1024]{1,0:T(8,128)(2,1)}, bf16[512,1024]{1,0:T(8,128)(2,1)S(1)}, u32[]{:S(2)}, u32[]{:S(2)}) %collective-permute-start.13) | collective-permute-done | bytes 1048608 | tf_op jit(solution)/shard_map/ppermute | solution.py:120
  237.0 2.4 collective-permute-start.15
  240.2 1.7 collective-permute-start.20
  244.2 10.9 %collective-permute-done.20 = bf16[512,512]{1,0:T(8,128)(2,1)S(1)} collective-permute-done((bf16[512,512]{1,0:T(8,128)(2,1)S(1)}, bf16[512,512]{1,0:T(8,128)(2,1)S(1)}, u32[]{:S(2)}, u32[]{:S(2)}) %collective-permute-start.20) | collective-permute-done | bytes 524320 | tf_op jit(solution)/shard_map/ppermute | solution.py:121
  255.8 12.6 %collective-permute-done.15 = bf16[512,1024]{1,0:T(8,128)(2,1)S(1)} collective-permute-done((bf16[512,1024]{1,0:T(8,128)(2,1)S(1)}, bf16[512,1024]{1,0:T(8,128)(2,1)S(1)}, u32[]{:S(2)}, u32[]{:S(2)}) %collective-permute-start.15) | collective-permute-done | bytes 1048608 | tf_op jit(solution)/shard_map/ppermute | solution.py:120
  268.4 1.5 collective-permute-start.22
  271.6 10.3 %collective-permute-done.22 = bf16[512,512]{1,0:T(8,128)(2,1)S(1)} collective-permute-done((bf16[512,512]{1,0:T(8,128)(2,1)S(1)}, bf16[512,512]{1,0:T(8,128)(2,1)S(1)}, u32[]{:S(2)}, u32[]{:S(2)}) %collective-permute-start.22) | collective-permute-done | bytes 524320 | tf_op jit(solution)/shard_map/ppermute | solution.py:121
  282.7 2.0 select_convert_fusion.1
  284.8 2.1 pad_maximum_fusion.2
  (87 shorter events, 33.9 us)
Async XLA Ops:
  8.3 30.7 %collective-permute-start.6 = (bf16[256,512]{0,1:T(8,128)(2,1)}, bf16[256,512]{0,1:T(8,128)(2,1)}, u32[]{:S(2)}, u32[]{:S(2)}) collective-permute-start(bf16[256,512]{0,1:T(8,128)(2,1)} %copy.77), channel_id=1, source_target_pairs={{0,8},{2,10},{4,12},{6,14},{1,9},{3,11},{5,13},{7,15},{16,24},{18,... | collective-permute-start | bytes 786440 | tf_op jit(solution)/shard_map/ppermute | solution.py:15
  15.0 29.9 %collective-permute-start.4 = (bf16[256,512]{0,1:T(8,128)(2,1)}, bf16[256,512]{0,1:T(8,128)(2,1)}, u32[]{:S(2)}, u32[]{:S(2)}) collective-permute-start(bf16[256,512]{0,1:T(8,128)(2,1)} %copy.77), channel_id=1, source_target_pairs={{0,6},{2,8},{4,10},{6,12},{8,14},{1,7},{3,9},{5,11},{7,13},{9,15},... | collective-permute-start | bytes 786440 | tf_op jit(solution)/shard_map/ppermute | solution.py:15
  20.1 30.7 %collective-permute-start.2 = (bf16[256,512]{0,1:T(8,128)(2,1)}, bf16[256,512]{0,1:T(8,128)(2,1)S(1)}, u32[]{:S(2)}, u32[]{:S(2)}) collective-permute-start(bf16[256,512]{0,1:T(8,128)(2,1)} %copy.77), channel_id=1, source_target_pairs={{0,4},{2,6},{4,8},{6,10},{8,12},{10,14},{1,5},{3,7},{5,9},{7,11},{... | collective-permute-start | bytes 786440 | tf_op jit(solution)/shard_map/ppermute | solution.py:15
  21.4 34.3 %collective-permute-start = (bf16[256,512]{0,1:T(8,128)(2,1)}, bf16[256,512]{0,1:T(8,128)(2,1)S(1)}, u32[]{:S(2)}, u32[]{:S(2)}) collective-permute-start(bf16[256,512]{0,1:T(8,128)(2,1)} %copy.77), channel_id=1, source_target_pairs={{0,2},{2,4},{4,6},{6,8},{8,10},{10,12},{12,14},{1,3},{3,5},{5,7},{... | collective-permute-start | bytes 786440 | tf_op jit(solution)/shard_map/ppermute | solution.py:15
  23.9 37.7 %collective-permute-start.1 = (bf16[256,512]{1,0:T(8,128)(2,1)}, bf16[256,512]{1,0:T(8,128)(2,1)}, u32[]{:S(2)}, u32[]{:S(2)}) collective-permute-start(bf16[256,512]{1,0:T(8,128)(2,1)} %param.9), channel_id=1, source_target_pairs={{0,2},{2,4},{4,6},{6,8},{8,10},{10,12},{12,14},{1,3},{3,5},{5,7},{... | collective-permute-start | bytes 786440 | tf_op jit(solution)/shard_map/ppermute | solution.py:15
  29.5 7.9 %copy-start.7 = (s32[16]{0:T(128)S(1)}, s32[16]{0:T(128)}, u32[]{:S(2)}) copy-start(s32[16]{0:T(128)} %param.10) | copy-start | bytes 196
  39.0 31.8 %collective-permute-start.3 = (bf16[256,512]{1,0:T(8,128)(2,1)}, bf16[256,512]{1,0:T(8,128)(2,1)}, u32[]{:S(2)}, u32[]{:S(2)}) collective-permute-start(bf16[256,512]{1,0:T(8,128)(2,1)} %param.9), channel_id=1, source_target_pairs={{0,4},{2,6},{4,8},{6,10},{8,12},{10,14},{1,5},{3,7},{5,9},{7,11},{... | collective-permute-start | bytes 786440 | tf_op jit(solution)/shard_map/ppermute | solution.py:15
  44.9 32.9 %collective-permute-start.5 = (bf16[256,512]{1,0:T(8,128)(2,1)}, bf16[256,512]{1,0:T(8,128)(2,1)}, u32[]{:S(2)}, u32[]{:S(2)}) collective-permute-start(bf16[256,512]{1,0:T(8,128)(2,1)} %param.9), channel_id=1, source_target_pairs={{0,6},{2,8},{4,10},{6,12},{8,14},{1,7},{3,9},{5,11},{7,13},{9,15},... | collective-permute-start | bytes 786440 | tf_op jit(solution)/shard_map/ppermute | solution.py:15
  50.8 34.0 %collective-permute-start.7 = (bf16[256,512]{1,0:T(8,128)(2,1)}, bf16[256,512]{1,0:T(8,128)(2,1)}, u32[]{:S(2)}, u32[]{:S(2)}) collective-permute-start(bf16[256,512]{1,0:T(8,128)(2,1)} %param.9), channel_id=1, source_target_pairs={{0,8},{2,10},{4,12},{6,14},{1,9},{3,11},{5,13},{7,15},{16,24},{18,... | collective-permute-start | bytes 786440 | tf_op jit(solution)/shard_map/ppermute | solution.py:15
  55.8 36.7 %collective-permute-start.9 = (bf16[512,1024]{1,0:T(8,128)(2,1)}, bf16[512,1024]{1,0:T(8,128)(2,1)}, u32[]{:S(2)}, u32[]{:S(2)}) collective-permute-start(bf16[512,1024]{1,0:T(8,128)(2,1)} %pad_maximum_fusion.1), channel_id=1, source_target_pairs={{0,4},{4,8},{8,12},{12,14},{14,10},{10,6},{6,2},{2,0},{1,5},{5,9},... | collective-permute-start | bytes 3145736 | tf_op jit(solution)/shard_map/ppermute | solution.py:120
  55.8 2.1 copy-start.5
  56.8 3.7 %copy-start.3 = (f32[4,256,256,4]{2,1,3,0:T(8,128)}, f32[4,256,256,4]{2,1,3,0:T(8,128)S(1)}, u32[]{:S(2)}) copy-start(f32[4,256,256,4]{2,1,3,0:T(8,128)S(1)} %get-tuple-element.47) | copy-start | bytes 12582916
  61.6 31.0 %collective-permute-start.10 = (bf16[512,1024]{1,0:T(8,128)(2,1)}, bf16[512,1024]{1,0:T(8,128)(2,1)}, u32[]{:S(2)}, u32[]{:S(2)}) collective-permute-start(bf16[512,1024]{1,0:T(8,128)(2,1)} %pad_maximum_fusion.1), channel_id=1, source_target_pairs={{0,2},{4,0},{8,4},{12,8},{14,12},{10,14},{6,10},{2,6},{1,3},{5,1},... | collective-permute-start | bytes 3145736 | tf_op jit(solution)/shard_map/ppermute | solution.py:124
  64.9 4.8 %copy-start.2 = (f32[4,256,256,4]{2,1,3,0:T(8,128)S(1)}, f32[4,256,256,4]{2,1,3,0:T(8,128)}, u32[]{:S(2)}) copy-start(f32[4,256,256,4]{2,1,3,0:T(8,128)} %get-tuple-element.45) | copy-start | bytes 12582916
  71.9 4.9 %copy-start.1 = (f32[4,256,256,4]{2,1,3,0:T(8,128)S(1)}, f32[4,256,256,4]{2,1,3,0:T(8,128)}, u32[]{:S(2)}) copy-start(f32[4,256,256,4]{2,1,3,0:T(8,128)} %get-tuple-element.43) | copy-start | bytes 12582916
  78.9 4.9 %copy-start = (f32[4,256,256,4]{2,1,3,0:T(8,128)S(1)}, f32[4,256,256,4]{2,1,3,0:T(8,128)}, u32[]{:S(2)}) copy-start(f32[4,256,256,4]{2,1,3,0:T(8,128)} %get-tuple-element.41) | copy-start | bytes 12582916
  92.4 4.6 %copy-start.4 = (bf16[256,4,4,128]{0,3,2,1:T(8,128)(2,1)}, bf16[256,4,4,128]{0,3,2,1:T(8,128)(2,1)S(1)}, u32[]{:S(2)}) copy-start(bf16[256,4,4,128]{0,3,2,1:T(8,128)(2,1)S(1)} %fusion.26) | copy-start | bytes 3145732
  92.4 4.6 %collective-permute-start.8 = (bf16[256,2048]{0,1:T(8,128)(2,1)S(1)}, bf16[256,2048]{0,1:T(8,128)(2,1)}, u32[]{:S(2)}, u32[]{:S(2)}) collective-permute-start(bf16[256,2048]{0,1:T(8,128)(2,1)S(1)} %bitcast.277), channel_id=1, source_target_pairs={{0,1},{1,0},{2,3},{3,2},{4,5},{5,4},{6,7},{7,6},{8,9},{9,8},{10,11... | collective-permute-start | bytes 3145736 | tf_op jit(solution)/shard_map/ppermute | solution.py:77
  92.5 28.5 %collective-permute-start.11 = (bf16[512,1024]{1,0:T(8,128)(2,1)}, bf16[512,1024]{1,0:T(8,128)(2,1)}, u32[]{:S(2)}, u32[]{:S(2)}) collective-permute-start(bf16[512,1024]{1,0:T(8,128)(2,1)} %collective-permute-done.9), channel_id=1, source_target_pairs={{0,4},{4,8},{8,12},{12,14},{14,10},{10,6},{6,2},{2,0},{1,5},{5,9},... | collective-permute-start | bytes 3145736 | tf_op jit(solution)/shard_map/ppermute | solution.py:120
  92.6 30.1 %collective-permute-start.12 = (bf16[512,1024]{1,0:T(8,128)(2,1)}, bf16[512,1024]{1,0:T(8,128)(2,1)}, u32[]{:S(2)}, u32[]{:S(2)}) collective-permute-start(bf16[512,1024]{1,0:T(8,128)(2,1)} %collective-permute-done.10), channel_id=1, source_target_pairs={{0,2},{4,0},{8,4},{12,8},{14,12},{10,14},{6,10},{2,6},{1,3},{5,1},... | collective-permute-start | bytes 3145736 | tf_op jit(solution)/shard_map/ppermute | solution.py:124
  98.7 37.1 %copy-start.8 = (s32[8]{0:T(128)S(1)}, s32[8]{0:T(128)}, u32[]{:S(2)}) copy-start(s32[8]{0:T(128)} %constant.180.clone) | copy-start | bytes 100
  98.7 42.3 %copy-start.6 = (s32[8]{0:T(128)S(1)}, s32[8]{0:T(128)}, u32[]{:S(2)}) copy-start(s32[8]{0:T(128)} %constant.181.clone) | copy-start | bytes 100
  122.6 60.5 %all-to-all-start = ((bf16[256,8,512]{0,2,1:T(8,128)(2,1)}), bf16[256,8,512]{0,2,1:T(8,128)(2,1)}, u32[]{:S(2)}, u32[]{:S(2)}) async-start(bf16[256,8,512]{0,2,1:T(8,128)(2,1)} %bitcast.275), calls=%async_computation | async-start | bytes 4194304 | tf_op jit(solution)/shard_map/all_to_all | solution.py:151
  135.5 149.3 %reduce-scatter.2.cloned.1.call-start = ((), (), s32[]{:S(2)}) async-start(), calls=%async_computation.2 | async-start | bytes 2359296 | tf_op jit(solution)/shard_map/reduce_scatter | solution.py:153
  148.2 48.3 %collective-permute-start.16 = (bf16[512,512]{1,0:T(8,128)(2,1)}, bf16[512,512]{1,0:T(8,128)(2,1)}, u32[]{:S(2)}, u32[]{:S(2)}) collective-permute-start(bf16[512,512]{1,0:T(8,128)(2,1)} %slice.53), channel_id=1, source_target_pairs={{0,16},{16,0},{1,17},{17,1},{2,18},{18,2},{3,19},{19,3},{4,20},{20... | collective-permute-start | bytes 1572872 | tf_op jit(solution)/shard_map/ppermute | solution.py:121
  151.5 46.7 %collective-permute-start.17 = (bf16[512,512]{1,0:T(8,128)(2,1)}, bf16[512,512]{1,0:T(8,128)(2,1)}, u32[]{:S(2)}, u32[]{:S(2)}) collective-permute-start(bf16[512,512]{1,0:T(8,128)(2,1)} %slice.54), channel_id=1, source_target_pairs={{0,16},{16,0},{1,17},{17,1},{2,18},{18,2},{3,19},{19,3},{4,20},{20... | collective-permute-start | bytes 1572872 | tf_op jit(solution)/shard_map/ppermute | solution.py:125
  198.2 38.8 %collective-permute-start.13 = (bf16[512,1024]{1,0:T(8,128)(2,1)}, bf16[512,1024]{1,0:T(8,128)(2,1)S(1)}, u32[]{:S(2)}, u32[]{:S(2)}) collective-permute-start(bf16[512,1024]{1,0:T(8,128)(2,1)} %collective-permute-done.11), channel_id=1, source_target_pairs={{0,4},{4,8},{8,12},{12,14},{14,10},{10,6},{6,2},{2,0},{1,5},{5,9},... | collective-permute-start | bytes 3145736 | tf_op jit(solution)/shard_map/ppermute | solution.py:120
  201.2 14.9 %collective-permute-start.18 = (bf16[512,512]{1,0:T(8,128)(2,1)S(1)}, bf16[512,512]{1,0:T(8,128)(2,1)S(1)}, u32[]{:S(2)}, u32[]{:S(2)}) collective-permute-start(bf16[512,512]{1,0:T(8,128)(2,1)S(1)} %slice.55), channel_id=1, source_target_pairs={{0,16},{16,0},{1,17},{17,1},{2,18},{18,2},{3,19},{19,3},{4,20},{20... | collective-permute-start | bytes 1572872 | tf_op jit(solution)/shard_map/ppermute | solution.py:121
  203.8 35.6 %collective-permute-start.19 = (bf16[512,512]{1,0:T(8,128)(2,1)S(1)}, bf16[512,512]{1,0:T(8,128)(2,1)S(1)}, u32[]{:S(2)}, u32[]{:S(2)}) collective-permute-start(bf16[512,512]{1,0:T(8,128)(2,1)S(1)} %slice.56), channel_id=1, source_target_pairs={{0,16},{16,0},{1,17},{17,1},{2,18},{18,2},{3,19},{19,3},{4,20},{20... | collective-permute-start | bytes 1572872 | tf_op jit(solution)/shard_map/ppermute | solution.py:125
  204.4 37.5 %collective-permute-start.14 = (bf16[512,1024]{1,0:T(8,128)(2,1)}, bf16[512,1024]{1,0:T(8,128)(2,1)S(1)}, u32[]{:S(2)}, u32[]{:S(2)}) collective-permute-start(bf16[512,1024]{1,0:T(8,128)(2,1)} %collective-permute-done.12), channel_id=1, source_target_pairs={{0,2},{4,0},{8,4},{12,8},{14,12},{10,14},{6,10},{2,6},{1,3},{5,1},... | collective-permute-start | bytes 3145736 | tf_op jit(solution)/shard_map/ppermute | solution.py:124
  237.0 31.4 %collective-permute-start.15 = (bf16[512,1024]{1,0:T(8,128)(2,1)S(1)}, bf16[512,1024]{1,0:T(8,128)(2,1)S(1)}, u32[]{:S(2)}, u32[]{:S(2)}) collective-permute-start(bf16[512,1024]{1,0:T(8,128)(2,1)S(1)} %collective-permute-done.13), channel_id=1, source_target_pairs={{0,4},{4,8},{8,12},{12,14},{14,10},{10,6},{6,2},{2,0},{1,5},{5,9},... | collective-permute-start | bytes 3145736 | tf_op jit(solution)/shard_map/ppermute | solution.py:120
  240.2 14.9 %collective-permute-start.20 = (bf16[512,512]{1,0:T(8,128)(2,1)S(1)}, bf16[512,512]{1,0:T(8,128)(2,1)S(1)}, u32[]{:S(2)}, u32[]{:S(2)}) collective-permute-start(bf16[512,512]{1,0:T(8,128)(2,1)S(1)} %slice.57), channel_id=1, source_target_pairs={{0,16},{16,0},{1,17},{17,1},{2,18},{18,2},{3,19},{19,3},{4,20},{20... | collective-permute-start | bytes 1572872 | tf_op jit(solution)/shard_map/ppermute | solution.py:121
  241.9 28.0 %collective-permute-start.21 = (bf16[512,512]{1,0:T(8,128)(2,1)S(1)}, bf16[512,512]{1,0:T(8,128)(2,1)S(1)}, u32[]{:S(2)}, u32[]{:S(2)}) collective-permute-start(bf16[512,512]{1,0:T(8,128)(2,1)S(1)} %slice.58), channel_id=1, source_target_pairs={{0,16},{16,0},{1,17},{17,1},{2,18},{18,2},{3,19},{19,3},{4,20},{20... | collective-permute-start | bytes 1572872 | tf_op jit(solution)/shard_map/ppermute | solution.py:125
  268.4 13.5 %collective-permute-start.22 = (bf16[512,512]{1,0:T(8,128)(2,1)S(1)}, bf16[512,512]{1,0:T(8,128)(2,1)S(1)}, u32[]{:S(2)}, u32[]{:S(2)}) collective-permute-start(bf16[512,512]{1,0:T(8,128)(2,1)S(1)} %slice.59), channel_id=1, source_target_pairs={{0,16},{16,0},{1,17},{17,1},{2,18},{18,2},{3,19},{19,3},{4,20},{20... | collective-permute-start | bytes 1572872 | tf_op jit(solution)/shard_map/ppermute | solution.py:121
Sparse Core Ops, SparseCore 0:
  191.5 81.8 reduce-scatter.1

commit v8 on v4

--- a/solution.py
+++ b/solution.py
@@ -168,8 +168,10 @@
     initial_state = fresh_state(kv_heads, group_width, tok_rows)
     state_now = attend(initial_state, keys, values, query_start)
     for distance in range(1, reach_devs + 1):
-        prior_keys, prior_values = passed_along((keys, values), "ctx", distance)
-        state_now = attend(state_now, prior_keys, prior_values, query_start - distance * tok_rows)
+        skipped = BLOCK_TOKENS if distance == reach_devs and tok_rows > BLOCK_TOKENS else 0
+        prior_keys, prior_values = passed_along((keys[skipped:], values[skipped:]), "ctx", distance)
+        key_start = query_start - distance * tok_rows + skipped
+        state_now = attend(state_now, prior_keys, prior_values, key_start)
     attended = finish(state_now, tok_rows, q_heads)
     features = head_features(attended)
     mixed = ring_project(features, arrivals, shared, own, out_weight.shape[0])

time: 222 us -> 224 us (level)
  matrix products: 56.1 us -> 50.9 us
  starting transfers between devices: 49.3 us -> 53 us
    ppermute x4, waiting for transfers between devices: 35.4 us -> 47.2 us  [ring_transfer(): forward = lax.ppermute(forward, 'ctx', ahead)]
    ppermute x8, starting transfers between devices: 24.6 us -> 35.7 us  [passed_along(): return lax.ppermute(array, axis, pairs)]
    ppermute x3, waiting for transfers between devices: 24.4 us -> 16.5 us  [ring_transfer(): crossed = lax.ppermute(backward[:, shared:], 'group', swap) if own else None]
    dot_general x5, matrix products: 23.5 us -> 18.1 us  [update(): jnp.einsum('hgqk,khd->hgqd', weights.astype(jnp.bfloat16), value_head_row...]
    ppermute x3, starting transfers between devices: 10.3 us -> 6.18 us  [ring_transfer(): backward = lax.ppermute(backward, 'ctx', behind)]
    ppermute x4, starting transfers between devices: 6.23 us -> 3.04 us  [ring_transfer(): forward = lax.ppermute(forward, 'ctx', ahead)]
  transfers between devices with their start and end apart: 23 -> 23, of which waited for: 9 -> 7; matrix products, arithmetic and copies ran while one was open for 35% -> 33% of each run, Pallas kernels for 0% -> 0%
where the time goes in v8:
time: 224 us; the launch traced here: 223 us
  waiting for transfers between devices  80.1 us (36%)
  starting transfers between devices  53 us (24%)
  matrix products  50.9 us (23%)
  local copies, waits for them, and re-layouts  19.1 us (9%)
  other arithmetic  9.79 us (4%)
  between operations  9.54 us (4%)
    ppermute x4, waiting for transfers between devices, ring_transfer(): forward = lax.ppermute(forward, 'ctx', ahead)  47.2 us
    ppermute x8, starting transfers between devices, passed_along(): return lax.ppermute(array, axis, pairs)  35.7 us
    dot_general x5, matrix products, update(): jnp.einsum('hgqk,khd->hgqd', weights.astype(jnp.bfloat16), value_head_row...  18.1 us
    ppermute x3, waiting for transfers between devices, ring_transfer(): crossed = lax.ppermute(backward[:, shared:], 'group', swap) if own else None  16.5 us
    dot_general x5, matrix products, update(): jnp.einsum('qhgd,khd->hgqk', query_head_rows, key_head_rows, preferred_el...  14.3 us
    dot_general x8, matrix products, ring_project(): terms = [jnp.dot(piece, carried_block, preferred_element_type=jnp.float32)]  10.7 us
    ppermute x4, waiting for transfers between devices, ring_transfer(): crossed = lax.ppermute(forward[:, shared:], 'group', swap) if own else None  9.72 us
    dot_general x8, matrix products, ring_project(): terms.append(jnp.dot(piece, crossed, preferred_element_type=jnp.float32))  7.83 us
  transfers between devices with their start and end apart: 23, of which 7 were waited for; matrix products, arithmetic and copies ran while one was open for 33% of the time, Pallas kernels for 0%

profile of v8, /device:TPU:0, one launch (start us, length us, event | category | flops | bytes accessed | tf_op | source)
XLA Modules:
  0.0 222.5 jit_solution(2641804940656520340)
XLA Ops:
  0.0 1.9 copy.52
  1.9 6.6 %collective-permute-start.4 = (bf16[256,512]{0,1:T(8,128)(2,1)}, bf16[256,512]{0,1:T(8,128)(2,1)}, u32[]{:S(2)}, u32[]{:S(2)}) collective-permute-start(bf16[256,512]{0,1:T(8,128)(2,1)} %copy.52), channel_id=1, source_target_pairs={{0,6},{2,8},{4,10},{6,12},{8,14},{1,7},{3,9},{5,11},{7,13},{9,15},... | collective-permute-start | bytes 786440 | tf_op jit(solution)/shard_map/ppermute | solution.py:15
  8.5 4.2 %collective-permute-start.2 = (bf16[256,512]{0,1:T(8,128)(2,1)}, bf16[256,512]{0,1:T(8,128)(2,1)}, u32[]{:S(2)}, u32[]{:S(2)}) collective-permute-start(bf16[256,512]{0,1:T(8,128)(2,1)} %copy.52), channel_id=1, source_target_pairs={{0,4},{2,6},{4,8},{6,10},{8,12},{10,14},{1,5},{3,7},{5,9},{7,11},{... | collective-permute-start | bytes 786440 | tf_op jit(solution)/shard_map/ppermute | solution.py:15
  12.6 3.5 %collective-permute-start = (bf16[256,512]{0,1:T(8,128)(2,1)}, bf16[256,512]{0,1:T(8,128)(2,1)}, u32[]{:S(2)}, u32[]{:S(2)}) collective-permute-start(bf16[256,512]{0,1:T(8,128)(2,1)} %copy.52), channel_id=1, source_target_pairs={{0,2},{2,4},{4,6},{6,8},{8,10},{10,12},{12,14},{1,3},{3,5},{5,7},{... | collective-permute-start | bytes 786440 | tf_op jit(solution)/shard_map/ppermute | solution.py:15
  17.0 1.3 collective-permute-start.6
  19.3 1.3 collective-permute-start.7
  21.7 1.8 copy.89
  24.3 1.2 slice.40
  25.5 1.4 constant_dynamic-slice_fusion
  27.0 1.2 pad_maximum_fusion
  29.3 2.9 %fusion = (f32[4,4,256]{2,1,0:T(4,128)S(1)}, f32[4,256,256,4]{2,1,3,0:T(8,128)}) fusion(pred[256,256]{0,1:T(8,128)(4,1)S(1)} %get-tuple-element.24, bf16[256,4,4,128]{3,2,1,0:T(4,128)(2,1)S(1)} %reshape.293, bf16[256,4,128,1]{2,1,0,3:T(4,128)(2,1)S(1)} %bitcast.267), kind=kOutput, calls=%fused_computation.24 | convolution fusion | flops 271577088 | bytes 5586944 | tf_op jit(solution)/shard_map/qhgd,khd->hgqk/dot_general | solution.py:33
  32.3 2.7 %collective-permute-start.1 = (bf16[256,512]{1,0:T(8,128)(2,1)}, bf16[256,512]{1,0:T(8,128)(2,1)}, u32[]{:S(2)}, u32[]{:S(2)}) collective-permute-start(bf16[256,512]{1,0:T(8,128)(2,1)} %param.9), channel_id=1, source_target_pairs={{0,2},{2,4},{4,6},{6,8},{8,10},{10,12},{12,14},{1,3},{3,5},{5,7},{... | collective-permute-start | bytes 786440 | tf_op jit(solution)/shard_map/ppermute | solution.py:15
  35.8 14.2 %collective-permute-start.3 = (bf16[256,512]{1,0:T(8,128)(2,1)}, bf16[256,512]{1,0:T(8,128)(2,1)}, u32[]{:S(2)}, u32[]{:S(2)}) collective-permute-start(bf16[256,512]{1,0:T(8,128)(2,1)} %param.9), channel_id=1, source_target_pairs={{0,4},{2,6},{4,8},{6,10},{8,12},{10,14},{1,5},{3,7},{5,9},{7,11},{... | collective-permute-start | bytes 786440 | tf_op jit(solution)/shard_map/ppermute | solution.py:15
  50.0 1.5 fusion.49
  51.5 2.0 collective-permute-start.5
  53.5 3.9 %fusion.3 = (f32[4,4,256]{2,1,0:T(4,128)S(1)}, f32[4,256,256,4]{2,1,3,0:T(8,128)}) fusion(pred[256,256]{0,1:T(8,128)(4,1)S(1)} %get-tuple-element.26, bf16[256,4,128,1]{0,2,3,1:T(8,128)(2,1)} %bitcast.70, bf16[256,4,4,128]{3,2,1,0:T(4,128)(2,1)S(1)} %reshape.293), kind=kOutput, calls=%fused_computation.27 | convolution fusion | flops 271577088 | bytes 5586944 | tf_op jit(solution)/shard_map/qhgd,khd->hgqk/dot_general | solution.py:33
  57.4 2.7 %collective-permute-start.9 = (bf16[512,1408]{1,0:T(8,128)(2,1)}, bf16[512,1408]{1,0:T(8,128)(2,1)}, u32[]{:S(2)}, u32[]{:S(2)}) collective-permute-start(bf16[512,1408]{1,0:T(8,128)(2,1)} %pad_maximum_fusion), channel_id=1, source_target_pairs={{0,4},{4,8},{8,12},{12,14},{14,10},{10,6},{6,2},{2,0},{1,5},{5,9},... | collective-permute-start | bytes 4325384 | tf_op jit(solution)/shard_map/ppermute | solution.py:120
  60.1 3.9 %fusion.2 = (f32[4,4,256]{2,1,0:T(4,128)S(1)}, f32[4,256,256,4]{2,1,3,0:T(8,128)}) fusion(pred[256,256]{0,1:T(8,128)(4,1)S(1)} %get-tuple-element.27, bf16[256,4,128,1]{0,2,3,1:T(8,128)(2,1)} %bitcast.66, bf16[256,4,4,128]{3,2,1,0:T(4,128)(2,1)S(1)} %reshape.293), kind=kOutput, calls=%fused_computation.26 | convolution fusion | flops 271577088 | bytes 5586944 | tf_op jit(solution)/shard_map/qhgd,khd->hgqk/dot_general | solution.py:33
  64.1 2.1 collective-permute-start.10
  66.2 2.1 fusion.1
  69.6 2.6 %fusion.21 = f32[4,4,256,128]{2,3,1,0:T(8,128)} fusion(bf16[256,4,128,1]{0,2,3,1:T(8,128)(2,1)S(1)} %bitcast.268, f32[4,256,256,4]{2,1,3,0:T(8,128)S(1)} %copy-done, f32[4,4,256]{2,1,0:T(4,128)S(1)} %get-tuple-element.23, pred[256,256]{0,1:T(8,128)(4,1)S(1)} %copy-done.11), kind=kOutput, calls=%fused_computation.46 | convolution fusion | flops 273678336 | bytes 6635520 | tf_op jit(solution)/shard_map/hgqk,khd->hgqd/dot_general | solution.py:42
  73.3 1.1 copy.55
  74.4 4.9 %fusion.19 = f32[4,4,256,128]{2,3,1,0:T(8,128)} fusion(bf16[256,4,128,1]{0,2,3,1:T(8,128)(2,1)S(1)} %bitcast.269, f32[4,256,256,4]{2,1,3,0:T(8,128)} %copy-done.3, f32[4,4,256]{2,1,0:T(4,128)S(1)} %get-tuple-element.16, pred[256,256]{0,1:T(8,128)(4,1)S(1)} %copy-done.9), kind=kOutput, calls=%fused_computation.45 | convolution fusion | flops 273678336 | bytes 6635520 | tf_op jit(solution)/shard_map/hgqk,khd->hgqd/dot_general | solution.py:42
  80.3 1.1 copy.60
  81.4 4.8 %fusion.17 = f32[4,4,256,128]{2,3,1,0:T(8,128)} fusion(bf16[256,4,128,1]{0,2,3,1:T(8,128)(2,1)S(1)} %bitcast.270, f32[4,256,256,4]{2,1,3,0:T(8,128)} %get-tuple-element.40, f32[4,4,256]{2,1,0:T(4,128)S(1)} %get-tuple-element.15, pred[256,256]{0,1:T(8,128)(4,1)S(1)} %get-tuple-element.27), kind=kOutput, calls=%fused_computation.44 | convolution fusion | flops 273678336 | bytes 6635520 | tf_op jit(solution)/shard_map/hgqk,khd->hgqd/dot_general | solution.py:42
  87.3 1.1 copy.65
  88.4 3.5 %fusion.15 = f32[4,4,256,128]{2,3,1,0:T(8,128)S(1)} fusion(bf16[256,4,128,1]{0,2,3,1:T(8,128)(2,1)S(1)} %bitcast.271, f32[4,256,256,4]{2,1,3,0:T(8,128)} %get-tuple-element.38, f32[4,4,256]{2,1,0:T(4,128)S(1)} %get-tuple-element.14, pred[256,256]{0,1:T(8,128)(4,1)S(1)} %get-tuple-element.26), kind=kOutput, calls=%fused_computation.43 | convolution fusion | flops 273678336 | bytes 6635520 | tf_op jit(solution)/shard_map/hgqk,khd->hgqd/dot_general | solution.py:42
  93.6 2.3 %fusion.24 = bf16[256,4,4,128]{0,3,2,1:T(8,128)(2,1)} fusion(f32[4,4,256,128]{2,3,1,0:T(8,128)S(1)} %fusion.15, f32[4,4,256,128]{2,3,1,0:T(8,128)S(1)} %copy-done.20, f32[4,4,256,128]{2,3,1,0:T(8,128)S(1)} %copy-done.19, f32[4,4,256,128]{2,3,1,0:T(8,128)S(1)} %copy-done.18, bf16[128,4,128,1]{0,2,3,1:T(8,128)(2,1)S(1)} %bitcast.273, ...), kind=kOutput, calls=%fused_computation.49 | convolution fusion | flops 142606336 | bytes 11812864 | tf_op jit(solution)/shard_map/hgqk,khd->hgqd/dot_general | solution.py:42
  106.2 2.1 collective-permute-start.12
  108.3 1.4 broadcast_select_fusion
  109.7 1.1 slice.53
  110.8 1.6 collective-permute-start.16
  112.4 1.1 slice.54
  114.1 2.3 %fusion.131 = f32[256,1408]{1,0:T(8,128)S(1)} fusion(bf16[512,1408]{1,0:T(8,128)(2,1)} %collective-permute-done.9, s32[]{:T(128)S(6)} %select_n.241, bf16[256,2048]{0,1:T(8,128)(2,1)S(1)} %get-tuple-element.18, bf16[256,2048]{0,1:T(8,128)(2,1)S(1)} %get-tuple-element.17), kind=kOutput, calls=%fused_computation.211 | convolution fusion | flops 369623040 | bytes 4980740 | tf_op jit(solution)/shard_map/dot_general | solution.py:135
  116.5 13.9 %collective-permute-done.11 = bf16[512,1408]{1,0:T(8,128)(2,1)S(1)} collective-permute-done((bf16[512,1408]{1,0:T(8,128)(2,1)}, bf16[512,1408]{1,0:T(8,128)(2,1)S(1)}, u32[]{:S(2)}, u32[]{:S(2)}) %collective-permute-start.11) | collective-permute-done | bytes 1441824 | tf_op jit(solution)/shard_map/ppermute | solution.py:120
  130.4 2.3 %fusion.127 = f32[256,1408]{1,0:T(8,128)S(1)} fusion(bf16[512,1408]{1,0:T(8,128)(2,1)} %collective-permute-done.10, s32[]{:T(128)S(6)} %select_n.244, bf16[256,2048]{0,1:T(8,128)(2,1)S(1)} %get-tuple-element.18, bf16[256,2048]{0,1:T(8,128)(2,1)S(1)} %get-tuple-element.17), kind=kOutput, calls=%fused_computation.209 | convolution fusion | flops 369623040 | bytes 4980740 | tf_op jit(solution)/shard_map/dot_general | solution.py:135
  133.8 6.7 %collective-permute-done.12 = bf16[512,1408]{1,0:T(8,128)(2,1)S(1)} collective-permute-done((bf16[512,1408]{1,0:T(8,128)(2,1)}, bf16[512,1408]{1,0:T(8,128)(2,1)S(1)}, u32[]{:S(2)}, u32[]{:S(2)}) %collective-permute-start.12) | collective-permute-done | bytes 1441824 | tf_op jit(solution)/shard_map/ppermute | solution.py:124
  140.5 2.0 collective-permute-start.14
  144.2 1.6 collective-permute-start.18
  147.4 16.4 %collective-permute-done.13 = bf16[512,1408]{1,0:T(8,128)(2,1)S(1)} collective-permute-done((bf16[512,1408]{1,0:T(8,128)(2,1)S(1)}, bf16[512,1408]{1,0:T(8,128)(2,1)S(1)}, u32[]{:S(2)}, u32[]{:S(2)}) %collective-permute-start.13) | collective-permute-done | bytes 1441824 | tf_op jit(solution)/shard_map/ppermute | solution.py:120
  165.9 8.4 %collective-permute-done.19 = bf16[512,640]{1,0:T(8,128)(2,1)S(1)} collective-permute-done((bf16[512,640]{1,0:T(8,128)(2,1)S(1)}, bf16[512,640]{1,0:T(8,128)(2,1)S(1)}, u32[]{:S(2)}, u32[]{:S(2)}) %collective-permute-start.19) | collective-permute-done | bytes 655392 | tf_op jit(solution)/shard_map/ppermute | solution.py:125
  175.2 1.6 collective-permute-start.20
  179.4 16.9 %collective-permute-done.15 = bf16[512,1408]{1,0:T(8,128)(2,1)S(1)} collective-permute-done((bf16[512,1408]{1,0:T(8,128)(2,1)S(1)}, bf16[512,1408]{1,0:T(8,128)(2,1)S(1)}, u32[]{:S(2)}, u32[]{:S(2)}) %collective-permute-start.15) | collective-permute-done | bytes 1441824 | tf_op jit(solution)/shard_map/ppermute | solution.py:120
  196.4 1.6 collective-permute-start.22
  198.8 8.1 %collective-permute-done.21 = bf16[512,640]{1,0:T(8,128)(2,1)S(1)} collective-permute-done((bf16[512,640]{1,0:T(8,128)(2,1)S(1)}, bf16[512,640]{1,0:T(8,128)(2,1)S(1)}, u32[]{:S(2)}, u32[]{:S(2)}) %collective-permute-start.21) | collective-permute-done | bytes 655392 | tf_op jit(solution)/shard_map/ppermute | solution.py:125
  208.7 9.7 %collective-permute-done.22 = bf16[512,640]{1,0:T(8,128)(2,1)S(1)} collective-permute-done((bf16[512,640]{1,0:T(8,128)(2,1)S(1)}, bf16[512,640]{1,0:T(8,128)(2,1)S(1)}, u32[]{:S(2)}, u32[]{:S(2)}) %collective-permute-start.22) | collective-permute-done | bytes 655392 | tf_op jit(solution)/shard_map/ppermute | solution.py:121
  219.3 2.2 select_convert_fusion.1
  221.4 1.1 pad_maximum_fusion.1
  (109 shorter events, 27.1 us)
Async XLA Ops:
  0.0 23.5 %copy-start.8 = (bf16[256,2048]{1,0:T(8,128)(2,1)S(1)}, bf16[256,2048]{1,0:T(8,128)(2,1)}, u32[]{:S(2)}) copy-start(bf16[256,2048]{1,0:T(8,128)(2,1)} %param.7) | copy-start | bytes 3145732
  1.9 49.6 %collective-permute-start.4 = (bf16[256,512]{0,1:T(8,128)(2,1)}, bf16[256,512]{0,1:T(8,128)(2,1)}, u32[]{:S(2)}, u32[]{:S(2)}) collective-permute-start(bf16[256,512]{0,1:T(8,128)(2,1)} %copy.52), channel_id=1, source_target_pairs={{0,6},{2,8},{4,10},{6,12},{8,14},{1,7},{3,9},{5,11},{7,13},{9,15},... | collective-permute-start | bytes 786440 | tf_op jit(solution)/shard_map/ppermute | solution.py:15
  8.5 48.9 %collective-permute-start.2 = (bf16[256,512]{0,1:T(8,128)(2,1)}, bf16[256,512]{0,1:T(8,128)(2,1)}, u32[]{:S(2)}, u32[]{:S(2)}) collective-permute-start(bf16[256,512]{0,1:T(8,128)(2,1)} %copy.52), channel_id=1, source_target_pairs={{0,4},{2,6},{4,8},{6,10},{8,12},{10,14},{1,5},{3,7},{5,9},{7,11},{... | collective-permute-start | bytes 786440 | tf_op jit(solution)/shard_map/ppermute | solution.py:15
  12.6 51.5 %collective-permute-start = (bf16[256,512]{0,1:T(8,128)(2,1)}, bf16[256,512]{0,1:T(8,128)(2,1)}, u32[]{:S(2)}, u32[]{:S(2)}) collective-permute-start(bf16[256,512]{0,1:T(8,128)(2,1)} %copy.52), channel_id=1, source_target_pairs={{0,2},{2,4},{4,6},{6,8},{8,10},{10,12},{12,14},{1,3},{3,5},{5,7},{... | collective-permute-start | bytes 786440 | tf_op jit(solution)/shard_map/ppermute | solution.py:15
  17.0 18.8 %collective-permute-start.6 = (bf16[128,512]{0,1:T(8,128)(2,1)S(1)}, bf16[128,512]{0,1:T(8,128)(2,1)S(1)}, u32[]{:S(2)}, u32[]{:S(2)}) collective-permute-start(bf16[128,512]{0,1:T(8,128)(2,1)S(1)} %slice.50), channel_id=1, source_target_pairs={{0,8},{2,10},{4,12},{6,14},{1,9},{3,11},{5,13},{7,15},{16,24},{18,... | collective-permute-start | bytes 393224 | tf_op jit(solution)/shard_map/ppermute | solution.py:15
  19.3 13.0 %collective-permute-start.7 = (bf16[128,512]{1,0:T(8,128)(2,1)S(1)}, bf16[128,512]{1,0:T(8,128)(2,1)S(1)}, u32[]{:S(2)}, u32[]{:S(2)}) collective-permute-start(bf16[128,512]{1,0:T(8,128)(2,1)S(1)} %slice.39), channel_id=1, source_target_pairs={{0,8},{2,10},{4,12},{6,14},{1,9},{3,11},{5,13},{7,15},{16,24},{18,... | collective-permute-start | bytes 393224 | tf_op jit(solution)/shard_map/ppermute | solution.py:15
  23.5 3.4 %copy-start.16 = (s32[16]{0:T(128)S(1)}, s32[16]{0:T(128)}, u32[]{:S(2)}) copy-start(s32[16]{0:T(128)} %param.10) | copy-start | bytes 196
  25.4 2.8 %copy-start.4 = (bf16[512,768]{1,0:T(8,128)(2,1)}, bf16[512,768]{1,0:T(8,128)(2,1)S(1)}, u32[]{:S(2)}) copy-start(bf16[512,768]{1,0:T(8,128)(2,1)S(1)} %slice.40) | copy-start | bytes 2359300
  26.9 5.3 %copy-start.6 = (bf16[512,640]{1,0:T(8,128)(2,1)}, bf16[512,640]{1,0:T(8,128)(2,1)S(1)}, u32[]{:S(2)}) copy-start(bf16[512,640]{1,0:T(8,128)(2,1)S(1)} %constant_dynamic-slice_fusion) | copy-start | bytes 1966084
  29.3 2.9 %copy-start.10 = (pred[256,256]{0,1:T(8,128)(4,1)}, pred[256,256]{0,1:T(8,128)(4,1)S(1)}, u32[]{:S(2)}) copy-start(pred[256,256]{0,1:T(8,128)(4,1)S(1)} %get-tuple-element.24) | copy-start | bytes 196612
  32.3 41.0 %collective-permute-start.1 = (bf16[256,512]{1,0:T(8,128)(2,1)}, bf16[256,512]{1,0:T(8,128)(2,1)}, u32[]{:S(2)}, u32[]{:S(2)}) collective-permute-start(bf16[256,512]{1,0:T(8,128)(2,1)} %param.9), channel_id=1, source_target_pairs={{0,2},{2,4},{4,6},{6,8},{8,10},{10,12},{12,14},{1,3},{3,5},{5,7},{... | collective-permute-start | bytes 786440 | tf_op jit(solution)/shard_map/ppermute | solution.py:15
  35.8 14.2 %copy-start.13 = (bf16[128,512]{0,1:T(8,128)(2,1)}, bf16[128,512]{0,1:T(8,128)(2,1)S(1)}, u32[]{:S(2)}) copy-start(bf16[128,512]{0,1:T(8,128)(2,1)S(1)} %collective-permute-done.6) | copy-start | bytes 393220
  35.8 44.5 %collective-permute-start.3 = (bf16[256,512]{1,0:T(8,128)(2,1)}, bf16[256,512]{1,0:T(8,128)(2,1)}, u32[]{:S(2)}, u32[]{:S(2)}) collective-permute-start(bf16[256,512]{1,0:T(8,128)(2,1)} %param.9), channel_id=1, source_target_pairs={{0,4},{2,6},{4,8},{6,10},{8,12},{10,14},{1,5},{3,7},{5,9},{7,11},{... | collective-permute-start | bytes 786440 | tf_op jit(solution)/shard_map/ppermute | solution.py:15
  51.5 35.8 %collective-permute-start.5 = (bf16[256,512]{1,0:T(8,128)(2,1)}, bf16[256,512]{1,0:T(8,128)(2,1)}, u32[]{:S(2)}, u32[]{:S(2)}) collective-permute-start(bf16[256,512]{1,0:T(8,128)(2,1)} %param.9), channel_id=1, source_target_pairs={{0,6},{2,8},{4,10},{6,12},{8,14},{1,7},{3,9},{5,11},{7,13},{9,15},... | collective-permute-start | bytes 786440 | tf_op jit(solution)/shard_map/ppermute | solution.py:15
  57.4 38.5 %collective-permute-start.9 = (bf16[512,1408]{1,0:T(8,128)(2,1)}, bf16[512,1408]{1,0:T(8,128)(2,1)}, u32[]{:S(2)}, u32[]{:S(2)}) collective-permute-start(bf16[512,1408]{1,0:T(8,128)(2,1)} %pad_maximum_fusion), channel_id=1, source_target_pairs={{0,4},{4,8},{8,12},{12,14},{14,10},{10,6},{6,2},{2,0},{1,5},{5,9},... | collective-permute-start | bytes 4325384 | tf_op jit(solution)/shard_map/ppermute | solution.py:120
  60.1 6.0 %copy-start.9 = (pred[256,256]{0,1:T(8,128)(4,1)S(1)}, pred[256,256]{0,1:T(8,128)(4,1)}, u32[]{:S(2)}) copy-start(pred[256,256]{0,1:T(8,128)(4,1)} %get-tuple-element.25) | copy-start | bytes 196612
  64.1 42.1 %collective-permute-start.10 = (bf16[512,1408]{1,0:T(8,128)(2,1)}, bf16[512,1408]{1,0:T(8,128)(2,1)}, u32[]{:S(2)}, u32[]{:S(2)}) collective-permute-start(bf16[512,1408]{1,0:T(8,128)(2,1)} %pad_maximum_fusion), channel_id=1, source_target_pairs={{0,2},{4,0},{8,4},{12,8},{14,12},{10,14},{6,10},{2,6},{1,3},{5,1},... | collective-permute-start | bytes 4325384 | tf_op jit(solution)/shard_map/ppermute | solution.py:124
  66.2 2.3 %copy-start = (f32[4,256,256,4]{2,1,3,0:T(8,128)S(1)}, f32[4,256,256,4]{2,1,3,0:T(8,128)}, u32[]{:S(2)}) copy-start(f32[4,256,256,4]{2,1,3,0:T(8,128)} %get-tuple-element.44) | copy-start | bytes 12582916
  66.2 2.3 %copy-start.11 = (pred[256,256]{0,1:T(8,128)(4,1)S(1)}, pred[256,256]{0,1:T(8,128)(4,1)}, u32[]{:S(2)}) copy-start(pred[256,256]{0,1:T(8,128)(4,1)} %copy-done.10) | copy-start | bytes 196612
  68.3 3.9 %copy-start.3 = (f32[4,256,256,4]{2,1,3,0:T(8,128)}, f32[4,256,256,4]{2,1,3,0:T(8,128)S(1)}, u32[]{:S(2)}) copy-start(f32[4,256,256,4]{2,1,3,0:T(8,128)S(1)} %get-tuple-element.42) | copy-start | bytes 12582916
  68.5 1.2 copy-start.12
  74.4 4.9 %copy-start.2 = (f32[4,256,256,4]{2,1,3,0:T(8,128)S(1)}, f32[4,256,256,4]{2,1,3,0:T(8,128)}, u32[]{:S(2)}) copy-start(f32[4,256,256,4]{2,1,3,0:T(8,128)} %get-tuple-element.40) | copy-start | bytes 12582916
  81.4 4.9 %copy-start.1 = (f32[4,256,256,4]{2,1,3,0:T(8,128)S(1)}, f32[4,256,256,4]{2,1,3,0:T(8,128)}, u32[]{:S(2)}) copy-start(f32[4,256,256,4]{2,1,3,0:T(8,128)} %get-tuple-element.38) | copy-start | bytes 12582916
  88.4 4.2 %copy-start.19 = (f32[4,4,256,128]{2,3,1,0:T(8,128)S(1)}, f32[4,4,256,128]{2,3,1,0:T(8,128)}, u32[]{:S(2)}) copy-start(f32[4,4,256,128]{2,3,1,0:T(8,128)} %fusion.19) | copy-start | bytes 6291460
  88.4 4.2 %copy-start.20 = (f32[4,4,256,128]{2,3,1,0:T(8,128)S(1)}, f32[4,4,256,128]{2,3,1,0:T(8,128)}, u32[]{:S(2)}) copy-start(f32[4,4,256,128]{2,3,1,0:T(8,128)} %fusion.17) | copy-start | bytes 6291460
  91.9 0.9 copy-start.14
  91.9 1.7 copy-start.18
  93.6 2.3 %copy-start.17 = (s32[8]{0:T(128)S(1)}, s32[8]{0:T(128)}, u32[]{:S(2)}) copy-start(s32[8]{0:T(128)} %constant.187.clone) | copy-start | bytes 100
  93.6 7.5 %copy-start.15 = (s32[8]{0:T(128)S(1)}, s32[8]{0:T(128)}, u32[]{:S(2)}) copy-start(s32[8]{0:T(128)} %constant.188.clone) | copy-start | bytes 100
  95.9 12.4 %collective-permute-start.8 = (bf16[256,2048]{0,1:T(8,128)(2,1)}, bf16[256,2048]{0,1:T(8,128)(2,1)S(1)}, u32[]{:S(2)}, u32[]{:S(2)}) collective-permute-start(bf16[256,2048]{0,1:T(8,128)(2,1)} %bitcast.44), channel_id=1, source_target_pairs={{0,1},{1,0},{2,3},{3,2},{4,5},{5,4},{6,7},{7,6},{8,9},{9,8},{10,11... | collective-permute-start | bytes 3145736 | tf_op jit(solution)/shard_map/ppermute | solution.py:77
  95.9 34.5 %collective-permute-start.11 = (bf16[512,1408]{1,0:T(8,128)(2,1)}, bf16[512,1408]{1,0:T(8,128)(2,1)S(1)}, u32[]{:S(2)}, u32[]{:S(2)}) collective-permute-start(bf16[512,1408]{1,0:T(8,128)(2,1)} %collective-permute-done.9), channel_id=1, source_target_pairs={{0,4},{4,8},{8,12},{12,14},{14,10},{10,6},{6,2},{2,0},{1,5},{5,9},... | collective-permute-start | bytes 4325384 | tf_op jit(solution)/shard_map/ppermute | solution.py:120
  106.2 34.2 %collective-permute-start.12 = (bf16[512,1408]{1,0:T(8,128)(2,1)}, bf16[512,1408]{1,0:T(8,128)(2,1)S(1)}, u32[]{:S(2)}, u32[]{:S(2)}) collective-permute-start(bf16[512,1408]{1,0:T(8,128)(2,1)} %collective-permute-done.10), channel_id=1, source_target_pairs={{0,2},{4,0},{8,4},{12,8},{14,12},{10,14},{6,10},{2,6},{1,3},{5,1},... | collective-permute-start | bytes 4325384 | tf_op jit(solution)/shard_map/ppermute | solution.py:124
  110.8 31.7 %collective-permute-start.16 = (bf16[512,640]{1,0:T(8,128)(2,1)S(1)}, bf16[512,640]{1,0:T(8,128)(2,1)S(1)}, u32[]{:S(2)}, u32[]{:S(2)}) collective-permute-start(bf16[512,640]{1,0:T(8,128)(2,1)S(1)} %slice.53), channel_id=1, source_target_pairs={{0,16},{16,0},{1,17},{17,1},{2,18},{18,2},{3,19},{19,3},{4,20},{20... | collective-permute-start | bytes 1966088 | tf_op jit(solution)/shard_map/ppermute | solution.py:121
  113.5 29.8 %collective-permute-start.17 = (bf16[512,640]{1,0:T(8,128)(2,1)S(1)}, bf16[512,640]{1,0:T(8,128)(2,1)S(1)}, u32[]{:S(2)}, u32[]{:S(2)}) collective-permute-start(bf16[512,640]{1,0:T(8,128)(2,1)S(1)} %slice.54), channel_id=1, source_target_pairs={{0,16},{16,0},{1,17},{17,1},{2,18},{18,2},{3,19},{19,3},{4,20},{20... | collective-permute-start | bytes 1966088 | tf_op jit(solution)/shard_map/ppermute | solution.py:125
  116.5 16.3 %copy-start.5 = (bf16[512,768]{1,0:T(8,128)(2,1)S(1)}, bf16[512,768]{1,0:T(8,128)(2,1)}, u32[]{:S(2)}) copy-start(bf16[512,768]{1,0:T(8,128)(2,1)} %copy-done.4) | copy-start | bytes 2359300
  116.5 16.3 %copy-start.7 = (bf16[512,640]{1,0:T(8,128)(2,1)S(1)}, bf16[512,640]{1,0:T(8,128)(2,1)}, u32[]{:S(2)}) copy-start(bf16[512,640]{1,0:T(8,128)(2,1)} %copy-done.6) | copy-start | bytes 1966084
  130.4 33.4 %collective-permute-start.13 = (bf16[512,1408]{1,0:T(8,128)(2,1)S(1)}, bf16[512,1408]{1,0:T(8,128)(2,1)S(1)}, u32[]{:S(2)}, u32[]{:S(2)}) collective-permute-start(bf16[512,1408]{1,0:T(8,128)(2,1)S(1)} %collective-permute-done.11), channel_id=1, source_target_pairs={{0,4},{4,8},{8,12},{12,14},{14,10},{10,6},{6,2},{2,0},{1,5},{5,9},... | collective-permute-start | bytes 4325384 | tf_op jit(solution)/shard_map/ppermute | solution.py:120
  140.5 36.3 %collective-permute-start.14 = (bf16[512,1408]{1,0:T(8,128)(2,1)S(1)}, bf16[512,1408]{1,0:T(8,128)(2,1)S(1)}, u32[]{:S(2)}, u32[]{:S(2)}) collective-permute-start(bf16[512,1408]{1,0:T(8,128)(2,1)S(1)} %collective-permute-done.12), channel_id=1, source_target_pairs={{0,2},{4,0},{8,4},{12,8},{14,12},{10,14},{6,10},{2,6},{1,3},{5,1},... | collective-permute-start | bytes 4325384 | tf_op jit(solution)/shard_map/ppermute | solution.py:124
  144.2 20.9 %collective-permute-start.18 = (bf16[512,640]{1,0:T(8,128)(2,1)S(1)}, bf16[512,640]{1,0:T(8,128)(2,1)S(1)}, u32[]{:S(2)}, u32[]{:S(2)}) collective-permute-start(bf16[512,640]{1,0:T(8,128)(2,1)S(1)} %slice.55), channel_id=1, source_target_pairs={{0,16},{16,0},{1,17},{17,1},{2,18},{18,2},{3,19},{19,3},{4,20},{20... | collective-permute-start | bytes 1966088 | tf_op jit(solution)/shard_map/ppermute | solution.py:121
  145.8 28.5 %collective-permute-start.19 = (bf16[512,640]{1,0:T(8,128)(2,1)S(1)}, bf16[512,640]{1,0:T(8,128)(2,1)S(1)}, u32[]{:S(2)}, u32[]{:S(2)}) collective-permute-start(bf16[512,640]{1,0:T(8,128)(2,1)S(1)} %slice.56), channel_id=1, source_target_pairs={{0,16},{16,0},{1,17},{17,1},{2,18},{18,2},{3,19},{19,3},{4,20},{20... | collective-permute-start | bytes 1966088 | tf_op jit(solution)/shard_map/ppermute | solution.py:125
  163.8 32.6 %collective-permute-start.15 = (bf16[512,1408]{1,0:T(8,128)(2,1)S(1)}, bf16[512,1408]{1,0:T(8,128)(2,1)S(1)}, u32[]{:S(2)}, u32[]{:S(2)}) collective-permute-start(bf16[512,1408]{1,0:T(8,128)(2,1)S(1)} %collective-permute-done.13), channel_id=1, source_target_pairs={{0,4},{4,8},{8,12},{12,14},{14,10},{10,6},{6,2},{2,0},{1,5},{5,9},... | collective-permute-start | bytes 4325384 | tf_op jit(solution)/shard_map/ppermute | solution.py:120
  175.2 22.8 %collective-permute-start.20 = (bf16[512,640]{1,0:T(8,128)(2,1)S(1)}, bf16[512,640]{1,0:T(8,128)(2,1)S(1)}, u32[]{:S(2)}, u32[]{:S(2)}) collective-permute-start(bf16[512,640]{1,0:T(8,128)(2,1)S(1)} %slice.57), channel_id=1, source_target_pairs={{0,16},{16,0},{1,17},{17,1},{2,18},{18,2},{3,19},{19,3},{4,20},{20... | collective-permute-start | bytes 1966088 | tf_op jit(solution)/shard_map/ppermute | solution.py:121
  176.8 30.1 %collective-permute-start.21 = (bf16[512,640]{1,0:T(8,128)(2,1)S(1)}, bf16[512,640]{1,0:T(8,128)(2,1)S(1)}, u32[]{:S(2)}, u32[]{:S(2)}) collective-permute-start(bf16[512,640]{1,0:T(8,128)(2,1)S(1)} %slice.58), channel_id=1, source_target_pairs={{0,16},{16,0},{1,17},{17,1},{2,18},{18,2},{3,19},{19,3},{4,20},{20... | collective-permute-start | bytes 1966088 | tf_op jit(solution)/shard_map/ppermute | solution.py:125
  196.4 22.1 %collective-permute-start.22 = (bf16[512,640]{1,0:T(8,128)(2,1)S(1)}, bf16[512,640]{1,0:T(8,128)(2,1)S(1)}, u32[]{:S(2)}, u32[]{:S(2)}) collective-permute-start(bf16[512,640]{1,0:T(8,128)(2,1)S(1)} %slice.59), channel_id=1, source_target_pairs={{0,16},{16,0},{1,17},{17,1},{2,18},{18,2},{3,19},{19,3},{4,20},{20... | collective-permute-start | bytes 1966088 | tf_op jit(solution)/shard_map/ppermute | solution.py:121

commit v9 on v4

--- a/solution.py
+++ b/solution.py
@@ -97,7 +97,7 @@
     columns = out_weight.shape[1]
     groups = lax.axis_size("group")
     group_index = lax.axis_index("group")
-    own = (columns // 3) // 128 * 128 if groups == 2 else 0
+    own = (columns // 4) // 128 * 128 if groups == 2 else 0
     shared = columns - groups * own if own else columns
     swap = [(0, 1), (1, 0)]
 

time: 222 us -> 215 us (0.968)
  waiting for transfers between devices: 78.9 us -> 57.3 us
  starting transfers between devices: 49.3 us -> 61.9 us
    ppermute x3, waiting for transfers between devices: 24.4 us -> 7.41 us  [ring_transfer(): crossed = lax.ppermute(backward[:, shared:], 'group', swap) if own else None]
    ppermute x3, starting transfers between devices: 10.3 us -> 19.1 us  [ring_transfer(): backward = lax.ppermute(backward, 'ctx', behind)]
    ppermute x4, waiting for transfers between devices: 35.4 us -> 29.5 us  [ring_transfer(): forward = lax.ppermute(forward, 'ctx', ahead)]
    dot_general x5, matrix products: 23.5 us -> 20 us  [update(): jnp.einsum('hgqk,khd->hgqd', weights.astype(jnp.bfloat16), value_head_row...]
    ppermute x4, waiting for transfers between devices: 11.6 us -> 14 us  [ring_transfer(): crossed = lax.ppermute(forward[:, shared:], 'group', swap) if own else None]
  transfers between devices with their start and end apart: 23 -> 23, of which waited for: 9 -> 9; matrix products, arithmetic and copies ran while one was open for 35% -> 37% of each run, Pallas kernels for 0% -> 0%
where the time goes in v9:
time: 215 us; the launch traced here: 214 us
  starting transfers between devices  61.9 us (29%)
  waiting for transfers between devices  57.3 us (27%)
  matrix products  54.6 us (25%)
  local copies, waits for them, and re-layouts  18.6 us (9%)
  other arithmetic  12 us (6%)
  between operations  9.61 us (4%)
    ppermute x4, waiting for transfers between devices, ring_transfer(): forward = lax.ppermute(forward, 'ctx', ahead)  29.5 us
    ppermute x8, starting transfers between devices, passed_along(): return lax.ppermute(array, axis, pairs)  25.8 us
    dot_general x5, matrix products, update(): jnp.einsum('hgqk,khd->hgqd', weights.astype(jnp.bfloat16), value_head_row...  20 us
    ppermute x3, starting transfers between devices, ring_transfer(): backward = lax.ppermute(backward, 'ctx', behind)  19.1 us
    ppermute x4, waiting for transfers between devices, ring_transfer(): crossed = lax.ppermute(forward[:, shared:], 'group', swap) if own else None  14 us
    dot_general x5, matrix products, update(): jnp.einsum('qhgd,khd->hgqk', query_head_rows, key_head_rows, preferred_el...  13.7 us
    dot_general x8, matrix products, ring_project(): terms = [jnp.dot(piece, carried_block, preferred_element_type=jnp.float32)]  13.7 us
    ppermute x4, starting transfers between devices, ring_transfer(): forward = lax.ppermute(forward, 'ctx', ahead)  8.06 us
  transfers between devices with their start and end apart: 23, of which 9 were waited for; matrix products, arithmetic and copies ran while one was open for 37% of the time, Pallas kernels for 0%

profile of v9, /device:TPU:0, one launch (start us, length us, event | category | flops | bytes accessed | tf_op | source)
XLA Modules:
  0.0 214.0 jit_solution(6619333861378954827)
XLA Ops:
  0.0 1.9 copy.52
  1.9 6.7 %collective-permute-start.6 = (bf16[256,512]{0,1:T(8,128)(2,1)}, bf16[256,512]{0,1:T(8,128)(2,1)}, u32[]{:S(2)}, u32[]{:S(2)}) collective-permute-start(bf16[256,512]{0,1:T(8,128)(2,1)} %copy.52), channel_id=1, source_target_pairs={{0,8},{2,10},{4,12},{6,14},{1,9},{3,11},{5,13},{7,15},{16,24},{18,... | collective-permute-start | bytes 786440 | tf_op jit(solution)/shard_map/ppermute | solution.py:15
  8.6 5.1 %collective-permute-start.4 = (bf16[256,512]{0,1:T(8,128)(2,1)}, bf16[256,512]{0,1:T(8,128)(2,1)}, u32[]{:S(2)}, u32[]{:S(2)}) collective-permute-start(bf16[256,512]{0,1:T(8,128)(2,1)} %copy.52), channel_id=1, source_target_pairs={{0,6},{2,8},{4,10},{6,12},{8,14},{1,7},{3,9},{5,11},{7,13},{9,15},... | collective-permute-start | bytes 786440 | tf_op jit(solution)/shard_map/ppermute | solution.py:15
  13.7 2.0 collective-permute-start.2
  15.7 2.4 %collective-permute-start = (bf16[256,512]{0,1:T(8,128)(2,1)}, bf16[256,512]{0,1:T(8,128)(2,1)S(1)}, u32[]{:S(2)}, u32[]{:S(2)}) collective-permute-start(bf16[256,512]{0,1:T(8,128)(2,1)} %copy.52), channel_id=1, source_target_pairs={{0,2},{2,4},{4,6},{6,8},{8,10},{10,12},{12,14},{1,3},{3,5},{5,7},{... | collective-permute-start | bytes 786440 | tf_op jit(solution)/shard_map/ppermute | solution.py:15
  18.1 2.6 %collective-permute-start.1 = (bf16[256,512]{1,0:T(8,128)(2,1)}, bf16[256,512]{1,0:T(8,128)(2,1)}, u32[]{:S(2)}, u32[]{:S(2)}) collective-permute-start(bf16[256,512]{1,0:T(8,128)(2,1)} %param.9), channel_id=1, source_target_pairs={{0,2},{2,4},{4,6},{6,8},{8,10},{10,12},{12,14},{1,3},{3,5},{5,7},{... | collective-permute-start | bytes 786440 | tf_op jit(solution)/shard_map/ppermute | solution.py:15
  21.8 1.8 copy.89
  24.4 1.3 slice.32
  25.7 1.1 constant_dynamic-slice_fusion
  28.4 1.3 pad_maximum_fusion
  29.7 2.0 collective-permute-start.3
  31.8 3.9 %fusion.4 = (f32[4,4,256]{2,1,0:T(4,128)S(1)}, f32[4,256,256,4]{2,1,3,0:T(8,128)}) fusion(pred[256,256]{0,1:T(8,128)(4,1)S(1)} %get-tuple-element.29, bf16[256,4,128,1]{0,2,3,1:T(8,128)(2,1)} %bitcast.74, bf16[256,4,4,128]{3,2,1,0:T(4,128)(2,1)S(1)} %reshape.293), kind=kOutput, calls=%fused_computation.30 | convolution fusion | flops 271577088 | bytes 5586944 | tf_op jit(solution)/shard_map/qhgd,khd->hgqk/dot_general | solution.py:33
  35.6 2.0 collective-permute-start.5
  37.7 3.9 %fusion.3 = (f32[4,4,256]{2,1,0:T(4,128)S(1)}, f32[4,256,256,4]{2,1,3,0:T(8,128)}) fusion(pred[256,256]{0,1:T(8,128)(4,1)S(1)} %get-tuple-element.27, bf16[256,4,128,1]{0,2,3,1:T(8,128)(2,1)} %bitcast.70, bf16[256,4,4,128]{3,2,1,0:T(4,128)(2,1)S(1)} %reshape.293), kind=kOutput, calls=%fused_computation.29 | convolution fusion | flops 271577088 | bytes 5586944 | tf_op jit(solution)/shard_map/qhgd,khd->hgqk/dot_general | solution.py:33
  41.6 2.9 %collective-permute-start.7 = (bf16[256,512]{1,0:T(8,128)(2,1)S(1)}, bf16[256,512]{1,0:T(8,128)(2,1)}, u32[]{:S(2)}, u32[]{:S(2)}) collective-permute-start(bf16[256,512]{1,0:T(8,128)(2,1)S(1)} %copy-done.5), channel_id=1, source_target_pairs={{0,8},{2,10},{4,12},{6,14},{1,9},{3,11},{5,13},{7,15},{16,24},{18,... | collective-permute-start | bytes 786440 | tf_op jit(solution)/shard_map/ppermute | solution.py:15
  44.5 3.9 %fusion.2 = (f32[4,4,256]{2,1,0:T(4,128)S(1)}, f32[4,256,256,4]{2,1,3,0:T(8,128)}) fusion(pred[256,256]{0,1:T(8,128)(4,1)S(1)} %get-tuple-element.28, bf16[256,4,128,1]{0,2,3,1:T(8,128)(2,1)} %bitcast.66, bf16[256,4,4,128]{3,2,1,0:T(4,128)(2,1)S(1)} %reshape.293), kind=kOutput, calls=%fused_computation.28 | convolution fusion | flops 271577088 | bytes 5586944 | tf_op jit(solution)/shard_map/qhgd,khd->hgqk/dot_general | solution.py:33
  48.4 1.3 collective-permute-start.9
  51.9 2.6 %fusion.26 = f32[4,4,256,128]{2,3,1,0:T(8,128)} fusion(bf16[256,4,128,1]{0,2,3,1:T(8,128)(2,1)S(1)} %bitcast.272, f32[4,256,256,4]{2,1,3,0:T(8,128)S(1)} %get-tuple-element.46, f32[4,4,256]{2,1,0:T(4,128)S(1)} %get-tuple-element.24, pred[256,256]{0,1:T(8,128)(4,1)S(1)} %get-tuple-element.25), kind=kOutput, calls=%fused_computation.52 | convolution fusion | flops 273678336 | bytes 6635520 | tf_op jit(solution)/shard_map/hgqk,khd->hgqd/dot_general | solution.py:42
  57.6 4.8 %fusion.24 = f32[4,4,256,128]{2,3,1,0:T(8,128)} fusion(bf16[256,4,128,1]{0,2,3,1:T(8,128)(2,1)S(1)} %bitcast.275, f32[4,256,256,4]{2,1,3,0:T(8,128)} %copy-done.3, f32[4,4,256]{2,1,0:T(4,128)S(1)} %get-tuple-element.17, pred[256,256]{0,1:T(8,128)(4,1)S(1)} %get-tuple-element.26), kind=kOutput, calls=%fused_computation.51 | convolution fusion | flops 273678336 | bytes 6635520 | tf_op jit(solution)/shard_map/hgqk,khd->hgqd/dot_general | solution.py:42
  63.5 1.1 copy.60
  64.6 4.9 %fusion.22 = f32[4,4,256,128]{2,3,1,0:T(8,128)} fusion(bf16[256,4,128,1]{0,2,3,1:T(8,128)(2,1)S(1)} %bitcast.276, f32[4,256,256,4]{2,1,3,0:T(8,128)} %get-tuple-element.42, f32[4,4,256]{2,1,0:T(4,128)S(1)} %get-tuple-element.16, pred[256,256]{0,1:T(8,128)(4,1)S(1)} %get-tuple-element.28), kind=kOutput, calls=%fused_computation.50 | convolution fusion | flops 273678336 | bytes 6635520 | tf_op jit(solution)/shard_map/hgqk,khd->hgqd/dot_general | solution.py:42
  71.6 3.2 %fusion.13 = f32[4,4,256]{2,1,0:T(4,128)S(1)} fusion(f32[4,256,256,4]{2,1,3,0:T(8,128)} %get-tuple-element.38, f32[4,4,256]{2,1,0:T(4,128)S(1)} %get-tuple-element.14, pred[256,256]{0,1:T(8,128)(4,1)S(1)} %get-tuple-element.29), kind=kLoop, calls=%fused_computation.39 | loop fusion | flops 5238784 | bytes 4292608 | tf_op jit(solution)/shard_map/reduce_sum | solution.py:49
  76.0 3.5 %fusion.20 = f32[4,4,256,128]{2,3,1,0:T(8,128)S(1)} fusion(bf16[256,4,128,1]{0,2,3,1:T(8,128)(2,1)S(1)} %bitcast.274, f32[4,256,256,4]{2,1,3,0:T(8,128)} %get-tuple-element.40, f32[4,4,256]{2,1,0:T(4,128)S(1)} %get-tuple-element.15, pred[256,256]{0,1:T(8,128)(4,1)S(1)} %get-tuple-element.27), kind=kOutput, calls=%fused_computation.49 | convolution fusion | flops 273678336 | bytes 6635520 | tf_op jit(solution)/shard_map/hgqk,khd->hgqd/dot_general | solution.py:42
  80.1 4.2 %fusion.29 = bf16[256,4,4,128]{0,3,2,1:T(8,128)(2,1)S(1)} fusion(f32[4,4,256,128]{2,3,1,0:T(8,128)S(1)} %fusion.20, f32[4,4,256,128]{2,3,1,0:T(8,128)} %fusion.22, f32[4,4,256,128]{2,3,1,0:T(8,128)} %fusion.24, f32[4,4,256,128]{2,3,1,0:T(8,128)S(1)} %copy-done.10, f32[256,4,4]{0,2,1:T(4,128)S(1)} %get-tuple-element.10, ...), kind=kOutput, calls=%fused_computation.55 | convolution fusion | flops 279445504 | bytes 14073856 | tf_op jit(solution)/shard_map/hgqk,khd->hgqd/dot_general | solution.py:42
  84.4 5.4 %collective-permute-start.11 = (bf16[512,1536]{1,0:T(8,128)(2,1)}, bf16[512,1536]{1,0:T(8,128)(2,1)}, u32[]{:S(2)}, u32[]{:S(2)}) collective-permute-start(bf16[512,1536]{1,0:T(8,128)(2,1)} %collective-permute-done.9), channel_id=1, source_target_pairs={{0,4},{4,8},{8,12},{12,14},{14,10},{10,6},{6,2},{2,0},{1,5},{5,9},... | collective-permute-start | bytes 4718600 | tf_op jit(solution)/shard_map/ppermute | solution.py:120
  89.9 1.6 collective-permute-done.10
  91.4 4.4 %collective-permute-start.12 = (bf16[512,1536]{1,0:T(8,128)(2,1)}, bf16[512,1536]{1,0:T(8,128)(2,1)}, u32[]{:S(2)}, u32[]{:S(2)}) collective-permute-start(bf16[512,1536]{1,0:T(8,128)(2,1)} %collective-permute-done.10), channel_id=1, source_target_pairs={{0,2},{4,0},{8,4},{12,8},{14,12},{10,14},{6,10},{2,6},{1,3},{5,1},... | collective-permute-start | bytes 4718600 | tf_op jit(solution)/shard_map/ppermute | solution.py:124
  106.3 1.4 broadcast_select_fusion
  108.7 1.6 collective-permute-start.16
  112.0 13.1 %collective-permute-done.11 = bf16[512,1536]{1,0:T(8,128)(2,1)} collective-permute-done((bf16[512,1536]{1,0:T(8,128)(2,1)}, bf16[512,1536]{1,0:T(8,128)(2,1)}, u32[]{:S(2)}, u32[]{:S(2)}) %collective-permute-start.11) | collective-permute-done | bytes 1572896 | tf_op jit(solution)/shard_map/ppermute | solution.py:120
  125.0 1.3 collective-permute-start.13
  126.3 2.4 %fusion.134 = f32[256,1536]{1,0:T(8,128)S(1)} fusion(bf16[512,1536]{1,0:T(8,128)(2,1)} %collective-permute-done.9, s32[]{:T(128)S(6)} %select_n.237, bf16[256,2048]{0,1:T(8,128)(2,1)S(1)} %get-tuple-element.19, bf16[256,2048]{0,1:T(8,128)(2,1)S(1)} %get-tuple-element.18), kind=kOutput, calls=%fused_computation.212 | convolution fusion | flops 403177472 | bytes 5242884 | tf_op jit(solution)/shard_map/dot_general | solution.py:135
  128.7 2.4 %fusion.130 = f32[256,1536]{1,0:T(8,128)S(1)} fusion(bf16[512,1536]{1,0:T(8,128)(2,1)} %collective-permute-done.10, s32[]{:T(128)S(6)} %select_n.240, bf16[256,2048]{0,1:T(8,128)(2,1)S(1)} %get-tuple-element.19, bf16[256,2048]{0,1:T(8,128)(2,1)S(1)} %get-tuple-element.18), kind=kOutput, calls=%fused_computation.210 | convolution fusion | flops 403177472 | bytes 5242884 | tf_op jit(solution)/shard_map/dot_general | solution.py:135
  132.7 13.7 %collective-permute-start.14 = (bf16[512,1536]{1,0:T(8,128)(2,1)}, bf16[512,1536]{1,0:T(8,128)(2,1)S(1)}, u32[]{:S(2)}, u32[]{:S(2)}) collective-permute-start(bf16[512,1536]{1,0:T(8,128)(2,1)} %collective-permute-done.12), channel_id=1, source_target_pairs={{0,2},{4,0},{8,4},{12,8},{14,12},{10,14},{6,10},{2,6},{1,3},{5,1},... | collective-permute-start | bytes 4718600 | tf_op jit(solution)/shard_map/ppermute | solution.py:124
  149.0 1.6 collective-permute-start.18
  152.3 2.4 %fusion.123 = f32[256,1536]{1,0:T(8,128)S(1)} fusion(bf16[512,1536]{1,0:T(8,128)(2,1)} %collective-permute-done.12, s32[]{:T(128)S(6)} %select_n.246, bf16[256,2048]{0,1:T(8,128)(2,1)S(1)} %get-tuple-element.19, bf16[256,2048]{0,1:T(8,128)(2,1)S(1)} %get-tuple-element.18), kind=kOutput, calls=%fused_computation.207 | convolution fusion | flops 403177472 | bytes 5242884 | tf_op jit(solution)/shard_map/dot_general | solution.py:135
  154.7 7.8 %collective-permute-done.13 = bf16[512,1536]{1,0:T(8,128)(2,1)S(1)} collective-permute-done((bf16[512,1536]{1,0:T(8,128)(2,1)}, bf16[512,1536]{1,0:T(8,128)(2,1)S(1)}, u32[]{:S(2)}, u32[]{:S(2)}) %collective-permute-start.13) | collective-permute-done | bytes 1572896 | tf_op jit(solution)/shard_map/ppermute | solution.py:120
  162.4 2.4 %fusion.16 = f32[256,1536]{1,0:T(8,128)S(1)} fusion(f32[256,1536]{1,0:T(8,128)S(1)} %fusion.123, f32[256,1536]{1,0:T(8,128)S(1)} %fusion.17, bf16[512,1536]{1,0:T(8,128)(2,1)} %collective-permute-done.11, s32[]{:T(128)S(6)} %select_n.243, bf16[256,2048]{0,1:T(8,128)(2,1)S(1)} %get-tuple-element.19, bf16[256,2048]{0,1:T(8,128)(2,1)S(1)} %get-tuple-element.18), kind=kOutput, calls=%fused_computation.45 | convolution fusion | flops 403963904 | bytes 8388612 | tf_op jit(solution)/shard_map/dot_general | solution.py:135
  165.6 7.4 %collective-permute-done.19 = bf16[512,512]{1,0:T(8,128)(2,1)S(1)} collective-permute-done((bf16[512,512]{1,0:T(8,128)(2,1)S(1)}, bf16[512,512]{1,0:T(8,128)(2,1)S(1)}, u32[]{:S(2)}, u32[]{:S(2)}) %collective-permute-start.19) | collective-permute-done | bytes 524320 | tf_op jit(solution)/shard_map/ppermute | solution.py:125
  173.8 1.6 collective-permute-start.20
  175.4 4.3 %collective-permute-done.14 = bf16[512,1536]{1,0:T(8,128)(2,1)S(1)} collective-permute-done((bf16[512,1536]{1,0:T(8,128)(2,1)}, bf16[512,1536]{1,0:T(8,128)(2,1)S(1)}, u32[]{:S(2)}, u32[]{:S(2)}) %collective-permute-start.14) | collective-permute-done | bytes 1572896 | tf_op jit(solution)/shard_map/ppermute | solution.py:124
  179.7 1.6 collective-permute-start.21
  183.4 5.3 %collective-permute-done.20 = bf16[512,512]{1,0:T(8,128)(2,1)S(1)} collective-permute-done((bf16[512,512]{1,0:T(8,128)(2,1)S(1)}, bf16[512,512]{1,0:T(8,128)(2,1)S(1)}, u32[]{:S(2)}, u32[]{:S(2)}) %collective-permute-start.20) | collective-permute-done | bytes 524320 | tf_op jit(solution)/shard_map/ppermute | solution.py:121
  189.5 8.7 %collective-permute-done.15 = bf16[512,1536]{1,0:T(8,128)(2,1)S(1)} collective-permute-done((bf16[512,1536]{1,0:T(8,128)(2,1)S(1)}, bf16[512,1536]{1,0:T(8,128)(2,1)S(1)}, u32[]{:S(2)}, u32[]{:S(2)}) %collective-permute-start.15) | collective-permute-done | bytes 1572896 | tf_op jit(solution)/shard_map/ppermute | solution.py:120
  198.2 1.5 collective-permute-start.22
  201.5 8.7 %collective-permute-done.22 = bf16[512,512]{1,0:T(8,128)(2,1)S(1)} collective-permute-done((bf16[512,512]{1,0:T(8,128)(2,1)S(1)}, bf16[512,512]{1,0:T(8,128)(2,1)S(1)}, u32[]{:S(2)}, u32[]{:S(2)}) %collective-permute-start.22) | collective-permute-done | bytes 524320 | tf_op jit(solution)/shard_map/ppermute | solution.py:121
  210.9 2.0 select_convert_fusion.1
  212.9 1.1 pad_maximum_fusion.1
  (83 shorter events, 30.5 us)
Async XLA Ops:
  0.0 23.6 %copy-start.4 = (bf16[256,2048]{1,0:T(8,128)(2,1)S(1)}, bf16[256,2048]{1,0:T(8,128)(2,1)}, u32[]{:S(2)}) copy-start(bf16[256,2048]{1,0:T(8,128)(2,1)} %param.7) | copy-start | bytes 3145732
  1.9 27.9 %collective-permute-start.6 = (bf16[256,512]{0,1:T(8,128)(2,1)}, bf16[256,512]{0,1:T(8,128)(2,1)}, u32[]{:S(2)}, u32[]{:S(2)}) collective-permute-start(bf16[256,512]{0,1:T(8,128)(2,1)} %copy.52), channel_id=1, source_target_pairs={{0,8},{2,10},{4,12},{6,14},{1,9},{3,11},{5,13},{7,15},{16,24},{18,... | collective-permute-start | bytes 786440 | tf_op jit(solution)/shard_map/ppermute | solution.py:15
  8.6 27.1 %collective-permute-start.4 = (bf16[256,512]{0,1:T(8,128)(2,1)}, bf16[256,512]{0,1:T(8,128)(2,1)}, u32[]{:S(2)}, u32[]{:S(2)}) collective-permute-start(bf16[256,512]{0,1:T(8,128)(2,1)} %copy.52), channel_id=1, source_target_pairs={{0,6},{2,8},{4,10},{6,12},{8,14},{1,7},{3,9},{5,11},{7,13},{9,15},... | collective-permute-start | bytes 786440 | tf_op jit(solution)/shard_map/ppermute | solution.py:15
  13.7 27.9 %collective-permute-start.2 = (bf16[256,512]{0,1:T(8,128)(2,1)}, bf16[256,512]{0,1:T(8,128)(2,1)}, u32[]{:S(2)}, u32[]{:S(2)}) collective-permute-start(bf16[256,512]{0,1:T(8,128)(2,1)} %copy.52), channel_id=1, source_target_pairs={{0,4},{2,6},{4,8},{6,10},{8,12},{10,14},{1,5},{3,7},{5,9},{7,11},{... | collective-permute-start | bytes 786440 | tf_op jit(solution)/shard_map/ppermute | solution.py:15
  15.7 32.7 %collective-permute-start = (bf16[256,512]{0,1:T(8,128)(2,1)}, bf16[256,512]{0,1:T(8,128)(2,1)S(1)}, u32[]{:S(2)}, u32[]{:S(2)}) collective-permute-start(bf16[256,512]{0,1:T(8,128)(2,1)} %copy.52), channel_id=1, source_target_pairs={{0,2},{2,4},{4,6},{6,8},{8,10},{10,12},{12,14},{1,3},{3,5},{5,7},{... | collective-permute-start | bytes 786440 | tf_op jit(solution)/shard_map/ppermute | solution.py:15
  18.1 37.5 %collective-permute-start.1 = (bf16[256,512]{1,0:T(8,128)(2,1)}, bf16[256,512]{1,0:T(8,128)(2,1)}, u32[]{:S(2)}, u32[]{:S(2)}) collective-permute-start(bf16[256,512]{1,0:T(8,128)(2,1)} %param.9), channel_id=1, source_target_pairs={{0,2},{2,4},{4,6},{6,8},{8,10},{10,12},{12,14},{1,3},{3,5},{5,7},{... | collective-permute-start | bytes 786440 | tf_op jit(solution)/shard_map/ppermute | solution.py:15
  24.3 2.4 %copy-start.8 = (s32[16]{0:T(128)S(1)}, s32[16]{0:T(128)}, u32[]{:S(2)}) copy-start(s32[16]{0:T(128)} %param.10) | copy-start | bytes 196
  28.4 1.4 copy-start.5
  29.7 33.8 %collective-permute-start.3 = (bf16[256,512]{1,0:T(8,128)(2,1)S(1)}, bf16[256,512]{1,0:T(8,128)(2,1)}, u32[]{:S(2)}, u32[]{:S(2)}) collective-permute-start(bf16[256,512]{1,0:T(8,128)(2,1)S(1)} %copy-done.5), channel_id=1, source_target_pairs={{0,4},{2,6},{4,8},{6,10},{8,12},{10,14},{1,5},{3,7},{5,9},{7,11},{... | collective-permute-start | bytes 786440 | tf_op jit(solution)/shard_map/ppermute | solution.py:15
  35.6 34.9 %collective-permute-start.5 = (bf16[256,512]{1,0:T(8,128)(2,1)S(1)}, bf16[256,512]{1,0:T(8,128)(2,1)}, u32[]{:S(2)}, u32[]{:S(2)}) collective-permute-start(bf16[256,512]{1,0:T(8,128)(2,1)S(1)} %copy-done.5), channel_id=1, source_target_pairs={{0,6},{2,8},{4,10},{6,12},{8,14},{1,7},{3,9},{5,11},{7,13},{9,15},... | collective-permute-start | bytes 786440 | tf_op jit(solution)/shard_map/ppermute | solution.py:15
  41.6 33.3 %collective-permute-start.7 = (bf16[256,512]{1,0:T(8,128)(2,1)S(1)}, bf16[256,512]{1,0:T(8,128)(2,1)}, u32[]{:S(2)}, u32[]{:S(2)}) collective-permute-start(bf16[256,512]{1,0:T(8,128)(2,1)S(1)} %copy-done.5), channel_id=1, source_target_pairs={{0,8},{2,10},{4,12},{6,14},{1,9},{3,11},{5,13},{7,15},{16,24},{18,... | collective-permute-start | bytes 786440 | tf_op jit(solution)/shard_map/ppermute | solution.py:15
  48.4 36.0 %collective-permute-start.9 = (bf16[512,1536]{1,0:T(8,128)(2,1)}, bf16[512,1536]{1,0:T(8,128)(2,1)}, u32[]{:S(2)}, u32[]{:S(2)}) collective-permute-start(bf16[512,1536]{1,0:T(8,128)(2,1)} %pad_maximum_fusion), channel_id=1, source_target_pairs={{0,4},{4,8},{8,12},{12,14},{14,10},{10,6},{6,2},{2,0},{1,5},{5,9},... | collective-permute-start | bytes 4718600 | tf_op jit(solution)/shard_map/ppermute | solution.py:120
  50.7 3.8 %copy-start.3 = (f32[4,256,256,4]{2,1,3,0:T(8,128)}, f32[4,256,256,4]{2,1,3,0:T(8,128)S(1)}, u32[]{:S(2)}) copy-start(f32[4,256,256,4]{2,1,3,0:T(8,128)S(1)} %get-tuple-element.44) | copy-start | bytes 12582916
  50.8 1.1 copy-start.6
  55.6 35.9 %collective-permute-start.10 = (bf16[512,1536]{1,0:T(8,128)(2,1)}, bf16[512,1536]{1,0:T(8,128)(2,1)}, u32[]{:S(2)}, u32[]{:S(2)}) collective-permute-start(bf16[512,1536]{1,0:T(8,128)(2,1)} %pad_maximum_fusion), channel_id=1, source_target_pairs={{0,2},{4,0},{8,4},{12,8},{14,12},{10,14},{6,10},{2,6},{1,3},{5,1},... | collective-permute-start | bytes 4718600 | tf_op jit(solution)/shard_map/ppermute | solution.py:124
  57.6 4.8 %copy-start.2 = (f32[4,256,256,4]{2,1,3,0:T(8,128)S(1)}, f32[4,256,256,4]{2,1,3,0:T(8,128)}, u32[]{:S(2)}) copy-start(f32[4,256,256,4]{2,1,3,0:T(8,128)} %get-tuple-element.42) | copy-start | bytes 12582916
  64.6 4.9 %copy-start.1 = (f32[4,256,256,4]{2,1,3,0:T(8,128)S(1)}, f32[4,256,256,4]{2,1,3,0:T(8,128)}, u32[]{:S(2)}) copy-start(f32[4,256,256,4]{2,1,3,0:T(8,128)} %get-tuple-element.40) | copy-start | bytes 12582916
  76.0 3.5 %copy-start = (f32[4,256,256,4]{2,1,3,0:T(8,128)S(1)}, f32[4,256,256,4]{2,1,3,0:T(8,128)}, u32[]{:S(2)}) copy-start(f32[4,256,256,4]{2,1,3,0:T(8,128)} %get-tuple-element.38) | copy-start | bytes 12582916
  76.0 4.1 %copy-start.10 = (f32[4,4,256,128]{2,3,1,0:T(8,128)S(1)}, f32[4,4,256,128]{2,3,1,0:T(8,128)}, u32[]{:S(2)}) copy-start(f32[4,4,256,128]{2,3,1,0:T(8,128)} %fusion.26) | copy-start | bytes 6291460
  80.1 15.7 %copy-start.9 = (s32[8]{0:T(128)S(1)}, s32[8]{0:T(128)}, u32[]{:S(2)}) copy-start(s32[8]{0:T(128)} %constant.181.clone) | copy-start | bytes 100
  80.1 20.9 %copy-start.7 = (s32[8]{0:T(128)S(1)}, s32[8]{0:T(128)}, u32[]{:S(2)}) copy-start(s32[8]{0:T(128)} %constant.182.clone) | copy-start | bytes 100
  84.3 21.9 %collective-permute-start.8 = (bf16[256,2048]{0,1:T(8,128)(2,1)S(1)}, bf16[256,2048]{0,1:T(8,128)(2,1)}, u32[]{:S(2)}, u32[]{:S(2)}) collective-permute-start(bf16[256,2048]{0,1:T(8,128)(2,1)S(1)} %bitcast.269), channel_id=1, source_target_pairs={{0,1},{1,0},{2,3},{3,2},{4,5},{5,4},{6,7},{7,6},{8,9},{9,8},{10,11... | collective-permute-start | bytes 3145736 | tf_op jit(solution)/shard_map/ppermute | solution.py:77
  84.4 40.6 %collective-permute-start.11 = (bf16[512,1536]{1,0:T(8,128)(2,1)}, bf16[512,1536]{1,0:T(8,128)(2,1)}, u32[]{:S(2)}, u32[]{:S(2)}) collective-permute-start(bf16[512,1536]{1,0:T(8,128)(2,1)} %collective-permute-done.9), channel_id=1, source_target_pairs={{0,4},{4,8},{8,12},{12,14},{14,10},{10,6},{6,2},{2,0},{1,5},{5,9},... | collective-permute-start | bytes 4718600 | tf_op jit(solution)/shard_map/ppermute | solution.py:120
  91.4 41.2 %collective-permute-start.12 = (bf16[512,1536]{1,0:T(8,128)(2,1)}, bf16[512,1536]{1,0:T(8,128)(2,1)}, u32[]{:S(2)}, u32[]{:S(2)}) collective-permute-start(bf16[512,1536]{1,0:T(8,128)(2,1)} %collective-permute-done.10), channel_id=1, source_target_pairs={{0,2},{4,0},{8,4},{12,8},{14,12},{10,14},{6,10},{2,6},{1,3},{5,1},... | collective-permute-start | bytes 4718600 | tf_op jit(solution)/shard_map/ppermute | solution.py:124
  108.7 37.7 %collective-permute-start.16 = (bf16[512,512]{1,0:T(8,128)(2,1)S(1)}, bf16[512,512]{1,0:T(8,128)(2,1)S(1)}, u32[]{:S(2)}, u32[]{:S(2)}) collective-permute-start(bf16[512,512]{1,0:T(8,128)(2,1)S(1)} %slice.44), channel_id=1, source_target_pairs={{0,16},{16,0},{1,17},{17,1},{2,18},{18,2},{3,19},{19,3},{4,20},{20... | collective-permute-start | bytes 1572872 | tf_op jit(solution)/shard_map/ppermute | solution.py:121
  111.4 35.8 %collective-permute-start.17 = (bf16[512,512]{1,0:T(8,128)(2,1)S(1)}, bf16[512,512]{1,0:T(8,128)(2,1)S(1)}, u32[]{:S(2)}, u32[]{:S(2)}) collective-permute-start(bf16[512,512]{1,0:T(8,128)(2,1)S(1)} %slice.45), channel_id=1, source_target_pairs={{0,16},{16,0},{1,17},{17,1},{2,18},{18,2},{3,19},{19,3},{4,20},{20... | collective-permute-start | bytes 1572872 | tf_op jit(solution)/shard_map/ppermute | solution.py:125
  125.0 37.4 %collective-permute-start.13 = (bf16[512,1536]{1,0:T(8,128)(2,1)}, bf16[512,1536]{1,0:T(8,128)(2,1)S(1)}, u32[]{:S(2)}, u32[]{:S(2)}) collective-permute-start(bf16[512,1536]{1,0:T(8,128)(2,1)} %collective-permute-done.11), channel_id=1, source_target_pairs={{0,4},{4,8},{8,12},{12,14},{14,10},{10,6},{6,2},{2,0},{1,5},{5,9},... | collective-permute-start | bytes 4718600 | tf_op jit(solution)/shard_map/ppermute | solution.py:120
  132.7 47.0 %collective-permute-start.14 = (bf16[512,1536]{1,0:T(8,128)(2,1)}, bf16[512,1536]{1,0:T(8,128)(2,1)S(1)}, u32[]{:S(2)}, u32[]{:S(2)}) collective-permute-start(bf16[512,1536]{1,0:T(8,128)(2,1)} %collective-permute-done.12), channel_id=1, source_target_pairs={{0,2},{4,0},{8,4},{12,8},{14,12},{10,14},{6,10},{2,6},{1,3},{5,1},... | collective-permute-start | bytes 4718600 | tf_op jit(solution)/shard_map/ppermute | solution.py:124
  149.0 15.8 %collective-permute-start.18 = (bf16[512,512]{1,0:T(8,128)(2,1)S(1)}, bf16[512,512]{1,0:T(8,128)(2,1)S(1)}, u32[]{:S(2)}, u32[]{:S(2)}) collective-permute-start(bf16[512,512]{1,0:T(8,128)(2,1)S(1)} %slice.46), channel_id=1, source_target_pairs={{0,16},{16,0},{1,17},{17,1},{2,18},{18,2},{3,19},{19,3},{4,20},{20... | collective-permute-start | bytes 1572872 | tf_op jit(solution)/shard_map/ppermute | solution.py:121
  151.7 21.4 %collective-permute-start.19 = (bf16[512,512]{1,0:T(8,128)(2,1)S(1)}, bf16[512,512]{1,0:T(8,128)(2,1)S(1)}, u32[]{:S(2)}, u32[]{:S(2)}) collective-permute-start(bf16[512,512]{1,0:T(8,128)(2,1)S(1)} %slice.47), channel_id=1, source_target_pairs={{0,16},{16,0},{1,17},{17,1},{2,18},{18,2},{3,19},{19,3},{4,20},{20... | collective-permute-start | bytes 1572872 | tf_op jit(solution)/shard_map/ppermute | solution.py:125
  162.4 35.7 %collective-permute-start.15 = (bf16[512,1536]{1,0:T(8,128)(2,1)S(1)}, bf16[512,1536]{1,0:T(8,128)(2,1)S(1)}, u32[]{:S(2)}, u32[]{:S(2)}) collective-permute-start(bf16[512,1536]{1,0:T(8,128)(2,1)S(1)} %collective-permute-done.13), channel_id=1, source_target_pairs={{0,4},{4,8},{8,12},{12,14},{14,10},{10,6},{6,2},{2,0},{1,5},{5,9},... | collective-permute-start | bytes 4718600 | tf_op jit(solution)/shard_map/ppermute | solution.py:120
  173.8 14.9 %collective-permute-start.20 = (bf16[512,512]{1,0:T(8,128)(2,1)S(1)}, bf16[512,512]{1,0:T(8,128)(2,1)S(1)}, u32[]{:S(2)}, u32[]{:S(2)}) collective-permute-start(bf16[512,512]{1,0:T(8,128)(2,1)S(1)} %slice.48), channel_id=1, source_target_pairs={{0,16},{16,0},{1,17},{17,1},{2,18},{18,2},{3,19},{19,3},{4,20},{20... | collective-permute-start | bytes 1572872 | tf_op jit(solution)/shard_map/ppermute | solution.py:121
  179.7 19.9 %collective-permute-start.21 = (bf16[512,512]{1,0:T(8,128)(2,1)S(1)}, bf16[512,512]{1,0:T(8,128)(2,1)S(1)}, u32[]{:S(2)}, u32[]{:S(2)}) collective-permute-start(bf16[512,512]{1,0:T(8,128)(2,1)S(1)} %slice.49), channel_id=1, source_target_pairs={{0,16},{16,0},{1,17},{17,1},{2,18},{18,2},{3,19},{19,3},{4,20},{20... | collective-permute-start | bytes 1572872 | tf_op jit(solution)/shard_map/ppermute | solution.py:125
  198.2 12.0 %collective-permute-start.22 = (bf16[512,512]{1,0:T(8,128)(2,1)S(1)}, bf16[512,512]{1,0:T(8,128)(2,1)S(1)}, u32[]{:S(2)}, u32[]{:S(2)}) collective-permute-start(bf16[512,512]{1,0:T(8,128)(2,1)S(1)} %slice.50), channel_id=1, source_target_pairs={{0,16},{16,0},{1,17},{17,1},{2,18},{18,2},{3,19},{19,3},{4,20},{20... | collective-permute-start | bytes 1572872 | tf_op jit(solution)/shard_map/ppermute | solution.py:121

commit v10 on v2

--- a/solution.py
+++ b/solution.py
@@ -85,33 +85,89 @@
     return jnp.concatenate(pieces, axis=1)
 
 
-def ring_project(features, out_weight):
+class Split:
+    def __init__(self, columns, own):
+        self.own = own
+        self.shared = columns - 2 * own if own else columns
+
+    def carried(self, block, group_index):
+        if not self.own:
+            return block
+        start = self.shared + group_index * self.own
+        mine = lax.dynamic_slice_in_dim(block, start, self.own, 1)
+        return jnp.concatenate([block[:, : self.shared], mine], axis=1)
+
+    def other_of(self, block, group_index):
+        start = self.shared + (1 - group_index) * self.own
+        return lax.dynamic_slice_in_dim(block, start, self.own, 1)
+
+
+def ring_transfer(out_weight):
     count = lax.axis_size("ctx")
-    order = [i for i in range(0, count, 2)] + sorted(range(1, count, 2), reverse=True)
+    order = list(range(0, count, 2)) + sorted(range(1, count, 2), reverse=True)
     position_of = [0] * count
     for position, index in enumerate(order):
         position_of[index] = position
     ctx_index = lax.axis_index("ctx")
     position = jnp.asarray(position_of, jnp.int32)[ctx_index]
     order_table = jnp.asarray(order, jnp.int32)
-    rows = out_weight.shape[0]
-
-    def term(block, source):
-        piece = lax.dynamic_slice_in_dim(features, source * rows, rows, 1)
-        return jnp.dot(piece, block, preferred_element_type=jnp.float32)
-
-    mixed = term(out_weight, ctx_index)
+    columns = out_weight.shape[1]
+    groups = lax.axis_size("group")
+    group_index = lax.axis_index("group")
+    lanes = columns // 128
+    ahead_split = Split(columns, (lanes * 5 // 16) * 128 if groups == 2 else 0)
+    behind_split = Split(columns, (lanes * 3 // 16) * 128 if groups == 2 else 0)
+    swap = [(0, 1), (1, 0)]
+
+    def cross(block, split):
+        if not split.own:
+            return None
+        return lax.ppermute(block[:, split.shared :], "group", swap)
+
+    own_other = ahead_split.other_of(out_weight, group_index) if ahead_split.own else None
+    arrivals = [(ctx_index, ahead_split.carried(out_weight, group_index), own_other, ahead_split)]
     ahead = [(order[p], order[(p + 1) % count]) for p in range(count)]
     behind = [(order[p], order[(p - 1) % count]) for p in range(count)]
-    forward = backward = out_weight
+    forward = ahead_split.carried(out_weight, group_index)
+    backward = behind_split.carried(out_weight, group_index)
     forward_steps = count // 2
     backward_steps = count - 1 - forward_steps
     for step in range(1, forward_steps + 1):
         forward = lax.ppermute(forward, "ctx", ahead)
-        mixed = mixed + term(forward, order_table[(position + count - step) % count])
+        arrivals.append(
+            (order_table[(position + count - step) % count], forward, cross(forward, ahead_split), ahead_split)
+        )
         if step <= backward_steps:
             backward = lax.ppermute(backward, "ctx", behind)
-            mixed = mixed + term(backward, order_table[(position + step) % count])
+            arrivals.append(
+                (order_table[(position + step) % count], backward, cross(backward, behind_split), behind_split)
+            )
+    return arrivals
+
+
+def ring_project(features, arrivals, rows):
+    group_index = lax.axis_index("group")
+    sums = {}
+    for source, carried_block, crossed, split in arrivals:
+        piece = lax.dynamic_slice_in_dim(features, source * rows, rows, 1)
+        terms = [jnp.dot(piece, carried_block, preferred_element_type=jnp.float32)]
+        if split.own:
+            terms.append(jnp.dot(piece, crossed, preferred_element_type=jnp.float32))
+        key = id(split)
+        if key in sums:
+            sums[key] = (split, [a + b for a, b in zip(sums[key][1], terms)])
+        else:
+            sums[key] = (split, terms)
+    mixed = None
+    for split, parts in sums.values():
+        if split.own:
+            mine, other = parts[0][:, split.shared :], parts[1]
+            first = jnp.where(group_index == 0, mine, other)
+            second = jnp.where(group_index == 0, other, mine)
+            full = jnp.concatenate([parts[0][:, : split.shared], first, second], axis=1)
+        else:
+            full = parts[0]
+        mixed = full if mixed is None else mixed + full
     return mixed
 
 
@@ -136,6 +192,7 @@
         )
         return update(state_now, query_head_rows, key_piece, value_piece, visible)
 
+    arrivals = ring_transfer(out_weight)
     initial_state = fresh_state(kv_heads, group_width, tok_rows)
     state_now = attend(initial_state, keys, values, query_start)
     for distance in range(1, reach_devs + 1):
@@ -143,7 +200,7 @@
         state_now = attend(state_now, prior_keys, prior_values, query_start - distance * tok_rows)
     attended = finish(state_now, tok_rows, q_heads)
     features = head_features(attended)
-    mixed = ring_project(features, out_weight)
+    mixed = ring_project(features, arrivals, out_weight.shape[0])
     return mixed.astype(jnp.bfloat16)
 
 

time: 238 us -> 219 us (0.920)
  waiting for transfers between devices: 115 us -> 57.8 us
  starting transfers between devices: 45.5 us -> 56.8 us
  local copies, waits for them, and re-layouts: 11.1 us -> 22 us
  matrix products: 46.2 us -> 57.1 us
  other arithmetic: 9.19 us -> 14 us
    ppermute x8, waiting for transfers between devices: 29 us -> 0.02 us  [passed_along(): return lax.ppermute(array, axis, pairs)]
    ppermute x7 -> x14, waiting for transfers between devices: 86.2 us -> 57.8 us  [the longest x7 28.3 us: cross(): return lax.ppermute(block[:, split.shared:], 'group', swap)]
    ppermute x7 -> x14, starting transfers between devices: 17.8 us -> 31.9 us  [the longest x3 17.6 us: ring_transfer(): backward = lax.ppermute(backward, 'ctx', behind)]
    dot_general x5, matrix products: 9.07 us -> 14.7 us  [update(): jnp.einsum('qhgd,khd->hgqk', query_head_rows, key_head_rows, preferred_el...]
    dot_general x5, matrix products: 19.1 us -> 23.6 us  [update(): jnp.einsum('hgqk,khd->hgqd', weights.astype(jnp.bfloat16), value_head_row...]
    slice x0 -> x13, local copies, waits for them, and re-layouts: none -> 3.97 us  [the longest x7 3.43 us: cross(): return lax.ppermute(block[:, split.shared:], 'group', swap)]
    ppermute x8, starting transfers between devices: 27.6 us -> 24.8 us  [passed_along(): return lax.ppermute(array, axis, pairs)]
    concatenate x0 -> x2, other arithmetic: none -> 2.6 us  [carried(): return jnp.concatenate([block[:, :self.shared], mine], axis=1)]
  transfers between devices with their start and end apart: 16 -> 23, of which waited for: 5 -> 8; matrix products, arithmetic and copies ran while one was open for 26% -> 39% of each run, Pallas kernels for 0% -> 0%
where the time goes in v10:
time: 219 us; the launch traced here: 218 us
  waiting for transfers between devices  57.8 us (26%)
  matrix products  57.1 us (26%)
  starting transfers between devices  56.8 us (26%)
  local copies, waits for them, and re-layouts  22 us (10%)
  other arithmetic  14 us (6%)
  between operations  9.94 us (5%)
    ppermute x7, waiting for transfers between devices, cross(): return lax.ppermute(block[:, split.shared:], 'group', swap)  28.3 us
    ppermute x8, starting transfers between devices, passed_along(): return lax.ppermute(array, axis, pairs)  24.8 us
    dot_general x5, matrix products, update(): jnp.einsum('hgqk,khd->hgqd', weights.astype(jnp.bfloat16), value_head_row...  23.6 us
    ppermute x4, waiting for transfers between devices, ring_transfer(): forward = lax.ppermute(forward, 'ctx', ahead)  23.2 us
    ppermute x3, starting transfers between devices, ring_transfer(): backward = lax.ppermute(backward, 'ctx', behind)  17.6 us
    dot_general x5, matrix products, update(): jnp.einsum('qhgd,khd->hgqk', query_head_rows, key_head_rows, preferred_el...  14.7 us
    dot_general x8, matrix products, ring_project(): terms = [jnp.dot(piece, carried_block, preferred_element_type=jnp.float32)]  12.4 us
    ppermute x7, starting transfers between devices, cross(): return lax.ppermute(block[:, split.shared:], 'group', swap)  10.1 us
  transfers between devices with their start and end apart: 23, of which 8 were waited for; matrix products, arithmetic and copies ran while one was open for 39% of the time, Pallas kernels for 0%

profile of v10, /device:TPU:0, one launch (start us, length us, event | category | flops | bytes accessed | tf_op | source)
XLA Modules:
  0.0 217.7 jit_solution(5770617452344045401)
XLA Ops:
  0.0 1.8 copy.52
  1.8 6.6 %collective-permute-start.6 = (bf16[256,512]{0,1:T(8,128)(2,1)}, bf16[256,512]{0,1:T(8,128)(2,1)}, u32[]{:S(2)}, u32[]{:S(2)}) collective-permute-start(bf16[256,512]{0,1:T(8,128)(2,1)} %copy.52), channel_id=1, source_target_pairs={{0,8},{2,10},{4,12},{6,14},{1,9},{3,11},{5,13},{7,15},{16,24},{18,... | collective-permute-start | bytes 786440 | tf_op jit(solution)/shard_map/ppermute | solution.py:15
  8.4 5.1 %collective-permute-start.4 = (bf16[256,512]{0,1:T(8,128)(2,1)}, bf16[256,512]{0,1:T(8,128)(2,1)}, u32[]{:S(2)}, u32[]{:S(2)}) collective-permute-start(bf16[256,512]{0,1:T(8,128)(2,1)} %copy.52), channel_id=1, source_target_pairs={{0,6},{2,8},{4,10},{6,12},{8,14},{1,7},{3,9},{5,11},{7,13},{9,15},... | collective-permute-start | bytes 786440 | tf_op jit(solution)/shard_map/ppermute | solution.py:15
  13.6 2.0 collective-permute-start.2
  15.5 3.1 %collective-permute-start = (bf16[256,512]{0,1:T(8,128)(2,1)}, bf16[256,512]{0,1:T(8,128)(2,1)}, u32[]{:S(2)}, u32[]{:S(2)}) collective-permute-start(bf16[256,512]{0,1:T(8,128)(2,1)} %copy.52), channel_id=1, source_target_pairs={{0,2},{2,4},{4,6},{6,8},{8,10},{10,12},{12,14},{1,3},{3,5},{5,7},{... | collective-permute-start | bytes 786440 | tf_op jit(solution)/shard_map/ppermute | solution.py:15
  18.6 2.0 collective-permute-start.1
  23.0 1.7 reshape.292
  24.7 1.8 copy.89
  26.5 1.6 copy-done.4
  28.2 1.9 reshape.293
  31.2 1.1 constant_dynamic-slice_fusion.1
  32.4 1.3 pad_maximum_fusion
  35.4 1.3 pad_maximum_fusion.1
  36.7 2.0 collective-permute-start.3
  38.7 3.9 %fusion.4 = (f32[4,4,256]{2,1,0:T(4,128)S(1)}, f32[4,256,256,4]{2,1,3,0:T(8,128)}) fusion(pred[256,256]{0,1:T(8,128)(4,1)S(1)} %get-tuple-element.31, bf16[256,4,128,1]{0,2,3,1:T(8,128)(2,1)} %bitcast.74, bf16[256,4,4,128]{3,2,1,0:T(4,128)(2,1)S(1)} %reshape.293), kind=kOutput, calls=%fused_computation.30 | convolution fusion | flops 271577088 | bytes 5586944 | tf_op jit(solution)/shard_map/qhgd,khd->hgqk/dot_general | solution.py:33
  42.6 2.0 collective-permute-start.5
  44.6 4.0 %fusion.3 = (f32[4,4,256]{2,1,0:T(4,128)S(1)}, f32[4,256,256,4]{2,1,3,0:T(8,128)}) fusion(pred[256,256]{0,1:T(8,128)(4,1)S(1)} %get-tuple-element.29, bf16[256,4,128,1]{0,2,3,1:T(8,128)(2,1)} %bitcast.70, bf16[256,4,4,128]{3,2,1,0:T(4,128)(2,1)S(1)} %reshape.293), kind=kOutput, calls=%fused_computation.29 | convolution fusion | flops 271577088 | bytes 5586944 | tf_op jit(solution)/shard_map/qhgd,khd->hgqk/dot_general | solution.py:33
  48.6 2.0 collective-permute-start.7
  50.5 3.9 %fusion.2 = (f32[4,4,256]{2,1,0:T(4,128)S(1)}, f32[4,256,256,4]{2,1,3,0:T(8,128)}) fusion(pred[256,256]{0,1:T(8,128)(4,1)S(1)} %get-tuple-element.30, bf16[256,4,128,1]{0,2,3,1:T(8,128)(2,1)} %bitcast.66, bf16[256,4,4,128]{3,2,1,0:T(4,128)(2,1)S(1)} %reshape.293), kind=kOutput, calls=%fused_computation.28 | convolution fusion | flops 271577088 | bytes 5586944 | tf_op jit(solution)/shard_map/qhgd,khd->hgqk/dot_general | solution.py:33
  54.5 2.0 fusion.1
  58.3 2.6 %fusion.23 = f32[4,4,256,128]{2,3,1,0:T(8,128)} fusion(bf16[256,4,128,1]{0,2,3,1:T(8,128)(2,1)S(1)} %bitcast.271, f32[4,256,256,4]{2,1,3,0:T(8,128)S(1)} %get-tuple-element.48, f32[4,4,256]{2,1,0:T(4,128)S(1)} %get-tuple-element.26, pred[256,256]{0,1:T(8,128)(4,1)S(1)} %get-tuple-element.27), kind=kOutput, calls=%fused_computation.51 | convolution fusion | flops 273678336 | bytes 6635520 | tf_op jit(solution)/shard_map/hgqk,khd->hgqd/dot_general | solution.py:42
  61.9 2.2 %collective-permute-start.9 = (bf16[512,1408]{1,0:T(8,128)(2,1)}, bf16[512,1408]{1,0:T(8,128)(2,1)S(1)}, u32[]{:S(2)}, u32[]{:S(2)}) collective-permute-start(bf16[512,1408]{1,0:T(8,128)(2,1)} %pad_maximum_fusion.1), channel_id=1, source_target_pairs={{0,4},{4,8},{8,12},{12,14},{14,10},{10,6},{6,2},{2,0},{1,5},{5,9},... | collective-permute-start | bytes 4325384 | tf_op jit(solution)/shard_map/ppermute | solution.py:136
  65.3 4.8 %fusion.21 = f32[4,4,256,128]{2,3,1,0:T(8,128)} fusion(bf16[256,4,128,1]{0,2,3,1:T(8,128)(2,1)S(1)} %bitcast.273, f32[4,256,256,4]{2,1,3,0:T(8,128)} %copy-done.3, f32[4,4,256]{2,1,0:T(4,128)S(1)} %get-tuple-element.17, pred[256,256]{0,1:T(8,128)(4,1)S(1)} %get-tuple-element.28), kind=kOutput, calls=%fused_computation.50 | convolution fusion | flops 273678336 | bytes 6635520 | tf_op jit(solution)/shard_map/hgqk,khd->hgqd/dot_general | solution.py:42
  72.2 4.8 %fusion.19 = f32[4,4,256,128]{2,3,1,0:T(8,128)} fusion(bf16[256,4,128,1]{0,2,3,1:T(8,128)(2,1)S(1)} %bitcast.274, f32[4,256,256,4]{2,1,3,0:T(8,128)} %get-tuple-element.44, f32[4,4,256]{2,1,0:T(4,128)S(1)} %get-tuple-element.16, pred[256,256]{0,1:T(8,128)(4,1)S(1)} %get-tuple-element.30), kind=kOutput, calls=%fused_computation.49 | convolution fusion | flops 273678336 | bytes 6635520 | tf_op jit(solution)/shard_map/hgqk,khd->hgqd/dot_general | solution.py:42
  79.2 4.8 %fusion.17 = f32[4,4,256,128]{2,3,1,0:T(8,128)} fusion(bf16[256,4,128,1]{0,2,3,1:T(8,128)(2,1)S(1)} %bitcast.275, f32[4,256,256,4]{2,1,3,0:T(8,128)} %get-tuple-element.42, f32[4,4,256]{2,1,0:T(4,128)S(1)} %get-tuple-element.15, pred[256,256]{0,1:T(8,128)(4,1)S(1)} %get-tuple-element.29), kind=kOutput, calls=%fused_computation.48 | convolution fusion | flops 273678336 | bytes 6635520 | tf_op jit(solution)/shard_map/hgqk,khd->hgqd/dot_general | solution.py:42
  85.8 1.8 copy.70
  87.6 6.5 %fusion.27 = bf16[256,4,4,128]{0,3,2,1:T(8,128)(2,1)S(1)} fusion(f32[4,4,256,128]{2,3,1,0:T(8,128)} %fusion.17, f32[4,4,256,128]{2,3,1,0:T(8,128)} %fusion.19, f32[4,4,256,128]{2,3,1,0:T(8,128)} %fusion.21, f32[4,4,256,128]{2,3,1,0:T(8,128)} %fusion.23, f32[256,4,4]{0,2,1:T(4,128)S(1)} %get-tuple-element.10, f32[256,4,4]{0,2,1:T(4,128)S(1)} %get-tuple-element.13, ...), kind=kOutput, calls=%fused_computation.56 | convolution fusion | flops 279445504 | bytes 14073856 | tf_op jit(solution)/shard_map/hgqk,khd->hgqd/dot_general | solution.py:42
  94.8 1.7 collective-permute-start.10
  107.5 1.4 broadcast_select_fusion
  109.0 1.6 collective-permute-start.13
  111.5 16.8 %collective-permute-done.10 = bf16[512,1408]{1,0:T(8,128)(2,1)} collective-permute-done((bf16[512,1408]{1,0:T(8,128)(2,1)S(1)}, bf16[512,1408]{1,0:T(8,128)(2,1)}, u32[]{:S(2)}, u32[]{:S(2)}) %collective-permute-start.10) | collective-permute-done | bytes 1441824 | tf_op jit(solution)/shard_map/ppermute | solution.py:136
  130.6 1.6 collective-permute-start.20
  132.2 2.5 %fusion.109 = f32[256,1664]{1,0:T(8,128)S(1)} fusion(bf16[512,1664]{1,0:T(8,128)(2,1)} %collective-permute-done.17, s32[]{:T(128)S(6)} %select_n.268, bf16[256,2048]{0,1:T(8,128)(2,1)S(1)} %get-tuple-element.23, bf16[256,2048]{0,1:T(8,128)(2,1)S(1)} %get-tuple-element.22), kind=kOutput, calls=%fused_computation.205 | convolution fusion | flops 436731904 | bytes 5505028 | tf_op jit(solution)/shard_map/dot_general | solution.py:153
  134.8 17.2 %collective-permute-start.19 = (bf16[512,1664]{1,0:T(8,128)(2,1)}, bf16[512,1664]{1,0:T(8,128)(2,1)S(1)}, u32[]{:S(2)}, u32[]{:S(2)}) collective-permute-start(bf16[512,1664]{1,0:T(8,128)(2,1)} %collective-permute-done.18), channel_id=1, source_target_pairs={{0,2},{4,0},{8,4},{12,8},{14,12},{10,14},{6,10},{2,6},{1,3},{5,1},... | collective-permute-start | bytes 5111816 | tf_op jit(solution)/shard_map/ppermute | solution.py:141
  152.8 1.1 slice.56
  153.9 1.6 collective-permute-start.14
  155.5 2.3 %convolution_add_fusion.2 = f32[256,1408]{1,0:T(8,128)S(1)} fusion(f32[256,1408]{1,0:T(8,128)S(1)} %convolution_add_fusion.3, bf16[512,1408]{1,0:T(8,128)(2,1)} %collective-permute-done.10, s32[]{:T(128)S(6)} %select_n.255, bf16[256,2048]{0,1:T(8,128)(2,1)S(1)} %get-tuple-element.23, bf16[256,2048]{0,1:T(8,128)(2,1)S(1)} %get-tuple-element.22), kind=kOutput, calls=%fused_computation.43 | convolution fusion | flops 369983488 | bytes 6422532 | tf_op jit(solution)/shard_map/dot_general | solution.py:153
  159.5 2.5 %convolution_add_fusion.5 = f32[256,1664]{1,0:T(8,128)S(1)} fusion(f32[256,1664]{1,0:T(8,128)S(1)} %fusion.109, bf16[512,1664]{1,0:T(8,128)(2,1)} %collective-permute-done.18, s32[]{:T(128)S(6)} %select_n.272, bf16[256,2048]{0,1:T(8,128)(2,1)S(1)} %get-tuple-element.23, bf16[256,2048]{0,1:T(8,128)(2,1)S(1)} %get-tuple-element.22), kind=kOutput, calls=%fused_computation.46 | convolution fusion | flops 437157888 | bytes 7208964 | tf_op jit(solution)/shard_map/dot_general | solution.py:153
  162.0 1.6 collective-permute-start.15
  163.6 7.9 %collective-permute-done.14 = bf16[512,640]{1,0:T(8,128)(2,1)S(1)} collective-permute-done((bf16[512,640]{1,0:T(8,128)(2,1)S(1)}, bf16[512,640]{1,0:T(8,128)(2,1)S(1)}, u32[]{:S(2)}, u32[]{:S(2)}) %collective-permute-start.14) | collective-permute-done | bytes 655392 | tf_op jit(solution)/shard_map/ppermute | solution.py:125
  172.4 7.6 %collective-permute-done.21 = bf16[512,384]{1,0:T(8,128)(2,1)S(1)} collective-permute-done((bf16[512,384]{1,0:T(8,128)(2,1)S(1)}, bf16[512,384]{1,0:T(8,128)(2,1)S(1)}, u32[]{:S(2)}, u32[]{:S(2)}) %collective-permute-start.21) | collective-permute-done | bytes 393248 | tf_op jit(solution)/shard_map/ppermute | solution.py:125
  181.8 6.3 %collective-permute-done.19 = bf16[512,1664]{1,0:T(8,128)(2,1)S(1)} collective-permute-done((bf16[512,1664]{1,0:T(8,128)(2,1)}, bf16[512,1664]{1,0:T(8,128)(2,1)S(1)}, u32[]{:S(2)}, u32[]{:S(2)}) %collective-permute-start.19) | collective-permute-done | bytes 1703968 | tf_op jit(solution)/shard_map/ppermute | solution.py:141
  188.1 1.6 collective-permute-start.22
  189.7 4.4 %collective-permute-done.15 = bf16[512,640]{1,0:T(8,128)(2,1)S(1)} collective-permute-done((bf16[512,640]{1,0:T(8,128)(2,1)S(1)}, bf16[512,640]{1,0:T(8,128)(2,1)S(1)}, u32[]{:S(2)}, u32[]{:S(2)}) %collective-permute-start.15) | collective-permute-done | bytes 655392 | tf_op jit(solution)/shard_map/ppermute | solution.py:125
  196.0 5.8 %collective-permute-done.12 = bf16[512,1408]{1,0:T(8,128)(2,1)S(1)} collective-permute-done((bf16[512,1408]{1,0:T(8,128)(2,1)S(1)}, bf16[512,1408]{1,0:T(8,128)(2,1)S(1)}, u32[]{:S(2)}, u32[]{:S(2)}) %collective-permute-start.12) | collective-permute-done | bytes 1441824 | tf_op jit(solution)/shard_map/ppermute | solution.py:136
  201.8 1.6 collective-permute-start.16
  206.0 8.4 %collective-permute-done.16 = bf16[512,640]{1,0:T(8,128)(2,1)S(1)} collective-permute-done((bf16[512,640]{1,0:T(8,128)(2,1)S(1)}, bf16[512,640]{1,0:T(8,128)(2,1)S(1)}, u32[]{:S(2)}, u32[]{:S(2)}) %collective-permute-start.16) | collective-permute-done | bytes 655392 | tf_op jit(solution)/shard_map/ppermute | solution.py:125
  216.6 1.2 fusion.25
  (125 shorter events, 32.4 us)
Async XLA Ops:
  1.8 34.9 %collective-permute-start.6 = (bf16[256,512]{0,1:T(8,128)(2,1)}, bf16[256,512]{0,1:T(8,128)(2,1)}, u32[]{:S(2)}, u32[]{:S(2)}) collective-permute-start(bf16[256,512]{0,1:T(8,128)(2,1)} %copy.52), channel_id=1, source_target_pairs={{0,8},{2,10},{4,12},{6,14},{1,9},{3,11},{5,13},{7,15},{16,24},{18,... | collective-permute-start | bytes 786440 | tf_op jit(solution)/shard_map/ppermute | solution.py:15
  8.4 34.1 %collective-permute-start.4 = (bf16[256,512]{0,1:T(8,128)(2,1)}, bf16[256,512]{0,1:T(8,128)(2,1)}, u32[]{:S(2)}, u32[]{:S(2)}) collective-permute-start(bf16[256,512]{0,1:T(8,128)(2,1)} %copy.52), channel_id=1, source_target_pairs={{0,6},{2,8},{4,10},{6,12},{8,14},{1,7},{3,9},{5,11},{7,13},{9,15},... | collective-permute-start | bytes 786440 | tf_op jit(solution)/shard_map/ppermute | solution.py:15
  13.6 35.0 %collective-permute-start.2 = (bf16[256,512]{0,1:T(8,128)(2,1)}, bf16[256,512]{0,1:T(8,128)(2,1)}, u32[]{:S(2)}, u32[]{:S(2)}) collective-permute-start(bf16[256,512]{0,1:T(8,128)(2,1)} %copy.52), channel_id=1, source_target_pairs={{0,4},{2,6},{4,8},{6,10},{8,12},{10,14},{1,5},{3,7},{5,9},{7,11},{... | collective-permute-start | bytes 786440 | tf_op jit(solution)/shard_map/ppermute | solution.py:15
  15.5 38.9 %collective-permute-start = (bf16[256,512]{0,1:T(8,128)(2,1)}, bf16[256,512]{0,1:T(8,128)(2,1)}, u32[]{:S(2)}, u32[]{:S(2)}) collective-permute-start(bf16[256,512]{0,1:T(8,128)(2,1)} %copy.52), channel_id=1, source_target_pairs={{0,2},{2,4},{4,6},{6,8},{8,10},{10,12},{12,14},{1,3},{3,5},{5,7},{... | collective-permute-start | bytes 786440 | tf_op jit(solution)/shard_map/ppermute | solution.py:15
  18.6 43.3 %collective-permute-start.1 = (bf16[256,512]{1,0:T(8,128)(2,1)}, bf16[256,512]{1,0:T(8,128)(2,1)}, u32[]{:S(2)}, u32[]{:S(2)}) collective-permute-start(bf16[256,512]{1,0:T(8,128)(2,1)} %param.9), channel_id=1, source_target_pairs={{0,2},{2,4},{4,6},{6,8},{8,10},{10,12},{12,14},{1,3},{3,5},{5,7},{... | collective-permute-start | bytes 786440 | tf_op jit(solution)/shard_map/ppermute | solution.py:15
  26.5 1.6 copy-start.4
  28.2 4.2 %slice-start = ((bf16[512,2048]{1,0:T(8,128)(2,1)}), bf16[512,1280]{1,0:T(8,128)(2,1)S(1)}, s32[]{:S(2)}) async-start(bf16[512,2048]{1,0:T(8,128)(2,1)} %param.11), calls=%async_computation | async-start | bytes 2621440 | tf_op jit(solution)/shard_map/slice | solution.py:98
  31.1 2.6 %copy-start.22 = (s32[256]{0:T(256)S(1)}, s32[256]{0:T(256)}, u32[]{:S(2)}) copy-start(s32[256]{0:T(256)} %get-tuple-element.49) | copy-start | bytes 3076
  31.1 2.6 %copy-start.23 = (s32[256]{0:T(256)S(1)}, s32[256]{0:T(256)}, u32[]{:S(2)}) copy-start(s32[256]{0:T(256)} %get-tuple-element.50) | copy-start | bytes 3076
  31.2 2.6 %copy-start.24 = (s32[256]{0:T(256)S(1)}, s32[256]{0:T(256)}, u32[]{:S(2)}) copy-start(s32[256]{0:T(256)} %get-tuple-element.51) | copy-start | bytes 3076
  31.2 2.5 %copy-start.25 = (s32[256]{0:T(256)S(1)}, s32[256]{0:T(256)}, u32[]{:S(2)}) copy-start(s32[256]{0:T(256)} %get-tuple-element.52) | copy-start | bytes 3076
  31.2 2.5 %copy-start.26 = (s32[256]{0:T(256)S(1)}, s32[256]{0:T(256)}, u32[]{:S(2)}) copy-start(s32[256]{0:T(256)} %get-tuple-element.53) | copy-start | bytes 3076
  31.2 2.5 %copy-start.27 = (s32[16]{0:T(128)S(1)}, s32[16]{0:T(128)}, u32[]{:S(2)}) copy-start(s32[16]{0:T(128)} %param.10) | copy-start | bytes 196
  31.2 2.6 %copy-start.21 = (s32[256]{0:T(256)S(1)}, s32[256]{0:T(256)}, u32[]{:S(2)}) copy-start(s32[256]{0:T(256)} %get-tuple-element.58) | copy-start | bytes 3076
  32.4 3.0 %copy-start.7 = (bf16[512,640]{1,0:T(8,128)(2,1)}, bf16[512,640]{1,0:T(8,128)(2,1)S(1)}, u32[]{:S(2)}) copy-start(bf16[512,640]{1,0:T(8,128)(2,1)S(1)} %constant_dynamic-slice_fusion.1) | copy-start | bytes 1966084
  32.4 2.0 copy-start.9
  36.7 34.4 %collective-permute-start.3 = (bf16[256,512]{1,0:T(8,128)(2,1)}, bf16[256,512]{1,0:T(8,128)(2,1)}, u32[]{:S(2)}, u32[]{:S(2)}) collective-permute-start(bf16[256,512]{1,0:T(8,128)(2,1)} %param.9), channel_id=1, source_target_pairs={{0,4},{2,6},{4,8},{6,10},{8,12},{10,14},{1,5},{3,7},{5,9},{7,11},{... | collective-permute-start | bytes 786440 | tf_op jit(solution)/shard_map/ppermute | solution.py:15
  42.6 14.0 %copy-start.11 = (f32[4,4,256]{2,1,0:T(4,128)}, f32[4,4,256]{2,1,0:T(4,128)S(1)}, u32[]{:S(2)}) copy-start(f32[4,4,256]{2,1,0:T(4,128)S(1)} %get-tuple-element.39) | copy-start | bytes 49156
  42.6 35.5 %collective-permute-start.5 = (bf16[256,512]{1,0:T(8,128)(2,1)}, bf16[256,512]{1,0:T(8,128)(2,1)}, u32[]{:S(2)}, u32[]{:S(2)}) collective-permute-start(bf16[256,512]{1,0:T(8,128)(2,1)} %param.9), channel_id=1, source_target_pairs={{0,6},{2,8},{4,10},{6,12},{8,14},{1,7},{3,9},{5,11},{7,13},{9,15},... | collective-permute-start | bytes 786440 | tf_op jit(solution)/shard_map/ppermute | solution.py:15
  48.5 8.0 %copy-start.13 = (f32[4,4,256]{2,1,0:T(4,128)}, f32[4,4,256]{2,1,0:T(4,128)S(1)}, u32[]{:S(2)}) copy-start(f32[4,4,256]{2,1,0:T(4,128)S(1)} %get-tuple-element.41) | copy-start | bytes 49156
  48.6 37.3 %collective-permute-start.7 = (bf16[256,512]{1,0:T(8,128)(2,1)}, bf16[256,512]{1,0:T(8,128)(2,1)}, u32[]{:S(2)}, u32[]{:S(2)}) collective-permute-start(bf16[256,512]{1,0:T(8,128)(2,1)} %param.9), channel_id=1, source_target_pairs={{0,8},{2,10},{4,12},{6,14},{1,9},{3,11},{5,13},{7,15},{16,24},{18,... | collective-permute-start | bytes 786440 | tf_op jit(solution)/shard_map/ppermute | solution.py:15
  54.5 2.1 copy-start.15
  54.5 42.1 %collective-permute-start.17 = (bf16[512,1664]{1,0:T(8,128)(2,1)}, bf16[512,1664]{1,0:T(8,128)(2,1)}, u32[]{:S(2)}, u32[]{:S(2)}) collective-permute-start(bf16[512,1664]{1,0:T(8,128)(2,1)} %pad_maximum_fusion), channel_id=1, source_target_pairs={{0,2},{4,0},{8,4},{12,8},{14,12},{10,14},{6,10},{2,6},{1,3},{5,1},... | collective-permute-start | bytes 5111816 | tf_op jit(solution)/shard_map/ppermute | solution.py:141
  56.5 4.3 %copy-start.3 = (f32[4,256,256,4]{2,1,3,0:T(8,128)}, f32[4,256,256,4]{2,1,3,0:T(8,128)S(1)}, u32[]{:S(2)}) copy-start(f32[4,256,256,4]{2,1,3,0:T(8,128)S(1)} %get-tuple-element.46) | copy-start | bytes 12582916
  56.6 27.5 %copy-start.19 = (f32[4,4,256]{2,1,0:T(4,128)}, f32[4,4,256]{2,1,0:T(4,128)S(1)}, u32[]{:S(2)}) copy-start(f32[4,4,256]{2,1,0:T(4,128)S(1)} %get-tuple-element.14) | copy-start | bytes 49156
  61.9 32.9 %collective-permute-start.9 = (bf16[512,1408]{1,0:T(8,128)(2,1)}, bf16[512,1408]{1,0:T(8,128)(2,1)S(1)}, u32[]{:S(2)}, u32[]{:S(2)}) collective-permute-start(bf16[512,1408]{1,0:T(8,128)(2,1)} %pad_maximum_fusion.1), channel_id=1, source_target_pairs={{0,4},{4,8},{8,12},{12,14},{14,10},{10,6},{6,2},{2,0},{1,5},{5,9},... | collective-permute-start | bytes 4325384 | tf_op jit(solution)/shard_map/ppermute | solution.py:136
  65.2 4.8 %copy-start.2 = (f32[4,256,256,4]{2,1,3,0:T(8,128)S(1)}, f32[4,256,256,4]{2,1,3,0:T(8,128)}, u32[]{:S(2)}) copy-start(f32[4,256,256,4]{2,1,3,0:T(8,128)} %get-tuple-element.44) | copy-start | bytes 12582916
  72.2 4.8 %copy-start.1 = (f32[4,256,256,4]{2,1,3,0:T(8,128)S(1)}, f32[4,256,256,4]{2,1,3,0:T(8,128)}, u32[]{:S(2)}) copy-start(f32[4,256,256,4]{2,1,3,0:T(8,128)} %get-tuple-element.42) | copy-start | bytes 12582916
  79.2 4.9 %copy-start = (f32[4,256,256,4]{2,1,3,0:T(8,128)S(1)}, f32[4,256,256,4]{2,1,3,0:T(8,128)}, u32[]{:S(2)}) copy-start(f32[4,256,256,4]{2,1,3,0:T(8,128)} %get-tuple-element.40) | copy-start | bytes 12582916
  87.6 9.3 %copy-start.28 = (s32[8]{0:T(128)S(1)}, s32[8]{0:T(128)}, u32[]{:S(2)}) copy-start(s32[8]{0:T(128)} %constant.189.clone) | copy-start | bytes 100
  87.6 14.8 %copy-start.20 = (s32[8]{0:T(128)S(1)}, s32[8]{0:T(128)}, u32[]{:S(2)}) copy-start(s32[8]{0:T(128)} %constant.190.clone) | copy-start | bytes 100
  94.1 13.4 %collective-permute-start.8 = (bf16[256,2048]{0,1:T(8,128)(2,1)S(1)}, bf16[256,2048]{0,1:T(8,128)(2,1)}, u32[]{:S(2)}, u32[]{:S(2)}) collective-permute-start(bf16[256,2048]{0,1:T(8,128)(2,1)S(1)} %bitcast.269), channel_id=1, source_target_pairs={{0,1},{1,0},{2,3},{3,2},{4,5},{5,4},{6,7},{7,6},{8,9},{9,8},{10,11... | collective-permute-start | bytes 3145736 | tf_op jit(solution)/shard_map/ppermute | solution.py:77
  94.8 33.5 %collective-permute-start.10 = (bf16[512,1408]{1,0:T(8,128)(2,1)S(1)}, bf16[512,1408]{1,0:T(8,128)(2,1)}, u32[]{:S(2)}, u32[]{:S(2)}) collective-permute-start(bf16[512,1408]{1,0:T(8,128)(2,1)S(1)} %collective-permute-done.9), channel_id=1, source_target_pairs={{0,4},{4,8},{8,12},{12,14},{14,10},{10,6},{6,2},{2,0},{1,5},{5,9},... | collective-permute-start | bytes 4325384 | tf_op jit(solution)/shard_map/ppermute | solution.py:136
  96.6 38.2 %collective-permute-start.18 = (bf16[512,1664]{1,0:T(8,128)(2,1)}, bf16[512,1664]{1,0:T(8,128)(2,1)}, u32[]{:S(2)}, u32[]{:S(2)}) collective-permute-start(bf16[512,1664]{1,0:T(8,128)(2,1)} %collective-permute-done.17), channel_id=1, source_target_pairs={{0,2},{4,0},{8,4},{12,8},{14,12},{10,14},{6,10},{2,6},{1,3},{5,1},... | collective-permute-start | bytes 5111816 | tf_op jit(solution)/shard_map/ppermute | solution.py:141
  109.0 43.0 %collective-permute-start.13 = (bf16[512,640]{1,0:T(8,128)(2,1)S(1)}, bf16[512,640]{1,0:T(8,128)(2,1)S(1)}, u32[]{:S(2)}, u32[]{:S(2)}) collective-permute-start(bf16[512,640]{1,0:T(8,128)(2,1)S(1)} %slice.55), channel_id=1, source_target_pairs={{0,16},{16,0},{1,17},{17,1},{2,18},{18,2},{3,19},{19,3},{4,20},{20... | collective-permute-start | bytes 1966088 | tf_op jit(solution)/shard_map/ppermute | solution.py:125
  110.6 18.1 %copy-start.8 = (bf16[512,640]{1,0:T(8,128)(2,1)S(1)}, bf16[512,640]{1,0:T(8,128)(2,1)}, u32[]{:S(2)}) copy-start(bf16[512,640]{1,0:T(8,128)(2,1)} %copy-done.7) | copy-start | bytes 1966084
  128.3 33.7 %collective-permute-start.11 = (bf16[512,1408]{1,0:T(8,128)(2,1)}, bf16[512,1408]{1,0:T(8,128)(2,1)S(1)}, u32[]{:S(2)}, u32[]{:S(2)}) collective-permute-start(bf16[512,1408]{1,0:T(8,128)(2,1)} %collective-permute-done.10), channel_id=1, source_target_pairs={{0,4},{4,8},{8,12},{12,14},{14,10},{10,6},{6,2},{2,0},{1,5},{5,9},... | collective-permute-start | bytes 4325384 | tf_op jit(solution)/shard_map/ppermute | solution.py:136
  130.6 73.5 %collective-permute-start.20 = (bf16[512,384]{1,0:T(8,128)(2,1)S(1)}, bf16[512,384]{1,0:T(8,128)(2,1)S(1)}, u32[]{:S(2)}, u32[]{:S(2)}) collective-permute-start(bf16[512,384]{1,0:T(8,128)(2,1)S(1)} %slice.61), channel_id=1, source_target_pairs={{0,16},{16,0},{1,17},{17,1},{2,18},{18,2},{3,19},{19,3},{4,20},{20... | collective-permute-start | bytes 1179656 | tf_op jit(solution)/shard_map/ppermute | solution.py:125
  134.8 53.3 %collective-permute-start.19 = (bf16[512,1664]{1,0:T(8,128)(2,1)}, bf16[512,1664]{1,0:T(8,128)(2,1)S(1)}, u32[]{:S(2)}, u32[]{:S(2)}) collective-permute-start(bf16[512,1664]{1,0:T(8,128)(2,1)} %collective-permute-done.18), channel_id=1, source_target_pairs={{0,2},{4,0},{8,4},{12,8},{14,12},{10,14},{6,10},{2,6},{1,3},{5,1},... | collective-permute-start | bytes 5111816 | tf_op jit(solution)/shard_map/ppermute | solution.py:141
  153.9 17.7 %collective-permute-start.14 = (bf16[512,640]{1,0:T(8,128)(2,1)S(1)}, bf16[512,640]{1,0:T(8,128)(2,1)S(1)}, u32[]{:S(2)}, u32[]{:S(2)}) collective-permute-start(bf16[512,640]{1,0:T(8,128)(2,1)S(1)} %slice.56), channel_id=1, source_target_pairs={{0,16},{16,0},{1,17},{17,1},{2,18},{18,2},{3,19},{19,3},{4,20},{20... | collective-permute-start | bytes 1966088 | tf_op jit(solution)/shard_map/ppermute | solution.py:125
  158.9 21.1 %collective-permute-start.21 = (bf16[512,384]{1,0:T(8,128)(2,1)S(1)}, bf16[512,384]{1,0:T(8,128)(2,1)S(1)}, u32[]{:S(2)}, u32[]{:S(2)}) collective-permute-start(bf16[512,384]{1,0:T(8,128)(2,1)S(1)} %slice.62), channel_id=1, source_target_pairs={{0,16},{16,0},{1,17},{17,1},{2,18},{18,2},{3,19},{19,3},{4,20},{20... | collective-permute-start | bytes 1179656 | tf_op jit(solution)/shard_map/ppermute | solution.py:125
  162.0 32.0 %collective-permute-start.15 = (bf16[512,640]{1,0:T(8,128)(2,1)S(1)}, bf16[512,640]{1,0:T(8,128)(2,1)S(1)}, u32[]{:S(2)}, u32[]{:S(2)}) collective-permute-start(bf16[512,640]{1,0:T(8,128)(2,1)S(1)} %slice.57), channel_id=1, source_target_pairs={{0,16},{16,0},{1,17},{17,1},{2,18},{18,2},{3,19},{19,3},{4,20},{20... | collective-permute-start | bytes 1966088 | tf_op jit(solution)/shard_map/ppermute | solution.py:125
  171.6 30.2 %collective-permute-start.12 = (bf16[512,1408]{1,0:T(8,128)(2,1)S(1)}, bf16[512,1408]{1,0:T(8,128)(2,1)S(1)}, u32[]{:S(2)}, u32[]{:S(2)}) collective-permute-start(bf16[512,1408]{1,0:T(8,128)(2,1)S(1)} %collective-permute-done.11), channel_id=1, source_target_pairs={{0,4},{4,8},{8,12},{12,14},{14,10},{10,6},{6,2},{2,0},{1,5},{5,9},... | collective-permute-start | bytes 4325384 | tf_op jit(solution)/shard_map/ppermute | solution.py:136
  188.1 15.3 %collective-permute-start.22 = (bf16[512,384]{1,0:T(8,128)(2,1)S(1)}, bf16[512,384]{1,0:T(8,128)(2,1)S(1)}, u32[]{:S(2)}, u32[]{:S(2)}) collective-permute-start(bf16[512,384]{1,0:T(8,128)(2,1)S(1)} %slice.63), channel_id=1, source_target_pairs={{0,16},{16,0},{1,17},{17,1},{2,18},{18,2},{3,19},{19,3},{4,20},{20... | collective-permute-start | bytes 1179656 | tf_op jit(solution)/shard_map/ppermute | solution.py:125
  195.9 8.2 %copy-start.6 = (f32[256,1664]{1,0:T(8,128)}, f32[256,1664]{1,0:T(8,128)S(1)}, u32[]{:S(2)}) copy-start(f32[256,1664]{1,0:T(8,128)S(1)} %convolution_add_fusion.4) | copy-start | bytes 5111812
  201.8 12.6 %collective-permute-start.16 = (bf16[512,640]{1,0:T(8,128)(2,1)S(1)}, bf16[512,640]{1,0:T(8,128)(2,1)S(1)}, u32[]{:S(2)}, u32[]{:S(2)}) collective-permute-start(bf16[512,640]{1,0:T(8,128)(2,1)S(1)} %slice.58), channel_id=1, source_target_pairs={{0,16},{16,0},{1,17},{17,1},{2,18},{18,2},{3,19},{19,3},{4,20},{20... | collective-permute-start | bytes 1966088 | tf_op jit(solution)/shard_map/ppermute | solution.py:125
  206.0 9.2 %copy-start.5 = (bf16[512,2048]{1,0:T(8,128)(2,1)S(1)}, bf16[512,2048]{1,0:T(8,128)(2,1)}, u32[]{:S(2)}) copy-start(bf16[512,2048]{1,0:T(8,128)(2,1)} %param.11) | copy-start | bytes 6291460
  215.3 1.3 slice-start.1
  (6 other events, 6.1 us)

commit v11 on v9

--- a/solution.py
+++ b/solution.py
@@ -97,7 +97,7 @@
     columns = out_weight.shape[1]
     groups = lax.axis_size("group")
     group_index = lax.axis_index("group")
-    own = (columns // 4) // 128 * 128 if groups == 2 else 0
+    own = (columns // 16 * 3) // 128 * 128 if groups == 2 else 0
     shared = columns - groups * own if own else columns
     swap = [(0, 1), (1, 0)]
 

time: 215 us -> 220 us (1.023)
  waiting for transfers between devices: 57.3 us -> 63.7 us
  starting transfers between devices: 61.9 us -> 58.7 us
    ppermute x4, waiting for transfers between devices: 29.5 us -> 42.9 us  [ring_transfer(): forward = lax.ppermute(forward, 'ctx', ahead)]
    ppermute x4, waiting for transfers between devices: 14 us -> 5.63 us  [ring_transfer(): crossed = lax.ppermute(forward[:, shared:], 'group', swap) if own else None]
    ppermute x3, waiting for transfers between devices: 6.38 us -> 14.6 us  [ring_transfer(): backward = lax.ppermute(backward, 'ctx', behind)]
    ppermute x3, waiting for transfers between devices: 7.41 us -> 0.58 us  [ring_transfer(): crossed = lax.ppermute(backward[:, shared:], 'group', swap) if own else None]
    ppermute x3, starting transfers between devices: 19.1 us -> 13.6 us  [ring_transfer(): backward = lax.ppermute(backward, 'ctx', behind)]
    ppermute x4, starting transfers between devices: 8.06 us -> 11.2 us  [ring_transfer(): forward = lax.ppermute(forward, 'ctx', ahead)]
  transfers between devices with their start and end apart: 23 -> 23, of which waited for: 9 -> 8; matrix products, arithmetic and copies ran while one was open for 37% -> 36% of each run, Pallas kernels for 0% -> 0%
where the time goes in v11:
time: 220 us; the launch traced here: 219 us
  waiting for transfers between devices  63.7 us (29%)
  starting transfers between devices  58.7 us (27%)
  matrix products  56.5 us (26%)
  local copies, waits for them, and re-layouts  19.6 us (9%)
  other arithmetic  11.1 us (5%)
  between operations  9.7 us (4%)
    ppermute x4, waiting for transfers between devices, ring_transfer(): forward = lax.ppermute(forward, 'ctx', ahead)  42.9 us
    ppermute x8, starting transfers between devices, passed_along(): return lax.ppermute(array, axis, pairs)  24.8 us
    dot_general x5, matrix products, update(): jnp.einsum('hgqk,khd->hgqd', weights.astype(jnp.bfloat16), value_head_row...  21.2 us
    ppermute x3, waiting for transfers between devices, ring_transfer(): backward = lax.ppermute(backward, 'ctx', behind)  14.6 us
    dot_general x8, matrix products, ring_project(): terms = [jnp.dot(piece, carried_block, preferred_element_type=jnp.float32)]  14.4 us
    dot_general x5, matrix products, update(): jnp.einsum('qhgd,khd->hgqk', query_head_rows, key_head_rows, preferred_el...  13.7 us
    ppermute x3, starting transfers between devices, ring_transfer(): backward = lax.ppermute(backward, 'ctx', behind)  13.6 us
    ppermute x4, starting transfers between devices, ring_transfer(): forward = lax.ppermute(forward, 'ctx', ahead)  11.2 us
  transfers between devices with their start and end apart: 23, of which 8 were waited for; matrix products, arithmetic and copies ran while one was open for 36% of the time, Pallas kernels for 0%

profile of v11, /device:TPU:0, one launch (start us, length us, event | category | flops | bytes accessed | tf_op | source)
XLA Modules:
  0.0 219.3 jit_solution(11946476433888855714)
XLA Ops:
  0.0 1.9 copy.52
  1.9 6.7 %collective-permute-start.6 = (bf16[256,512]{0,1:T(8,128)(2,1)}, bf16[256,512]{0,1:T(8,128)(2,1)}, u32[]{:S(2)}, u32[]{:S(2)}) collective-permute-start(bf16[256,512]{0,1:T(8,128)(2,1)} %copy.52), channel_id=1, source_target_pairs={{0,8},{2,10},{4,12},{6,14},{1,9},{3,11},{5,13},{7,15},{16,24},{18,... | collective-permute-start | bytes 786440 | tf_op jit(solution)/shard_map/ppermute | solution.py:15
  8.6 5.1 %collective-permute-start.4 = (bf16[256,512]{0,1:T(8,128)(2,1)}, bf16[256,512]{0,1:T(8,128)(2,1)}, u32[]{:S(2)}, u32[]{:S(2)}) collective-permute-start(bf16[256,512]{0,1:T(8,128)(2,1)} %copy.52), channel_id=1, source_target_pairs={{0,6},{2,8},{4,10},{6,12},{8,14},{1,7},{3,9},{5,11},{7,13},{9,15},... | collective-permute-start | bytes 786440 | tf_op jit(solution)/shard_map/ppermute | solution.py:15
  13.7 2.0 collective-permute-start.2
  15.7 2.4 %collective-permute-start = (bf16[256,512]{0,1:T(8,128)(2,1)}, bf16[256,512]{0,1:T(8,128)(2,1)S(1)}, u32[]{:S(2)}, u32[]{:S(2)}) collective-permute-start(bf16[256,512]{0,1:T(8,128)(2,1)} %copy.52), channel_id=1, source_target_pairs={{0,2},{2,4},{4,6},{6,8},{8,10},{10,12},{12,14},{1,3},{3,5},{5,7},{... | collective-permute-start | bytes 786440 | tf_op jit(solution)/shard_map/ppermute | solution.py:15
  18.1 2.6 %collective-permute-start.1 = (bf16[256,512]{1,0:T(8,128)(2,1)}, bf16[256,512]{1,0:T(8,128)(2,1)}, u32[]{:S(2)}, u32[]{:S(2)}) collective-permute-start(bf16[256,512]{1,0:T(8,128)(2,1)} %param.9), channel_id=1, source_target_pairs={{0,2},{2,4},{4,6},{6,8},{8,10},{10,12},{12,14},{1,3},{3,5},{5,7},{... | collective-permute-start | bytes 786440 | tf_op jit(solution)/shard_map/ppermute | solution.py:15
  22.4 1.8 copy.89
  24.9 1.4 slice.32
  27.5 1.2 compare_and_fusion.4
  29.7 1.4 pad_maximum_fusion
  31.1 2.0 collective-permute-start.3
  33.1 3.9 %fusion.4 = (f32[4,4,256]{2,1,0:T(4,128)S(1)}, f32[4,256,256,4]{2,1,3,0:T(8,128)}) fusion(pred[256,256]{0,1:T(8,128)(4,1)S(1)} %get-tuple-element.29, bf16[256,4,128,1]{0,2,3,1:T(8,128)(2,1)} %bitcast.74, bf16[256,4,4,128]{3,2,1,0:T(4,128)(2,1)S(1)} %reshape.293), kind=kOutput, calls=%fused_computation.30 | convolution fusion | flops 271577088 | bytes 5586944 | tf_op jit(solution)/shard_map/qhgd,khd->hgqk/dot_general | solution.py:33
  37.0 2.0 collective-permute-start.5
  39.0 3.9 %fusion.3 = (f32[4,4,256]{2,1,0:T(4,128)S(1)}, f32[4,256,256,4]{2,1,3,0:T(8,128)}) fusion(pred[256,256]{0,1:T(8,128)(4,1)S(1)} %get-tuple-element.27, bf16[256,4,128,1]{0,2,3,1:T(8,128)(2,1)} %bitcast.70, bf16[256,4,4,128]{3,2,1,0:T(4,128)(2,1)S(1)} %reshape.293), kind=kOutput, calls=%fused_computation.29 | convolution fusion | flops 271577088 | bytes 5586944 | tf_op jit(solution)/shard_map/qhgd,khd->hgqk/dot_general | solution.py:33
  42.9 2.0 collective-permute-start.7
  44.9 3.9 %fusion.2 = (f32[4,4,256]{2,1,0:T(4,128)S(1)}, f32[4,256,256,4]{2,1,3,0:T(8,128)}) fusion(pred[256,256]{0,1:T(8,128)(4,1)S(1)} %get-tuple-element.28, bf16[256,4,128,1]{0,2,3,1:T(8,128)(2,1)} %bitcast.66, bf16[256,4,4,128]{3,2,1,0:T(4,128)(2,1)S(1)} %reshape.293), kind=kOutput, calls=%fused_computation.28 | convolution fusion | flops 271577088 | bytes 5586944 | tf_op jit(solution)/shard_map/qhgd,khd->hgqk/dot_general | solution.py:33
  52.5 2.6 %fusion.26 = f32[4,4,256,128]{2,3,1,0:T(8,128)} fusion(bf16[256,4,128,1]{0,2,3,1:T(8,128)(2,1)S(1)} %bitcast.272, f32[4,256,256,4]{2,1,3,0:T(8,128)S(1)} %get-tuple-element.46, f32[4,4,256]{2,1,0:T(4,128)S(1)} %get-tuple-element.24, pred[256,256]{0,1:T(8,128)(4,1)S(1)} %get-tuple-element.25), kind=kOutput, calls=%fused_computation.52 | convolution fusion | flops 273678336 | bytes 6635520 | tf_op jit(solution)/shard_map/hgqk,khd->hgqd/dot_general | solution.py:42
  56.2 1.3 collective-permute-start.10
  58.6 4.8 %fusion.24 = f32[4,4,256,128]{2,3,1,0:T(8,128)} fusion(bf16[256,4,128,1]{0,2,3,1:T(8,128)(2,1)S(1)} %bitcast.276, f32[4,256,256,4]{2,1,3,0:T(8,128)} %copy-done.4, f32[4,4,256]{2,1,0:T(4,128)S(1)} %get-tuple-element.17, pred[256,256]{0,1:T(8,128)(4,1)S(1)} %get-tuple-element.26), kind=kOutput, calls=%fused_computation.51 | convolution fusion | flops 273678336 | bytes 6635520 | tf_op jit(solution)/shard_map/hgqk,khd->hgqd/dot_general | solution.py:42
  64.5 1.1 copy-done.3
  68.9 4.8 %fusion.22 = f32[4,4,256,128]{2,3,1,0:T(8,128)} fusion(bf16[256,4,128,1]{0,2,3,1:T(8,128)(2,1)S(1)} %bitcast.274, f32[4,256,256,4]{2,1,3,0:T(8,128)} %get-tuple-element.42, f32[4,4,256]{2,1,0:T(4,128)S(1)} %get-tuple-element.16, pred[256,256]{0,1:T(8,128)(4,1)S(1)} %get-tuple-element.28), kind=kOutput, calls=%fused_computation.50 | convolution fusion | flops 273678336 | bytes 6635520 | tf_op jit(solution)/shard_map/hgqk,khd->hgqd/dot_general | solution.py:42
  73.8 2.6 %fusion.20 = f32[4,4,256,128]{2,3,1,0:T(8,128)} fusion(bf16[256,4,128,1]{0,2,3,1:T(8,128)(2,1)S(1)} %bitcast.275, f32[4,256,256,4]{2,1,3,0:T(8,128)S(1)} %copy-done.2, f32[4,4,256]{2,1,0:T(4,128)S(1)} %get-tuple-element.15, pred[256,256]{0,1:T(8,128)(4,1)S(1)} %get-tuple-element.27), kind=kOutput, calls=%fused_computation.49 | convolution fusion | flops 273678336 | bytes 6635520 | tf_op jit(solution)/shard_map/hgqk,khd->hgqd/dot_general | solution.py:42
  78.6 8.7 %collective-permute-done.9 = bf16[512,1664]{1,0:T(8,128)(2,1)} collective-permute-done((bf16[512,1664]{1,0:T(8,128)(2,1)}, bf16[512,1664]{1,0:T(8,128)(2,1)}, u32[]{:S(2)}, u32[]{:S(2)}) %collective-permute-start.9) | collective-permute-done | bytes 1703968 | tf_op jit(solution)/shard_map/ppermute | solution.py:120
  87.3 5.4 %collective-permute-start.11 = (bf16[512,1664]{1,0:T(8,128)(2,1)}, bf16[512,1664]{1,0:T(8,128)(2,1)}, u32[]{:S(2)}, u32[]{:S(2)}) collective-permute-start(bf16[512,1664]{1,0:T(8,128)(2,1)} %collective-permute-done.9), channel_id=1, source_target_pairs={{0,4},{4,8},{8,12},{12,14},{14,10},{10,6},{6,2},{2,0},{1,5},{5,9},... | collective-permute-start | bytes 5111816 | tf_op jit(solution)/shard_map/ppermute | solution.py:120
  92.7 6.4 %fusion.29 = bf16[256,4,4,128]{0,3,2,1:T(8,128)(2,1)S(1)} fusion(f32[4,4,256,128]{2,3,1,0:T(8,128)} %fusion.20, f32[4,4,256,128]{2,3,1,0:T(8,128)} %fusion.22, f32[4,4,256,128]{2,3,1,0:T(8,128)} %fusion.24, f32[4,4,256,128]{2,3,1,0:T(8,128)} %fusion.26, f32[256,4,4]{0,2,1:T(4,128)S(1)} %get-tuple-element.10, f32[256,4,4]{0,2,1:T(4,128)S(1)} %get-tuple-element.13, ...), kind=kOutput, calls=%fused_computation.55 | convolution fusion | flops 279445504 | bytes 14073856 | tf_op jit(solution)/shard_map/hgqk,khd->hgqd/dot_general | solution.py:42
  109.8 1.4 broadcast_select_fusion
  112.2 1.6 collective-permute-start.16
  115.4 14.0 %collective-permute-done.11 = bf16[512,1664]{1,0:T(8,128)(2,1)} collective-permute-done((bf16[512,1664]{1,0:T(8,128)(2,1)}, bf16[512,1664]{1,0:T(8,128)(2,1)}, u32[]{:S(2)}, u32[]{:S(2)}) %collective-permute-start.11) | collective-permute-done | bytes 1703968 | tf_op jit(solution)/shard_map/ppermute | solution.py:120
  129.4 2.5 %collective-permute-start.13 = (bf16[512,1664]{1,0:T(8,128)(2,1)}, bf16[512,1664]{1,0:T(8,128)(2,1)S(1)}, u32[]{:S(2)}, u32[]{:S(2)}) collective-permute-start(bf16[512,1664]{1,0:T(8,128)(2,1)} %collective-permute-done.11), channel_id=1, source_target_pairs={{0,4},{4,8},{8,12},{12,14},{14,10},{10,6},{6,2},{2,0},{1,5},{5,9},... | collective-permute-start | bytes 5111816 | tf_op jit(solution)/shard_map/ppermute | solution.py:120
  131.9 2.5 %fusion.134 = f32[256,1664]{1,0:T(8,128)S(1)} fusion(bf16[512,1664]{1,0:T(8,128)(2,1)} %collective-permute-done.9, s32[]{:T(128)S(6)} %select_n.237, bf16[256,2048]{0,1:T(8,128)(2,1)S(1)} %get-tuple-element.19, bf16[256,2048]{0,1:T(8,128)(2,1)S(1)} %get-tuple-element.18), kind=kOutput, calls=%fused_computation.212 | convolution fusion | flops 436731904 | bytes 5505028 | tf_op jit(solution)/shard_map/dot_general | solution.py:135
  134.4 2.5 %fusion.130 = f32[256,1664]{1,0:T(8,128)S(1)} fusion(bf16[512,1664]{1,0:T(8,128)(2,1)} %collective-permute-done.10, s32[]{:T(128)S(6)} %select_n.240, bf16[256,2048]{0,1:T(8,128)(2,1)S(1)} %get-tuple-element.19, bf16[256,2048]{0,1:T(8,128)(2,1)S(1)} %get-tuple-element.18), kind=kOutput, calls=%fused_computation.210 | convolution fusion | flops 436731904 | bytes 5505028 | tf_op jit(solution)/shard_map/dot_general | solution.py:135
  136.9 2.9 %collective-permute-done.12 = bf16[512,1664]{1,0:T(8,128)(2,1)} collective-permute-done((bf16[512,1664]{1,0:T(8,128)(2,1)}, bf16[512,1664]{1,0:T(8,128)(2,1)}, u32[]{:S(2)}, u32[]{:S(2)}) %collective-permute-start.12) | collective-permute-done | bytes 1703968 | tf_op jit(solution)/shard_map/ppermute | solution.py:124
  139.8 12.2 %collective-permute-start.14 = (bf16[512,1664]{1,0:T(8,128)(2,1)}, bf16[512,1664]{1,0:T(8,128)(2,1)S(1)}, u32[]{:S(2)}, u32[]{:S(2)}) collective-permute-start(bf16[512,1664]{1,0:T(8,128)(2,1)} %collective-permute-done.12), channel_id=1, source_target_pairs={{0,2},{4,0},{8,4},{12,8},{14,12},{10,14},{6,10},{2,6},{1,3},{5,1},... | collective-permute-start | bytes 5111816 | tf_op jit(solution)/shard_map/ppermute | solution.py:124
  155.7 1.6 collective-permute-start.18
  158.9 2.5 %fusion.123 = f32[256,1664]{1,0:T(8,128)S(1)} fusion(bf16[512,1664]{1,0:T(8,128)(2,1)} %collective-permute-done.12, s32[]{:T(128)S(6)} %select_n.246, bf16[256,2048]{0,1:T(8,128)(2,1)S(1)} %get-tuple-element.19, bf16[256,2048]{0,1:T(8,128)(2,1)S(1)} %get-tuple-element.18), kind=kOutput, calls=%fused_computation.207 | convolution fusion | flops 436731904 | bytes 5505028 | tf_op jit(solution)/shard_map/dot_general | solution.py:135
  161.4 6.5 %collective-permute-done.13 = bf16[512,1664]{1,0:T(8,128)(2,1)S(1)} collective-permute-done((bf16[512,1664]{1,0:T(8,128)(2,1)}, bf16[512,1664]{1,0:T(8,128)(2,1)S(1)}, u32[]{:S(2)}, u32[]{:S(2)}) %collective-permute-start.13) | collective-permute-done | bytes 1703968 | tf_op jit(solution)/shard_map/ppermute | solution.py:120
  167.9 2.3 %collective-permute-start.15 = (bf16[512,1664]{1,0:T(8,128)(2,1)S(1)}, bf16[512,1664]{1,0:T(8,128)(2,1)S(1)}, u32[]{:S(2)}, u32[]{:S(2)}) collective-permute-start(bf16[512,1664]{1,0:T(8,128)(2,1)S(1)} %collective-permute-done.13), channel_id=1, source_target_pairs={{0,4},{4,8},{8,12},{12,14},{14,10},{10,6},{6,2},{2,0},{1,5},{5,9},... | collective-permute-start | bytes 5111816 | tf_op jit(solution)/shard_map/ppermute | solution.py:120
  170.2 2.5 %fusion.16 = f32[256,1664]{1,0:T(8,128)S(1)} fusion(f32[256,1664]{1,0:T(8,128)S(1)} %fusion.123, f32[256,1664]{1,0:T(8,128)S(1)} %fusion.17, bf16[512,1664]{1,0:T(8,128)(2,1)} %collective-permute-done.11, s32[]{:T(128)S(6)} %select_n.243, bf16[256,2048]{0,1:T(8,128)(2,1)S(1)} %get-tuple-element.19, bf16[256,2048]{0,1:T(8,128)(2,1)S(1)} %get-tuple-element.18), kind=kOutput, calls=%fused_computation.45 | convolution fusion | flops 437583872 | bytes 8912900 | tf_op jit(solution)/shard_map/dot_general | solution.py:135
  174.9 1.6 collective-permute-start.20
  176.5 11.6 %collective-permute-done.14 = bf16[512,1664]{1,0:T(8,128)(2,1)S(1)} collective-permute-done((bf16[512,1664]{1,0:T(8,128)(2,1)}, bf16[512,1664]{1,0:T(8,128)(2,1)S(1)}, u32[]{:S(2)}, u32[]{:S(2)}) %collective-permute-start.14) | collective-permute-done | bytes 1703968 | tf_op jit(solution)/shard_map/ppermute | solution.py:124
  188.2 1.6 collective-permute-start.21
  190.8 1.1 fusion.15
  192.7 13.7 %collective-permute-done.15 = bf16[512,1664]{1,0:T(8,128)(2,1)S(1)} collective-permute-done((bf16[512,1664]{1,0:T(8,128)(2,1)S(1)}, bf16[512,1664]{1,0:T(8,128)(2,1)S(1)}, u32[]{:S(2)}, u32[]{:S(2)}) %collective-permute-start.15) | collective-permute-done | bytes 1703968 | tf_op jit(solution)/shard_map/ppermute | solution.py:120
  206.4 1.6 collective-permute-start.22
  208.7 1.1 convolution_add_fusion
  209.9 5.6 %collective-permute-done.22 = bf16[512,384]{1,0:T(8,128)(2,1)S(1)} collective-permute-done((bf16[512,384]{1,0:T(8,128)(2,1)S(1)}, bf16[512,384]{1,0:T(8,128)(2,1)S(1)}, u32[]{:S(2)}, u32[]{:S(2)}) %collective-permute-start.22) | collective-permute-done | bytes 393248 | tf_op jit(solution)/shard_map/ppermute | solution.py:121
  216.3 1.9 select_convert_fusion.1
  218.2 1.1 pad_maximum_fusion.1
  (99 shorter events, 31.8 us)
Async XLA Ops:
  0.0 24.1 %copy-start.5 = (bf16[256,2048]{1,0:T(8,128)(2,1)S(1)}, bf16[256,2048]{1,0:T(8,128)(2,1)}, u32[]{:S(2)}) copy-start(bf16[256,2048]{1,0:T(8,128)(2,1)} %param.7) | copy-start | bytes 3145732
  1.9 29.2 %collective-permute-start.6 = (bf16[256,512]{0,1:T(8,128)(2,1)}, bf16[256,512]{0,1:T(8,128)(2,1)}, u32[]{:S(2)}, u32[]{:S(2)}) collective-permute-start(bf16[256,512]{0,1:T(8,128)(2,1)} %copy.52), channel_id=1, source_target_pairs={{0,8},{2,10},{4,12},{6,14},{1,9},{3,11},{5,13},{7,15},{16,24},{18,... | collective-permute-start | bytes 786440 | tf_op jit(solution)/shard_map/ppermute | solution.py:15
  8.6 28.4 %collective-permute-start.4 = (bf16[256,512]{0,1:T(8,128)(2,1)}, bf16[256,512]{0,1:T(8,128)(2,1)}, u32[]{:S(2)}, u32[]{:S(2)}) collective-permute-start(bf16[256,512]{0,1:T(8,128)(2,1)} %copy.52), channel_id=1, source_target_pairs={{0,6},{2,8},{4,10},{6,12},{8,14},{1,7},{3,9},{5,11},{7,13},{9,15},... | collective-permute-start | bytes 786440 | tf_op jit(solution)/shard_map/ppermute | solution.py:15
  13.7 29.2 %collective-permute-start.2 = (bf16[256,512]{0,1:T(8,128)(2,1)}, bf16[256,512]{0,1:T(8,128)(2,1)}, u32[]{:S(2)}, u32[]{:S(2)}) collective-permute-start(bf16[256,512]{0,1:T(8,128)(2,1)} %copy.52), channel_id=1, source_target_pairs={{0,4},{2,6},{4,8},{6,10},{8,12},{10,14},{1,5},{3,7},{5,9},{7,11},{... | collective-permute-start | bytes 786440 | tf_op jit(solution)/shard_map/ppermute | solution.py:15
  15.7 33.1 %collective-permute-start = (bf16[256,512]{0,1:T(8,128)(2,1)}, bf16[256,512]{0,1:T(8,128)(2,1)S(1)}, u32[]{:S(2)}, u32[]{:S(2)}) collective-permute-start(bf16[256,512]{0,1:T(8,128)(2,1)} %copy.52), channel_id=1, source_target_pairs={{0,2},{2,4},{4,6},{6,8},{8,10},{10,12},{12,14},{1,3},{3,5},{5,7},{... | collective-permute-start | bytes 786440 | tf_op jit(solution)/shard_map/ppermute | solution.py:15
  18.1 38.1 %collective-permute-start.1 = (bf16[256,512]{1,0:T(8,128)(2,1)}, bf16[256,512]{1,0:T(8,128)(2,1)}, u32[]{:S(2)}, u32[]{:S(2)}) collective-permute-start(bf16[256,512]{1,0:T(8,128)(2,1)} %param.9), channel_id=1, source_target_pairs={{0,2},{2,4},{4,6},{6,8},{8,10},{10,12},{12,14},{1,3},{3,5},{5,7},{... | collective-permute-start | bytes 786440 | tf_op jit(solution)/shard_map/ppermute | solution.py:15
  24.9 2.5 %copy-start.17 = (s32[16]{0:T(128)S(1)}, s32[16]{0:T(128)}, u32[]{:S(2)}) copy-start(s32[16]{0:T(128)} %param.10) | copy-start | bytes 196
  29.7 1.4 copy-start.6
  31.1 35.6 %collective-permute-start.3 = (bf16[256,512]{1,0:T(8,128)(2,1)S(1)}, bf16[256,512]{1,0:T(8,128)(2,1)}, u32[]{:S(2)}, u32[]{:S(2)}) collective-permute-start(bf16[256,512]{1,0:T(8,128)(2,1)S(1)} %copy-done.6), channel_id=1, source_target_pairs={{0,4},{2,6},{4,8},{6,10},{8,12},{10,14},{1,5},{3,7},{5,9},{7,11},{... | collective-permute-start | bytes 786440 | tf_op jit(solution)/shard_map/ppermute | solution.py:15
  37.0 13.8 %copy-start.8 = (f32[4,4,256]{2,1,0:T(4,128)}, f32[4,4,256]{2,1,0:T(4,128)S(1)}, u32[]{:S(2)}) copy-start(f32[4,4,256]{2,1,0:T(4,128)S(1)} %get-tuple-element.37) | copy-start | bytes 49156
  37.0 30.8 %collective-permute-start.5 = (bf16[256,512]{1,0:T(8,128)(2,1)S(1)}, bf16[256,512]{1,0:T(8,128)(2,1)}, u32[]{:S(2)}, u32[]{:S(2)}) collective-permute-start(bf16[256,512]{1,0:T(8,128)(2,1)S(1)} %copy-done.6), channel_id=1, source_target_pairs={{0,6},{2,8},{4,10},{6,12},{8,14},{1,7},{3,9},{5,11},{7,13},{9,15},... | collective-permute-start | bytes 786440 | tf_op jit(solution)/shard_map/ppermute | solution.py:15
  42.9 7.9 %copy-start.10 = (f32[4,4,256]{2,1,0:T(4,128)}, f32[4,4,256]{2,1,0:T(4,128)S(1)}, u32[]{:S(2)}) copy-start(f32[4,4,256]{2,1,0:T(4,128)S(1)} %get-tuple-element.39) | copy-start | bytes 49156
  42.9 34.5 %collective-permute-start.7 = (bf16[256,512]{1,0:T(8,128)(2,1)S(1)}, bf16[256,512]{1,0:T(8,128)(2,1)}, u32[]{:S(2)}, u32[]{:S(2)}) collective-permute-start(bf16[256,512]{1,0:T(8,128)(2,1)S(1)} %copy-done.6), channel_id=1, source_target_pairs={{0,8},{2,10},{4,12},{6,14},{1,9},{3,11},{5,13},{7,15},{16,24},{18,... | collective-permute-start | bytes 786440 | tf_op jit(solution)/shard_map/ppermute | solution.py:15
  48.8 2.0 copy-start.12
  48.8 38.5 %collective-permute-start.9 = (bf16[512,1664]{1,0:T(8,128)(2,1)}, bf16[512,1664]{1,0:T(8,128)(2,1)}, u32[]{:S(2)}, u32[]{:S(2)}) collective-permute-start(bf16[512,1664]{1,0:T(8,128)(2,1)} %pad_maximum_fusion), channel_id=1, source_target_pairs={{0,4},{4,8},{8,12},{12,14},{14,10},{10,6},{6,2},{2,0},{1,5},{5,9},... | collective-permute-start | bytes 5111816 | tf_op jit(solution)/shard_map/ppermute | solution.py:120
  50.8 0.6 copy-start.14
  50.8 4.3 %copy-start.4 = (f32[4,256,256,4]{2,1,3,0:T(8,128)}, f32[4,256,256,4]{2,1,3,0:T(8,128)S(1)}, u32[]{:S(2)}) copy-start(f32[4,256,256,4]{2,1,3,0:T(8,128)S(1)} %get-tuple-element.44) | copy-start | bytes 12582916
  51.4 1.1 copy-start.7
  56.2 43.0 %collective-permute-start.10 = (bf16[512,1664]{1,0:T(8,128)(2,1)}, bf16[512,1664]{1,0:T(8,128)(2,1)}, u32[]{:S(2)}, u32[]{:S(2)}) collective-permute-start(bf16[512,1664]{1,0:T(8,128)(2,1)} %pad_maximum_fusion), channel_id=1, source_target_pairs={{0,2},{4,0},{8,4},{12,8},{14,12},{10,14},{6,10},{2,6},{1,3},{5,1},... | collective-permute-start | bytes 5111816 | tf_op jit(solution)/shard_map/ppermute | solution.py:124
  58.6 4.9 %copy-start.1 = (f32[4,256,256,4]{2,1,3,0:T(8,128)S(1)}, f32[4,256,256,4]{2,1,3,0:T(8,128)}, u32[]{:S(2)}) copy-start(f32[4,256,256,4]{2,1,3,0:T(8,128)} %get-tuple-element.40) | copy-start | bytes 12582916
  63.5 2.2 copy-start.3
  68.9 4.9 %copy-start.2 = (f32[4,256,256,4]{2,1,3,0:T(8,128)S(1)}, f32[4,256,256,4]{2,1,3,0:T(8,128)}, u32[]{:S(2)}) copy-start(f32[4,256,256,4]{2,1,3,0:T(8,128)} %get-tuple-element.40) | copy-start | bytes 12582916
  73.8 2.6 %copy-start = (f32[4,256,256,4]{2,1,3,0:T(8,128)S(1)}, f32[4,256,256,4]{2,1,3,0:T(8,128)}, u32[]{:S(2)}) copy-start(f32[4,256,256,4]{2,1,3,0:T(8,128)} %get-tuple-element.38) | copy-start | bytes 12582916
  76.3 2.2 copy-start.9
  76.3 2.2 copy-start.11
  76.3 2.2 copy-start.13
  76.3 2.2 copy-start.15
  87.3 42.1 %collective-permute-start.11 = (bf16[512,1664]{1,0:T(8,128)(2,1)}, bf16[512,1664]{1,0:T(8,128)(2,1)}, u32[]{:S(2)}, u32[]{:S(2)}) collective-permute-start(bf16[512,1664]{1,0:T(8,128)(2,1)} %collective-permute-done.9), channel_id=1, source_target_pairs={{0,4},{4,8},{8,12},{12,14},{14,10},{10,6},{6,2},{2,0},{1,5},{5,9},... | collective-permute-start | bytes 5111816 | tf_op jit(solution)/shard_map/ppermute | solution.py:120
  92.7 6.6 %copy-start.18 = (s32[8]{0:T(128)S(1)}, s32[8]{0:T(128)}, u32[]{:S(2)}) copy-start(s32[8]{0:T(128)} %constant.184.clone) | copy-start | bytes 100
  92.7 11.9 %copy-start.16 = (s32[8]{0:T(128)S(1)}, s32[8]{0:T(128)}, u32[]{:S(2)}) copy-start(s32[8]{0:T(128)} %constant.185.clone) | copy-start | bytes 100
  99.1 10.7 %collective-permute-start.8 = (bf16[256,2048]{0,1:T(8,128)(2,1)S(1)}, bf16[256,2048]{0,1:T(8,128)(2,1)}, u32[]{:S(2)}, u32[]{:S(2)}) collective-permute-start(bf16[256,2048]{0,1:T(8,128)(2,1)S(1)} %bitcast.269), channel_id=1, source_target_pairs={{0,1},{1,0},{2,3},{3,2},{4,5},{5,4},{6,7},{7,6},{8,9},{9,8},{10,11... | collective-permute-start | bytes 3145736 | tf_op jit(solution)/shard_map/ppermute | solution.py:77
  99.2 40.6 %collective-permute-start.12 = (bf16[512,1664]{1,0:T(8,128)(2,1)}, bf16[512,1664]{1,0:T(8,128)(2,1)}, u32[]{:S(2)}, u32[]{:S(2)}) collective-permute-start(bf16[512,1664]{1,0:T(8,128)(2,1)} %collective-permute-done.10), channel_id=1, source_target_pairs={{0,2},{4,0},{8,4},{12,8},{14,12},{10,14},{6,10},{2,6},{1,3},{5,1},... | collective-permute-start | bytes 5111816 | tf_op jit(solution)/shard_map/ppermute | solution.py:124
  112.2 40.9 %collective-permute-start.16 = (bf16[512,384]{1,0:T(8,128)(2,1)S(1)}, bf16[512,384]{1,0:T(8,128)(2,1)S(1)}, u32[]{:S(2)}, u32[]{:S(2)}) collective-permute-start(bf16[512,384]{1,0:T(8,128)(2,1)S(1)} %slice.44), channel_id=1, source_target_pairs={{0,16},{16,0},{1,17},{17,1},{2,18},{18,2},{3,19},{19,3},{4,20},{20... | collective-permute-start | bytes 1179656 | tf_op jit(solution)/shard_map/ppermute | solution.py:121
  114.8 39.1 %collective-permute-start.17 = (bf16[512,384]{1,0:T(8,128)(2,1)S(1)}, bf16[512,384]{1,0:T(8,128)(2,1)S(1)}, u32[]{:S(2)}, u32[]{:S(2)}) collective-permute-start(bf16[512,384]{1,0:T(8,128)(2,1)S(1)} %slice.45), channel_id=1, source_target_pairs={{0,16},{16,0},{1,17},{17,1},{2,18},{18,2},{3,19},{19,3},{4,20},{20... | collective-permute-start | bytes 1179656 | tf_op jit(solution)/shard_map/ppermute | solution.py:125
  129.4 38.5 %collective-permute-start.13 = (bf16[512,1664]{1,0:T(8,128)(2,1)}, bf16[512,1664]{1,0:T(8,128)(2,1)S(1)}, u32[]{:S(2)}, u32[]{:S(2)}) collective-permute-start(bf16[512,1664]{1,0:T(8,128)(2,1)} %collective-permute-done.11), channel_id=1, source_target_pairs={{0,4},{4,8},{8,12},{12,14},{14,10},{10,6},{6,2},{2,0},{1,5},{5,9},... | collective-permute-start | bytes 5111816 | tf_op jit(solution)/shard_map/ppermute | solution.py:120
  139.8 48.3 %collective-permute-start.14 = (bf16[512,1664]{1,0:T(8,128)(2,1)}, bf16[512,1664]{1,0:T(8,128)(2,1)S(1)}, u32[]{:S(2)}, u32[]{:S(2)}) collective-permute-start(bf16[512,1664]{1,0:T(8,128)(2,1)} %collective-permute-done.12), channel_id=1, source_target_pairs={{0,2},{4,0},{8,4},{12,8},{14,12},{10,14},{6,10},{2,6},{1,3},{5,1},... | collective-permute-start | bytes 5111816 | tf_op jit(solution)/shard_map/ppermute | solution.py:124
  155.7 17.0 %collective-permute-start.18 = (bf16[512,384]{1,0:T(8,128)(2,1)S(1)}, bf16[512,384]{1,0:T(8,128)(2,1)S(1)}, u32[]{:S(2)}, u32[]{:S(2)}) collective-permute-start(bf16[512,384]{1,0:T(8,128)(2,1)S(1)} %slice.46), channel_id=1, source_target_pairs={{0,16},{16,0},{1,17},{17,1},{2,18},{18,2},{3,19},{19,3},{4,20},{20... | collective-permute-start | bytes 1179656 | tf_op jit(solution)/shard_map/ppermute | solution.py:121
  158.3 15.8 %collective-permute-start.19 = (bf16[512,384]{1,0:T(8,128)(2,1)S(1)}, bf16[512,384]{1,0:T(8,128)(2,1)S(1)}, u32[]{:S(2)}, u32[]{:S(2)}) collective-permute-start(bf16[512,384]{1,0:T(8,128)(2,1)S(1)} %slice.47), channel_id=1, source_target_pairs={{0,16},{16,0},{1,17},{17,1},{2,18},{18,2},{3,19},{19,3},{4,20},{20... | collective-permute-start | bytes 1179656 | tf_op jit(solution)/shard_map/ppermute | solution.py:125
  167.9 38.4 %collective-permute-start.15 = (bf16[512,1664]{1,0:T(8,128)(2,1)S(1)}, bf16[512,1664]{1,0:T(8,128)(2,1)S(1)}, u32[]{:S(2)}, u32[]{:S(2)}) collective-permute-start(bf16[512,1664]{1,0:T(8,128)(2,1)S(1)} %collective-permute-done.13), channel_id=1, source_target_pairs={{0,4},{4,8},{8,12},{12,14},{14,10},{10,6},{6,2},{2,0},{1,5},{5,9},... | collective-permute-start | bytes 5111816 | tf_op jit(solution)/shard_map/ppermute | solution.py:120
  174.9 17.0 %collective-permute-start.20 = (bf16[512,384]{1,0:T(8,128)(2,1)S(1)}, bf16[512,384]{1,0:T(8,128)(2,1)S(1)}, u32[]{:S(2)}, u32[]{:S(2)}) collective-permute-start(bf16[512,384]{1,0:T(8,128)(2,1)S(1)} %slice.48), channel_id=1, source_target_pairs={{0,16},{16,0},{1,17},{17,1},{2,18},{18,2},{3,19},{19,3},{4,20},{20... | collective-permute-start | bytes 1179656 | tf_op jit(solution)/shard_map/ppermute | solution.py:121
  188.2 19.8 %collective-permute-start.21 = (bf16[512,384]{1,0:T(8,128)(2,1)S(1)}, bf16[512,384]{1,0:T(8,128)(2,1)S(1)}, u32[]{:S(2)}, u32[]{:S(2)}) collective-permute-start(bf16[512,384]{1,0:T(8,128)(2,1)S(1)} %slice.49), channel_id=1, source_target_pairs={{0,16},{16,0},{1,17},{17,1},{2,18},{18,2},{3,19},{19,3},{4,20},{20... | collective-permute-start | bytes 1179656 | tf_op jit(solution)/shard_map/ppermute | solution.py:125
  206.4 9.1 %collective-permute-start.22 = (bf16[512,384]{1,0:T(8,128)(2,1)S(1)}, bf16[512,384]{1,0:T(8,128)(2,1)S(1)}, u32[]{:S(2)}, u32[]{:S(2)}) collective-permute-start(bf16[512,384]{1,0:T(8,128)(2,1)S(1)} %slice.50), channel_id=1, source_target_pairs={{0,16},{16,0},{1,17},{17,1},{2,18},{18,2},{3,19},{19,3},{4,20},{20... | collective-permute-start | bytes 1179656 | tf_op jit(solution)/shard_map/ppermute | solution.py:121

commit v12 on v8

--- a/solution.py
+++ b/solution.py
@@ -97,7 +97,7 @@
     columns = out_weight.shape[1]
     groups = lax.axis_size("group")
     group_index = lax.axis_index("group")
-    own = (columns // 3) // 128 * 128 if groups == 2 else 0
+    own = (columns // 4) // 128 * 128 if groups == 2 else 0
     shared = columns - groups * own if own else columns
     swap = [(0, 1), (1, 0)]
 
@@ -167,9 +167,11 @@
     arrivals, shared, own = ring_transfer(out_weight)
     initial_state = fresh_state(kv_heads, group_width, tok_rows)
     state_now = attend(initial_state, keys, values, query_start)
+    joined = jnp.concatenate([keys, values], axis=1)
     for distance in range(1, reach_devs + 1):
         skipped = BLOCK_TOKENS if distance == reach_devs and tok_rows > BLOCK_TOKENS else 0
-        prior_keys, prior_values = passed_along((keys[skipped:], values[skipped:]), "ctx", distance)
+        prior = passed_along(joined[skipped:], "ctx", distance)
+        prior_keys, prior_values = prior[:, : keys.shape[1]], prior[:, keys.shape[1] :]
         key_start = query_start - distance * tok_rows + skipped
         state_now = attend(state_now, prior_keys, prior_values, key_start)
     attended = finish(state_now, tok_rows, q_heads)

time: 224 us -> 213 us (0.951)
  matrix products: 50.9 us -> 31.8 us
  starting transfers between devices: 53 us -> 66.5 us
  local copies, waits for them, and re-layouts: 19.1 us -> 16.4 us
  waiting for transfers between devices: 80.1 us -> 77.4 us
    ppermute x3, starting transfers between devices: 6.18 us -> 33.4 us  [ring_transfer(): backward = lax.ppermute(backward, 'ctx', behind)]
    ppermute x8 -> x4, starting transfers between devices: 35.7 us -> 16.4 us  [passed_along(): return lax.ppermute(array, axis, pairs)]
    ppermute x3, waiting for transfers between devices: 16.5 us -> 2.22 us  [ring_transfer(): crossed = lax.ppermute(backward[:, shared:], 'group', swap) if own else None]
    ppermute x4, waiting for transfers between devices: 47.2 us -> 32.9 us  [ring_transfer(): forward = lax.ppermute(forward, 'ctx', ahead)]
    dot_general x5, matrix products: 18.1 us -> 6.31 us  [update(): jnp.einsum('hgqk,khd->hgqd', weights.astype(jnp.bfloat16), value_head_row...]
    ppermute x8 -> x4, waiting for transfers between devices: 0.02 us -> 11.6 us  [passed_along(): return lax.ppermute(array, axis, pairs)]
    dot_general x5, matrix products: 14.3 us -> 4.62 us  [update(): jnp.einsum('qhgd,khd->hgqk', query_head_rows, key_head_rows, preferred_el...]
    ppermute x3, waiting for transfers between devices: 6.71 us -> 15.8 us  [ring_transfer(): backward = lax.ppermute(backward, 'ctx', behind)]
  transfers between devices with their start and end apart: 23 -> 19, of which waited for: 7 -> 12; matrix products, arithmetic and copies ran while one was open for 33% -> 24% of each run, Pallas kernels for 0% -> 0%
where the time goes in v12:
time: 213 us; the launch traced here: 212 us
  waiting for transfers between devices  77.4 us (36%)
  starting transfers between devices  66.5 us (31%)
  matrix products  31.8 us (15%)
  local copies, waits for them, and re-layouts  16.4 us (8%)
  other arithmetic  10.1 us (5%)
  between operations  9.67 us (5%)
    ppermute x3, starting transfers between devices, ring_transfer(): backward = lax.ppermute(backward, 'ctx', behind)  33.4 us
    ppermute x4, waiting for transfers between devices, ring_transfer(): forward = lax.ppermute(forward, 'ctx', ahead)  32.9 us
    ppermute x4, starting transfers between devices, passed_along(): return lax.ppermute(array, axis, pairs)  16.4 us
    ppermute x3, waiting for transfers between devices, ring_transfer(): backward = lax.ppermute(backward, 'ctx', behind)  15.8 us
    ppermute x4, waiting for transfers between devices, ring_transfer(): crossed = lax.ppermute(forward[:, shared:], 'group', swap) if own else None  15 us
    dot_general x8, matrix products, ring_project(): terms = [jnp.dot(piece, carried_block, preferred_element_type=jnp.float32)]  13.6 us
    ppermute x4, waiting for transfers between devices, passed_along(): return lax.ppermute(array, axis, pairs)  11.6 us
    ppermute x4, starting transfers between devices, ring_transfer(): forward = lax.ppermute(forward, 'ctx', ahead)  7.48 us
  transfers between devices with their start and end apart: 19, of which 12 were waited for; matrix products, arithmetic and copies ran while one was open for 24% of the time, Pallas kernels for 0%

profile of v12, /device:TPU:0, one launch (start us, length us, event | category | flops | bytes accessed | tf_op | source)
XLA Modules:
  0.0 211.8 jit_solution(15712025459334749188)
XLA Ops:
  0.0 1.1 copy.77
  1.1 1.1 copy.46
  3.0 6.7 %collective-permute-start.2 = (bf16[256,1024]{0,1:T(8,128)(2,1)}, bf16[256,1024]{0,1:T(8,128)(2,1)}, u32[]{:S(2)}, u32[]{:S(2)}) collective-permute-start(bf16[256,1024]{0,1:T(8,128)(2,1)} %pad_maximum_fusion.2), channel_id=1, source_target_pairs={{0,6},{2,8},{4,10},{6,12},{8,14},{1,7},{3,9},{5,11},{7,13},{9,15},... | collective-permute-start | bytes 1572872 | tf_op jit(solution)/shard_map/ppermute | solution.py:15
  9.7 4.3 %collective-permute-start.1 = (bf16[256,1024]{0,1:T(8,128)(2,1)}, bf16[256,1024]{0,1:T(8,128)(2,1)}, u32[]{:S(2)}, u32[]{:S(2)}) collective-permute-start(bf16[256,1024]{0,1:T(8,128)(2,1)} %pad_maximum_fusion.2), channel_id=1, source_target_pairs={{0,4},{2,6},{4,8},{6,10},{8,12},{10,14},{1,5},{3,7},{5,9},{7,11},{... | collective-permute-start | bytes 1572872 | tf_op jit(solution)/shard_map/ppermute | solution.py:15
  14.0 3.5 %collective-permute-start = (bf16[256,1024]{0,1:T(8,128)(2,1)}, bf16[256,1024]{0,1:T(8,128)(2,1)}, u32[]{:S(2)}, u32[]{:S(2)}) collective-permute-start(bf16[256,1024]{0,1:T(8,128)(2,1)} %pad_maximum_fusion.2), channel_id=1, source_target_pairs={{0,2},{2,4},{4,6},{6,8},{8,10},{10,12},{12,14},{1,3},{3,5},{5,7},{... | collective-permute-start | bytes 1572872 | tf_op jit(solution)/shard_map/ppermute | solution.py:15
  17.5 2.0 collective-permute-start.3
  19.5 1.3 slice.68
  20.8 1.1 constant_dynamic-slice_fusion
  21.9 1.3 pad_maximum_fusion
  23.3 1.8 reshape.293
  26.8 11.5 %collective-permute-done.3 = bf16[128,1024]{0,1:T(8,128)(2,1)} collective-permute-done((bf16[128,1024]{0,1:T(8,128)(2,1)S(1)}, bf16[128,1024]{0,1:T(8,128)(2,1)}, u32[]{:S(2)}, u32[]{:S(2)}) %collective-permute-start.3) | collective-permute-done | bytes 262176 | tf_op jit(solution)/shard_map/ppermute | solution.py:15
  38.3 11.7 %collective-permute-start.6 = (bf16[512,1536]{1,0:T(8,128)(2,1)}, bf16[512,1536]{1,0:T(8,128)(2,1)}, u32[]{:S(2)}, u32[]{:S(2)}) collective-permute-start(bf16[512,1536]{1,0:T(8,128)(2,1)} %pad_maximum_fusion), channel_id=1, source_target_pairs={{0,2},{4,0},{8,4},{12,8},{14,12},{10,14},{6,10},{2,6},{1,3},{5,1},... | collective-permute-start | bytes 4718600 | tf_op jit(solution)/shard_map/ppermute | solution.py:124
  53.7 1.1 fusion.141
  55.8 1.1 fusion.140
  59.0 1.2 fusion.21
  61.2 1.2 fusion.19
  65.1 1.2 fusion.17
  66.3 1.4 fusion.15
  67.8 1.3 fusion.24
  69.2 1.8 collective-permute-done.5
  71.0 7.2 %collective-permute-start.7 = (bf16[512,1536]{1,0:T(8,128)(2,1)}, bf16[512,1536]{1,0:T(8,128)(2,1)}, u32[]{:S(2)}, u32[]{:S(2)}) collective-permute-start(bf16[512,1536]{1,0:T(8,128)(2,1)} %collective-permute-done.5), channel_id=1, source_target_pairs={{0,4},{4,8},{8,12},{12,14},{14,10},{10,6},{6,2},{2,0},{1,5},{5,9},... | collective-permute-start | bytes 4718600 | tf_op jit(solution)/shard_map/ppermute | solution.py:120
  78.2 4.9 %collective-permute-done.6 = bf16[512,1536]{1,0:T(8,128)(2,1)} collective-permute-done((bf16[512,1536]{1,0:T(8,128)(2,1)}, bf16[512,1536]{1,0:T(8,128)(2,1)}, u32[]{:S(2)}, u32[]{:S(2)}) %collective-permute-start.6) | collective-permute-done | bytes 1572896 | tf_op jit(solution)/shard_map/ppermute | solution.py:124
  83.1 19.3 %collective-permute-start.8 = (bf16[512,1536]{1,0:T(8,128)(2,1)}, bf16[512,1536]{1,0:T(8,128)(2,1)}, u32[]{:S(2)}, u32[]{:S(2)}) collective-permute-start(bf16[512,1536]{1,0:T(8,128)(2,1)} %collective-permute-done.6), channel_id=1, source_target_pairs={{0,2},{4,0},{8,4},{12,8},{14,12},{10,14},{6,10},{2,6},{1,3},{5,1},... | collective-permute-start | bytes 4718600 | tf_op jit(solution)/shard_map/ppermute | solution.py:124
  112.9 1.4 broadcast_select_fusion
  114.3 1.1 slice.90
  115.4 1.6 collective-permute-start.12
  117.0 1.1 slice.91
  118.6 4.2 %collective-permute-done.7 = bf16[512,1536]{1,0:T(8,128)(2,1)} collective-permute-done((bf16[512,1536]{1,0:T(8,128)(2,1)}, bf16[512,1536]{1,0:T(8,128)(2,1)}, u32[]{:S(2)}, u32[]{:S(2)}) %collective-permute-start.7) | collective-permute-done | bytes 1572896 | tf_op jit(solution)/shard_map/ppermute | solution.py:120
  122.8 2.4 %fusion.132 = f32[256,1536]{1,0:T(8,128)S(1)} fusion(bf16[512,1536]{1,0:T(8,128)(2,1)} %collective-permute-done.5, s32[]{:T(128)S(6)} %select_n.241, bf16[256,2048]{0,1:T(8,128)(2,1)S(1)} %get-tuple-element.18, bf16[256,2048]{0,1:T(8,128)(2,1)S(1)} %get-tuple-element.17), kind=kOutput, calls=%fused_computation.215 | convolution fusion | flops 403177472 | bytes 5242884 | tf_op jit(solution)/shard_map/dot_general | solution.py:135
  125.2 2.4 %fusion.128 = f32[256,1536]{1,0:T(8,128)S(1)} fusion(bf16[512,1536]{1,0:T(8,128)(2,1)} %collective-permute-done.6, s32[]{:T(128)S(6)} %select_n.244, bf16[256,2048]{0,1:T(8,128)(2,1)S(1)} %get-tuple-element.18, bf16[256,2048]{0,1:T(8,128)(2,1)S(1)} %get-tuple-element.17), kind=kOutput, calls=%fused_computation.213 | convolution fusion | flops 403177472 | bytes 5242884 | tf_op jit(solution)/shard_map/dot_general | solution.py:135
  128.6 7.1 %collective-permute-done.8 = bf16[512,1536]{1,0:T(8,128)(2,1)} collective-permute-done((bf16[512,1536]{1,0:T(8,128)(2,1)}, bf16[512,1536]{1,0:T(8,128)(2,1)}, u32[]{:S(2)}, u32[]{:S(2)}) %collective-permute-start.8) | collective-permute-done | bytes 1572896 | tf_op jit(solution)/shard_map/ppermute | solution.py:124
  135.7 2.5 %collective-permute-start.10 = (bf16[512,1536]{1,0:T(8,128)(2,1)}, bf16[512,1536]{1,0:T(8,128)(2,1)S(1)}, u32[]{:S(2)}, u32[]{:S(2)}) collective-permute-start(bf16[512,1536]{1,0:T(8,128)(2,1)} %collective-permute-done.8), channel_id=1, source_target_pairs={{0,2},{4,0},{8,4},{12,8},{14,12},{10,14},{6,10},{2,6},{1,3},{5,1},... | collective-permute-start | bytes 4718600 | tf_op jit(solution)/shard_map/ppermute | solution.py:124
  140.2 1.1 slice.92
  141.2 1.6 collective-permute-start.14
  142.8 1.1 slice.93
  144.5 2.4 %fusion.121 = f32[256,1536]{1,0:T(8,128)S(1)} fusion(bf16[512,1536]{1,0:T(8,128)(2,1)} %collective-permute-done.8, s32[]{:T(128)S(6)} %select_n.250, bf16[256,2048]{0,1:T(8,128)(2,1)S(1)} %get-tuple-element.18, bf16[256,2048]{0,1:T(8,128)(2,1)S(1)} %get-tuple-element.17), kind=kOutput, calls=%fused_computation.210 | convolution fusion | flops 403177472 | bytes 5242884 | tf_op jit(solution)/shard_map/dot_general | solution.py:135
  146.9 12.3 %collective-permute-done.9 = bf16[512,1536]{1,0:T(8,128)(2,1)S(1)} collective-permute-done((bf16[512,1536]{1,0:T(8,128)(2,1)}, bf16[512,1536]{1,0:T(8,128)(2,1)S(1)}, u32[]{:S(2)}, u32[]{:S(2)}) %collective-permute-start.9) | collective-permute-done | bytes 1572896 | tf_op jit(solution)/shard_map/ppermute | solution.py:120
  159.5 2.4 %fusion.13 = f32[256,1536]{1,0:T(8,128)S(1)} fusion(f32[256,1536]{1,0:T(8,128)S(1)} %fusion.121, f32[256,1536]{1,0:T(8,128)S(1)} %fusion.14, bf16[512,1536]{1,0:T(8,128)(2,1)} %collective-permute-done.7, s32[]{:T(128)S(6)} %select_n.247, bf16[256,2048]{0,1:T(8,128)(2,1)S(1)} %get-tuple-element.18, bf16[256,2048]{0,1:T(8,128)(2,1)S(1)} %get-tuple-element.17), kind=kOutput, calls=%fused_computation.40 | convolution fusion | flops 403963904 | bytes 8388612 | tf_op jit(solution)/shard_map/dot_general | solution.py:135
  162.6 1.8 collective-permute-done.15
  165.2 1.6 collective-permute-start.16
  166.8 3.8 %collective-permute-done.10 = bf16[512,1536]{1,0:T(8,128)(2,1)S(1)} collective-permute-done((bf16[512,1536]{1,0:T(8,128)(2,1)}, bf16[512,1536]{1,0:T(8,128)(2,1)S(1)}, u32[]{:S(2)}, u32[]{:S(2)}) %collective-permute-start.10) | collective-permute-done | bytes 1572896 | tf_op jit(solution)/shard_map/ppermute | solution.py:124
  170.7 1.6 collective-permute-start.17
  174.3 5.8 %collective-permute-done.16 = bf16[512,512]{1,0:T(8,128)(2,1)S(1)} collective-permute-done((bf16[512,512]{1,0:T(8,128)(2,1)S(1)}, bf16[512,512]{1,0:T(8,128)(2,1)S(1)}, u32[]{:S(2)}, u32[]{:S(2)}) %collective-permute-start.16) | collective-permute-done | bytes 524320 | tf_op jit(solution)/shard_map/ppermute | solution.py:121
  180.8 14.5 %collective-permute-done.11 = bf16[512,1536]{1,0:T(8,128)(2,1)S(1)} collective-permute-done((bf16[512,1536]{1,0:T(8,128)(2,1)S(1)}, bf16[512,1536]{1,0:T(8,128)(2,1)S(1)}, u32[]{:S(2)}, u32[]{:S(2)}) %collective-permute-start.11) | collective-permute-done | bytes 1572896 | tf_op jit(solution)/shard_map/ppermute | solution.py:120
  195.4 1.6 collective-permute-start.18
  198.8 9.2 %collective-permute-done.18 = bf16[512,512]{1,0:T(8,128)(2,1)S(1)} collective-permute-done((bf16[512,512]{1,0:T(8,128)(2,1)S(1)}, bf16[512,512]{1,0:T(8,128)(2,1)S(1)}, u32[]{:S(2)}, u32[]{:S(2)}) %collective-permute-start.18) | collective-permute-done | bytes 524320 | tf_op jit(solution)/shard_map/ppermute | solution.py:121
  208.7 2.0 select_convert_fusion.1
  210.7 1.1 pad_maximum_fusion.1
  (67 shorter events, 25.8 us)
Async XLA Ops:
  3.0 48.6 %collective-permute-start.2 = (bf16[256,1024]{0,1:T(8,128)(2,1)}, bf16[256,1024]{0,1:T(8,128)(2,1)}, u32[]{:S(2)}, u32[]{:S(2)}) collective-permute-start(bf16[256,1024]{0,1:T(8,128)(2,1)} %pad_maximum_fusion.2), channel_id=1, source_target_pairs={{0,6},{2,8},{4,10},{6,12},{8,14},{1,7},{3,9},{5,11},{7,13},{9,15},... | collective-permute-start | bytes 1572872 | tf_op jit(solution)/shard_map/ppermute | solution.py:15
  9.7 44.0 %collective-permute-start.1 = (bf16[256,1024]{0,1:T(8,128)(2,1)}, bf16[256,1024]{0,1:T(8,128)(2,1)}, u32[]{:S(2)}, u32[]{:S(2)}) collective-permute-start(bf16[256,1024]{0,1:T(8,128)(2,1)} %pad_maximum_fusion.2), channel_id=1, source_target_pairs={{0,4},{2,6},{4,8},{6,10},{8,12},{10,14},{1,5},{3,7},{5,9},{7,11},{... | collective-permute-start | bytes 1572872 | tf_op jit(solution)/shard_map/ppermute | solution.py:15
  14.0 41.8 %collective-permute-start = (bf16[256,1024]{0,1:T(8,128)(2,1)}, bf16[256,1024]{0,1:T(8,128)(2,1)}, u32[]{:S(2)}, u32[]{:S(2)}) collective-permute-start(bf16[256,1024]{0,1:T(8,128)(2,1)} %pad_maximum_fusion.2), channel_id=1, source_target_pairs={{0,2},{2,4},{4,6},{6,8},{8,10},{10,12},{12,14},{1,3},{3,5},{5,7},{... | collective-permute-start | bytes 1572872 | tf_op jit(solution)/shard_map/ppermute | solution.py:15
  17.5 20.9 %collective-permute-start.3 = (bf16[128,1024]{0,1:T(8,128)(2,1)S(1)}, bf16[128,1024]{0,1:T(8,128)(2,1)}, u32[]{:S(2)}, u32[]{:S(2)}) collective-permute-start(bf16[128,1024]{0,1:T(8,128)(2,1)S(1)} %fusion.83), channel_id=1, source_target_pairs={{0,8},{2,10},{4,12},{6,14},{1,9},{3,11},{5,13},{7,15},{16,24},{18,... | collective-permute-start | bytes 786440 | tf_op jit(solution)/shard_map/ppermute | solution.py:15
  20.8 2.5 %copy-start = (bf16[256,512]{1,0:T(8,128)(2,1)S(1)}, bf16[256,512]{1,0:T(8,128)(2,1)}, u32[]{:S(2)}) copy-start(bf16[256,512]{1,0:T(8,128)(2,1)} %param.8) | copy-start | bytes 786436
  23.2 2.0 copy-start.2
  23.2 47.8 %collective-permute-start.5 = (bf16[512,1536]{1,0:T(8,128)(2,1)}, bf16[512,1536]{1,0:T(8,128)(2,1)}, u32[]{:S(2)}, u32[]{:S(2)}) collective-permute-start(bf16[512,1536]{1,0:T(8,128)(2,1)} %pad_maximum_fusion), channel_id=1, source_target_pairs={{0,4},{4,8},{8,12},{12,14},{14,10},{10,6},{6,2},{2,0},{1,5},{5,9},... | collective-permute-start | bytes 4718600 | tf_op jit(solution)/shard_map/ppermute | solution.py:120
  38.3 44.8 %collective-permute-start.6 = (bf16[512,1536]{1,0:T(8,128)(2,1)}, bf16[512,1536]{1,0:T(8,128)(2,1)}, u32[]{:S(2)}, u32[]{:S(2)}) collective-permute-start(bf16[512,1536]{1,0:T(8,128)(2,1)} %pad_maximum_fusion), channel_id=1, source_target_pairs={{0,2},{4,0},{8,4},{12,8},{14,12},{10,14},{6,10},{2,6},{1,3},{5,1},... | collective-permute-start | bytes 4718600 | tf_op jit(solution)/shard_map/ppermute | solution.py:124
  67.8 34.7 %copy-start.3 = (s32[8]{0:T(128)S(1)}, s32[8]{0:T(128)}, u32[]{:S(2)}) copy-start(s32[8]{0:T(128)} %constant.185.clone) | copy-start | bytes 100
  67.8 39.9 %copy-start.1 = (s32[8]{0:T(128)S(1)}, s32[8]{0:T(128)}, u32[]{:S(2)}) copy-start(s32[8]{0:T(128)} %constant.186.clone) | copy-start | bytes 100
  69.1 43.9 %collective-permute-start.4 = (bf16[256,2048]{0,1:T(8,128)(2,1)S(1)}, bf16[256,2048]{0,1:T(8,128)(2,1)}, u32[]{:S(2)}, u32[]{:S(2)}) collective-permute-start(bf16[256,2048]{0,1:T(8,128)(2,1)S(1)} %bitcast.268), channel_id=1, source_target_pairs={{0,1},{1,0},{2,3},{3,2},{4,5},{5,4},{6,7},{7,6},{8,9},{9,8},{10,11... | collective-permute-start | bytes 3145736 | tf_op jit(solution)/shard_map/ppermute | solution.py:77
  71.0 51.8 %collective-permute-start.7 = (bf16[512,1536]{1,0:T(8,128)(2,1)}, bf16[512,1536]{1,0:T(8,128)(2,1)}, u32[]{:S(2)}, u32[]{:S(2)}) collective-permute-start(bf16[512,1536]{1,0:T(8,128)(2,1)} %collective-permute-done.5), channel_id=1, source_target_pairs={{0,4},{4,8},{8,12},{12,14},{14,10},{10,6},{6,2},{2,0},{1,5},{5,9},... | collective-permute-start | bytes 4718600 | tf_op jit(solution)/shard_map/ppermute | solution.py:120
  83.1 52.6 %collective-permute-start.8 = (bf16[512,1536]{1,0:T(8,128)(2,1)}, bf16[512,1536]{1,0:T(8,128)(2,1)}, u32[]{:S(2)}, u32[]{:S(2)}) collective-permute-start(bf16[512,1536]{1,0:T(8,128)(2,1)} %collective-permute-done.6), channel_id=1, source_target_pairs={{0,2},{4,0},{8,4},{12,8},{14,12},{10,14},{6,10},{2,6},{1,3},{5,1},... | collective-permute-start | bytes 4718600 | tf_op jit(solution)/shard_map/ppermute | solution.py:124
  115.4 22.8 %collective-permute-start.12 = (bf16[512,512]{1,0:T(8,128)(2,1)S(1)}, bf16[512,512]{1,0:T(8,128)(2,1)S(1)}, u32[]{:S(2)}, u32[]{:S(2)}) collective-permute-start(bf16[512,512]{1,0:T(8,128)(2,1)S(1)} %slice.90), channel_id=1, source_target_pairs={{0,16},{16,0},{1,17},{17,1},{2,18},{18,2},{3,19},{19,3},{4,20},{20... | collective-permute-start | bytes 1572872 | tf_op jit(solution)/shard_map/ppermute | solution.py:121
  118.1 21.3 %collective-permute-start.13 = (bf16[512,512]{1,0:T(8,128)(2,1)S(1)}, bf16[512,512]{1,0:T(8,128)(2,1)S(1)}, u32[]{:S(2)}, u32[]{:S(2)}) collective-permute-start(bf16[512,512]{1,0:T(8,128)(2,1)S(1)} %slice.91), channel_id=1, source_target_pairs={{0,16},{16,0},{1,17},{17,1},{2,18},{18,2},{3,19},{19,3},{4,20},{20... | collective-permute-start | bytes 1572872 | tf_op jit(solution)/shard_map/ppermute | solution.py:125
  122.8 36.4 %collective-permute-start.9 = (bf16[512,1536]{1,0:T(8,128)(2,1)}, bf16[512,1536]{1,0:T(8,128)(2,1)S(1)}, u32[]{:S(2)}, u32[]{:S(2)}) collective-permute-start(bf16[512,1536]{1,0:T(8,128)(2,1)} %collective-permute-done.7), channel_id=1, source_target_pairs={{0,4},{4,8},{8,12},{12,14},{14,10},{10,6},{6,2},{2,0},{1,5},{5,9},... | collective-permute-start | bytes 4718600 | tf_op jit(solution)/shard_map/ppermute | solution.py:120
  135.7 34.9 %collective-permute-start.10 = (bf16[512,1536]{1,0:T(8,128)(2,1)}, bf16[512,1536]{1,0:T(8,128)(2,1)S(1)}, u32[]{:S(2)}, u32[]{:S(2)}) collective-permute-start(bf16[512,1536]{1,0:T(8,128)(2,1)} %collective-permute-done.8), channel_id=1, source_target_pairs={{0,2},{4,0},{8,4},{12,8},{14,12},{10,14},{6,10},{2,6},{1,3},{5,1},... | collective-permute-start | bytes 4718600 | tf_op jit(solution)/shard_map/ppermute | solution.py:124
  141.2 20.6 %collective-permute-start.14 = (bf16[512,512]{1,0:T(8,128)(2,1)S(1)}, bf16[512,512]{1,0:T(8,128)(2,1)S(1)}, u32[]{:S(2)}, u32[]{:S(2)}) collective-permute-start(bf16[512,512]{1,0:T(8,128)(2,1)S(1)} %slice.92), channel_id=1, source_target_pairs={{0,16},{16,0},{1,17},{17,1},{2,18},{18,2},{3,19},{19,3},{4,20},{20... | collective-permute-start | bytes 1572872 | tf_op jit(solution)/shard_map/ppermute | solution.py:121
  143.9 20.5 %collective-permute-start.15 = (bf16[512,512]{1,0:T(8,128)(2,1)S(1)}, bf16[512,512]{1,0:T(8,128)(2,1)S(1)}, u32[]{:S(2)}, u32[]{:S(2)}) collective-permute-start(bf16[512,512]{1,0:T(8,128)(2,1)S(1)} %slice.93), channel_id=1, source_target_pairs={{0,16},{16,0},{1,17},{17,1},{2,18},{18,2},{3,19},{19,3},{4,20},{20... | collective-permute-start | bytes 1572872 | tf_op jit(solution)/shard_map/ppermute | solution.py:125
  159.2 36.1 %collective-permute-start.11 = (bf16[512,1536]{1,0:T(8,128)(2,1)S(1)}, bf16[512,1536]{1,0:T(8,128)(2,1)S(1)}, u32[]{:S(2)}, u32[]{:S(2)}) collective-permute-start(bf16[512,1536]{1,0:T(8,128)(2,1)S(1)} %collective-permute-done.9), channel_id=1, source_target_pairs={{0,4},{4,8},{8,12},{12,14},{14,10},{10,6},{6,2},{2,0},{1,5},{5,9},... | collective-permute-start | bytes 4718600 | tf_op jit(solution)/shard_map/ppermute | solution.py:120
  165.2 14.9 %collective-permute-start.16 = (bf16[512,512]{1,0:T(8,128)(2,1)S(1)}, bf16[512,512]{1,0:T(8,128)(2,1)S(1)}, u32[]{:S(2)}, u32[]{:S(2)}) collective-permute-start(bf16[512,512]{1,0:T(8,128)(2,1)S(1)} %slice.94), channel_id=1, source_target_pairs={{0,16},{16,0},{1,17},{17,1},{2,18},{18,2},{3,19},{19,3},{4,20},{20... | collective-permute-start | bytes 1572872 | tf_op jit(solution)/shard_map/ppermute | solution.py:121
  170.7 26.3 %collective-permute-start.17 = (bf16[512,512]{1,0:T(8,128)(2,1)S(1)}, bf16[512,512]{1,0:T(8,128)(2,1)S(1)}, u32[]{:S(2)}, u32[]{:S(2)}) collective-permute-start(bf16[512,512]{1,0:T(8,128)(2,1)S(1)} %slice.95), channel_id=1, source_target_pairs={{0,16},{16,0},{1,17},{17,1},{2,18},{18,2},{3,19},{19,3},{4,20},{20... | collective-permute-start | bytes 1572872 | tf_op jit(solution)/shard_map/ppermute | solution.py:125
  195.4 12.6 %collective-permute-start.18 = (bf16[512,512]{1,0:T(8,128)(2,1)S(1)}, bf16[512,512]{1,0:T(8,128)(2,1)S(1)}, u32[]{:S(2)}, u32[]{:S(2)}) collective-permute-start(bf16[512,512]{1,0:T(8,128)(2,1)S(1)} %slice.96), channel_id=1, source_target_pairs={{0,16},{16,0},{1,17},{17,1},{2,18},{18,2},{3,19},{19,3},{4,20},{20... | collective-permute-start | bytes 1572872 | tf_op jit(solution)/shard_map/ppermute | solution.py:121

commit v13 on v12

--- a/solution.py
+++ b/solution.py
@@ -97,7 +97,7 @@
     columns = out_weight.shape[1]
     groups = lax.axis_size("group")
     group_index = lax.axis_index("group")
-    own = (columns // 4) // 128 * 128 if groups == 2 else 0
+    own = (columns // 3) // 128 * 128 if groups == 2 else 0
     shared = columns - groups * own if own else columns
     swap = [(0, 1), (1, 0)]
 

time: 213 us -> 216 us (1.014)
  waiting for transfers between devices: 77.4 us -> 93 us
  starting transfers between devices: 66.5 us -> 57.3 us
    ppermute x3, waiting for transfers between devices: 2.22 us -> 22.4 us  [ring_transfer(): crossed = lax.ppermute(backward[:, shared:], 'group', swap) if own else None]
    ppermute x3, starting transfers between devices: 33.4 us -> 26.2 us  [ring_transfer(): backward = lax.ppermute(backward, 'ctx', behind)]
    ppermute x4, waiting for transfers between devices: 32.9 us -> 40 us  [ring_transfer(): forward = lax.ppermute(forward, 'ctx', ahead)]
    ppermute x4, waiting for transfers between devices: 15 us -> 9.26 us  [ring_transfer(): crossed = lax.ppermute(forward[:, shared:], 'group', swap) if own else None]
    ppermute x3, waiting for transfers between devices: 15.8 us -> 10.2 us  [ring_transfer(): backward = lax.ppermute(backward, 'ctx', behind)]
  transfers between devices with their start and end apart: 19 -> 19, of which waited for: 12 -> 9; matrix products, arithmetic and copies ran while one was open for 24% -> 23% of each run, Pallas kernels for 0% -> 0%
where the time goes in v13:
time: 216 us
  waiting for transfers between devices  93 us (43%)
  starting transfers between devices  57.3 us (27%)
  matrix products  30.7 us (14%)
  local copies, waits for them, and re-layouts  15.6 us (7%)
  between operations  9.59 us (4%)
  other arithmetic  9.52 us (4%)
    ppermute x4, waiting for transfers between devices, ring_transfer(): forward = lax.ppermute(forward, 'ctx', ahead)  40 us
    ppermute x3, starting transfers between devices, ring_transfer(): backward = lax.ppermute(backward, 'ctx', behind)  26.2 us
    ppermute x3, waiting for transfers between devices, ring_transfer(): crossed = lax.ppermute(backward[:, shared:], 'group', swap) if own else None  22.4 us
    ppermute x4, starting transfers between devices, passed_along(): return lax.ppermute(array, axis, pairs)  16.4 us
    dot_general x8, matrix products, ring_project(): terms = [jnp.dot(piece, carried_block, preferred_element_type=jnp.float32)]  12.1 us
    ppermute x4, waiting for transfers between devices, passed_along(): return lax.ppermute(array, axis, pairs)  11.1 us
    ppermute x3, waiting for transfers between devices, ring_transfer(): backward = lax.ppermute(backward, 'ctx', behind)  10.2 us
    ppermute x4, waiting for transfers between devices, ring_transfer(): crossed = lax.ppermute(forward[:, shared:], 'group', swap) if own else None  9.26 us
  transfers between devices with their start and end apart: 19, of which 9 were waited for; matrix products, arithmetic and copies ran while one was open for 23% of the time, Pallas kernels for 0%

profile of v13, /device:TPU:0, one launch (start us, length us, event | category | flops | bytes accessed | tf_op | source)
XLA Modules:
  0.0 215.7 jit_solution(14855695510687581307)
XLA Ops:
  0.0 1.1 copy.77
  1.1 1.1 copy.46
  3.0 6.7 %collective-permute-start.2 = (bf16[256,1024]{0,1:T(8,128)(2,1)}, bf16[256,1024]{0,1:T(8,128)(2,1)}, u32[]{:S(2)}, u32[]{:S(2)}) collective-permute-start(bf16[256,1024]{0,1:T(8,128)(2,1)} %pad_maximum_fusion.2), channel_id=1, source_target_pairs={{0,6},{2,8},{4,10},{6,12},{8,14},{1,7},{3,9},{5,11},{7,13},{9,15},... | collective-permute-start | bytes 1572872 | tf_op jit(solution)/shard_map/ppermute | solution.py:15
  9.7 4.3 %collective-permute-start.1 = (bf16[256,1024]{0,1:T(8,128)(2,1)}, bf16[256,1024]{0,1:T(8,128)(2,1)}, u32[]{:S(2)}, u32[]{:S(2)}) collective-permute-start(bf16[256,1024]{0,1:T(8,128)(2,1)} %pad_maximum_fusion.2), channel_id=1, source_target_pairs={{0,4},{2,6},{4,8},{6,10},{8,12},{10,14},{1,5},{3,7},{5,9},{7,11},{... | collective-permute-start | bytes 1572872 | tf_op jit(solution)/shard_map/ppermute | solution.py:15
  14.0 3.5 %collective-permute-start = (bf16[256,1024]{0,1:T(8,128)(2,1)}, bf16[256,1024]{0,1:T(8,128)(2,1)}, u32[]{:S(2)}, u32[]{:S(2)}) collective-permute-start(bf16[256,1024]{0,1:T(8,128)(2,1)} %pad_maximum_fusion.2), channel_id=1, source_target_pairs={{0,2},{2,4},{4,6},{6,8},{8,10},{10,12},{12,14},{1,3},{3,5},{5,7},{... | collective-permute-start | bytes 1572872 | tf_op jit(solution)/shard_map/ppermute | solution.py:15
  18.2 2.0 collective-permute-start.3
  20.2 1.2 slice.68
  21.4 1.2 constant_dynamic-slice_fusion
  22.6 1.2 pad_maximum_fusion
  23.9 1.8 reshape.293
  27.4 11.0 %collective-permute-done.3 = bf16[128,1024]{0,1:T(8,128)(2,1)} collective-permute-done((bf16[128,1024]{0,1:T(8,128)(2,1)}, bf16[128,1024]{0,1:T(8,128)(2,1)}, u32[]{:S(2)}, u32[]{:S(2)}) %collective-permute-start.3) | collective-permute-done | bytes 262176 | tf_op jit(solution)/shard_map/ppermute | solution.py:15
  38.4 11.7 %collective-permute-start.6 = (bf16[512,1408]{1,0:T(8,128)(2,1)}, bf16[512,1408]{1,0:T(8,128)(2,1)}, u32[]{:S(2)}, u32[]{:S(2)}) collective-permute-start(bf16[512,1408]{1,0:T(8,128)(2,1)} %pad_maximum_fusion), channel_id=1, source_target_pairs={{0,2},{4,0},{8,4},{12,8},{14,12},{10,14},{6,10},{2,6},{1,3},{5,1},... | collective-permute-start | bytes 4325384 | tf_op jit(solution)/shard_map/ppermute | solution.py:124
  51.7 1.1 fusion.142
  53.8 1.1 fusion.141
  55.9 1.1 fusion.140
  58.0 1.0 fusion.4
  59.0 1.2 fusion.21
  60.2 1.0 fusion.6
  61.2 1.2 fusion.19
  62.4 1.0 fusion.8
  63.5 1.2 fusion.17
  64.7 1.0 fusion.10
  65.7 1.4 fusion.15
  67.7 1.3 fusion.24
  69.1 6.3 %collective-permute-start.7 = (bf16[512,1408]{1,0:T(8,128)(2,1)}, bf16[512,1408]{1,0:T(8,128)(2,1)}, u32[]{:S(2)}, u32[]{:S(2)}) collective-permute-start(bf16[512,1408]{1,0:T(8,128)(2,1)} %collective-permute-done.5), channel_id=1, source_target_pairs={{0,4},{4,8},{8,12},{12,14},{14,10},{10,6},{6,2},{2,0},{1,5},{5,9},... | collective-permute-start | bytes 4325384 | tf_op jit(solution)/shard_map/ppermute | solution.py:120
  85.8 1.1 slice.90
  87.0 1.6 collective-permute-start.12
  88.6 1.1 slice.91
  90.3 12.1 %collective-permute-start.8 = (bf16[512,1408]{1,0:T(8,128)(2,1)}, bf16[512,1408]{1,0:T(8,128)(2,1)S(1)}, u32[]{:S(2)}, u32[]{:S(2)}) collective-permute-start(bf16[512,1408]{1,0:T(8,128)(2,1)} %collective-permute-done.6), channel_id=1, source_target_pairs={{0,2},{4,0},{8,4},{12,8},{14,12},{10,14},{6,10},{2,6},{1,3},{5,1},... | collective-permute-start | bytes 4325384 | tf_op jit(solution)/shard_map/ppermute | solution.py:124
  102.7 2.4 %fusion.132 = f32[256,1408]{1,0:T(8,128)S(1)} fusion(bf16[512,1408]{1,0:T(8,128)(2,1)} %collective-permute-done.5, s32[]{:T(128)S(6)} %select_n.241, bf16[256,2048]{0,1:T(8,128)(2,1)S(1)} %get-tuple-element.18, bf16[256,2048]{0,1:T(8,128)(2,1)S(1)} %get-tuple-element.17), kind=kOutput, calls=%fused_computation.215 | convolution fusion | flops 369623040 | bytes 4980740 | tf_op jit(solution)/shard_map/dot_general | solution.py:135
  105.0 14.9 %collective-permute-done.7 = bf16[512,1408]{1,0:T(8,128)(2,1)} collective-permute-done((bf16[512,1408]{1,0:T(8,128)(2,1)}, bf16[512,1408]{1,0:T(8,128)(2,1)}, u32[]{:S(2)}, u32[]{:S(2)}) %collective-permute-start.7) | collective-permute-done | bytes 1441824 | tf_op jit(solution)/shard_map/ppermute | solution.py:120
  119.9 2.3 %fusion.128 = f32[256,1408]{1,0:T(8,128)S(1)} fusion(bf16[512,1408]{1,0:T(8,128)(2,1)} %collective-permute-done.6, s32[]{:T(128)S(6)} %select_n.244, bf16[256,2048]{0,1:T(8,128)(2,1)S(1)} %get-tuple-element.18, bf16[256,2048]{0,1:T(8,128)(2,1)S(1)} %get-tuple-element.17), kind=kOutput, calls=%fused_computation.213 | convolution fusion | flops 369623040 | bytes 4980740 | tf_op jit(solution)/shard_map/dot_general | solution.py:135
  122.3 1.0 fusion.14
  123.3 10.2 %collective-permute-done.8 = bf16[512,1408]{1,0:T(8,128)(2,1)S(1)} collective-permute-done((bf16[512,1408]{1,0:T(8,128)(2,1)}, bf16[512,1408]{1,0:T(8,128)(2,1)S(1)}, u32[]{:S(2)}, u32[]{:S(2)}) %collective-permute-start.8) | collective-permute-done | bytes 1441824 | tf_op jit(solution)/shard_map/ppermute | solution.py:124
  133.5 2.4 %collective-permute-start.10 = (bf16[512,1408]{1,0:T(8,128)(2,1)S(1)}, bf16[512,1408]{1,0:T(8,128)(2,1)S(1)}, u32[]{:S(2)}, u32[]{:S(2)}) collective-permute-start(bf16[512,1408]{1,0:T(8,128)(2,1)S(1)} %collective-permute-done.8), channel_id=1, source_target_pairs={{0,2},{4,0},{8,4},{12,8},{14,12},{10,14},{6,10},{2,6},{1,3},{5,1},... | collective-permute-start | bytes 4325384 | tf_op jit(solution)/shard_map/ppermute | solution.py:124
  137.6 1.1 slice.92
  138.7 1.6 collective-permute-start.14
  141.9 11.6 %collective-permute-done.9 = bf16[512,1408]{1,0:T(8,128)(2,1)S(1)} collective-permute-done((bf16[512,1408]{1,0:T(8,128)(2,1)}, bf16[512,1408]{1,0:T(8,128)(2,1)S(1)}, u32[]{:S(2)}, u32[]{:S(2)}) %collective-permute-start.9) | collective-permute-done | bytes 1441824 | tf_op jit(solution)/shard_map/ppermute | solution.py:120
  153.8 2.3 %fusion.13 = f32[256,1408]{1,0:T(8,128)S(1)} fusion(f32[256,1408]{1,0:T(8,128)S(1)} %fusion.121, f32[256,1408]{1,0:T(8,128)S(1)} %fusion.14, bf16[512,1408]{1,0:T(8,128)(2,1)} %collective-permute-done.7, s32[]{:T(128)S(6)} %select_n.247, bf16[256,2048]{0,1:T(8,128)(2,1)S(1)} %get-tuple-element.18, bf16[256,2048]{0,1:T(8,128)(2,1)S(1)} %get-tuple-element.17), kind=kOutput, calls=%fused_computation.40 | convolution fusion | flops 370343936 | bytes 7864324 | tf_op jit(solution)/shard_map/dot_general | solution.py:135
  157.2 10.9 %collective-permute-done.15 = bf16[512,640]{1,0:T(8,128)(2,1)S(1)} collective-permute-done((bf16[512,640]{1,0:T(8,128)(2,1)S(1)}, bf16[512,640]{1,0:T(8,128)(2,1)S(1)}, u32[]{:S(2)}, u32[]{:S(2)}) %collective-permute-start.15) | collective-permute-done | bytes 655392 | tf_op jit(solution)/shard_map/ppermute | solution.py:125
  169.0 1.7 collective-permute-start.16
  172.2 1.0 fusion.12
  173.2 13.5 %collective-permute-done.11 = bf16[512,1408]{1,0:T(8,128)(2,1)S(1)} collective-permute-done((bf16[512,1408]{1,0:T(8,128)(2,1)S(1)}, bf16[512,1408]{1,0:T(8,128)(2,1)S(1)}, u32[]{:S(2)}, u32[]{:S(2)}) %collective-permute-start.11) | collective-permute-done | bytes 1441824 | tf_op jit(solution)/shard_map/ppermute | solution.py:120
  186.8 1.6 collective-permute-start.18
  189.2 11.5 %collective-permute-done.17 = bf16[512,640]{1,0:T(8,128)(2,1)S(1)} collective-permute-done((bf16[512,640]{1,0:T(8,128)(2,1)S(1)}, bf16[512,640]{1,0:T(8,128)(2,1)S(1)}, u32[]{:S(2)}, u32[]{:S(2)}) %collective-permute-start.17) | collective-permute-done | bytes 655392 | tf_op jit(solution)/shard_map/ppermute | solution.py:125
  202.6 9.0 %collective-permute-done.18 = bf16[512,640]{1,0:T(8,128)(2,1)S(1)} collective-permute-done((bf16[512,640]{1,0:T(8,128)(2,1)S(1)}, bf16[512,640]{1,0:T(8,128)(2,1)S(1)}, u32[]{:S(2)}, u32[]{:S(2)}) %collective-permute-start.18) | collective-permute-done | bytes 655392 | tf_op jit(solution)/shard_map/ppermute | solution.py:121
  212.4 2.2 %select_convert_fusion.1 = (bf16[256,640]{1,0:T(8,128)(2,1)S(1)}, bf16[256,640]{1,0:T(8,128)(2,1)S(1)}) fusion(bf16[256,1408]{1,0:T(8,128)(2,1)S(1)} %convolution_add_fusion, pred[]{:T(512)S(6)} %eq.180, f32[256,640]{1,0:T(8,128)S(1)} %fusion.135, f32[256,640]{1,0:T(8,128)S(1)} %fusion.112, f32[256,640]{1,0:T(8,128)S(1)} %fusion.116, ...), kind=kOutput, calls=%fused_computation.101 | convolution fusion | flops 169934848 | bytes 8323081 | tf_op jit(solution)/shard_map/dot_general | solution.py:137
  214.6 1.1 pad_maximum_fusion.1
  (67 shorter events, 21.2 us)
Async XLA Ops:
  3.0 48.7 %collective-permute-start.2 = (bf16[256,1024]{0,1:T(8,128)(2,1)}, bf16[256,1024]{0,1:T(8,128)(2,1)}, u32[]{:S(2)}, u32[]{:S(2)}) collective-permute-start(bf16[256,1024]{0,1:T(8,128)(2,1)} %pad_maximum_fusion.2), channel_id=1, source_target_pairs={{0,6},{2,8},{4,10},{6,12},{8,14},{1,7},{3,9},{5,11},{7,13},{9,15},... | collective-permute-start | bytes 1572872 | tf_op jit(solution)/shard_map/ppermute | solution.py:15
  9.7 44.1 %collective-permute-start.1 = (bf16[256,1024]{0,1:T(8,128)(2,1)}, bf16[256,1024]{0,1:T(8,128)(2,1)}, u32[]{:S(2)}, u32[]{:S(2)}) collective-permute-start(bf16[256,1024]{0,1:T(8,128)(2,1)} %pad_maximum_fusion.2), channel_id=1, source_target_pairs={{0,4},{2,6},{4,8},{6,10},{8,12},{10,14},{1,5},{3,7},{5,9},{7,11},{... | collective-permute-start | bytes 1572872 | tf_op jit(solution)/shard_map/ppermute | solution.py:15
  14.0 41.9 %collective-permute-start = (bf16[256,1024]{0,1:T(8,128)(2,1)}, bf16[256,1024]{0,1:T(8,128)(2,1)}, u32[]{:S(2)}, u32[]{:S(2)}) collective-permute-start(bf16[256,1024]{0,1:T(8,128)(2,1)} %pad_maximum_fusion.2), channel_id=1, source_target_pairs={{0,2},{2,4},{4,6},{6,8},{8,10},{10,12},{12,14},{1,3},{3,5},{5,7},{... | collective-permute-start | bytes 1572872 | tf_op jit(solution)/shard_map/ppermute | solution.py:15
  18.2 20.3 %collective-permute-start.3 = (bf16[128,1024]{0,1:T(8,128)(2,1)}, bf16[128,1024]{0,1:T(8,128)(2,1)}, u32[]{:S(2)}, u32[]{:S(2)}) collective-permute-start(bf16[128,1024]{0,1:T(8,128)(2,1)} %fusion.83), channel_id=1, source_target_pairs={{0,8},{2,10},{4,12},{6,14},{1,9},{3,11},{5,13},{7,15},{16,24},{18,... | collective-permute-start | bytes 786440 | tf_op jit(solution)/shard_map/ppermute | solution.py:15
  21.3 2.5 %copy-start = (bf16[256,512]{1,0:T(8,128)(2,1)S(1)}, bf16[256,512]{1,0:T(8,128)(2,1)}, u32[]{:S(2)}) copy-start(bf16[256,512]{1,0:T(8,128)(2,1)} %param.8) | copy-start | bytes 786436
  22.6 3.2 %copy-start.2 = (s32[16]{0:T(128)S(1)}, s32[16]{0:T(128)}, u32[]{:S(2)}) copy-start(s32[16]{0:T(128)} %param.10) | copy-start | bytes 196
  23.8 45.3 %collective-permute-start.5 = (bf16[512,1408]{1,0:T(8,128)(2,1)}, bf16[512,1408]{1,0:T(8,128)(2,1)}, u32[]{:S(2)}, u32[]{:S(2)}) collective-permute-start(bf16[512,1408]{1,0:T(8,128)(2,1)} %pad_maximum_fusion), channel_id=1, source_target_pairs={{0,4},{4,8},{8,12},{12,14},{14,10},{10,6},{6,2},{2,0},{1,5},{5,9},... | collective-permute-start | bytes 4325384 | tf_op jit(solution)/shard_map/ppermute | solution.py:120
  38.4 50.1 %collective-permute-start.6 = (bf16[512,1408]{1,0:T(8,128)(2,1)}, bf16[512,1408]{1,0:T(8,128)(2,1)}, u32[]{:S(2)}, u32[]{:S(2)}) collective-permute-start(bf16[512,1408]{1,0:T(8,128)(2,1)} %pad_maximum_fusion), channel_id=1, source_target_pairs={{0,2},{4,0},{8,4},{12,8},{14,12},{10,14},{6,10},{2,6},{1,3},{5,1},... | collective-permute-start | bytes 4325384 | tf_op jit(solution)/shard_map/ppermute | solution.py:124
  67.7 7.7 %copy-start.3 = (s32[8]{0:T(128)S(1)}, s32[8]{0:T(128)}, u32[]{:S(2)}) copy-start(s32[8]{0:T(128)} %constant.187.clone) | copy-start | bytes 100
  67.7 13.0 %copy-start.1 = (s32[8]{0:T(128)S(1)}, s32[8]{0:T(128)}, u32[]{:S(2)}) copy-start(s32[8]{0:T(128)} %constant.188.clone) | copy-start | bytes 100
  69.0 33.4 %collective-permute-start.4 = (bf16[256,2048]{0,1:T(8,128)(2,1)S(1)}, bf16[256,2048]{0,1:T(8,128)(2,1)S(1)}, u32[]{:S(2)}, u32[]{:S(2)}) collective-permute-start(bf16[256,2048]{0,1:T(8,128)(2,1)S(1)} %bitcast.268), channel_id=1, source_target_pairs={{0,1},{1,0},{2,3},{3,2},{4,5},{5,4},{6,7},{7,6},{8,9},{9,8},{10,11... | collective-permute-start | bytes 3145736 | tf_op jit(solution)/shard_map/ppermute | solution.py:77
  69.1 50.8 %collective-permute-start.7 = (bf16[512,1408]{1,0:T(8,128)(2,1)}, bf16[512,1408]{1,0:T(8,128)(2,1)}, u32[]{:S(2)}, u32[]{:S(2)}) collective-permute-start(bf16[512,1408]{1,0:T(8,128)(2,1)} %collective-permute-done.5), channel_id=1, source_target_pairs={{0,4},{4,8},{8,12},{12,14},{14,10},{10,6},{6,2},{2,0},{1,5},{5,9},... | collective-permute-start | bytes 4325384 | tf_op jit(solution)/shard_map/ppermute | solution.py:120
  87.0 48.9 %collective-permute-start.12 = (bf16[512,640]{1,0:T(8,128)(2,1)S(1)}, bf16[512,640]{1,0:T(8,128)(2,1)S(1)}, u32[]{:S(2)}, u32[]{:S(2)}) collective-permute-start(bf16[512,640]{1,0:T(8,128)(2,1)S(1)} %slice.90), channel_id=1, source_target_pairs={{0,16},{16,0},{1,17},{17,1},{2,18},{18,2},{3,19},{19,3},{4,20},{20... | collective-permute-start | bytes 1966088 | tf_op jit(solution)/shard_map/ppermute | solution.py:121
  89.7 47.0 %collective-permute-start.13 = (bf16[512,640]{1,0:T(8,128)(2,1)S(1)}, bf16[512,640]{1,0:T(8,128)(2,1)S(1)}, u32[]{:S(2)}, u32[]{:S(2)}) collective-permute-start(bf16[512,640]{1,0:T(8,128)(2,1)S(1)} %slice.91), channel_id=1, source_target_pairs={{0,16},{16,0},{1,17},{17,1},{2,18},{18,2},{3,19},{19,3},{4,20},{20... | collective-permute-start | bytes 1966088 | tf_op jit(solution)/shard_map/ppermute | solution.py:125
  90.3 43.2 %collective-permute-start.8 = (bf16[512,1408]{1,0:T(8,128)(2,1)}, bf16[512,1408]{1,0:T(8,128)(2,1)S(1)}, u32[]{:S(2)}, u32[]{:S(2)}) collective-permute-start(bf16[512,1408]{1,0:T(8,128)(2,1)} %collective-permute-done.6), channel_id=1, source_target_pairs={{0,2},{4,0},{8,4},{12,8},{14,12},{10,14},{6,10},{2,6},{1,3},{5,1},... | collective-permute-start | bytes 4325384 | tf_op jit(solution)/shard_map/ppermute | solution.py:124
  119.9 33.6 %collective-permute-start.9 = (bf16[512,1408]{1,0:T(8,128)(2,1)}, bf16[512,1408]{1,0:T(8,128)(2,1)S(1)}, u32[]{:S(2)}, u32[]{:S(2)}) collective-permute-start(bf16[512,1408]{1,0:T(8,128)(2,1)} %collective-permute-done.7), channel_id=1, source_target_pairs={{0,4},{4,8},{8,12},{12,14},{14,10},{10,6},{6,2},{2,0},{1,5},{5,9},... | collective-permute-start | bytes 4325384 | tf_op jit(solution)/shard_map/ppermute | solution.py:120
  133.5 37.1 %collective-permute-start.10 = (bf16[512,1408]{1,0:T(8,128)(2,1)S(1)}, bf16[512,1408]{1,0:T(8,128)(2,1)S(1)}, u32[]{:S(2)}, u32[]{:S(2)}) collective-permute-start(bf16[512,1408]{1,0:T(8,128)(2,1)S(1)} %collective-permute-done.8), channel_id=1, source_target_pairs={{0,2},{4,0},{8,4},{12,8},{14,12},{10,14},{6,10},{2,6},{1,3},{5,1},... | collective-permute-start | bytes 4325384 | tf_op jit(solution)/shard_map/ppermute | solution.py:124
  138.7 17.7 %collective-permute-start.14 = (bf16[512,640]{1,0:T(8,128)(2,1)S(1)}, bf16[512,640]{1,0:T(8,128)(2,1)S(1)}, u32[]{:S(2)}, u32[]{:S(2)}) collective-permute-start(bf16[512,640]{1,0:T(8,128)(2,1)S(1)} %slice.92), channel_id=1, source_target_pairs={{0,16},{16,0},{1,17},{17,1},{2,18},{18,2},{3,19},{19,3},{4,20},{20... | collective-permute-start | bytes 1966088 | tf_op jit(solution)/shard_map/ppermute | solution.py:121
  140.4 27.7 %collective-permute-start.15 = (bf16[512,640]{1,0:T(8,128)(2,1)S(1)}, bf16[512,640]{1,0:T(8,128)(2,1)S(1)}, u32[]{:S(2)}, u32[]{:S(2)}) collective-permute-start(bf16[512,640]{1,0:T(8,128)(2,1)S(1)} %slice.93), channel_id=1, source_target_pairs={{0,16},{16,0},{1,17},{17,1},{2,18},{18,2},{3,19},{19,3},{4,20},{20... | collective-permute-start | bytes 1966088 | tf_op jit(solution)/shard_map/ppermute | solution.py:125
  153.5 33.2 %collective-permute-start.11 = (bf16[512,1408]{1,0:T(8,128)(2,1)S(1)}, bf16[512,1408]{1,0:T(8,128)(2,1)S(1)}, u32[]{:S(2)}, u32[]{:S(2)}) collective-permute-start(bf16[512,1408]{1,0:T(8,128)(2,1)S(1)} %collective-permute-done.9), channel_id=1, source_target_pairs={{0,4},{4,8},{8,12},{12,14},{14,10},{10,6},{6,2},{2,0},{1,5},{5,9},... | collective-permute-start | bytes 4325384 | tf_op jit(solution)/shard_map/ppermute | solution.py:120
  169.0 19.4 %collective-permute-start.16 = (bf16[512,640]{1,0:T(8,128)(2,1)S(1)}, bf16[512,640]{1,0:T(8,128)(2,1)S(1)}, u32[]{:S(2)}, u32[]{:S(2)}) collective-permute-start(bf16[512,640]{1,0:T(8,128)(2,1)S(1)} %slice.94), channel_id=1, source_target_pairs={{0,16},{16,0},{1,17},{17,1},{2,18},{18,2},{3,19},{19,3},{4,20},{20... | collective-permute-start | bytes 1966088 | tf_op jit(solution)/shard_map/ppermute | solution.py:121
  170.7 30.0 %collective-permute-start.17 = (bf16[512,640]{1,0:T(8,128)(2,1)S(1)}, bf16[512,640]{1,0:T(8,128)(2,1)S(1)}, u32[]{:S(2)}, u32[]{:S(2)}) collective-permute-start(bf16[512,640]{1,0:T(8,128)(2,1)S(1)} %slice.95), channel_id=1, source_target_pairs={{0,16},{16,0},{1,17},{17,1},{2,18},{18,2},{3,19},{19,3},{4,20},{20... | collective-permute-start | bytes 1966088 | tf_op jit(solution)/shard_map/ppermute | solution.py:125
  186.8 24.8 %collective-permute-start.18 = (bf16[512,640]{1,0:T(8,128)(2,1)S(1)}, bf16[512,640]{1,0:T(8,128)(2,1)S(1)}, u32[]{:S(2)}, u32[]{:S(2)}) collective-permute-start(bf16[512,640]{1,0:T(8,128)(2,1)S(1)} %slice.96), channel_id=1, source_target_pairs={{0,16},{16,0},{1,17},{17,1},{2,18},{18,2},{3,19},{19,3},{4,20},{20... | collective-permute-start | bytes 1966088 | tf_op jit(solution)/shard_map/ppermute | solution.py:121

commit v14 on v12

--- a/solution.py
+++ b/solution.py
@@ -175,6 +175,10 @@
         key_start = query_start - distance * tok_rows + skipped
         state_now = attend(state_now, prior_keys, prior_values, key_start)
     attended = finish(state_now, tok_rows, q_heads)
+    first = [index for index in (1, 2) if index < len(arrivals) and arrivals[index][2] is not None]
+    attended, crossed = lax.optimization_barrier((attended, [arrivals[i][2] for i in first]))
+    for index, value in zip(first, crossed):
+        arrivals[index] = (arrivals[index][0], arrivals[index][1], value)
     features = head_features(attended)
     mixed = ring_project(features, arrivals, shared, own, out_weight.shape[0])
     return mixed.astype(jnp.bfloat16)

time: 213 us -> 242 us (1.14)
  waiting for transfers between devices: 77.4 us -> 111 us
  starting transfers between devices: 66.5 us -> 62.1 us
    ppermute x4, waiting for transfers between devices: 32.9 us -> 61.9 us  [ring_transfer(): forward = lax.ppermute(forward, 'ctx', ahead)]
    ppermute x3, waiting for transfers between devices: 2.22 us -> 9.12 us  [ring_transfer(): crossed = lax.ppermute(backward[:, shared:], 'group', swap) if own else None]
    ppermute x3, starting transfers between devices: 33.4 us -> 27.4 us  [ring_transfer(): backward = lax.ppermute(backward, 'ctx', behind)]
    ppermute x3, waiting for transfers between devices: 15.8 us -> 9.79 us  [ring_transfer(): backward = lax.ppermute(backward, 'ctx', behind)]
    ppermute x4, waiting for transfers between devices: 15 us -> 18.2 us  [ring_transfer(): crossed = lax.ppermute(forward[:, shared:], 'group', swap) if own else None]
  transfers between devices with their start and end apart: 19 -> 19, of which waited for: 12 -> 10; matrix products, arithmetic and copies ran while one was open for 24% -> 21% of each run, Pallas kernels for 0% -> 0%
where the time goes in v14:
time: 242 us; the launch traced here: 241 us
  waiting for transfers between devices  111 us (46%)
  starting transfers between devices  62.1 us (26%)
  matrix products  31.8 us (13%)
  local copies, waits for them, and re-layouts  16.4 us (7%)
  other arithmetic  10.1 us (4%)
  between operations  9.94 us (4%)
    ppermute x4, waiting for transfers between devices, ring_transfer(): forward = lax.ppermute(forward, 'ctx', ahead)  61.9 us
    ppermute x3, starting transfers between devices, ring_transfer(): backward = lax.ppermute(backward, 'ctx', behind)  27.4 us
    ppermute x4, waiting for transfers between devices, ring_transfer(): crossed = lax.ppermute(forward[:, shared:], 'group', swap) if own else None  18.2 us
    ppermute x4, starting transfers between devices, passed_along(): return lax.ppermute(array, axis, pairs)  16.4 us
    dot_general x8, matrix products, ring_project(): terms = [jnp.dot(piece, carried_block, preferred_element_type=jnp.float32)]  13.7 us
    ppermute x4, waiting for transfers between devices, passed_along(): return lax.ppermute(array, axis, pairs)  11.6 us
    ppermute x3, waiting for transfers between devices, ring_transfer(): backward = lax.ppermute(backward, 'ctx', behind)  9.79 us
    ppermute x3, waiting for transfers between devices, ring_transfer(): crossed = lax.ppermute(backward[:, shared:], 'group', swap) if own else None  9.12 us
  transfers between devices with their start and end apart: 19, of which 10 were waited for; matrix products, arithmetic and copies ran while one was open for 21% of the time, Pallas kernels for 0%

profile of v14, /device:TPU:0, one launch (start us, length us, event | category | flops | bytes accessed | tf_op | source)
XLA Modules:
  0.0 241.0 jit_solution(6972398454443899113)
XLA Ops:
  0.0 1.1 copy.77
  1.1 1.1 copy.46
  3.0 6.7 %collective-permute-start.2 = (bf16[256,1024]{0,1:T(8,128)(2,1)}, bf16[256,1024]{0,1:T(8,128)(2,1)}, u32[]{:S(2)}, u32[]{:S(2)}) collective-permute-start(bf16[256,1024]{0,1:T(8,128)(2,1)} %pad_maximum_fusion.2), channel_id=1, source_target_pairs={{0,6},{2,8},{4,10},{6,12},{8,14},{1,7},{3,9},{5,11},{7,13},{9,15},... | collective-permute-start | bytes 1572872 | tf_op jit(solution)/shard_map/ppermute | solution.py:15
  9.7 4.3 %collective-permute-start.1 = (bf16[256,1024]{0,1:T(8,128)(2,1)}, bf16[256,1024]{0,1:T(8,128)(2,1)}, u32[]{:S(2)}, u32[]{:S(2)}) collective-permute-start(bf16[256,1024]{0,1:T(8,128)(2,1)} %pad_maximum_fusion.2), channel_id=1, source_target_pairs={{0,4},{2,6},{4,8},{6,10},{8,12},{10,14},{1,5},{3,7},{5,9},{7,11},{... | collective-permute-start | bytes 1572872 | tf_op jit(solution)/shard_map/ppermute | solution.py:15
  14.0 3.5 %collective-permute-start = (bf16[256,1024]{0,1:T(8,128)(2,1)}, bf16[256,1024]{0,1:T(8,128)(2,1)}, u32[]{:S(2)}, u32[]{:S(2)}) collective-permute-start(bf16[256,1024]{0,1:T(8,128)(2,1)} %pad_maximum_fusion.2), channel_id=1, source_target_pairs={{0,2},{2,4},{4,6},{6,8},{8,10},{10,12},{12,14},{1,3},{3,5},{5,7},{... | collective-permute-start | bytes 1572872 | tf_op jit(solution)/shard_map/ppermute | solution.py:15
  17.5 2.0 collective-permute-start.3
  19.5 1.3 slice.68
  20.8 1.1 constant_dynamic-slice_fusion
  21.9 1.2 pad_maximum_fusion
  23.3 1.8 reshape.293
  26.8 11.6 %collective-permute-done.3 = bf16[128,1024]{0,1:T(8,128)(2,1)} collective-permute-done((bf16[128,1024]{0,1:T(8,128)(2,1)S(1)}, bf16[128,1024]{0,1:T(8,128)(2,1)}, u32[]{:S(2)}, u32[]{:S(2)}) %collective-permute-start.3) | collective-permute-done | bytes 262176 | tf_op jit(solution)/shard_map/ppermute | solution.py:15
  38.3 11.7 %collective-permute-start.6 = (bf16[512,1536]{1,0:T(8,128)(2,1)}, bf16[512,1536]{1,0:T(8,128)(2,1)}, u32[]{:S(2)}, u32[]{:S(2)}) collective-permute-start(bf16[512,1536]{1,0:T(8,128)(2,1)} %pad_maximum_fusion), channel_id=1, source_target_pairs={{0,2},{4,0},{8,4},{12,8},{14,12},{10,14},{6,10},{2,6},{1,3},{5,1},... | collective-permute-start | bytes 4718600 | tf_op jit(solution)/shard_map/ppermute | solution.py:124
  51.6 1.1 fusion.142
  53.7 1.1 fusion.141
  55.8 1.1 fusion.140
  59.0 1.2 fusion.21
  63.9 1.2 fusion.19
  65.1 1.2 fusion.17
  66.3 1.4 fusion.15
  67.8 3.3 %collective-permute-done.4 = bf16[512,1536]{1,0:T(8,128)(2,1)} collective-permute-done((bf16[512,1536]{1,0:T(8,128)(2,1)}, bf16[512,1536]{1,0:T(8,128)(2,1)}, u32[]{:S(2)}, u32[]{:S(2)}) %collective-permute-start.4) | collective-permute-done | bytes 1572896 | tf_op jit(solution)/shard_map/ppermute | solution.py:120
  71.0 1.1 slice.88
  72.1 1.6 collective-permute-start.5
  73.7 9.4 %collective-permute-done.6 = bf16[512,1536]{1,0:T(8,128)(2,1)} collective-permute-done((bf16[512,1536]{1,0:T(8,128)(2,1)}, bf16[512,1536]{1,0:T(8,128)(2,1)}, u32[]{:S(2)}, u32[]{:S(2)}) %collective-permute-start.6) | collective-permute-done | bytes 1572896 | tf_op jit(solution)/shard_map/ppermute | solution.py:124
  83.1 1.1 slice.89
  84.2 1.6 collective-permute-start.7
  85.8 1.3 fusion.24
  87.1 9.1 %collective-permute-done.7 = bf16[512,512]{1,0:T(8,128)(2,1)S(1)} collective-permute-done((bf16[512,512]{1,0:T(8,128)(2,1)S(1)}, bf16[512,512]{1,0:T(8,128)(2,1)S(1)}, u32[]{:S(2)}, u32[]{:S(2)}) %collective-permute-start.7) | collective-permute-done | bytes 524320 | tf_op jit(solution)/shard_map/ppermute | solution.py:125
  96.2 7.2 %collective-permute-start.9 = (bf16[512,1536]{1,0:T(8,128)(2,1)}, bf16[512,1536]{1,0:T(8,128)(2,1)}, u32[]{:S(2)}, u32[]{:S(2)}) collective-permute-start(bf16[512,1536]{1,0:T(8,128)(2,1)} %collective-permute-done.4), channel_id=1, source_target_pairs={{0,4},{4,8},{8,12},{12,14},{14,10},{10,6},{6,2},{2,0},{1,5},{5,9},... | collective-permute-start | bytes 4718600 | tf_op jit(solution)/shard_map/ppermute | solution.py:120
  103.4 13.2 %collective-permute-start.10 = (bf16[512,1536]{1,0:T(8,128)(2,1)}, bf16[512,1536]{1,0:T(8,128)(2,1)}, u32[]{:S(2)}, u32[]{:S(2)}) collective-permute-start(bf16[512,1536]{1,0:T(8,128)(2,1)} %collective-permute-done.6), channel_id=1, source_target_pairs={{0,2},{4,0},{8,4},{12,8},{14,12},{10,14},{6,10},{2,6},{1,3},{5,1},... | collective-permute-start | bytes 4718600 | tf_op jit(solution)/shard_map/ppermute | solution.py:124
  127.5 1.4 broadcast_select_fusion
  128.9 23.0 %collective-permute-done.9 = bf16[512,1536]{1,0:T(8,128)(2,1)} collective-permute-done((bf16[512,1536]{1,0:T(8,128)(2,1)}, bf16[512,1536]{1,0:T(8,128)(2,1)}, u32[]{:S(2)}, u32[]{:S(2)}) %collective-permute-start.9) | collective-permute-done | bytes 1572896 | tf_op jit(solution)/shard_map/ppermute | solution.py:120
  152.7 2.4 fusion.132
  155.1 2.4 fusion.128
  157.5 2.5 %collective-permute-start.12 = (bf16[512,1536]{1,0:T(8,128)(2,1)}, bf16[512,1536]{1,0:T(8,128)(2,1)S(1)}, u32[]{:S(2)}, u32[]{:S(2)}) collective-permute-start(bf16[512,1536]{1,0:T(8,128)(2,1)} %collective-permute-done.10), channel_id=1, source_target_pairs={{0,2},{4,0},{8,4},{12,8},{14,12},{10,14},{6,10},{2,6},{1,3},{5,1},... | collective-permute-start | bytes 4718600 | tf_op jit(solution)/shard_map/ppermute | solution.py:124
  161.8 1.1 slice.92
  162.9 1.6 collective-permute-start.14
  164.5 1.1 slice.93
  166.1 2.4 fusion.121
  168.5 20.6 %collective-permute-done.11 = bf16[512,1536]{1,0:T(8,128)(2,1)S(1)} collective-permute-done((bf16[512,1536]{1,0:T(8,128)(2,1)}, bf16[512,1536]{1,0:T(8,128)(2,1)S(1)}, u32[]{:S(2)}, u32[]{:S(2)}) %collective-permute-start.11) | collective-permute-done | bytes 1572896 | tf_op jit(solution)/shard_map/ppermute | solution.py:120
  190.0 2.4 %fusion.13 = f32[256,1536]{1,0:T(8,128)S(1)} fusion(f32[256,1536]{1,0:T(8,128)S(1)} %fusion.121, f32[256,1536]{1,0:T(8,128)S(1)} %fusion.14, bf16[512,1536]{1,0:T(8,128)(2,1)} %collective-permute-done.9, s32[]{:T(128)S(6)} %select_n.247, bf16[256,2048]{0,1:T(8,128)(2,1)S(1)} %get-tuple-element.24, bf16[256,2048]{0,1:T(8,128)(2,1)S(1)} %get-tuple-element.23), kind=kOutput, calls=%fused_computation.40 | convolution fusion | flops 403963904 | bytes 8388612 | tf_op jit(solution)/shard_map/dot_general | solution.py:135
  194.1 1.6 collective-permute-start.16
  196.1 1.6 collective-permute-start.17
  199.7 9.2 %collective-permute-done.16 = bf16[512,512]{1,0:T(8,128)(2,1)S(1)} collective-permute-done((bf16[512,512]{1,0:T(8,128)(2,1)S(1)}, bf16[512,512]{1,0:T(8,128)(2,1)S(1)}, u32[]{:S(2)}, u32[]{:S(2)}) %collective-permute-start.16) | collective-permute-done | bytes 524320 | tf_op jit(solution)/shard_map/ppermute | solution.py:121
  209.7 15.1 %collective-permute-done.13 = bf16[512,1536]{1,0:T(8,128)(2,1)S(1)} collective-permute-done((bf16[512,1536]{1,0:T(8,128)(2,1)S(1)}, bf16[512,1536]{1,0:T(8,128)(2,1)S(1)}, u32[]{:S(2)}, u32[]{:S(2)}) %collective-permute-start.13) | collective-permute-done | bytes 1572896 | tf_op jit(solution)/shard_map/ppermute | solution.py:120
  224.8 1.6 collective-permute-start.18
  228.2 9.0 %collective-permute-done.18 = bf16[512,512]{1,0:T(8,128)(2,1)S(1)} collective-permute-done((bf16[512,512]{1,0:T(8,128)(2,1)S(1)}, bf16[512,512]{1,0:T(8,128)(2,1)S(1)}, u32[]{:S(2)}, u32[]{:S(2)}) %collective-permute-start.18) | collective-permute-done | bytes 524320 | tf_op jit(solution)/shard_map/ppermute | solution.py:121
  237.9 2.0 select_convert_fusion.1
  239.9 1.1 pad_maximum_fusion.1
  (71 shorter events, 24.8 us)
Async XLA Ops:
  3.0 48.6 %collective-permute-start.2 = (bf16[256,1024]{0,1:T(8,128)(2,1)}, bf16[256,1024]{0,1:T(8,128)(2,1)}, u32[]{:S(2)}, u32[]{:S(2)}) collective-permute-start(bf16[256,1024]{0,1:T(8,128)(2,1)} %pad_maximum_fusion.2), channel_id=1, source_target_pairs={{0,6},{2,8},{4,10},{6,12},{8,14},{1,7},{3,9},{5,11},{7,13},{9,15},... | collective-permute-start | bytes 1572872 | tf_op jit(solution)/shard_map/ppermute | solution.py:15
  9.7 44.0 %collective-permute-start.1 = (bf16[256,1024]{0,1:T(8,128)(2,1)}, bf16[256,1024]{0,1:T(8,128)(2,1)}, u32[]{:S(2)}, u32[]{:S(2)}) collective-permute-start(bf16[256,1024]{0,1:T(8,128)(2,1)} %pad_maximum_fusion.2), channel_id=1, source_target_pairs={{0,4},{2,6},{4,8},{6,10},{8,12},{10,14},{1,5},{3,7},{5,9},{7,11},{... | collective-permute-start | bytes 1572872 | tf_op jit(solution)/shard_map/ppermute | solution.py:15
  14.0 41.8 %collective-permute-start = (bf16[256,1024]{0,1:T(8,128)(2,1)}, bf16[256,1024]{0,1:T(8,128)(2,1)}, u32[]{:S(2)}, u32[]{:S(2)}) collective-permute-start(bf16[256,1024]{0,1:T(8,128)(2,1)} %pad_maximum_fusion.2), channel_id=1, source_target_pairs={{0,2},{2,4},{4,6},{6,8},{8,10},{10,12},{12,14},{1,3},{3,5},{5,7},{... | collective-permute-start | bytes 1572872 | tf_op jit(solution)/shard_map/ppermute | solution.py:15
  17.5 20.9 %collective-permute-start.3 = (bf16[128,1024]{0,1:T(8,128)(2,1)S(1)}, bf16[128,1024]{0,1:T(8,128)(2,1)}, u32[]{:S(2)}, u32[]{:S(2)}) collective-permute-start(bf16[128,1024]{0,1:T(8,128)(2,1)S(1)} %fusion.83), channel_id=1, source_target_pairs={{0,8},{2,10},{4,12},{6,14},{1,9},{3,11},{5,13},{7,15},{16,24},{18,... | collective-permute-start | bytes 786440 | tf_op jit(solution)/shard_map/ppermute | solution.py:15
  20.8 2.5 %copy-start = (bf16[256,512]{1,0:T(8,128)(2,1)S(1)}, bf16[256,512]{1,0:T(8,128)(2,1)}, u32[]{:S(2)}) copy-start(bf16[256,512]{1,0:T(8,128)(2,1)} %param.8) | copy-start | bytes 786436
  23.2 2.0 copy-start.4
  23.2 47.9 %collective-permute-start.4 = (bf16[512,1536]{1,0:T(8,128)(2,1)}, bf16[512,1536]{1,0:T(8,128)(2,1)}, u32[]{:S(2)}, u32[]{:S(2)}) collective-permute-start(bf16[512,1536]{1,0:T(8,128)(2,1)} %pad_maximum_fusion), channel_id=1, source_target_pairs={{0,4},{4,8},{8,12},{12,14},{14,10},{10,6},{6,2},{2,0},{1,5},{5,9},... | collective-permute-start | bytes 4718600 | tf_op jit(solution)/shard_map/ppermute | solution.py:120
  38.3 44.8 %collective-permute-start.6 = (bf16[512,1536]{1,0:T(8,128)(2,1)}, bf16[512,1536]{1,0:T(8,128)(2,1)}, u32[]{:S(2)}, u32[]{:S(2)}) collective-permute-start(bf16[512,1536]{1,0:T(8,128)(2,1)} %pad_maximum_fusion), channel_id=1, source_target_pairs={{0,2},{4,0},{8,4},{12,8},{14,12},{10,14},{6,10},{2,6},{1,3},{5,1},... | collective-permute-start | bytes 4718600 | tf_op jit(solution)/shard_map/ppermute | solution.py:124
  72.1 15.0 %collective-permute-start.5 = (bf16[512,512]{1,0:T(8,128)(2,1)S(1)}, bf16[512,512]{1,0:T(8,128)(2,1)S(1)}, u32[]{:S(2)}, u32[]{:S(2)}) collective-permute-start(bf16[512,512]{1,0:T(8,128)(2,1)S(1)} %slice.88), channel_id=1, source_target_pairs={{0,16},{16,0},{1,17},{17,1},{2,18},{18,2},{3,19},{19,3},{4,20},{20... | collective-permute-start | bytes 1572872 | tf_op jit(solution)/shard_map/ppermute | solution.py:121
  84.2 12.0 %collective-permute-start.7 = (bf16[512,512]{1,0:T(8,128)(2,1)S(1)}, bf16[512,512]{1,0:T(8,128)(2,1)S(1)}, u32[]{:S(2)}, u32[]{:S(2)}) collective-permute-start(bf16[512,512]{1,0:T(8,128)(2,1)S(1)} %slice.89), channel_id=1, source_target_pairs={{0,16},{16,0},{1,17},{17,1},{2,18},{18,2},{3,19},{19,3},{4,20},{20... | collective-permute-start | bytes 1572872 | tf_op jit(solution)/shard_map/ppermute | solution.py:125
  85.8 30.9 %copy-start.5 = (s32[8]{0:T(128)S(1)}, s32[8]{0:T(128)}, u32[]{:S(2)}) copy-start(s32[8]{0:T(128)} %constant.185.clone) | copy-start | bytes 100
  85.8 36.5 %copy-start.3 = (s32[8]{0:T(128)S(1)}, s32[8]{0:T(128)}, u32[]{:S(2)}) copy-start(s32[8]{0:T(128)} %constant.186.clone) | copy-start | bytes 100
  87.1 9.1 %copy-start.1 = (bf16[512,512]{1,0:T(8,128)(2,1)}, bf16[512,512]{1,0:T(8,128)(2,1)S(1)}, u32[]{:S(2)}) copy-start(bf16[512,512]{1,0:T(8,128)(2,1)S(1)} %collective-permute-done.5) | copy-start | bytes 1572868
  96.2 31.3 %collective-permute-start.8 = (bf16[256,2048]{0,1:T(8,128)(2,1)S(1)}, bf16[256,2048]{0,1:T(8,128)(2,1)}, u32[]{:S(2)}, u32[]{:S(2)}) collective-permute-start(bf16[256,2048]{0,1:T(8,128)(2,1)S(1)} %bitcast.266), channel_id=1, source_target_pairs={{0,1},{1,0},{2,3},{3,2},{4,5},{5,4},{6,7},{7,6},{8,9},{9,8},{10,11... | collective-permute-start | bytes 3145736 | tf_op jit(solution)/shard_map/ppermute | solution.py:77
  96.2 55.7 %collective-permute-start.9 = (bf16[512,1536]{1,0:T(8,128)(2,1)}, bf16[512,1536]{1,0:T(8,128)(2,1)}, u32[]{:S(2)}, u32[]{:S(2)}) collective-permute-start(bf16[512,1536]{1,0:T(8,128)(2,1)} %collective-permute-done.4), channel_id=1, source_target_pairs={{0,4},{4,8},{8,12},{12,14},{14,10},{10,6},{6,2},{2,0},{1,5},{5,9},... | collective-permute-start | bytes 4718600 | tf_op jit(solution)/shard_map/ppermute | solution.py:120
  103.4 54.1 %collective-permute-start.10 = (bf16[512,1536]{1,0:T(8,128)(2,1)}, bf16[512,1536]{1,0:T(8,128)(2,1)}, u32[]{:S(2)}, u32[]{:S(2)}) collective-permute-start(bf16[512,1536]{1,0:T(8,128)(2,1)} %collective-permute-done.6), channel_id=1, source_target_pairs={{0,2},{4,0},{8,4},{12,8},{14,12},{10,14},{6,10},{2,6},{1,3},{5,1},... | collective-permute-start | bytes 4718600 | tf_op jit(solution)/shard_map/ppermute | solution.py:124
  127.5 24.5 %copy-start.2 = (bf16[512,512]{1,0:T(8,128)(2,1)S(1)}, bf16[512,512]{1,0:T(8,128)(2,1)}, u32[]{:S(2)}) copy-start(bf16[512,512]{1,0:T(8,128)(2,1)} %copy-done.1) | copy-start | bytes 1572868
  151.9 37.2 %collective-permute-start.11 = (bf16[512,1536]{1,0:T(8,128)(2,1)}, bf16[512,1536]{1,0:T(8,128)(2,1)S(1)}, u32[]{:S(2)}, u32[]{:S(2)}) collective-permute-start(bf16[512,1536]{1,0:T(8,128)(2,1)} %collective-permute-done.9), channel_id=1, source_target_pairs={{0,4},{4,8},{8,12},{12,14},{14,10},{10,6},{6,2},{2,0},{1,5},{5,9},... | collective-permute-start | bytes 4718600 | tf_op jit(solution)/shard_map/ppermute | solution.py:120
  157.5 38.5 %collective-permute-start.12 = (bf16[512,1536]{1,0:T(8,128)(2,1)}, bf16[512,1536]{1,0:T(8,128)(2,1)S(1)}, u32[]{:S(2)}, u32[]{:S(2)}) collective-permute-start(bf16[512,1536]{1,0:T(8,128)(2,1)} %collective-permute-done.10), channel_id=1, source_target_pairs={{0,2},{4,0},{8,4},{12,8},{14,12},{10,14},{6,10},{2,6},{1,3},{5,1},... | collective-permute-start | bytes 4718600 | tf_op jit(solution)/shard_map/ppermute | solution.py:124
  162.9 29.6 %collective-permute-start.14 = (bf16[512,512]{1,0:T(8,128)(2,1)S(1)}, bf16[512,512]{1,0:T(8,128)(2,1)S(1)}, u32[]{:S(2)}, u32[]{:S(2)}) collective-permute-start(bf16[512,512]{1,0:T(8,128)(2,1)S(1)} %slice.92), channel_id=1, source_target_pairs={{0,16},{16,0},{1,17},{17,1},{2,18},{18,2},{3,19},{19,3},{4,20},{20... | collective-permute-start | bytes 1572872 | tf_op jit(solution)/shard_map/ppermute | solution.py:121
  165.6 27.7 %collective-permute-start.15 = (bf16[512,512]{1,0:T(8,128)(2,1)S(1)}, bf16[512,512]{1,0:T(8,128)(2,1)S(1)}, u32[]{:S(2)}, u32[]{:S(2)}) collective-permute-start(bf16[512,512]{1,0:T(8,128)(2,1)S(1)} %slice.93), channel_id=1, source_target_pairs={{0,16},{16,0},{1,17},{17,1},{2,18},{18,2},{3,19},{19,3},{4,20},{20... | collective-permute-start | bytes 1572872 | tf_op jit(solution)/shard_map/ppermute | solution.py:125
  189.1 35.7 %collective-permute-start.13 = (bf16[512,1536]{1,0:T(8,128)(2,1)S(1)}, bf16[512,1536]{1,0:T(8,128)(2,1)S(1)}, u32[]{:S(2)}, u32[]{:S(2)}) collective-permute-start(bf16[512,1536]{1,0:T(8,128)(2,1)S(1)} %collective-permute-done.11), channel_id=1, source_target_pairs={{0,4},{4,8},{8,12},{12,14},{14,10},{10,6},{6,2},{2,0},{1,5},{5,9},... | collective-permute-start | bytes 4718600 | tf_op jit(solution)/shard_map/ppermute | solution.py:120
  194.1 14.9 %collective-permute-start.16 = (bf16[512,512]{1,0:T(8,128)(2,1)S(1)}, bf16[512,512]{1,0:T(8,128)(2,1)S(1)}, u32[]{:S(2)}, u32[]{:S(2)}) collective-permute-start(bf16[512,512]{1,0:T(8,128)(2,1)S(1)} %slice.94), channel_id=1, source_target_pairs={{0,16},{16,0},{1,17},{17,1},{2,18},{18,2},{3,19},{19,3},{4,20},{20... | collective-permute-start | bytes 1572872 | tf_op jit(solution)/shard_map/ppermute | solution.py:121
  196.1 30.3 %collective-permute-start.17 = (bf16[512,512]{1,0:T(8,128)(2,1)S(1)}, bf16[512,512]{1,0:T(8,128)(2,1)S(1)}, u32[]{:S(2)}, u32[]{:S(2)}) collective-permute-start(bf16[512,512]{1,0:T(8,128)(2,1)S(1)} %slice.95), channel_id=1, source_target_pairs={{0,16},{16,0},{1,17},{17,1},{2,18},{18,2},{3,19},{19,3},{4,20},{20... | collective-permute-start | bytes 1572872 | tf_op jit(solution)/shard_map/ppermute | solution.py:125
  224.8 12.4 %collective-permute-start.18 = (bf16[512,512]{1,0:T(8,128)(2,1)S(1)}, bf16[512,512]{1,0:T(8,128)(2,1)S(1)}, u32[]{:S(2)}, u32[]{:S(2)}) collective-permute-start(bf16[512,512]{1,0:T(8,128)(2,1)S(1)} %slice.96), channel_id=1, source_target_pairs={{0,16},{16,0},{1,17},{17,1},{2,18},{18,2},{3,19},{19,3},{4,20},{20... | collective-permute-start | bytes 1572872 | tf_op jit(solution)/shard_map/ppermute | solution.py:121

commit v15 on v12

--- a/solution.py
+++ b/solution.py
@@ -118,12 +118,21 @@
     backward_steps = count - 1 - forward_steps
     for step in range(1, forward_steps + 1):
         forward = lax.ppermute(forward, "ctx", ahead)
-        crossed = lax.ppermute(forward[:, shared:], "group", swap) if own else None
-        arrivals.append((order_table[(position + count - step) % count], forward, crossed))
-        if step <= backward_steps:
-            backward = lax.ppermute(backward, "ctx", behind)
-            crossed = lax.ppermute(backward[:, shared:], "group", swap) if own else None
-            arrivals.append((order_table[(position + step) % count], backward, crossed))
+        if step > backward_steps:
+            crossed = lax.ppermute(forward[:, shared:], "group", swap) if own else None
+            arrivals.append((order_table[(position + count - step) % count], forward, crossed))
+            continue
+        backward = lax.ppermute(backward, "ctx", behind)
+        both = None
+        if own:
+            both = lax.ppermute(
+                jnp.concatenate([forward[:, shared:], backward[:, shared:]], axis=0), "group", swap
+            )
+        rows = forward.shape[0]
+        arrivals.append(
+            (order_table[(position + count - step) % count], forward, both[:rows] if own else None)
+        )
+        arrivals.append((order_table[(position + step) % count], backward, both[rows:] if own else None))
     return arrivals, shared, own
 
 

time: 213 us -> 213 us (level)
    ppermute x4, waiting for transfers between devices: 32.9 us -> 12.6 us  [ring_transfer(): forward = lax.ppermute(forward, 'ctx', ahead)]
    ppermute x3, waiting for transfers between devices: 2.22 us -> 17.4 us  [ring_transfer(): lax.ppermute(jnp.concatenate([forward[:, shared:], backward[:, shared:]],...]
    ppermute x3, waiting for transfers between devices: 15.8 us -> 28.4 us  [ring_transfer(): backward = lax.ppermute(backward, 'ctx', behind)]
    ppermute x4 -> x1, waiting for transfers between devices: 15 us -> 8.97 us  [ring_transfer(): crossed = lax.ppermute(forward[:, shared:], 'group', swap) if own else None]
    ppermute x4 -> x1, starting transfers between devices: 6.33 us -> 2.23 us  [ring_transfer(): crossed = lax.ppermute(forward[:, shared:], 'group', swap) if own else None]
    slice x3 -> x6, local copies, waits for them, and re-layouts: 2.19 us -> 4.38 us  [the longest x3 2.19 us: ring_transfer(): forward[:, shared:]]
    slice x4 -> x1, local copies, waits for them, and re-layouts: 2.23 us -> 0.03 us  [ring_transfer(): crossed = lax.ppermute(forward[:, shared:], 'group', swap) if own else None]
  transfers between devices with their start and end apart: 19 -> 16, of which waited for: 12 -> 9; matrix products, arithmetic and copies ran while one was open for 24% -> 24% of each run, Pallas kernels for 0% -> 0%
where the time goes in v15:
time: 213 us; the launch traced here: 212 us
  waiting for transfers between devices  78.9 us (37%)
  starting transfers between devices  64.8 us (30%)
  matrix products  31.9 us (15%)
  local copies, waits for them, and re-layouts  16.4 us (8%)
  other arithmetic  10.3 us (5%)
  between operations  9.7 us (5%)
    ppermute x3, starting transfers between devices, ring_transfer(): backward = lax.ppermute(backward, 'ctx', behind)  33.4 us
    ppermute x3, waiting for transfers between devices, ring_transfer(): backward = lax.ppermute(backward, 'ctx', behind)  28.4 us
    ppermute x3, waiting for transfers between devices, ring_transfer(): lax.ppermute(jnp.concatenate([forward[:, shared:], backward[:, shared:]],...  17.4 us
    ppermute x4, starting transfers between devices, passed_along(): return lax.ppermute(array, axis, pairs)  16.4 us
    dot_general x8, matrix products, ring_project(): terms = [jnp.dot(piece, carried_block, preferred_element_type=jnp.float32)]  13.7 us
    ppermute x4, waiting for transfers between devices, ring_transfer(): forward = lax.ppermute(forward, 'ctx', ahead)  12.6 us
    ppermute x4, waiting for transfers between devices, passed_along(): return lax.ppermute(array, axis, pairs)  11.6 us
    ppermute x1, waiting for transfers between devices, ring_transfer(): crossed = lax.ppermute(forward[:, shared:], 'group', swap) if own else None  8.97 us
  transfers between devices with their start and end apart: 16, of which 9 were waited for; matrix products, arithmetic and copies ran while one was open for 24% of the time, Pallas kernels for 0%

profile of v15, /device:TPU:0, one launch (start us, length us, event | category | flops | bytes accessed | tf_op | source)
XLA Modules:
  0.0 211.9 jit_solution(12837000577807943096)
XLA Ops:
  0.0 1.1 copy.77
  1.1 1.1 copy.46
  3.0 6.7 %collective-permute-start.2 = (bf16[256,1024]{0,1:T(8,128)(2,1)}, bf16[256,1024]{0,1:T(8,128)(2,1)}, u32[]{:S(2)}, u32[]{:S(2)}) collective-permute-start(bf16[256,1024]{0,1:T(8,128)(2,1)} %pad_maximum_fusion.5), channel_id=1, source_target_pairs={{0,6},{2,8},{4,10},{6,12},{8,14},{1,7},{3,9},{5,11},{7,13},{9,15},... | collective-permute-start | bytes 1572872 | tf_op jit(solution)/shard_map/ppermute | solution.py:15
  9.7 4.3 %collective-permute-start.1 = (bf16[256,1024]{0,1:T(8,128)(2,1)}, bf16[256,1024]{0,1:T(8,128)(2,1)}, u32[]{:S(2)}, u32[]{:S(2)}) collective-permute-start(bf16[256,1024]{0,1:T(8,128)(2,1)} %pad_maximum_fusion.5), channel_id=1, source_target_pairs={{0,4},{2,6},{4,8},{6,10},{8,12},{10,14},{1,5},{3,7},{5,9},{7,11},{... | collective-permute-start | bytes 1572872 | tf_op jit(solution)/shard_map/ppermute | solution.py:15
  14.0 3.5 %collective-permute-start = (bf16[256,1024]{0,1:T(8,128)(2,1)}, bf16[256,1024]{0,1:T(8,128)(2,1)}, u32[]{:S(2)}, u32[]{:S(2)}) collective-permute-start(bf16[256,1024]{0,1:T(8,128)(2,1)} %pad_maximum_fusion.5), channel_id=1, source_target_pairs={{0,2},{2,4},{4,6},{6,8},{8,10},{10,12},{12,14},{1,3},{3,5},{5,7},{... | collective-permute-start | bytes 1572872 | tf_op jit(solution)/shard_map/ppermute | solution.py:15
  17.5 2.0 collective-permute-start.3
  19.5 1.3 slice.86
  20.8 1.1 constant_dynamic-slice_fusion
  21.9 1.3 pad_maximum_fusion
  23.3 1.8 reshape.293
  26.8 11.5 %collective-permute-done.3 = bf16[128,1024]{0,1:T(8,128)(2,1)} collective-permute-done((bf16[128,1024]{0,1:T(8,128)(2,1)S(1)}, bf16[128,1024]{0,1:T(8,128)(2,1)}, u32[]{:S(2)}, u32[]{:S(2)}) %collective-permute-start.3) | collective-permute-done | bytes 262176 | tf_op jit(solution)/shard_map/ppermute | solution.py:15
  38.3 11.7 %collective-permute-start.6 = (bf16[512,1536]{1,0:T(8,128)(2,1)}, bf16[512,1536]{1,0:T(8,128)(2,1)}, u32[]{:S(2)}, u32[]{:S(2)}) collective-permute-start(bf16[512,1536]{1,0:T(8,128)(2,1)} %pad_maximum_fusion), channel_id=1, source_target_pairs={{0,2},{4,0},{8,4},{12,8},{14,12},{10,14},{6,10},{2,6},{1,3},{5,1},... | collective-permute-start | bytes 4718600 | tf_op jit(solution)/shard_map/ppermute | solution.py:125
  51.6 1.1 fusion.148
  53.7 1.1 fusion.147
  55.8 1.1 fusion.146
  57.9 1.1 fusion.4
  59.0 1.2 fusion.21
  60.2 1.1 fusion.6
  61.2 1.2 fusion.19
  63.5 1.2 fusion.17
  64.7 1.1 fusion.10
  65.7 1.4 fusion.15
  67.8 1.3 fusion.24
  69.2 1.9 collective-permute-done.5
  71.0 7.2 %collective-permute-start.7 = (bf16[512,1536]{1,0:T(8,128)(2,1)}, bf16[512,1536]{1,0:T(8,128)(2,1)}, u32[]{:S(2)}, u32[]{:S(2)}) collective-permute-start(bf16[512,1536]{1,0:T(8,128)(2,1)} %collective-permute-done.5), channel_id=1, source_target_pairs={{0,4},{4,8},{8,12},{12,14},{14,10},{10,6},{6,2},{2,0},{1,5},{5,9},... | collective-permute-start | bytes 4718600 | tf_op jit(solution)/shard_map/ppermute | solution.py:120
  78.2 4.9 %collective-permute-done.6 = bf16[512,1536]{1,0:T(8,128)(2,1)} collective-permute-done((bf16[512,1536]{1,0:T(8,128)(2,1)}, bf16[512,1536]{1,0:T(8,128)(2,1)}, u32[]{:S(2)}, u32[]{:S(2)}) %collective-permute-start.6) | collective-permute-done | bytes 1572896 | tf_op jit(solution)/shard_map/ppermute | solution.py:125
  83.1 19.3 %collective-permute-start.8 = (bf16[512,1536]{1,0:T(8,128)(2,1)}, bf16[512,1536]{1,0:T(8,128)(2,1)}, u32[]{:S(2)}, u32[]{:S(2)}) collective-permute-start(bf16[512,1536]{1,0:T(8,128)(2,1)} %collective-permute-done.6), channel_id=1, source_target_pairs={{0,2},{4,0},{8,4},{12,8},{14,12},{10,14},{6,10},{2,6},{1,3},{5,1},... | collective-permute-start | bytes 4718600 | tf_op jit(solution)/shard_map/ppermute | solution.py:125
  112.9 1.1 slice.114
  114.0 1.1 slice.115
  115.2 1.6 collective-permute-start.12
  116.8 1.4 broadcast_select_fusion
  118.1 2.4 %fusion.136 = f32[256,1536]{1,0:T(8,128)S(1)} fusion(bf16[512,1536]{1,0:T(8,128)(2,1)} %collective-permute-done.5, s32[]{:T(128)S(6)} %select_n.241, bf16[256,2048]{0,1:T(8,128)(2,1)S(1)} %get-tuple-element.18, bf16[256,2048]{0,1:T(8,128)(2,1)S(1)} %get-tuple-element.17), kind=kOutput, calls=%fused_computation.224 | convolution fusion | flops 403177472 | bytes 5242884 | tf_op jit(solution)/shard_map/dot_general | solution.py:144
  120.5 2.4 %fusion.133 = f32[256,1536]{1,0:T(8,128)S(1)} fusion(bf16[512,1536]{1,0:T(8,128)(2,1)} %collective-permute-done.6, s32[]{:T(128)S(6)} %select_n.244, bf16[256,2048]{0,1:T(8,128)(2,1)S(1)} %get-tuple-element.18, bf16[256,2048]{0,1:T(8,128)(2,1)S(1)} %get-tuple-element.17), kind=kOutput, calls=%fused_computation.223 | convolution fusion | flops 403177472 | bytes 5242884 | tf_op jit(solution)/shard_map/dot_general | solution.py:144
  123.0 12.7 %collective-permute-done.8 = bf16[512,1536]{1,0:T(8,128)(2,1)} collective-permute-done((bf16[512,1536]{1,0:T(8,128)(2,1)}, bf16[512,1536]{1,0:T(8,128)(2,1)}, u32[]{:S(2)}, u32[]{:S(2)}) %collective-permute-start.8) | collective-permute-done | bytes 1572896 | tf_op jit(solution)/shard_map/ppermute | solution.py:125
  135.7 2.5 %collective-permute-start.10 = (bf16[512,1536]{1,0:T(8,128)(2,1)}, bf16[512,1536]{1,0:T(8,128)(2,1)S(1)}, u32[]{:S(2)}, u32[]{:S(2)}) collective-permute-start(bf16[512,1536]{1,0:T(8,128)(2,1)} %collective-permute-done.8), channel_id=1, source_target_pairs={{0,2},{4,0},{8,4},{12,8},{14,12},{10,14},{6,10},{2,6},{1,3},{5,1},... | collective-permute-start | bytes 4718600 | tf_op jit(solution)/shard_map/ppermute | solution.py:125
  140.0 1.1 slice.118
  141.1 1.1 slice.119
  142.2 1.6 collective-permute-start.13
  144.6 2.4 %fusion.128 = f32[256,1536]{1,0:T(8,128)S(1)} fusion(bf16[512,1536]{1,0:T(8,128)(2,1)} %collective-permute-done.8, s32[]{:T(128)S(6)} %select_n.250, bf16[256,2048]{0,1:T(8,128)(2,1)S(1)} %get-tuple-element.18, bf16[256,2048]{0,1:T(8,128)(2,1)S(1)} %get-tuple-element.17), kind=kOutput, calls=%fused_computation.222 | convolution fusion | flops 403177472 | bytes 5242884 | tf_op jit(solution)/shard_map/dot_general | solution.py:144
  147.0 2.4 %fusion.13 = f32[256,1536]{1,0:T(8,128)S(1)} fusion(f32[256,1536]{1,0:T(8,128)S(1)} %fusion.128, f32[256,1536]{1,0:T(8,128)S(1)} %fusion.14, bf16[512,1536]{1,0:T(8,128)(2,1)} %collective-permute-done.7, s32[]{:T(128)S(6)} %select_n.247, bf16[256,2048]{0,1:T(8,128)(2,1)S(1)} %get-tuple-element.18, bf16[256,2048]{0,1:T(8,128)(2,1)S(1)} %get-tuple-element.17), kind=kOutput, calls=%fused_computation.40 | convolution fusion | flops 403963904 | bytes 8388612 | tf_op jit(solution)/shard_map/dot_general | solution.py:144
  149.4 9.8 %collective-permute-done.9 = bf16[512,1536]{1,0:T(8,128)(2,1)S(1)} collective-permute-done((bf16[512,1536]{1,0:T(8,128)(2,1)}, bf16[512,1536]{1,0:T(8,128)(2,1)S(1)}, u32[]{:S(2)}, u32[]{:S(2)}) %collective-permute-start.9) | collective-permute-done | bytes 1572896 | tf_op jit(solution)/shard_map/ppermute | solution.py:120
  159.8 10.8 %collective-permute-done.10 = bf16[512,1536]{1,0:T(8,128)(2,1)S(1)} collective-permute-done((bf16[512,1536]{1,0:T(8,128)(2,1)}, bf16[512,1536]{1,0:T(8,128)(2,1)S(1)}, u32[]{:S(2)}, u32[]{:S(2)}) %collective-permute-start.10) | collective-permute-done | bytes 1572896 | tf_op jit(solution)/shard_map/ppermute | solution.py:125
  170.7 1.6 collective-permute-start.14
  175.9 17.4 %collective-permute-done.14 = bf16[1024,512]{1,0:T(8,128)(2,1)S(1)} collective-permute-done((bf16[1024,512]{1,0:T(8,128)(2,1)S(1)}, bf16[1024,512]{1,0:T(8,128)(2,1)S(1)}, u32[]{:S(2)}, u32[]{:S(2)}) %collective-permute-start.14) | collective-permute-done | bytes 1048608 | tf_op jit(solution)/shard_map/ppermute | solution.py:128
  195.1 2.2 %collective-permute-start.15 = (bf16[512,512]{1,0:T(8,128)(2,1)S(1)}, bf16[512,512]{1,0:T(8,128)(2,1)S(1)}, u32[]{:S(2)}, u32[]{:S(2)}) collective-permute-start(bf16[512,512]{1,0:T(8,128)(2,1)S(1)} %slice.126), channel_id=1, source_target_pairs={{0,16},{16,0},{1,17},{17,1},{2,18},{18,2},{3,19},{19,3},{4,20},{20... | collective-permute-start | bytes 1572872 | tf_op jit(solution)/shard_map/ppermute | solution.py:122
  199.1 9.0 %collective-permute-done.15 = bf16[512,512]{1,0:T(8,128)(2,1)S(1)} collective-permute-done((bf16[512,512]{1,0:T(8,128)(2,1)S(1)}, bf16[512,512]{1,0:T(8,128)(2,1)S(1)}, u32[]{:S(2)}, u32[]{:S(2)}) %collective-permute-start.15) | collective-permute-done | bytes 524320 | tf_op jit(solution)/shard_map/ppermute | solution.py:122
  208.8 2.0 select_convert_fusion.1
  210.8 1.1 pad_maximum_fusion.4
  (64 shorter events, 21.5 us)
Async XLA Ops:
  3.0 48.6 %collective-permute-start.2 = (bf16[256,1024]{0,1:T(8,128)(2,1)}, bf16[256,1024]{0,1:T(8,128)(2,1)}, u32[]{:S(2)}, u32[]{:S(2)}) collective-permute-start(bf16[256,1024]{0,1:T(8,128)(2,1)} %pad_maximum_fusion.5), channel_id=1, source_target_pairs={{0,6},{2,8},{4,10},{6,12},{8,14},{1,7},{3,9},{5,11},{7,13},{9,15},... | collective-permute-start | bytes 1572872 | tf_op jit(solution)/shard_map/ppermute | solution.py:15
  9.7 44.0 %collective-permute-start.1 = (bf16[256,1024]{0,1:T(8,128)(2,1)}, bf16[256,1024]{0,1:T(8,128)(2,1)}, u32[]{:S(2)}, u32[]{:S(2)}) collective-permute-start(bf16[256,1024]{0,1:T(8,128)(2,1)} %pad_maximum_fusion.5), channel_id=1, source_target_pairs={{0,4},{2,6},{4,8},{6,10},{8,12},{10,14},{1,5},{3,7},{5,9},{7,11},{... | collective-permute-start | bytes 1572872 | tf_op jit(solution)/shard_map/ppermute | solution.py:15
  14.0 41.8 %collective-permute-start = (bf16[256,1024]{0,1:T(8,128)(2,1)}, bf16[256,1024]{0,1:T(8,128)(2,1)}, u32[]{:S(2)}, u32[]{:S(2)}) collective-permute-start(bf16[256,1024]{0,1:T(8,128)(2,1)} %pad_maximum_fusion.5), channel_id=1, source_target_pairs={{0,2},{2,4},{4,6},{6,8},{8,10},{10,12},{12,14},{1,3},{3,5},{5,7},{... | collective-permute-start | bytes 1572872 | tf_op jit(solution)/shard_map/ppermute | solution.py:15
  17.5 20.9 %collective-permute-start.3 = (bf16[128,1024]{0,1:T(8,128)(2,1)S(1)}, bf16[128,1024]{0,1:T(8,128)(2,1)}, u32[]{:S(2)}, u32[]{:S(2)}) collective-permute-start(bf16[128,1024]{0,1:T(8,128)(2,1)S(1)} %fusion.95), channel_id=1, source_target_pairs={{0,8},{2,10},{4,12},{6,14},{1,9},{3,11},{5,13},{7,15},{16,24},{18,... | collective-permute-start | bytes 786440 | tf_op jit(solution)/shard_map/ppermute | solution.py:15
  20.8 2.5 %copy-start = (bf16[256,512]{1,0:T(8,128)(2,1)S(1)}, bf16[256,512]{1,0:T(8,128)(2,1)}, u32[]{:S(2)}) copy-start(bf16[256,512]{1,0:T(8,128)(2,1)} %param.8) | copy-start | bytes 786436
  23.2 2.0 copy-start.2
  23.2 47.8 %collective-permute-start.5 = (bf16[512,1536]{1,0:T(8,128)(2,1)}, bf16[512,1536]{1,0:T(8,128)(2,1)}, u32[]{:S(2)}, u32[]{:S(2)}) collective-permute-start(bf16[512,1536]{1,0:T(8,128)(2,1)} %pad_maximum_fusion), channel_id=1, source_target_pairs={{0,4},{4,8},{8,12},{12,14},{14,10},{10,6},{6,2},{2,0},{1,5},{5,9},... | collective-permute-start | bytes 4718600 | tf_op jit(solution)/shard_map/ppermute | solution.py:120
  38.3 44.8 %collective-permute-start.6 = (bf16[512,1536]{1,0:T(8,128)(2,1)}, bf16[512,1536]{1,0:T(8,128)(2,1)}, u32[]{:S(2)}, u32[]{:S(2)}) collective-permute-start(bf16[512,1536]{1,0:T(8,128)(2,1)} %pad_maximum_fusion), channel_id=1, source_target_pairs={{0,2},{4,0},{8,4},{12,8},{14,12},{10,14},{6,10},{2,6},{1,3},{5,1},... | collective-permute-start | bytes 4718600 | tf_op jit(solution)/shard_map/ppermute | solution.py:125
  67.7 34.7 %copy-start.3 = (s32[8]{0:T(128)S(1)}, s32[8]{0:T(128)}, u32[]{:S(2)}) copy-start(s32[8]{0:T(128)} %constant.185.clone) | copy-start | bytes 100
  67.8 39.9 %copy-start.1 = (s32[8]{0:T(128)S(1)}, s32[8]{0:T(128)}, u32[]{:S(2)}) copy-start(s32[8]{0:T(128)} %constant.186.clone) | copy-start | bytes 100
  69.1 47.7 %collective-permute-start.4 = (bf16[256,2048]{0,1:T(8,128)(2,1)S(1)}, bf16[256,2048]{0,1:T(8,128)(2,1)}, u32[]{:S(2)}, u32[]{:S(2)}) collective-permute-start(bf16[256,2048]{0,1:T(8,128)(2,1)S(1)} %bitcast.262), channel_id=1, source_target_pairs={{0,1},{1,0},{2,3},{3,2},{4,5},{5,4},{6,7},{7,6},{8,9},{9,8},{10,11... | collective-permute-start | bytes 3145736 | tf_op jit(solution)/shard_map/ppermute | solution.py:77
  71.0 51.9 %collective-permute-start.7 = (bf16[512,1536]{1,0:T(8,128)(2,1)}, bf16[512,1536]{1,0:T(8,128)(2,1)}, u32[]{:S(2)}, u32[]{:S(2)}) collective-permute-start(bf16[512,1536]{1,0:T(8,128)(2,1)} %collective-permute-done.5), channel_id=1, source_target_pairs={{0,4},{4,8},{8,12},{12,14},{14,10},{10,6},{6,2},{2,0},{1,5},{5,9},... | collective-permute-start | bytes 4718600 | tf_op jit(solution)/shard_map/ppermute | solution.py:120
  83.1 52.6 %collective-permute-start.8 = (bf16[512,1536]{1,0:T(8,128)(2,1)}, bf16[512,1536]{1,0:T(8,128)(2,1)}, u32[]{:S(2)}, u32[]{:S(2)}) collective-permute-start(bf16[512,1536]{1,0:T(8,128)(2,1)} %collective-permute-done.6), channel_id=1, source_target_pairs={{0,2},{4,0},{8,4},{12,8},{14,12},{10,14},{6,10},{2,6},{1,3},{5,1},... | collective-permute-start | bytes 4718600 | tf_op jit(solution)/shard_map/ppermute | solution.py:125
  115.2 24.0 %collective-permute-start.12 = (bf16[1024,512]{1,0:T(8,128)(2,1)S(1)}, bf16[1024,512]{1,0:T(8,128)(2,1)S(1)}, u32[]{:S(2)}, u32[]{:S(2)}) collective-permute-start(bf16[1024,512]{1,0:T(8,128)(2,1)S(1)} %pad_maximum_fusion.1), channel_id=1, source_target_pairs={{0,16},{16,0},{1,17},{17,1},{2,18},{18,2},{3,19},{19,3},{4,20},{20... | collective-permute-start | bytes 3145736 | tf_op jit(solution)/shard_map/ppermute | solution.py:128
  123.0 36.2 %collective-permute-start.9 = (bf16[512,1536]{1,0:T(8,128)(2,1)}, bf16[512,1536]{1,0:T(8,128)(2,1)S(1)}, u32[]{:S(2)}, u32[]{:S(2)}) collective-permute-start(bf16[512,1536]{1,0:T(8,128)(2,1)} %collective-permute-done.7), channel_id=1, source_target_pairs={{0,4},{4,8},{8,12},{12,14},{14,10},{10,6},{6,2},{2,0},{1,5},{5,9},... | collective-permute-start | bytes 4718600 | tf_op jit(solution)/shard_map/ppermute | solution.py:120
  135.7 34.9 %collective-permute-start.10 = (bf16[512,1536]{1,0:T(8,128)(2,1)}, bf16[512,1536]{1,0:T(8,128)(2,1)S(1)}, u32[]{:S(2)}, u32[]{:S(2)}) collective-permute-start(bf16[512,1536]{1,0:T(8,128)(2,1)} %collective-permute-done.8), channel_id=1, source_target_pairs={{0,2},{4,0},{8,4},{12,8},{14,12},{10,14},{6,10},{2,6},{1,3},{5,1},... | collective-permute-start | bytes 4718600 | tf_op jit(solution)/shard_map/ppermute | solution.py:125
  142.2 30.1 %collective-permute-start.13 = (bf16[1024,512]{1,0:T(8,128)(2,1)S(1)}, bf16[1024,512]{1,0:T(8,128)(2,1)S(1)}, u32[]{:S(2)}, u32[]{:S(2)}) collective-permute-start(bf16[1024,512]{1,0:T(8,128)(2,1)S(1)} %pad_maximum_fusion.2), channel_id=1, source_target_pairs={{0,16},{16,0},{1,17},{17,1},{2,18},{18,2},{3,19},{19,3},{4,20},{20... | collective-permute-start | bytes 3145736 | tf_op jit(solution)/shard_map/ppermute | solution.py:128
  159.2 35.8 %collective-permute-start.11 = (bf16[512,1536]{1,0:T(8,128)(2,1)S(1)}, bf16[512,1536]{1,0:T(8,128)(2,1)S(1)}, u32[]{:S(2)}, u32[]{:S(2)}) collective-permute-start(bf16[512,1536]{1,0:T(8,128)(2,1)S(1)} %collective-permute-done.9), channel_id=1, source_target_pairs={{0,4},{4,8},{8,12},{12,14},{14,10},{10,6},{6,2},{2,0},{1,5},{5,9},... | collective-permute-start | bytes 4718600 | tf_op jit(solution)/shard_map/ppermute | solution.py:120
  170.7 22.6 %collective-permute-start.14 = (bf16[1024,512]{1,0:T(8,128)(2,1)S(1)}, bf16[1024,512]{1,0:T(8,128)(2,1)S(1)}, u32[]{:S(2)}, u32[]{:S(2)}) collective-permute-start(bf16[1024,512]{1,0:T(8,128)(2,1)S(1)} %pad_maximum_fusion.3), channel_id=1, source_target_pairs={{0,16},{16,0},{1,17},{17,1},{2,18},{18,2},{3,19},{19,3},{4,20},{20... | collective-permute-start | bytes 3145736 | tf_op jit(solution)/shard_map/ppermute | solution.py:128
  195.1 13.0 %collective-permute-start.15 = (bf16[512,512]{1,0:T(8,128)(2,1)S(1)}, bf16[512,512]{1,0:T(8,128)(2,1)S(1)}, u32[]{:S(2)}, u32[]{:S(2)}) collective-permute-start(bf16[512,512]{1,0:T(8,128)(2,1)S(1)} %slice.126), channel_id=1, source_target_pairs={{0,16},{16,0},{1,17},{17,1},{2,18},{18,2},{3,19},{19,3},{4,20},{20... | collective-permute-start | bytes 1572872 | tf_op jit(solution)/shard_map/ppermute | solution.py:122

commit v16 on v12

--- a/solution.py
+++ b/solution.py
@@ -138,10 +138,13 @@
         parts = terms if parts is None else [a + b for a, b in zip(parts, terms)]
     if not own:
         return parts[0]
-    mine, other = parts[0][:, shared:], parts[1]
-    first = jnp.where(group_index == 0, mine, other)
-    second = jnp.where(group_index == 0, other, mine)
-    return jnp.concatenate([parts[0][:, :shared], first, second], axis=1)
+    full = jnp.concatenate([parts[0], parts[1]], axis=1)
+    return lax.dynamic_update_slice_in_dim(
+        lax.dynamic_update_slice_in_dim(full, parts[0][:, shared:], shared + group_index * own, 1),
+        parts[1],
+        shared + (1 - group_index) * own,
+        1,
+    )
 
 def per_device(queries, keys, values, doc_of_block, out_weight):
     tok_rows = queries.shape[0]

time: 213 us -> 213 us (level)
  no operation moved by 1% of the time
where the time goes in v16:
time: 213 us
  waiting for transfers between devices  77.5 us (36%)
  starting transfers between devices  66.5 us (31%)
  matrix products  31.7 us (15%)
  local copies, waits for them, and re-layouts  18 us (8%)
  between operations  9.59 us (5%)
  other arithmetic  9.11 us (4%)
    ppermute x3, starting transfers between devices, ring_transfer(): backward = lax.ppermute(backward, 'ctx', behind)  33.4 us
    ppermute x4, waiting for transfers between devices, ring_transfer(): forward = lax.ppermute(forward, 'ctx', ahead)  33.1 us
    ppermute x4, starting transfers between devices, passed_along(): return lax.ppermute(array, axis, pairs)  16.4 us
    ppermute x3, waiting for transfers between devices, ring_transfer(): backward = lax.ppermute(backward, 'ctx', behind)  15.9 us
    ppermute x4, waiting for transfers between devices, ring_transfer(): crossed = lax.ppermute(forward[:, shared:], 'group', swap) if own else None  14.9 us
    dot_general x8, matrix products, ring_project(): terms = [jnp.dot(piece, carried_block, preferred_element_type=jnp.float32)]  13.6 us
    ppermute x4, waiting for transfers between devices, passed_along(): return lax.ppermute(array, axis, pairs)  11.6 us
    ppermute x4, starting transfers between devices, ring_transfer(): forward = lax.ppermute(forward, 'ctx', ahead)  7.48 us
  transfers between devices with their start and end apart: 19, of which 12 were waited for; matrix products, arithmetic and copies ran while one was open for 24% of the time, Pallas kernels for 0%

profile of v16, /device:TPU:0, one launch (start us, length us, event | category | flops | bytes accessed | tf_op | source)
XLA Modules:
  0.0 212.5 jit_solution(17890278616102562635)
XLA Ops:
  0.0 1.1 copy.77
  1.1 1.1 copy.46
  3.0 6.7 %collective-permute-start.2 = (bf16[256,1024]{0,1:T(8,128)(2,1)}, bf16[256,1024]{0,1:T(8,128)(2,1)}, u32[]{:S(2)}, u32[]{:S(2)}) collective-permute-start(bf16[256,1024]{0,1:T(8,128)(2,1)} %pad_maximum_fusion.2), channel_id=1, source_target_pairs={{0,6},{2,8},{4,10},{6,12},{8,14},{1,7},{3,9},{5,11},{7,13},{9,15},... | collective-permute-start | bytes 1572872 | tf_op jit(solution)/shard_map/ppermute | solution.py:15
  9.7 4.3 %collective-permute-start.1 = (bf16[256,1024]{0,1:T(8,128)(2,1)}, bf16[256,1024]{0,1:T(8,128)(2,1)}, u32[]{:S(2)}, u32[]{:S(2)}) collective-permute-start(bf16[256,1024]{0,1:T(8,128)(2,1)} %pad_maximum_fusion.2), channel_id=1, source_target_pairs={{0,4},{2,6},{4,8},{6,10},{8,12},{10,14},{1,5},{3,7},{5,9},{7,11},{... | collective-permute-start | bytes 1572872 | tf_op jit(solution)/shard_map/ppermute | solution.py:15
  14.0 3.5 %collective-permute-start = (bf16[256,1024]{0,1:T(8,128)(2,1)}, bf16[256,1024]{0,1:T(8,128)(2,1)}, u32[]{:S(2)}, u32[]{:S(2)}) collective-permute-start(bf16[256,1024]{0,1:T(8,128)(2,1)} %pad_maximum_fusion.2), channel_id=1, source_target_pairs={{0,2},{2,4},{4,6},{6,8},{8,10},{10,12},{12,14},{1,3},{3,5},{5,7},{... | collective-permute-start | bytes 1572872 | tf_op jit(solution)/shard_map/ppermute | solution.py:15
  17.5 2.0 collective-permute-start.3
  19.5 1.3 slice.64
  20.8 1.1 constant_dynamic-slice_fusion
  21.9 1.3 pad_maximum_fusion.1
  23.3 1.8 reshape.293
  26.8 11.5 %collective-permute-done.3 = bf16[128,1024]{0,1:T(8,128)(2,1)} collective-permute-done((bf16[128,1024]{0,1:T(8,128)(2,1)S(1)}, bf16[128,1024]{0,1:T(8,128)(2,1)}, u32[]{:S(2)}, u32[]{:S(2)}) %collective-permute-start.3) | collective-permute-done | bytes 262176 | tf_op jit(solution)/shard_map/ppermute | solution.py:15
  38.3 11.7 %collective-permute-start.6 = (bf16[512,1536]{1,0:T(8,128)(2,1)}, bf16[512,1536]{1,0:T(8,128)(2,1)}, u32[]{:S(2)}, u32[]{:S(2)}) collective-permute-start(bf16[512,1536]{1,0:T(8,128)(2,1)} %pad_maximum_fusion.1), channel_id=1, source_target_pairs={{0,2},{4,0},{8,4},{12,8},{14,12},{10,14},{6,10},{2,6},{1,3},{5,1},... | collective-permute-start | bytes 4718600 | tf_op jit(solution)/shard_map/ppermute | solution.py:124
  51.6 1.1 fusion.142
  53.7 1.1 fusion.141
  55.8 1.1 fusion.140
  59.0 1.2 fusion.21
  61.2 1.2 fusion.19
  65.1 1.2 fusion.17
  66.3 1.4 fusion.15
  67.8 1.3 fusion.24
  69.2 1.8 collective-permute-done.5
  71.0 7.2 %collective-permute-start.7 = (bf16[512,1536]{1,0:T(8,128)(2,1)}, bf16[512,1536]{1,0:T(8,128)(2,1)}, u32[]{:S(2)}, u32[]{:S(2)}) collective-permute-start(bf16[512,1536]{1,0:T(8,128)(2,1)} %collective-permute-done.5), channel_id=1, source_target_pairs={{0,4},{4,8},{8,12},{12,14},{14,10},{10,6},{6,2},{2,0},{1,5},{5,9},... | collective-permute-start | bytes 4718600 | tf_op jit(solution)/shard_map/ppermute | solution.py:120
  78.2 4.9 %collective-permute-done.6 = bf16[512,1536]{1,0:T(8,128)(2,1)} collective-permute-done((bf16[512,1536]{1,0:T(8,128)(2,1)}, bf16[512,1536]{1,0:T(8,128)(2,1)}, u32[]{:S(2)}, u32[]{:S(2)}) %collective-permute-start.6) | collective-permute-done | bytes 1572896 | tf_op jit(solution)/shard_map/ppermute | solution.py:124
  83.1 19.3 %collective-permute-start.8 = (bf16[512,1536]{1,0:T(8,128)(2,1)}, bf16[512,1536]{1,0:T(8,128)(2,1)}, u32[]{:S(2)}, u32[]{:S(2)}) collective-permute-start(bf16[512,1536]{1,0:T(8,128)(2,1)} %collective-permute-done.6), channel_id=1, source_target_pairs={{0,2},{4,0},{8,4},{12,8},{14,12},{10,14},{6,10},{2,6},{1,3},{5,1},... | collective-permute-start | bytes 4718600 | tf_op jit(solution)/shard_map/ppermute | solution.py:124
  112.8 1.4 broadcast_select_fusion
  114.2 1.1 slice.83
  115.3 1.6 collective-permute-start.12
  116.9 1.1 slice.84
  118.5 4.3 %collective-permute-done.7 = bf16[512,1536]{1,0:T(8,128)(2,1)} collective-permute-done((bf16[512,1536]{1,0:T(8,128)(2,1)}, bf16[512,1536]{1,0:T(8,128)(2,1)}, u32[]{:S(2)}, u32[]{:S(2)}) %collective-permute-start.7) | collective-permute-done | bytes 1572896 | tf_op jit(solution)/shard_map/ppermute | solution.py:120
  122.8 2.4 %fusion.132 = f32[256,1536]{1,0:T(8,128)S(1)} fusion(bf16[512,1536]{1,0:T(8,128)(2,1)} %collective-permute-done.5, s32[]{:T(128)S(6)} %select_n.231, bf16[256,2048]{0,1:T(8,128)(2,1)S(1)} %get-tuple-element.18, bf16[256,2048]{0,1:T(8,128)(2,1)S(1)} %get-tuple-element.17), kind=kOutput, calls=%fused_computation.214 | convolution fusion | flops 403177472 | bytes 5242884 | tf_op jit(solution)/shard_map/dot_general | solution.py:135
  125.2 2.4 %fusion.128 = f32[256,1536]{1,0:T(8,128)S(1)} fusion(bf16[512,1536]{1,0:T(8,128)(2,1)} %collective-permute-done.6, s32[]{:T(128)S(6)} %select_n.234, bf16[256,2048]{0,1:T(8,128)(2,1)S(1)} %get-tuple-element.18, bf16[256,2048]{0,1:T(8,128)(2,1)S(1)} %get-tuple-element.17), kind=kOutput, calls=%fused_computation.212 | convolution fusion | flops 403177472 | bytes 5242884 | tf_op jit(solution)/shard_map/dot_general | solution.py:135
  128.6 7.1 %collective-permute-done.8 = bf16[512,1536]{1,0:T(8,128)(2,1)} collective-permute-done((bf16[512,1536]{1,0:T(8,128)(2,1)}, bf16[512,1536]{1,0:T(8,128)(2,1)}, u32[]{:S(2)}, u32[]{:S(2)}) %collective-permute-start.8) | collective-permute-done | bytes 1572896 | tf_op jit(solution)/shard_map/ppermute | solution.py:124
  135.7 2.5 %collective-permute-start.10 = (bf16[512,1536]{1,0:T(8,128)(2,1)}, bf16[512,1536]{1,0:T(8,128)(2,1)S(1)}, u32[]{:S(2)}, u32[]{:S(2)}) collective-permute-start(bf16[512,1536]{1,0:T(8,128)(2,1)} %collective-permute-done.8), channel_id=1, source_target_pairs={{0,2},{4,0},{8,4},{12,8},{14,12},{10,14},{6,10},{2,6},{1,3},{5,1},... | collective-permute-start | bytes 4718600 | tf_op jit(solution)/shard_map/ppermute | solution.py:124
  140.1 1.1 slice.85
  141.1 1.6 collective-permute-start.14
  142.7 1.1 slice.86
  144.4 2.4 %fusion.121 = f32[256,1536]{1,0:T(8,128)S(1)} fusion(bf16[512,1536]{1,0:T(8,128)(2,1)} %collective-permute-done.8, s32[]{:T(128)S(6)} %select_n.240, bf16[256,2048]{0,1:T(8,128)(2,1)S(1)} %get-tuple-element.18, bf16[256,2048]{0,1:T(8,128)(2,1)S(1)} %get-tuple-element.17), kind=kOutput, calls=%fused_computation.209 | convolution fusion | flops 403177472 | bytes 5242884 | tf_op jit(solution)/shard_map/dot_general | solution.py:135
  146.8 12.4 %collective-permute-done.9 = bf16[512,1536]{1,0:T(8,128)(2,1)S(1)} collective-permute-done((bf16[512,1536]{1,0:T(8,128)(2,1)}, bf16[512,1536]{1,0:T(8,128)(2,1)S(1)}, u32[]{:S(2)}, u32[]{:S(2)}) %collective-permute-start.9) | collective-permute-done | bytes 1572896 | tf_op jit(solution)/shard_map/ppermute | solution.py:120
  159.5 2.4 %fusion.13 = f32[256,1536]{1,0:T(8,128)S(1)} fusion(f32[256,1536]{1,0:T(8,128)S(1)} %fusion.121, f32[256,1536]{1,0:T(8,128)S(1)} %fusion.14, bf16[512,1536]{1,0:T(8,128)(2,1)} %collective-permute-done.7, s32[]{:T(128)S(6)} %select_n.237, bf16[256,2048]{0,1:T(8,128)(2,1)S(1)} %get-tuple-element.18, bf16[256,2048]{0,1:T(8,128)(2,1)S(1)} %get-tuple-element.17), kind=kOutput, calls=%fused_computation.40 | convolution fusion | flops 403963904 | bytes 8388612 | tf_op jit(solution)/shard_map/dot_general | solution.py:135
  162.6 1.7 collective-permute-done.15
  165.1 1.6 collective-permute-start.16
  166.7 3.9 %collective-permute-done.10 = bf16[512,1536]{1,0:T(8,128)(2,1)S(1)} collective-permute-done((bf16[512,1536]{1,0:T(8,128)(2,1)}, bf16[512,1536]{1,0:T(8,128)(2,1)S(1)}, u32[]{:S(2)}, u32[]{:S(2)}) %collective-permute-start.10) | collective-permute-done | bytes 1572896 | tf_op jit(solution)/shard_map/ppermute | solution.py:124
  170.7 1.6 collective-permute-start.17
  174.3 5.7 %collective-permute-done.16 = bf16[512,512]{1,0:T(8,128)(2,1)S(1)} collective-permute-done((bf16[512,512]{1,0:T(8,128)(2,1)S(1)}, bf16[512,512]{1,0:T(8,128)(2,1)S(1)}, u32[]{:S(2)}, u32[]{:S(2)}) %collective-permute-start.16) | collective-permute-done | bytes 524320 | tf_op jit(solution)/shard_map/ppermute | solution.py:121
  180.7 14.6 %collective-permute-done.11 = bf16[512,1536]{1,0:T(8,128)(2,1)S(1)} collective-permute-done((bf16[512,1536]{1,0:T(8,128)(2,1)S(1)}, bf16[512,1536]{1,0:T(8,128)(2,1)S(1)}, u32[]{:S(2)}, u32[]{:S(2)}) %collective-permute-start.11) | collective-permute-done | bytes 1572896 | tf_op jit(solution)/shard_map/ppermute | solution.py:120
  195.4 1.6 collective-permute-start.18
  198.7 9.3 %collective-permute-done.18 = bf16[512,512]{1,0:T(8,128)(2,1)S(1)} collective-permute-done((bf16[512,512]{1,0:T(8,128)(2,1)S(1)}, bf16[512,512]{1,0:T(8,128)(2,1)S(1)}, u32[]{:S(2)}, u32[]{:S(2)}) %collective-permute-start.18) | collective-permute-done | bytes 524320 | tf_op jit(solution)/shard_map/ppermute | solution.py:121
  208.7 1.9 fusion.57
  (70 shorter events, 26.4 us)
Async XLA Ops:
  3.0 48.6 %collective-permute-start.2 = (bf16[256,1024]{0,1:T(8,128)(2,1)}, bf16[256,1024]{0,1:T(8,128)(2,1)}, u32[]{:S(2)}, u32[]{:S(2)}) collective-permute-start(bf16[256,1024]{0,1:T(8,128)(2,1)} %pad_maximum_fusion.2), channel_id=1, source_target_pairs={{0,6},{2,8},{4,10},{6,12},{8,14},{1,7},{3,9},{5,11},{7,13},{9,15},... | collective-permute-start | bytes 1572872 | tf_op jit(solution)/shard_map/ppermute | solution.py:15
  9.7 44.0 %collective-permute-start.1 = (bf16[256,1024]{0,1:T(8,128)(2,1)}, bf16[256,1024]{0,1:T(8,128)(2,1)}, u32[]{:S(2)}, u32[]{:S(2)}) collective-permute-start(bf16[256,1024]{0,1:T(8,128)(2,1)} %pad_maximum_fusion.2), channel_id=1, source_target_pairs={{0,4},{2,6},{4,8},{6,10},{8,12},{10,14},{1,5},{3,7},{5,9},{7,11},{... | collective-permute-start | bytes 1572872 | tf_op jit(solution)/shard_map/ppermute | solution.py:15
  14.0 41.8 %collective-permute-start = (bf16[256,1024]{0,1:T(8,128)(2,1)}, bf16[256,1024]{0,1:T(8,128)(2,1)}, u32[]{:S(2)}, u32[]{:S(2)}) collective-permute-start(bf16[256,1024]{0,1:T(8,128)(2,1)} %pad_maximum_fusion.2), channel_id=1, source_target_pairs={{0,2},{2,4},{4,6},{6,8},{8,10},{10,12},{12,14},{1,3},{3,5},{5,7},{... | collective-permute-start | bytes 1572872 | tf_op jit(solution)/shard_map/ppermute | solution.py:15
  17.5 20.9 %collective-permute-start.3 = (bf16[128,1024]{0,1:T(8,128)(2,1)S(1)}, bf16[128,1024]{0,1:T(8,128)(2,1)}, u32[]{:S(2)}, u32[]{:S(2)}) collective-permute-start(bf16[128,1024]{0,1:T(8,128)(2,1)S(1)} %fusion.83), channel_id=1, source_target_pairs={{0,8},{2,10},{4,12},{6,14},{1,9},{3,11},{5,13},{7,15},{16,24},{18,... | collective-permute-start | bytes 786440 | tf_op jit(solution)/shard_map/ppermute | solution.py:15
  20.8 2.5 %copy-start.1 = (bf16[256,512]{1,0:T(8,128)(2,1)S(1)}, bf16[256,512]{1,0:T(8,128)(2,1)}, u32[]{:S(2)}) copy-start(bf16[256,512]{1,0:T(8,128)(2,1)} %param.8) | copy-start | bytes 786436
  23.2 2.0 copy-start.3
  23.2 47.8 %collective-permute-start.5 = (bf16[512,1536]{1,0:T(8,128)(2,1)}, bf16[512,1536]{1,0:T(8,128)(2,1)}, u32[]{:S(2)}, u32[]{:S(2)}) collective-permute-start(bf16[512,1536]{1,0:T(8,128)(2,1)} %pad_maximum_fusion.1), channel_id=1, source_target_pairs={{0,4},{4,8},{8,12},{12,14},{14,10},{10,6},{6,2},{2,0},{1,5},{5,9},... | collective-permute-start | bytes 4718600 | tf_op jit(solution)/shard_map/ppermute | solution.py:120
  38.3 44.8 %collective-permute-start.6 = (bf16[512,1536]{1,0:T(8,128)(2,1)}, bf16[512,1536]{1,0:T(8,128)(2,1)}, u32[]{:S(2)}, u32[]{:S(2)}) collective-permute-start(bf16[512,1536]{1,0:T(8,128)(2,1)} %pad_maximum_fusion.1), channel_id=1, source_target_pairs={{0,2},{4,0},{8,4},{12,8},{14,12},{10,14},{6,10},{2,6},{1,3},{5,1},... | collective-permute-start | bytes 4718600 | tf_op jit(solution)/shard_map/ppermute | solution.py:124
  67.8 34.7 %copy-start.4 = (s32[8]{0:T(128)S(1)}, s32[8]{0:T(128)}, u32[]{:S(2)}) copy-start(s32[8]{0:T(128)} %constant.185.clone) | copy-start | bytes 100
  67.8 39.9 %copy-start.2 = (s32[8]{0:T(128)S(1)}, s32[8]{0:T(128)}, u32[]{:S(2)}) copy-start(s32[8]{0:T(128)} %constant.186.clone) | copy-start | bytes 100
  69.1 43.8 %collective-permute-start.4 = (bf16[256,2048]{0,1:T(8,128)(2,1)S(1)}, bf16[256,2048]{0,1:T(8,128)(2,1)}, u32[]{:S(2)}, u32[]{:S(2)}) collective-permute-start(bf16[256,2048]{0,1:T(8,128)(2,1)S(1)} %bitcast.268), channel_id=1, source_target_pairs={{0,1},{1,0},{2,3},{3,2},{4,5},{5,4},{6,7},{7,6},{8,9},{9,8},{10,11... | collective-permute-start | bytes 3145736 | tf_op jit(solution)/shard_map/ppermute | solution.py:77
  71.0 51.8 %collective-permute-start.7 = (bf16[512,1536]{1,0:T(8,128)(2,1)}, bf16[512,1536]{1,0:T(8,128)(2,1)}, u32[]{:S(2)}, u32[]{:S(2)}) collective-permute-start(bf16[512,1536]{1,0:T(8,128)(2,1)} %collective-permute-done.5), channel_id=1, source_target_pairs={{0,4},{4,8},{8,12},{12,14},{14,10},{10,6},{6,2},{2,0},{1,5},{5,9},... | collective-permute-start | bytes 4718600 | tf_op jit(solution)/shard_map/ppermute | solution.py:120
  83.1 52.6 %collective-permute-start.8 = (bf16[512,1536]{1,0:T(8,128)(2,1)}, bf16[512,1536]{1,0:T(8,128)(2,1)}, u32[]{:S(2)}, u32[]{:S(2)}) collective-permute-start(bf16[512,1536]{1,0:T(8,128)(2,1)} %collective-permute-done.6), channel_id=1, source_target_pairs={{0,2},{4,0},{8,4},{12,8},{14,12},{10,14},{6,10},{2,6},{1,3},{5,1},... | collective-permute-start | bytes 4718600 | tf_op jit(solution)/shard_map/ppermute | solution.py:124
  115.3 22.9 %collective-permute-start.12 = (bf16[512,512]{1,0:T(8,128)(2,1)S(1)}, bf16[512,512]{1,0:T(8,128)(2,1)S(1)}, u32[]{:S(2)}, u32[]{:S(2)}) collective-permute-start(bf16[512,512]{1,0:T(8,128)(2,1)S(1)} %slice.83), channel_id=1, source_target_pairs={{0,16},{16,0},{1,17},{17,1},{2,18},{18,2},{3,19},{19,3},{4,20},{20... | collective-permute-start | bytes 1572872 | tf_op jit(solution)/shard_map/ppermute | solution.py:121
  118.0 21.3 %collective-permute-start.13 = (bf16[512,512]{1,0:T(8,128)(2,1)S(1)}, bf16[512,512]{1,0:T(8,128)(2,1)S(1)}, u32[]{:S(2)}, u32[]{:S(2)}) collective-permute-start(bf16[512,512]{1,0:T(8,128)(2,1)S(1)} %slice.84), channel_id=1, source_target_pairs={{0,16},{16,0},{1,17},{17,1},{2,18},{18,2},{3,19},{19,3},{4,20},{20... | collective-permute-start | bytes 1572872 | tf_op jit(solution)/shard_map/ppermute | solution.py:125
  122.8 36.4 %collective-permute-start.9 = (bf16[512,1536]{1,0:T(8,128)(2,1)}, bf16[512,1536]{1,0:T(8,128)(2,1)S(1)}, u32[]{:S(2)}, u32[]{:S(2)}) collective-permute-start(bf16[512,1536]{1,0:T(8,128)(2,1)} %collective-permute-done.7), channel_id=1, source_target_pairs={{0,4},{4,8},{8,12},{12,14},{14,10},{10,6},{6,2},{2,0},{1,5},{5,9},... | collective-permute-start | bytes 4718600 | tf_op jit(solution)/shard_map/ppermute | solution.py:120
  135.7 34.9 %collective-permute-start.10 = (bf16[512,1536]{1,0:T(8,128)(2,1)}, bf16[512,1536]{1,0:T(8,128)(2,1)S(1)}, u32[]{:S(2)}, u32[]{:S(2)}) collective-permute-start(bf16[512,1536]{1,0:T(8,128)(2,1)} %collective-permute-done.8), channel_id=1, source_target_pairs={{0,2},{4,0},{8,4},{12,8},{14,12},{10,14},{6,10},{2,6},{1,3},{5,1},... | collective-permute-start | bytes 4718600 | tf_op jit(solution)/shard_map/ppermute | solution.py:124
  141.1 20.7 %collective-permute-start.14 = (bf16[512,512]{1,0:T(8,128)(2,1)S(1)}, bf16[512,512]{1,0:T(8,128)(2,1)S(1)}, u32[]{:S(2)}, u32[]{:S(2)}) collective-permute-start(bf16[512,512]{1,0:T(8,128)(2,1)S(1)} %slice.85), channel_id=1, source_target_pairs={{0,16},{16,0},{1,17},{17,1},{2,18},{18,2},{3,19},{19,3},{4,20},{20... | collective-permute-start | bytes 1572872 | tf_op jit(solution)/shard_map/ppermute | solution.py:121
  143.8 20.5 %collective-permute-start.15 = (bf16[512,512]{1,0:T(8,128)(2,1)S(1)}, bf16[512,512]{1,0:T(8,128)(2,1)S(1)}, u32[]{:S(2)}, u32[]{:S(2)}) collective-permute-start(bf16[512,512]{1,0:T(8,128)(2,1)S(1)} %slice.86), channel_id=1, source_target_pairs={{0,16},{16,0},{1,17},{17,1},{2,18},{18,2},{3,19},{19,3},{4,20},{20... | collective-permute-start | bytes 1572872 | tf_op jit(solution)/shard_map/ppermute | solution.py:125
  159.2 36.1 %collective-permute-start.11 = (bf16[512,1536]{1,0:T(8,128)(2,1)S(1)}, bf16[512,1536]{1,0:T(8,128)(2,1)S(1)}, u32[]{:S(2)}, u32[]{:S(2)}) collective-permute-start(bf16[512,1536]{1,0:T(8,128)(2,1)S(1)} %collective-permute-done.9), channel_id=1, source_target_pairs={{0,4},{4,8},{8,12},{12,14},{14,10},{10,6},{6,2},{2,0},{1,5},{5,9},... | collective-permute-start | bytes 4718600 | tf_op jit(solution)/shard_map/ppermute | solution.py:120
  165.1 14.9 %collective-permute-start.16 = (bf16[512,512]{1,0:T(8,128)(2,1)S(1)}, bf16[512,512]{1,0:T(8,128)(2,1)S(1)}, u32[]{:S(2)}, u32[]{:S(2)}) collective-permute-start(bf16[512,512]{1,0:T(8,128)(2,1)S(1)} %slice.87), channel_id=1, source_target_pairs={{0,16},{16,0},{1,17},{17,1},{2,18},{18,2},{3,19},{19,3},{4,20},{20... | collective-permute-start | bytes 1572872 | tf_op jit(solution)/shard_map/ppermute | solution.py:121
  170.7 26.3 %collective-permute-start.17 = (bf16[512,512]{1,0:T(8,128)(2,1)S(1)}, bf16[512,512]{1,0:T(8,128)(2,1)S(1)}, u32[]{:S(2)}, u32[]{:S(2)}) collective-permute-start(bf16[512,512]{1,0:T(8,128)(2,1)S(1)} %slice.88), channel_id=1, source_target_pairs={{0,16},{16,0},{1,17},{17,1},{2,18},{18,2},{3,19},{19,3},{4,20},{20... | collective-permute-start | bytes 1572872 | tf_op jit(solution)/shard_map/ppermute | solution.py:125
  195.4 12.6 %collective-permute-start.18 = (bf16[512,512]{1,0:T(8,128)(2,1)S(1)}, bf16[512,512]{1,0:T(8,128)(2,1)S(1)}, u32[]{:S(2)}, u32[]{:S(2)}) collective-permute-start(bf16[512,512]{1,0:T(8,128)(2,1)S(1)} %slice.89), channel_id=1, source_target_pairs={{0,16},{16,0},{1,17},{17,1},{2,18},{18,2},{3,19},{19,3},{4,20},{20... | collective-permute-start | bytes 1572872 | tf_op jit(solution)/shard_map/ppermute | solution.py:121
  210.8 1.0 copy-start
